TPU v7x, 128 devices: a whole 4x4x4 slice. The times are simulated.
128 devices in a mesh: pairs: 8 (over x, core), win: 16 (over z, y).
Axes of the slice: x: 4, y: 4, z: 4, core: 2. Of those that a mesh axis runs over, the one named last changes fastest.
Arguments:
- records: bfloat16 [8, 96, 128, 4096], P('pairs', 'win'), may hold values from -6 to 6
- pair_list: int32 [8, 2, 2], replicated, may hold values from 0 to 7, as said below
- pair_count: int32 [8], replicated, may hold values from 1 to 2, as said below
Outputs:
- correlations: bfloat16 [8, 2, 128, 128, 128], P('pairs', None, 'win')
Inputs may be any that keep to these rules, and one draw needn't show every extreme that they name: `pair_list`: the 4 block numbers in one owner's row are all distinct. `pair_count`: slots at or beyond an owner's count are unused and their correlations are zero; some owner has exactly 2 live slots and another exactly 1.
All inputs are finite; a program needn't handle non-finite values.
Results may differ from a plain program's by a relative error of at most 0.019.
Values may be sent and summed in bfloat16 or wider, within the bound.
No kernel may reach another device: no remote copies, remote signals or barrier semaphores. Data moves between devices by JAX's collectives and lax.ppermute only.
A program may use at most 128 MiB of HBM per device.

v0:
```python
import math

import jax
import jax.numpy as jnp
from jax import lax
from jax.sharding import PartitionSpec as P

NSAMP = 4096
FREQS = 32
LOW_BIN = 16
LAGS = 128


WATER = 0.1


def band_table():
    sample_idx = jnp.arange(NSAMP, dtype=jnp.int32)
    bin_idx = jnp.arange(FREQS, dtype=jnp.int32) + LOW_BIN
    phase = (sample_idx[:, None] * bin_idx[None, :] % NSAMP).astype(jnp.float32) * (
        2.0 * math.pi / NSAMP
    )
    scaled = jnp.concatenate([jnp.cos(phase), -jnp.sin(phase)], axis=1) * (1.0 / math.sqrt(NSAMP))
    return scaled.astype(jnp.bfloat16)


def lag_table(segments):
    bin_idx = jnp.arange(FREQS, dtype=jnp.int32) + LOW_BIN
    lag_idx = (jnp.arange(LAGS, dtype=jnp.int32) - LAGS // 2) * (NSAMP // LAGS)
    phase = (bin_idx[:, None] * lag_idx[None, :] % NSAMP).astype(jnp.float32) * (
        2.0 * math.pi / NSAMP
    )
    return jnp.concatenate([jnp.cos(phase), -jnp.sin(phase)], axis=0) * (
        1.0 / math.sqrt(segments * FREQS)
    )


def whiten(spectra):
    real_part = spectra[..., :FREQS]
    imag_part = spectra[..., FREQS:]
    power_bins = real_part * real_part + imag_part * imag_part
    widths = [(0, 0)] * (power_bins.ndim - 1) + [(2, 2)]
    padded = jnp.pad(power_bins, widths)
    smooth = (
        padded[..., 0:FREQS]
        + padded[..., 1 : FREQS + 1]
        + padded[..., 2 : FREQS + 2]
        + padded[..., 3 : FREQS + 3]
        + padded[..., 4 : FREQS + 4]
    ) * 0.2
    water_level = smooth + WATER * jnp.mean(power_bins, axis=-1, keepdims=True) + 1e-06
    factor = lax.rsqrt(water_level)
    return jnp.concatenate([real_part * factor, imag_part * factor], axis=-1).astype(jnp.bfloat16)


def pair_cross(left_spec, right_spec, einsum_form):
    left_real = left_spec[..., :FREQS]
    left_imag = left_spec[..., FREQS:]
    right_real = right_spec[..., :FREQS]
    right_imag = right_spec[..., FREQS:]
    real_sum = jnp.einsum(
        einsum_form, left_real, right_real, preferred_element_type=jnp.float32
    ) + jnp.einsum(einsum_form, left_imag, right_imag, preferred_element_type=jnp.float32)
    imag_sum = jnp.einsum(
        einsum_form, left_real, right_imag, preferred_element_type=jnp.float32
    ) - jnp.einsum(einsum_form, left_imag, right_real, preferred_element_type=jnp.float32)
    return jnp.concatenate([real_sum, imag_sum], axis=-1)


def shards(records, pair_list, pair_count):
    seg_dev = records.shape[1]
    block_width = records.shape[2]
    freq_width = 2 * FREQS
    slot_count = pair_list.shape[1]
    spectra = whiten(jnp.dot(records[0], band_table(), preferred_element_type=jnp.float32))
    owner_index = lax.axis_index("pairs")
    live_slots = jnp.arange(slot_count, dtype=jnp.int32)[None, :] < pair_count[:, None]
    wanted = jnp.any((pair_list == owner_index) & live_slots[:, :, None], axis=(1, 2))
    flat_spec = spectra.reshape(seg_dev, block_width * freq_width)
    outgoing = jnp.where(wanted[:, None, None], flat_spec[None], jnp.zeros((), jnp.bfloat16))
    incoming = lax.all_to_all(outgoing, "pairs", split_axis=0, concat_axis=0, tiled=True)
    own_pairs = lax.dynamic_index_in_dim(pair_list, owner_index, 0, keepdims=False)
    own_live = lax.dynamic_index_in_dim(live_slots, owner_index, 0, keepdims=False)
    chosen = jnp.take(incoming, own_pairs.reshape(-1), axis=0)
    win_count = lax.axis_size("win")
    lag_weights = lag_table(seg_dev * win_count)
    local_block = chosen.reshape(slot_count, 2, seg_dev, block_width, freq_width)
    left_spec = local_block[:, 0]
    stacked = lax.psum_scatter(
        pair_cross(left_spec, local_block[:, 1], "psif,psjf->ipjf").astype(jnp.bfloat16),
        "win",
        scatter_dimension=0,
        tiled=True,
    ).astype(jnp.float32)
    lag_form = "ipjq,qt->pijt"
    correlation = jnp.einsum(
        lag_form,
        stacked,
        lag_weights,
        precision=lax.Precision.HIGHEST,
        preferred_element_type=jnp.float32,
    )
    masked = correlation * own_live.astype(jnp.float32)[:, None, None, None]
    return masked.astype(jnp.bfloat16)[None]


def solution(mesh):
    in_specs = (P("pairs", "win", None, None), P(), P())
    out_specs = P("pairs", None, "win", None, None)
    return jax.shard_map(shards, mesh=mesh, in_specs=in_specs, out_specs=out_specs, check_vma=False)
```

profile of v0, /device:TPU:0, one launch (start us, length us, event | category | flops | bytes accessed | tf_op | source)
XLA Modules:
  0.0 137.9 jit_solution(14604570088383224623)
XLA Ops:
  6.5 2.1 %fusion.19 = (f32[4096,32]{0,1:T(8,128)S(1)}, f32[4096,32]{0,1:T(8,128)S(1)}) fusion(s32[32]{0:T(128)S(1)} %iota_add_fusion), kind=kLoop, calls=%fused_computation.30 | loop fusion | flops 1966080 | bytes 1048704 | tf_op jit(solution)/shard_map/cos | solution.py:23
  8.7 0.0 copy-start.1
  8.7 0.0 copy-start
  8.7 4.8 %fusion.6 = f32[6,128,64]{1,2,0:T(8,128)S(1)} fusion(bf16[1,6,128,4096]{3,2,1,0:T(8,128)(2,1)} %param.3, f32[4096,32]{0,1:T(8,128)S(1)} %get-tuple-element.12, f32[4096,32]{0,1:T(8,128)S(1)} %get-tuple-element.11), kind=kOutput, calls=%fused_computation.11 | convolution fusion | flops 403439616 | bytes 7536640 | tf_op jit(solution)/shard_map/dot_general | solution.py:75
  13.6 0.1 multiply_convert_fusion.1
  13.7 0.2 copy.18
  13.9 0.2 convert_element_type.44
  14.1 0.0 copy-done.1
  14.1 0.1 iota_compare_fusion
  14.1 0.1 copy.17
  14.2 0.0 copy-done
  14.3 1.1 broadcast_select_fusion
  15.4 4.4 %all-to-all-start = ((bf16[8,6,8192]{2,1,0:T(8,128)(2,1)}), bf16[8,6,8192]{2,1,0:T(8,128)(2,1)S(1)}, u32[]{:S(2)}, u32[]{:S(2)}) async-start(bf16[8,6,8192]{2,1,0:T(8,128)(2,1)} %broadcast_select_fusion), calls=%async_computation | async-start | bytes 2097152 | tf_op jit(solution)/shard_map/all_to_all | solution.py:81
  19.8 0.0 reduce-scatter.2.cloned.1.call-start
  19.8 0.2 dynamic-slice_reduce_fusion
  20.1 0.1 reshape.97
  20.1 0.1 copy.16
  20.3 15.5 %all-to-all-done = bf16[8,6,8192]{2,1,0:T(8,128)(2,1)S(1)} async-done(((bf16[8,6,8192]{2,1,0:T(8,128)(2,1)}), bf16[8,6,8192]{2,1,0:T(8,128)(2,1)S(1)}, u32[]{:S(2)}, u32[]{:S(2)}) %all-to-all-start) | async-done | bytes 786464 | tf_op jit(solution)/shard_map/all_to_all | solution.py:81
  35.8 0.6 gather_fusion
  36.3 0.8 reshape.109
  37.2 0.4 copy.20
  37.6 0.1 broadcast_select_fusion.1
  37.8 0.8 fusion.20
  38.6 0.8 fusion.21
  39.4 0.8 fusion.2
  40.2 0.8 fusion.3
  41.0 2.3 %pad_maximum_fusion = bf16[128,2,128,64]{0,2,3,1:T(8,128)(2,1)} fusion(bf16[128,2,128,32]{0,2,3,1:T(8,128)(2,1)S(1)} %fusion.3, bf16[128,2,128,32]{0,2,3,1:T(8,128)(2,1)S(1)} %fusion.2), kind=kLoop, calls=%fused_computation.3 | loop fusion | flops 2097152 | bytes 8388608 | tf_op jit(solution)/shard_map/concatenate | solution.py:67
  43.3 6.6 %copy.21 = bf16[128,2,128,64]{2,3,1,0:T(8,128)(2,1)} copy(bf16[128,2,128,64]{0,2,3,1:T(8,128)(2,1)} %pad_maximum_fusion) | data formatting | bytes 8388608 | tf_op jit(solution)/shard_map/concatenate | solution.py:67
  49.9 0.0 reduce-scatter.2.cloned.1.call-update
  50.0 0.2 fusion.42
  50.1 78.3 %reduce-scatter.2.cloned.1.call-done = bf16[8,2,128,64]{2,3,1,0:T(8,128)(2,1)} async-done(((bf16[128,2,128,64]{2,3,1,0:T(8,128)(2,1)}), bf16[8,2,128,64]{2,3,1,0:T(8,128)(2,1)}) %reduce-scatter.2.cloned.1.call-update) | async-done | bytes 262160 | tf_op jit(solution)/shard_map/reduce_scatter | solution.py:89
  128.4 1.6 %fusion.5 = bf16[1,2,8,128,128]{3,4,1,2,0:T(8,128)(2,1)S(1)} fusion(bf16[8,2,128,64]{2,3,1,0:T(8,128)(2,1)} %reduce-scatter.2.cloned.1.call-done, f32[2]{0:T(128)S(1)} %fusion.43, f32[32,128]{1,0:T(8,128)S(1)} %get-tuple-element.10, f32[32,128]{1,0:T(8,128)S(1)} %get-tuple-element.9), kind=kOutput, calls=%fused_computation.10 | convolution fusion | flops 201867264 | bytes 819208 | tf_op jit(solution)/shard_map/ipjq,qt->pijt/dot_general | solution.py:96
  130.0 1.0 copy.22
  (16 shorter events, 0.2 us)
Async XLA Ops:
  8.7 5.4 %copy-start.1 = (s32[8]{0:T(128)S(1)}, s32[8]{0:T(128)}, u32[]{:S(2)}) copy-start(s32[8]{0:T(128)} %param.5) | copy-start | bytes 100
  8.7 5.6 %copy-start = (s32[8,2,2]{0,2,1:T(2,128)S(1)}, s32[8,2,2]{0,2,1:T(2,128)}, u32[]{:S(2)}) copy-start(s32[8,2,2]{0,2,1:T(2,128)} %param.4) | copy-start | bytes 388
  15.4 20.4 %all-to-all-start = ((bf16[8,6,8192]{2,1,0:T(8,128)(2,1)}), bf16[8,6,8192]{2,1,0:T(8,128)(2,1)S(1)}, u32[]{:S(2)}, u32[]{:S(2)}) async-start(bf16[8,6,8192]{2,1,0:T(8,128)(2,1)} %broadcast_select_fusion), calls=%async_computation | async-start | bytes 2097152 | tf_op jit(solution)/shard_map/all_to_all | solution.py:81
  19.8 108.6 %reduce-scatter.2.cloned.1.call-start = ((), (), s32[]{:S(2)}) async-start(), calls=%async_computation.2 | async-start | bytes 4456448 | tf_op jit(solution)/shard_map/reduce_scatter | solution.py:89
Sparse Core Ops, SparseCore 0:
  50.1 78.3 reduce-scatter.1
where the time goes:
time: 138 us
  waiting for transfers between devices  93.8 us (68%)
  between operations  13.6 us (10%)
  local copies, waits for them, and re-layouts  10.4 us (8%)
  matrix products  9.54 us (7%)
  other arithmetic  6.14 us (4%)
  starting transfers between devices  4.42 us (3%)
    reduce_scatter x1, waiting for transfers between devices, shards(): lax.psum_scatter(pair_cross(left_spec, local_block[:, 1], 'psif,psjf->ipj...  78.3 us
    all_to_all x1, waiting for transfers between devices, shards(): lax.all_to_all(outgoing, 'pairs', split_axis=0, concat_axis=0, tiled=True)  15.5 us
    concatenate x1, local copies, waits for them, and re-layouts, pair_cross(): return jnp.concatenate([real_sum, imag_sum], axis=-1)  6.58 us
    dot_general x1, matrix products, shards(): jnp.dot(records[0], band_table(), preferred_element_type=jnp.float32)  4.83 us
    all_to_all x1, starting transfers between devices, shards(): lax.all_to_all(outgoing, 'pairs', split_axis=0, concat_axis=0, tiled=True)  4.39 us
  transfers between devices with their start and end apart: 2, of which 2 were waited for; matrix products, arithmetic and copies ran while one was open for 0% of the time, Pallas kernels for 0%

commit v1 on v0

v1 whole, which is shorter than its diff:
```python
import math

import jax
import jax.numpy as jnp
import ml_dtypes
import numpy as np
from jax import lax
from jax.sharding import Mesh
from jax.sharding import PartitionSpec as P

NSAMP = 4096
FREQS = 32
LOW_BIN = 16
LAGS = 128


WATER = 0.1


def band_table():
    sample_idx = np.arange(NSAMP, dtype=np.int64)
    bin_idx = np.arange(FREQS, dtype=np.int64) + LOW_BIN
    phase = (sample_idx[:, None] * bin_idx[None, :] % NSAMP).astype(np.float64) * (
        2.0 * math.pi / NSAMP
    )
    scaled = np.concatenate([np.cos(phase), -np.sin(phase)], axis=1) * (1.0 / math.sqrt(NSAMP))
    return jnp.asarray(scaled.astype(ml_dtypes.bfloat16))


def lag_table(segments):
    bin_idx = jnp.arange(FREQS, dtype=jnp.int32) + LOW_BIN
    lag_idx = (jnp.arange(LAGS, dtype=jnp.int32) - LAGS // 2) * (NSAMP // LAGS)
    phase = (bin_idx[:, None] * lag_idx[None, :] % NSAMP).astype(jnp.float32) * (
        2.0 * math.pi / NSAMP
    )
    return jnp.concatenate([jnp.cos(phase), -jnp.sin(phase)], axis=0) * (
        1.0 / math.sqrt(segments * FREQS)
    )


def whiten(spectra):
    real_part = spectra[..., :FREQS]
    imag_part = spectra[..., FREQS:]
    power_bins = real_part * real_part + imag_part * imag_part
    widths = [(0, 0)] * (power_bins.ndim - 1) + [(2, 2)]
    padded = jnp.pad(power_bins, widths)
    smooth = (
        padded[..., 0:FREQS]
        + padded[..., 1 : FREQS + 1]
        + padded[..., 2 : FREQS + 2]
        + padded[..., 3 : FREQS + 3]
        + padded[..., 4 : FREQS + 4]
    ) * 0.2
    water_level = smooth + WATER * jnp.mean(power_bins, axis=-1, keepdims=True) + 1e-06
    factor = lax.rsqrt(water_level)
    return jnp.concatenate([real_part * factor, imag_part * factor], axis=-1).astype(jnp.bfloat16)


def shards(records, pair_list, pair_count):
    seg_dev = records.shape[1]
    block_width = records.shape[2]
    slot_count = pair_list.shape[1]
    z_count = lax.axis_size("z")
    y_count = lax.axis_size("y")
    rows = block_width // (z_count * y_count)
    spectra = whiten(jnp.dot(records[0], band_table(), preferred_element_type=jnp.float32))
    owner_index = lax.axis_index("pairs")
    y_index = lax.axis_index("y")
    every_block = lax.all_gather(spectra, "pairs", axis=0, tiled=False)
    own_pairs = lax.dynamic_index_in_dim(pair_list, owner_index, 0, keepdims=False)
    live_slots = jnp.arange(slot_count, dtype=jnp.int32) < pair_count[owner_index]
    left = jnp.take(every_block, own_pairs[:, 0], axis=0)
    right = jnp.take(every_block, own_pairs[:, 1], axis=0)
    right_all = lax.all_gather(right, "y", axis=0, tiled=False)
    left_rows = left.reshape(slot_count, seg_dev, z_count, y_count, rows, 2 * FREQS)
    left_send = jnp.transpose(left_rows, (3, 0, 1, 2, 4, 5))
    left_all = lax.all_to_all(left_send, "y", 0, 0, tiled=True)
    lr = left_all[..., :FREQS]
    li = left_all[..., FREQS:]
    rr = right_all[..., :FREQS]
    ri = right_all[..., FREQS:]
    lhs = jnp.stack([lr, li], axis=0)
    rhs_real = jnp.stack([rr, ri], axis=0)
    rhs_imag = jnp.stack([ri, -rr], axis=0)
    rhs = jnp.stack([rhs_real, rhs_imag], axis=-2)
    partial_value = jnp.einsum(
        "cyksz rf,cyksjpf->zkrjpf".replace(" ", ""),
        lhs,
        rhs,
        preferred_element_type=jnp.float32,
    )
    partial_value = partial_value.reshape(z_count, slot_count, rows, block_width, 2 * FREQS)
    stacked = lax.psum_scatter(
        partial_value.astype(jnp.bfloat16), "z", scatter_dimension=0, tiled=True
    ).astype(jnp.float32)[0]
    lag_weights = lag_table(seg_dev * z_count * y_count)
    correlation = jnp.einsum(
        "krjq,qt->krjt",
        stacked,
        lag_weights,
        precision=lax.Precision.HIGHEST,
        preferred_element_type=jnp.float32,
    )
    masked = correlation * live_slots.astype(jnp.float32)[:, None, None, None]
    return masked.astype(jnp.bfloat16)[None]


def solution(mesh):
    pairs_count, win_count = mesh.devices.shape
    y_count = 4 if win_count % 4 == 0 else 1
    grid = Mesh(
        mesh.devices.reshape(pairs_count, win_count // y_count, y_count), ("pairs", "z", "y")
    )
    in_specs = (P("pairs", ("z", "y"), None, None), P(), P())
    out_specs = P("pairs", None, ("z", "y"), None, None)
    return jax.shard_map(shards, mesh=grid, in_specs=in_specs, out_specs=out_specs, check_vma=False)
```

time: 138 us -> 98.5 us (0.71)
  waiting for transfers between devices: 93.8 us -> 23.1 us
  blocking collectives: 0 us -> 28.9 us
  other arithmetic: 6.14 us -> 1.92 us
  local copies, waits for them, and re-layouts: 10.4 us -> 14.5 us
  matrix products: 9.54 us -> 11.8 us
    reduce_scatter x1, waiting for transfers between devices: 78.3 us -> 23 us  [shards(): lax.psum_scatter(partial_value.astype(jnp.bfloat16), 'z', scatter_dimensi...]
    all_gather x0 -> x2, blocking collectives: none -> 28.9 us  [the longest x1 15.1 us: shards(): right_all = lax.all_gather(right, 'y', axis=0, tiled=False)]
    all_to_all x1, waiting for transfers between devices: 15.5 us -> 0.01 us  [shards(): left_all = lax.all_to_all(left_send, 'y', 0, 0, tiled=True)]
    another operation x0 -> x2, local copies, waits for them, and re-layouts: none -> 8.29 us  [shards(): lhs = jnp.stack([lr, li], axis=0)]
    concatenate x2 -> x0, local copies, waits for them, and re-layouts: 6.76 us -> none  [the longest x1 6.58 us: pair_cross(): return jnp.concatenate([real_sum, imag_sum], axis=-1)]
    concatenate x1 -> x0, other arithmetic: 2.33 us -> none  [pair_cross(): return jnp.concatenate([real_sum, imag_sum], axis=-1)]
    cos x1 -> x0, other arithmetic: 2.13 us -> none  [band_table(): jnp.cos(phase)]
    dot_general x5 -> x2, matrix products: 4.71 us -> 6.76 us  [the longest x1 4.32 us: shards(): jnp.einsum('cyksz rf,cyksjpf->zkrjpf'.replace(' ', ''), lhs, rhs, preferr...]
  transfers between devices with their start and end apart: 2 -> 2, of which waited for: 2 -> 1; matrix products, arithmetic and copies ran while one was open for 0% -> 3% of each run, Pallas kernels for 0% -> 0%
where the time goes in v1:
time: 98.5 us; the launch traced here: 98.2 us
  blocking collectives  28.9 us (29%)
  waiting for transfers between devices  23.1 us (23%)
  local copies, waits for them, and re-layouts  14.5 us (15%)
  between operations  13.6 us (14%)
  matrix products  11.8 us (12%)
  starting transfers between devices  4.47 us (5%)
  other arithmetic  1.92 us (2%)
    reduce_scatter x1, waiting for transfers between devices, shards(): lax.psum_scatter(partial_value.astype(jnp.bfloat16), 'z', scatter_dimensi...  23 us
    all_gather x1, blocking collectives, shards(): right_all = lax.all_gather(right, 'y', axis=0, tiled=False)  15.1 us
    all_gather x1, blocking collectives, shards(): every_block = lax.all_gather(spectra, 'pairs', axis=0, tiled=False)  13.8 us
    another operation x2, local copies, waits for them, and re-layouts, shards(): lhs = jnp.stack([lr, li], axis=0)  8.29 us
    dot_general x1, matrix products, shards(): jnp.dot(records[0], band_table(), preferred_element_type=jnp.float32)  5 us
    all_to_all x1, starting transfers between devices, shards(): left_all = lax.all_to_all(left_send, 'y', 0, 0, tiled=True)  4.47 us
    dot_general x1, matrix products, shards(): jnp.einsum('cyksz rf,cyksjpf->zkrjpf'.replace(' ', ''), lhs, rhs, preferr...  4.32 us
    dot_general x1, matrix products, shards(): jnp.einsum('krjq,qt->krjt', stacked, lag_weights, precision=lax.Precision...  2.44 us
  transfers between devices with their start and end apart: 2, of which 1 were waited for; matrix products, arithmetic and copies ran while one was open for 3% of the time, Pallas kernels for 0%

profile of v1, /device:TPU:0, one launch (start us, length us, event | category | flops | bytes accessed | tf_op | source)
XLA Modules:
  0.0 98.2 jit_solution(12367641855093840118)
XLA Ops:
  6.5 0.0 copy-start
  6.5 0.7 copy-done
  7.2 0.2 dynamic-slice_reduce_fusion
  7.4 0.2 slice_reduce_fusion.1
  7.6 5.0 %fusion.8 = f32[6,128,64]{1,2,0:T(8,128)S(1)} fusion(bf16[4096,64,1]{0,1,2:T(8,128)(2,1)} %constant.67, bf16[1,6,128,4096]{3,2,1,0:T(8,128)(2,1)} %param.6), kind=kOutput, calls=%fused_computation.13 | convolution fusion | flops 402653184 | bytes 7012352 | tf_op jit(solution)/shard_map/dot_general | solution.py:66
  12.7 0.1 fusion.21
  12.8 13.8 %all_gather.10 = bf16[8,6,128,64]{2,3,1,0:T(8,128)(2,1)S(1)} all-gather(bf16[1,6,128,64]{2,3,1,0:T(8,128)(2,1)S(1)} %pad_maximum_fusion), channel_id=1, replica_groups=mesh['pairs'=8,'z'=4,'y'=4] {'pairs'}, dimensions={0}, use_global_device_ids=true | all-gather | bytes 884736 | tf_op jit(solution)/shard_map/all_gather | solution.py:69
  26.6 0.6 gather_fusion.1
  27.2 0.1 broadcast_select_fusion
  27.3 0.2 copy.28
  27.6 0.1 copy.29
  27.6 1.0 %reshape.91 = bf16[4,2,12288]{2,1,0:T(2,128)(2,1)} reshape(bf16[4,2,6,4,8,64]{5,4,3,2,1,0:T(8,128)(2,1)S(1)} %copy.29) | data formatting | bytes 393216
  28.6 4.5 %all-to-all-start = ((bf16[4,2,12288]{2,1,0:T(2,128)(2,1)}), bf16[4,2,12288]{2,1,0:T(2,128)(2,1)S(1)}, u32[]{:S(2)}, u32[]{:S(2)}) async-start(bf16[4,2,12288]{2,1,0:T(2,128)(2,1)} %reshape.91), calls=%async_computation | async-start | bytes 393216 | tf_op jit(solution)/shard_map/all_to_all | solution.py:77
  33.1 0.0 reduce-scatter.2.cloned.1.call-start
  33.1 0.6 gather_fusion
  33.7 0.1 broadcast_select_fusion.1
  33.8 15.1 %all-gather = bf16[8,6,128,64]{2,3,1,0:T(8,128)(2,1)S(1)} all-gather(bf16[2,6,128,64]{2,3,1,0:T(8,128)(2,1)S(1)} %broadcast_select_fusion.1), channel_id=2, replica_groups=mesh['pairs'=8,'z'=4,'y'=4] {'y'}, dimensions={0}, use_global_device_ids=true | all-gather | bytes 983040 | tf_op jit(solution)/shard_map/all_gather | solution.py:74
  48.9 0.1 fusion.37
  49.0 0.4 copy_bitcast_fusion.1
  49.4 0.2 maximum_bitcast_fusion.7
  49.6 0.0 all-to-all-done
  49.6 0.3 reshape.92
  49.9 0.2 slice_bitcast_fusion.1
  50.1 0.2 maximum_bitcast_fusion.8
  50.3 8.1 %copy.33 = bf16[2,4,2,6,4,8,32,1]{3,5,1,0,4,7,6,2:T(8,128)(2,1)} copy(bf16[2,4,2,6,4,8,32,1]{6,5,4,3,2,1,0,7:T(8,128)(2,1)S(1)} %maximum_bitcast_fusion.8) | data formatting | bytes 393216 | tf_op jit(solution)/shard_map/stack | solution.py:82
  58.4 0.0 copy-start.1
  58.4 4.3 %fusion.5 = bf16[4,2,8,128,2,32]{3,2,0,4,5,1:T(8,128)(2,1)S(1)} fusion(bf16[2,4,2,6,4,8,32,1]{3,5,1,0,4,7,6,2:T(8,128)(2,1)} %copy.33, bf16[2,4,2,6,128,1,32]{4,3,1,0,5,6,2:T(8,128)(2,1)S(1)} %maximum_bitcast_fusion.7, bf16[1,4,2,6,128,32]{4,3,1,5,2,0:T(8,128)(2,1)S(1)} %get-tuple-element.16, bf16[1,4,2,6,128,32]{4,3,1,5,2,0:T(8,128)(2,1)S(1)} %get-tuple-element.23), kind=kOutput, calls=%fused_computation.9 | convolution fusion | flops 54394880 | bytes 2818048 | tf_op jit(solution)/shard_map/cykszrf,cyksjpf->zkrjpf/dot_general | solution.py:86
  62.7 1.7 %copy.31 = bf16[4,2,8,128,2,32]{3,5,4,2,1,0:T(8,128)(2,1)} copy(bf16[4,2,8,128,2,32]{3,2,0,4,5,1:T(8,128)(2,1)S(1)} %fusion.5) | data formatting | bytes 2097152 | tf_op jit(solution)/shard_map/convert_element_type | solution.py:94
  64.4 0.0 reduce-scatter.2.cloned.1.call-update
  64.4 0.0 copy-done.1
  64.4 0.6 dynamic_slice.8
  65.0 0.6 compare_convert_fusion
  65.7 0.2 fusion.31
  65.9 23.0 %reduce-scatter.2.cloned.1.call-done = bf16[1,2,8,128,64]{3,4,2,1,0:T(8,128)(2,1)} async-done(((bf16[4,2,8,128,64]{3,4,2,1,0:T(8,128)(2,1)}), bf16[1,2,8,128,64]{3,4,2,1,0:T(8,128)(2,1)}) %reduce-scatter.2.cloned.1.call-update) | async-done | bytes 262160 | tf_op jit(solution)/shard_map/reduce_scatter | solution.py:93
  88.9 2.4 %fusion.7 = bf16[1,2,8,128,128]{4,3,2,1,0:T(8,128)(2,1)} fusion(f32[2]{0:T(128)S(1)} %compare_convert_fusion, bf16[1,2,8,128,64]{3,4,2,1,0:T(8,128)(2,1)} %reduce-scatter.2.cloned.1.call-done, f32[32,128]{1,0:T(8,128)S(1)} %get-tuple-element.21, f32[32,128]{1,0:T(8,128)S(1)} %get-tuple-element.20), kind=kOutput, calls=%fused_computation.12 | convolution fusion | flops 201867264 | bytes 819208 | tf_op jit(solution)/shard_map/krjq,qt->krjt/dot_general | solution.py:97
  (12 shorter events, 0.1 us)
Async XLA Ops:
  6.5 0.7 copy-start
  28.6 21.0 %all-to-all-start = ((bf16[4,2,12288]{2,1,0:T(2,128)(2,1)}), bf16[4,2,12288]{2,1,0:T(2,128)(2,1)S(1)}, u32[]{:S(2)}, u32[]{:S(2)}) async-start(bf16[4,2,12288]{2,1,0:T(2,128)(2,1)} %reshape.91), calls=%async_computation | async-start | bytes 393216 | tf_op jit(solution)/shard_map/all_to_all | solution.py:77
  33.1 55.8 %reduce-scatter.2.cloned.1.call-start = ((), (), s32[]{:S(2)}) async-start(), calls=%async_computation.2 | async-start | bytes 1310720 | tf_op jit(solution)/shard_map/reduce_scatter | solution.py:93
  58.4 6.0 %copy-start.1 = (s32[8]{0:T(128)S(1)}, s32[8]{0:T(128)}, u32[]{:S(2)}) copy-start(s32[8]{0:T(128)} %param.8) | copy-start | bytes 100
Sparse Core Ops, SparseCore 0:
  64.6 24.3 reduce-scatter.1

commit v2 on v1

--- a/solution.py
+++ b/solution.py
@@ -60,42 +60,114 @@
     seg_dev = records.shape[1]
     block_width = records.shape[2]
     slot_count = pair_list.shape[1]
-    z_count = lax.axis_size("z")
-    y_count = lax.axis_size("y")
-    rows = block_width // (z_count * y_count)
+    pairs_count = lax.axis_size("pairs")
+    side = lax.axis_size("y")
+    rows = block_width // (side * side)
+    chips = pairs_count // 2
+    half_seg = seg_dev // 2
     spectra = whiten(jnp.dot(records[0], band_table(), preferred_element_type=jnp.float32))
+    own = jnp.transpose(spectra, (2, 0, 1))
     owner_index = lax.axis_index("pairs")
+    core = owner_index % 2
+    chip = owner_index // 2
+    first_core = core == 0
+    z_index = lax.axis_index("z")
     y_index = lax.axis_index("y")
-    every_block = lax.all_gather(spectra, "pairs", axis=0, tiled=False)
+    gather_pos = jnp.where(first_core, y_index, z_index)
+    reduce_pos = jnp.where(first_core, z_index, y_index)
+
+    swap = [(p, p ^ 1) for p in range(pairs_count)]
+    ring = [(2 * x, 2 * ((x + 1) % chips)) for x in range(chips)] + [
+        (2 * x + 1, 2 * ((x - 1) % chips) + 1) for x in range(chips)
+    ]
+    partner = lax.ppermute(own, "pairs", swap)
+    here = jnp.where(first_core, jnp.stack([own, partner]), jnp.stack([partner, own]))
+    near = lax.ppermute(here, "pairs", ring)
+    relay = jnp.where(first_core, near[:, :, :half_seg], near[:, :, half_seg:])
+    far_part = lax.ppermute(relay, "pairs", ring)
+    other = lax.ppermute(jnp.concatenate([near, far_part], axis=2), "pairs", swap)
+    other_near = other[:, :, :seg_dev]
+    other_far = other[:, :, seg_dev:]
+    next_chip = jnp.where(first_core, other_near, near)
+    prev_chip = jnp.where(first_core, near, other_near)
+    far_chip = jnp.where(
+        first_core,
+        jnp.concatenate([far_part, other_far], axis=2),
+        jnp.concatenate([other_far, far_part], axis=2),
+    )
+    table = jnp.stack([here, next_chip, far_chip, prev_chip]).reshape(
+        (pairs_count,) + own.shape
+    )
     own_pairs = lax.dynamic_index_in_dim(pair_list, owner_index, 0, keepdims=False)
     live_slots = jnp.arange(slot_count, dtype=jnp.int32) < pair_count[owner_index]
-    left = jnp.take(every_block, own_pairs[:, 0], axis=0)
-    right = jnp.take(every_block, own_pairs[:, 1], axis=0)
-    right_all = lax.all_gather(right, "y", axis=0, tiled=False)
-    left_rows = left.reshape(slot_count, seg_dev, z_count, y_count, rows, 2 * FREQS)
-    left_send = jnp.transpose(left_rows, (3, 0, 1, 2, 4, 5))
-    left_all = lax.all_to_all(left_send, "y", 0, 0, tiled=True)
-    lr = left_all[..., :FREQS]
-    li = left_all[..., FREQS:]
-    rr = right_all[..., :FREQS]
-    ri = right_all[..., FREQS:]
+    position = ((own_pairs // 2 - chip) % chips) * 2 + own_pairs % 2
+    left = jnp.take(table, position[:, 0], axis=0)
+    right = jnp.take(table, position[:, 1], axis=0)
+    left6 = left.reshape(left.shape[:3] + (side, side, rows))
+    left_view = jnp.where(first_core, left6, jnp.swapaxes(left6, 3, 4))
+
+    def rows_for(pos):
+        picked = lax.dynamic_index_in_dim(left_view, pos, axis=4, keepdims=False)
+        return picked.reshape(picked.shape[:3] + (side * rows,))
+
+    def gather_perm(d):
+        perm = []
+        for p in range(pairs_count):
+            for z in range(side):
+                for y in range(side):
+                    src = (p * side + z) * side + y
+                    if p % 2 == 0:
+                        dst = (p * side + z) * side + (y + d) % side
+                    else:
+                        dst = (p * side + (z + d) % side) * side + y
+                    perm.append((src, dst))
+        return perm
+
+    def reduce_perm(e):
+        perm = []
+        for p in range(pairs_count):
+            for z in range(side):
+                for y in range(side):
+                    src = (p * side + z) * side + y
+                    if p % 2 == 0:
+                        dst = (p * side + (z + e) % side) * side + y
+                    else:
+                        dst = (p * side + z) * side + (y + e) % side
+                    perm.append((src, dst))
+        return perm
+
+    axes = ("pairs", "z", "y")
+    pieces = [jnp.concatenate([right, rows_for(gather_pos)], axis=-1)]
+    for d in range(1, side):
+        message = jnp.concatenate([right, rows_for((gather_pos + d) % side)], axis=-1)
+        pieces.append(lax.ppermute(message, axes, gather_perm(d)))
+    gathered = jnp.stack(pieces)
+    right_all = gathered[..., :block_width]
+    left_all = gathered[..., block_width:]
+    lr = left_all[:, :, :FREQS]
+    li = left_all[:, :, FREQS:]
+    rr = right_all[:, :, :FREQS]
+    ri = right_all[:, :, FREQS:]
     lhs = jnp.stack([lr, li], axis=0)
     rhs_real = jnp.stack([rr, ri], axis=0)
     rhs_imag = jnp.stack([ri, -rr], axis=0)
     rhs = jnp.stack([rhs_real, rhs_imag], axis=-2)
     partial_value = jnp.einsum(
-        "cyksz rf,cyksjpf->zkrjpf".replace(" ", ""),
-        lhs,
-        rhs,
-        preferred_element_type=jnp.float32,
+        "cakfsm,cakfspj->kfmpj", lhs, rhs, preferred_element_type=jnp.float32
     )
-    partial_value = partial_value.reshape(z_count, slot_count, rows, block_width, 2 * FREQS)
-    stacked = lax.psum_scatter(
-        partial_value.astype(jnp.bfloat16), "z", scatter_dimension=0, tiled=True
-    ).astype(jnp.float32)[0]
-    lag_weights = lag_table(seg_dev * z_count * y_count)
+    partial_value = partial_value.reshape(
+        (slot_count, FREQS, side, rows, 2, block_width)
+    )
+    partial_value = jnp.transpose(partial_value, (2, 0, 4, 1, 3, 5)).astype(jnp.bfloat16)
+    stacked = lax.dynamic_index_in_dim(partial_value, reduce_pos, 0, keepdims=False).astype(
+        jnp.float32
+    )
+    for e in range(1, side):
+        chunk = lax.dynamic_index_in_dim(partial_value, (reduce_pos + e) % side, 0, keepdims=False)
+        stacked = stacked + lax.ppermute(chunk, axes, reduce_perm(e)).astype(jnp.float32)
+    lag_weights = lag_table(seg_dev * side * side).reshape(2, FREQS, LAGS)
     correlation = jnp.einsum(
-        "krjq,qt->krjt",
+        "kpfrj,pft->krjt",
         stacked,
         lag_weights,
         precision=lax.Precision.HIGHEST,
@@ -107,10 +179,8 @@
 
 def solution(mesh):
     pairs_count, win_count = mesh.devices.shape
-    y_count = 4 if win_count % 4 == 0 else 1
-    grid = Mesh(
-        mesh.devices.reshape(pairs_count, win_count // y_count, y_count), ("pairs", "z", "y")
-    )
+    side = math.isqrt(win_count)
+    grid = Mesh(mesh.devices.reshape(pairs_count, side, side), ("pairs", "z", "y"))
     in_specs = (P("pairs", ("z", "y"), None, None), P(), P())
     out_specs = P("pairs", None, ("z", "y"), None, None)
     return jax.shard_map(shards, mesh=grid, in_specs=in_specs, out_specs=out_specs, check_vma=False)

time: 98.5 us -> 64.2 us (0.65)
  blocking collectives: 28.9 us -> 0 us
  between operations: 13.6 us -> 0.34 us
  local copies, waits for them, and re-layouts: 14.5 us -> 4.12 us
  starting transfers between devices: 4.47 us -> 14.2 us
  waiting for transfers between devices: 23.1 us -> 31.6 us
  matrix products: 11.8 us -> 8.98 us
  other arithmetic: 1.92 us -> 4.65 us
    ppermute x0 -> x10, waiting for transfers between devices: none -> 31.6 us  [the longest x3 11.4 us: shards(): pieces.append(lax.ppermute(message, axes, gather_perm(d)))]
    all_gather x2 -> x0, blocking collectives: 28.9 us -> none  [the longest x1 15.1 us: shards(): right_all = lax.all_gather(right, 'y', axis=0, tiled=False)]
    reduce_scatter x1 -> x0, waiting for transfers between devices: 23 us -> none  [shards(): lax.psum_scatter(partial_value.astype(jnp.bfloat16), 'z', scatter_dimensi...]
    ppermute x0 -> x10, starting transfers between devices: none -> 14.2 us  [the longest x3 5.98 us: shards(): pieces.append(lax.ppermute(message, axes, gather_perm(d)))]
    another operation x2 -> x1, local copies, waits for them, and re-layouts: 8.29 us -> 0.22 us  [shards(): lhs = jnp.stack([lr, li], axis=0)]
    all_to_all x1 -> x0, starting transfers between devices: 4.47 us -> none  [shards(): left_all = lax.all_to_all(left_send, 'y', 0, 0, tiled=True)]
    dot_general x2, matrix products: 6.76 us -> 3.98 us  [the longest x1 2.61 us: shards(): jnp.einsum('kpfrj,pft->krjt', stacked, lag_weights, precision=lax.Precisi...]
    another operation x1 -> x7, other arithmetic: 0.18 us -> 2.26 us  [the longest x2 1.98 us: shards(): gathered = jnp.stack(pieces)]
  transfers between devices with their start and end apart: 2 -> 10, of which waited for: 1 -> 8; matrix products, arithmetic and copies ran while one was open for 3% -> 3% of each run, Pallas kernels for 0% -> 0%
where the time goes in v2:
time: 64.2 us; the launch traced here: 63.9 us
  waiting for transfers between devices  31.6 us (49%)
  starting transfers between devices  14.2 us (22%)
  matrix products  8.98 us (14%)
  other arithmetic  4.65 us (7%)
  local copies, waits for them, and re-layouts  4.12 us (6%)
    ppermute x3, waiting for transfers between devices, shards(): pieces.append(lax.ppermute(message, axes, gather_perm(d)))  11.4 us
    ppermute x3, waiting for transfers between devices, shards(): lax.ppermute(chunk, axes, reduce_perm(e)).astype(jnp.float32)  7.1 us
    ppermute x3, starting transfers between devices, shards(): pieces.append(lax.ppermute(message, axes, gather_perm(d)))  5.98 us
    ppermute x3, starting transfers between devices, shards(): lax.ppermute(chunk, axes, reduce_perm(e)).astype(jnp.float32)  5.97 us
    ppermute x1, waiting for transfers between devices, shards(): far_part = lax.ppermute(relay, 'pairs', ring)  5.46 us
    ppermute x1, waiting for transfers between devices, shards(): near = lax.ppermute(here, 'pairs', ring)  5.29 us
    dot_general x1, matrix products, shards(): jnp.dot(records[0], band_table(), preferred_element_type=jnp.float32)  5 us
    dot_general x1, matrix products, shards(): jnp.einsum('kpfrj,pft->krjt', stacked, lag_weights, precision=lax.Precisi...  2.61 us
  transfers between devices with their start and end apart: 10, of which 8 were waited for; matrix products, arithmetic and copies ran while one was open for 3% of the time, Pallas kernels for 0%

profile of v2, /device:TPU:0, one launch (start us, length us, event | category | flops | bytes accessed | tf_op | source)
XLA Modules:
  0.0 63.9 jit_solution(7624023304075728179)
XLA Ops:
  0.0 0.0 copy-start
  0.0 5.0 %fusion.7 = f32[6,128,64]{1,2,0:T(8,128)S(1)} fusion(bf16[4096,64,1]{0,1,2:T(8,128)(2,1)} %constant.172, bf16[1,6,128,4096]{3,2,1,0:T(8,128)(2,1)} %param.6), kind=kOutput, calls=%fused_computation.13 | convolution fusion | flops 402653184 | bytes 7012352 | tf_op jit(solution)/shard_map/dot_general | solution.py:68
  5.1 0.1 multiply_convert_fusion.1
  5.2 0.1 fusion.30
  5.2 0.1 collective-permute-start
  5.3 0.0 copy-done
  5.3 0.2 fusion.36
  5.6 0.2 slice_reduce_fusion
  5.8 0.8 %collective-permute-done = bf16[64,6,128]{2,0,1:T(8,128)(2,1)S(1)} collective-permute-done((bf16[64,6,128]{2,0,1:T(8,128)(2,1)S(1)}, bf16[64,6,128]{2,0,1:T(8,128)(2,1)S(1)}, u32[]{:S(2)}, u32[]{:S(2)}) %collective-permute-start) | collective-permute-done | bytes 98336 | tf_op jit(solution)/shard_map/ppermute | solution.py:83
  6.6 1.6 %collective-permute-start.1 = (bf16[2,64,6,128]{3,1,2,0:T(8,128)(2,1)S(1)}, bf16[2,64,6,128]{3,1,2,0:T(8,128)(2,1)S(1)}, u32[]{:S(2)}, u32[]{:S(2)}) collective-permute-start(bf16[2,64,6,128]{3,1,2,0:T(8,128)(2,1)S(1)} %maximum_select_fusion.1), channel_id=1, source_target_pairs={{0,32},{32,64},{64,96},{96,0},{16,112},{48,16},{80,48},{112,80},{1... | collective-permute-start | bytes 589832 | tf_op jit(solution)/shard_map/ppermute | solution.py:85
  8.3 5.3 %collective-permute-done.1 = bf16[2,64,6,128]{3,1,2,0:T(8,128)(2,1)S(1)} collective-permute-done((bf16[2,64,6,128]{3,1,2,0:T(8,128)(2,1)S(1)}, bf16[2,64,6,128]{3,1,2,0:T(8,128)(2,1)S(1)}, u32[]{:S(2)}, u32[]{:S(2)}) %collective-permute-start.1) | collective-permute-done | bytes 196640 | tf_op jit(solution)/shard_map/ppermute | solution.py:85
  13.6 0.4 collective-permute-start.2
  14.0 5.5 %collective-permute-done.2 = bf16[2,64,3,128]{3,1,2,0:T(8,128)(2,1)S(1)} collective-permute-done((bf16[2,64,3,128]{3,1,2,0:T(8,128)(2,1)S(1)}, bf16[2,64,3,128]{3,1,2,0:T(8,128)(2,1)S(1)}, u32[]{:S(2)}, u32[]{:S(2)}) %collective-permute-start.2) | collective-permute-done | bytes 98336 | tf_op jit(solution)/shard_map/ppermute | solution.py:87
  19.5 0.1 collective-permute-start.3
  19.7 1.5 %collective-permute-done.3 = bf16[2,64,9,128]{3,1,2,0:T(8,128)(2,1)S(1)} collective-permute-done((bf16[2,64,9,128]{3,1,2,0:T(8,128)(2,1)S(1)}, bf16[2,64,9,128]{3,1,2,0:T(8,128)(2,1)S(1)}, u32[]{:S(2)}, u32[]{:S(2)}) %collective-permute-start.3) | collective-permute-done | bytes 294944 | tf_op jit(solution)/shard_map/ppermute | solution.py:88
  21.3 0.1 pad_maximum_fusion.2
  21.4 0.6 gather_fusion.1
  22.0 0.6 gather_fusion
  22.6 0.1 broadcast_select_fusion
  22.6 0.2 copy.18
  23.0 0.1 dynamic-slice_bitcast_fusion.3
  23.0 0.2 copy.20
  23.3 0.2 copy.23
  23.5 0.2 copy.22
  23.7 0.2 copy.21
  23.9 0.1 copy_select_fusion
  24.0 0.4 fusion.12
  24.4 1.7 %collective-permute-start.4 = (bf16[2,64,6,160]{3,2,1,0:T(8,128)(2,1)S(1)}, bf16[2,64,6,160]{3,2,1,0:T(8,128)(2,1)S(1)}, u32[]{:S(2)}, u32[]{:S(2)}) collective-permute-start(bf16[2,64,6,160]{3,2,1,0:T(8,128)(2,1)S(1)} %get-tuple-element.29), channel_id=1, source_target_pairs={{0,1},{1,2},{2,3},{3,0},{4,5},{5,6},{6,7},{7,4},{8,9},{9,10},{10,1... | collective-permute-start | bytes 737288 | tf_op jit(solution)/shard_map/ppermute | solution.py:143
  26.1 2.9 %collective-permute-start.5 = (bf16[2,64,6,160]{3,2,1,0:T(8,128)(2,1)S(1)}, bf16[2,64,6,160]{3,2,1,0:T(8,128)(2,1)S(1)}, u32[]{:S(2)}, u32[]{:S(2)}) collective-permute-start(bf16[2,64,6,160]{3,2,1,0:T(8,128)(2,1)S(1)} %get-tuple-element.30), channel_id=1, source_target_pairs={{0,2},{1,3},{2,0},{3,1},{4,6},{5,7},{6,4},{7,5},{8,10},{9,11},{10,... | collective-permute-start | bytes 737288 | tf_op jit(solution)/shard_map/ppermute | solution.py:143
  29.0 1.3 %collective-permute-start.6 = (bf16[2,64,6,160]{3,2,1,0:T(8,128)(2,1)S(1)}, bf16[2,64,6,160]{3,2,1,0:T(8,128)(2,1)}, u32[]{:S(2)}, u32[]{:S(2)}) collective-permute-start(bf16[2,64,6,160]{3,2,1,0:T(8,128)(2,1)S(1)} %get-tuple-element.31), channel_id=1, source_target_pairs={{0,3},{1,0},{2,1},{3,2},{4,7},{5,4},{6,5},{7,6},{8,11},{9,8},{10,9... | collective-permute-start | bytes 737288 | tf_op jit(solution)/shard_map/ppermute | solution.py:143
  30.4 4.5 %collective-permute-done.4 = bf16[2,64,6,160]{3,2,1,0:T(8,128)(2,1)S(1)} collective-permute-done((bf16[2,64,6,160]{3,2,1,0:T(8,128)(2,1)S(1)}, bf16[2,64,6,160]{3,2,1,0:T(8,128)(2,1)S(1)}, u32[]{:S(2)}, u32[]{:S(2)}) %collective-permute-start.4) | collective-permute-done | bytes 245792 | tf_op jit(solution)/shard_map/ppermute | solution.py:143
  34.9 6.9 %collective-permute-done.5 = bf16[2,64,6,160]{3,2,1,0:T(8,128)(2,1)S(1)} collective-permute-done((bf16[2,64,6,160]{3,2,1,0:T(8,128)(2,1)S(1)}, bf16[2,64,6,160]{3,2,1,0:T(8,128)(2,1)S(1)}, u32[]{:S(2)}, u32[]{:S(2)}) %collective-permute-start.5) | collective-permute-done | bytes 245792 | tf_op jit(solution)/shard_map/ppermute | solution.py:143
  41.8 0.0 collective-permute-done.6
  41.8 1.6 %pad_maximum_fusion = bf16[4,2,64,6,160]{4,3,0,2,1:T(8,128)(2,1)S(1)} fusion(bf16[1,2,64,6,160]{4,3,0,2,1:T(8,128)(2,1)} %bitcast.27, bf16[1,2,64,6,160]{4,3,0,2,1:T(8,128)(2,1)S(1)} %bitcast.127, bf16[1,2,64,6,160]{4,3,0,2,1:T(8,128)(2,1)S(1)} %bitcast.126, bf16[1,2,64,6,160]{4,3,0,2,1:T(8,128)(2,1)S(1)} %get-tuple-element.28), kind=kLoop, calls=%fused_computation.4 | loop fusion | flops 1474560 | bytes 1966080 | tf_op jit(solution)/shard_map/stack | solution.py:144
  43.4 0.2 slice_bitcast_fusion.1
  43.6 0.2 slice_bitcast_fusion.4
  43.8 0.2 maximum_bitcast_fusion.2
  44.1 0.7 %pad_maximum_fusion.1 = bf16[2,4,2,32,6,2,128]{6,4,0,1,5,3,2:T(8,128)(2,1)S(1)} fusion(bf16[2,4,2,32,6,1,128]{6,4,0,1,5,3,2:T(8,128)(2,1)S(1)} %maximum_bitcast_fusion.2, bf16[1,4,2,32,6,128]{5,4,1,3,2,0:T(8,128)(2,1)S(1)} %get-tuple-element.17, bf16[1,4,2,32,6,128]{5,4,1,3,2,0:T(8,128)(2,1)S(1)} %get-tuple-element.14), kind=kLoop, calls=%fused_computation.5 | loop fusion | flops 3538944 | bytes 3145728 | tf_op jit(solution)/shard_map/stack | solution.py:154
  44.8 1.4 %fusion.2 = bf16[2,32,32,2,128,1,1]{4,2,5,0,3,1,6:T(8,128)(2,1)S(1)} fusion(bf16[2,4,2,32,6,2,128]{6,4,0,1,5,3,2:T(8,128)(2,1)S(1)} %pad_maximum_fusion.1, bf16[1,4,2,32,6,32]{5,4,1,3,2,0:T(8,128)(2,1)S(1)} %get-tuple-element.13, bf16[1,4,2,32,6,32]{5,4,1,3,2,0:T(8,128)(2,1)S(1)} %get-tuple-element.12), kind=kOutput, calls=%fused_computation.7 | convolution fusion | flops 50429952 | bytes 2818048 | tf_op jit(solution)/shard_map/cakfsm,cakfspj->kfmpj/dot_general | solution.py:155
  46.2 0.1 copy.63
  46.3 0.0 copy-start.1
  46.3 0.3 constant_dynamic-slice_fusion.3
  46.6 0.1 copy.65
  46.6 0.1 copy.66
  46.7 0.1 copy.64
  46.8 4.1 %collective-permute-start.9 = (bf16[2,2,32,8,128]{4,2,1,3,0:T(8,128)(2,1)S(1)}, bf16[2,2,32,8,128]{4,2,1,3,0:T(8,128)(2,1)S(1)}, u32[]{:S(2)}, u32[]{:S(2)}) collective-permute-start(bf16[2,2,32,8,128]{4,2,1,3,0:T(8,128)(2,1)S(1)} %bitcast.133), channel_id=1, source_target_pairs={{0,12},{1,13},{2,14},{3,15},{4,0},{5,1},{6,2},{7,3},{8,4},{9,5},{1... | collective-permute-start | bytes 786440 | tf_op jit(solution)/shard_map/ppermute | solution.py:167
  50.9 0.0 collective-permute-start.7
  50.9 1.9 %collective-permute-start.8 = (bf16[2,2,32,8,128]{4,2,1,3,0:T(8,128)(2,1)S(1)}, bf16[2,2,32,8,128]{4,2,1,3,0:T(8,128)(2,1)S(1)}, u32[]{:S(2)}, u32[]{:S(2)}) collective-permute-start(bf16[2,2,32,8,128]{4,2,1,3,0:T(8,128)(2,1)S(1)} %bitcast.131), channel_id=1, source_target_pairs={{0,8},{1,9},{2,10},{3,11},{4,12},{5,13},{6,14},{7,15},{8,0},{9,1},... | collective-permute-start | bytes 786440 | tf_op jit(solution)/shard_map/ppermute | solution.py:167
  52.8 0.2 fusion.35
  52.9 0.0 copy-done.1
  52.9 0.6 dynamic_slice.42
  53.5 0.6 %compare_convert_fusion = f32[2]{0:T(128)S(1)} fusion(s32[]{:T(128)} %bitcast.52), kind=kLoop, calls=%fused_computation.102 | loop fusion | flops 4 | bytes 12 | tf_op jit(solution)/shard_map/convert_element_type | solution.py:176
  54.2 0.6 collective-permute-done.9
  54.8 6.5 %collective-permute-done.7 = bf16[2,2,32,8,128]{4,2,1,3,0:T(8,128)(2,1)S(1)} collective-permute-done((bf16[2,2,32,8,128]{4,2,1,3,0:T(8,128)(2,1)S(1)}, bf16[2,2,32,8,128]{4,2,1,3,0:T(8,128)(2,1)S(1)}, u32[]{:S(2)}, u32[]{:S(2)}) %collective-permute-start.7) | collective-permute-done | bytes 262176 | tf_op jit(solution)/shard_map/ppermute | solution.py:167
  61.3 0.0 collective-permute-done.8
  61.3 2.6 %fusion.6 = bf16[1,2,8,128,128]{4,3,2,1,0:T(8,128)(2,1)} fusion(f32[2,32,128,1,1]{2,1,0,4,3:T(8,128)S(1)} %bitcast.134, f32[2]{0:T(128)S(1)} %compare_convert_fusion, bf16[2,2,32,8,128]{4,2,1,3,0:T(8,128)(2,1)S(1)} %collective-permute-done.9, bf16[2,2,32,8,128]{4,2,1,3,0:T(8,128)(2,1)S(1)} %collective-permute-done.8, ...), kind=kOutput, calls=%fused_computation.12 | convolution fusion | flops 202768384 | bytes 1605640 | tf_op jit(solution)/shard_map/kpfrj,pft->krjt/dot_general | solution.py:169
  (19 shorter events, 0.3 us)
Async XLA Ops:
  0.0 5.3 %copy-start = (s32[8,2,2]{0,2,1:T(2,128)S(1)}, s32[8,2,2]{0,2,1:T(2,128)}, u32[]{:S(2)}) copy-start(s32[8,2,2]{0,2,1:T(2,128)} %param.7) | copy-start | bytes 388
  5.2 1.4 %collective-permute-start = (bf16[64,6,128]{2,0,1:T(8,128)(2,1)S(1)}, bf16[64,6,128]{2,0,1:T(8,128)(2,1)S(1)}, u32[]{:S(2)}, u32[]{:S(2)}) collective-permute-start(bf16[64,6,128]{2,0,1:T(8,128)(2,1)S(1)} %get-tuple-element.34), channel_id=1, source_target_pairs={{0,16},{16,0},{32,48},{48,32},{64,80},{80,64},{96,112},{112,96},{1... | collective-permute-start | bytes 294920 | tf_op jit(solution)/shard_map/ppermute | solution.py:83
  6.6 6.9 %collective-permute-start.1 = (bf16[2,64,6,128]{3,1,2,0:T(8,128)(2,1)S(1)}, bf16[2,64,6,128]{3,1,2,0:T(8,128)(2,1)S(1)}, u32[]{:S(2)}, u32[]{:S(2)}) collective-permute-start(bf16[2,64,6,128]{3,1,2,0:T(8,128)(2,1)S(1)} %maximum_select_fusion.1), channel_id=1, source_target_pairs={{0,32},{32,64},{64,96},{96,0},{16,112},{48,16},{80,48},{112,80},{1... | collective-permute-start | bytes 589832 | tf_op jit(solution)/shard_map/ppermute | solution.py:85
  13.6 5.9 %collective-permute-start.2 = (bf16[2,64,3,128]{3,1,2,0:T(8,128)(2,1)S(1)}, bf16[2,64,3,128]{3,1,2,0:T(8,128)(2,1)S(1)}, u32[]{:S(2)}, u32[]{:S(2)}) collective-permute-start(bf16[2,64,3,128]{3,1,2,0:T(8,128)(2,1)S(1)} %slice_select_fusion), channel_id=1, source_target_pairs={{0,32},{32,64},{64,96},{96,0},{16,112},{48,16},{80,48},{112,80},{1... | collective-permute-start | bytes 294920 | tf_op jit(solution)/shard_map/ppermute | solution.py:87
  19.5 1.7 %collective-permute-start.3 = (bf16[2,64,9,128]{3,1,2,0:T(8,128)(2,1)S(1)}, bf16[2,64,9,128]{3,1,2,0:T(8,128)(2,1)S(1)}, u32[]{:S(2)}, u32[]{:S(2)}) collective-permute-start(bf16[2,64,9,128]{3,1,2,0:T(8,128)(2,1)S(1)} %pad_maximum_fusion.7), channel_id=1, source_target_pairs={{0,16},{16,0},{32,48},{48,32},{64,80},{80,64},{96,112},{112,96},{1... | collective-permute-start | bytes 884744 | tf_op jit(solution)/shard_map/ppermute | solution.py:88
  24.4 10.5 %collective-permute-start.4 = (bf16[2,64,6,160]{3,2,1,0:T(8,128)(2,1)S(1)}, bf16[2,64,6,160]{3,2,1,0:T(8,128)(2,1)S(1)}, u32[]{:S(2)}, u32[]{:S(2)}) collective-permute-start(bf16[2,64,6,160]{3,2,1,0:T(8,128)(2,1)S(1)} %get-tuple-element.29), channel_id=1, source_target_pairs={{0,1},{1,2},{2,3},{3,0},{4,5},{5,6},{6,7},{7,4},{8,9},{9,10},{10,1... | collective-permute-start | bytes 737288 | tf_op jit(solution)/shard_map/ppermute | solution.py:143
  26.1 15.7 %collective-permute-start.5 = (bf16[2,64,6,160]{3,2,1,0:T(8,128)(2,1)S(1)}, bf16[2,64,6,160]{3,2,1,0:T(8,128)(2,1)S(1)}, u32[]{:S(2)}, u32[]{:S(2)}) collective-permute-start(bf16[2,64,6,160]{3,2,1,0:T(8,128)(2,1)S(1)} %get-tuple-element.30), channel_id=1, source_target_pairs={{0,2},{1,3},{2,0},{3,1},{4,6},{5,7},{6,4},{7,5},{8,10},{9,11},{10,... | collective-permute-start | bytes 737288 | tf_op jit(solution)/shard_map/ppermute | solution.py:143
  29.0 12.8 %collective-permute-start.6 = (bf16[2,64,6,160]{3,2,1,0:T(8,128)(2,1)S(1)}, bf16[2,64,6,160]{3,2,1,0:T(8,128)(2,1)}, u32[]{:S(2)}, u32[]{:S(2)}) collective-permute-start(bf16[2,64,6,160]{3,2,1,0:T(8,128)(2,1)S(1)} %get-tuple-element.31), channel_id=1, source_target_pairs={{0,3},{1,0},{2,1},{3,2},{4,7},{5,4},{6,5},{7,6},{8,11},{9,8},{10,9... | collective-permute-start | bytes 737288 | tf_op jit(solution)/shard_map/ppermute | solution.py:143
  46.3 6.6 %copy-start.1 = (s32[8]{0:T(128)S(1)}, s32[8]{0:T(128)}, u32[]{:S(2)}) copy-start(s32[8]{0:T(128)} %param.8) | copy-start | bytes 100
  46.8 8.0 %collective-permute-start.9 = (bf16[2,2,32,8,128]{4,2,1,3,0:T(8,128)(2,1)S(1)}, bf16[2,2,32,8,128]{4,2,1,3,0:T(8,128)(2,1)S(1)}, u32[]{:S(2)}, u32[]{:S(2)}) collective-permute-start(bf16[2,2,32,8,128]{4,2,1,3,0:T(8,128)(2,1)S(1)} %bitcast.133), channel_id=1, source_target_pairs={{0,12},{1,13},{2,14},{3,15},{4,0},{5,1},{6,2},{7,3},{8,4},{9,5},{1... | collective-permute-start | bytes 786440 | tf_op jit(solution)/shard_map/ppermute | solution.py:167
  50.9 10.4 %collective-permute-start.7 = (bf16[2,2,32,8,128]{4,2,1,3,0:T(8,128)(2,1)S(1)}, bf16[2,2,32,8,128]{4,2,1,3,0:T(8,128)(2,1)S(1)}, u32[]{:S(2)}, u32[]{:S(2)}) collective-permute-start(bf16[2,2,32,8,128]{4,2,1,3,0:T(8,128)(2,1)S(1)} %bitcast.132), channel_id=1, source_target_pairs={{0,4},{1,5},{2,6},{3,7},{4,8},{5,9},{6,10},{7,11},{8,12},{9,13},{1... | collective-permute-start | bytes 786440 | tf_op jit(solution)/shard_map/ppermute | solution.py:167
  50.9 10.4 %collective-permute-start.8 = (bf16[2,2,32,8,128]{4,2,1,3,0:T(8,128)(2,1)S(1)}, bf16[2,2,32,8,128]{4,2,1,3,0:T(8,128)(2,1)S(1)}, u32[]{:S(2)}, u32[]{:S(2)}) collective-permute-start(bf16[2,2,32,8,128]{4,2,1,3,0:T(8,128)(2,1)S(1)} %bitcast.131), channel_id=1, source_target_pairs={{0,8},{1,9},{2,10},{3,11},{4,12},{5,13},{6,14},{7,15},{8,0},{9,1},... | collective-permute-start | bytes 786440 | tf_op jit(solution)/shard_map/ppermute | solution.py:167

commit v3 on v2

--- a/solution.py
+++ b/solution.py
@@ -64,9 +64,11 @@
     side = lax.axis_size("y")
     rows = block_width // (side * side)
     chips = pairs_count // 2
-    half_seg = seg_dev // 2
+    width = 2 * FREQS
+    spec_rows = seg_dev * width
+    half_rows = spec_rows // 2
     spectra = whiten(jnp.dot(records[0], band_table(), preferred_element_type=jnp.float32))
-    own = jnp.transpose(spectra, (2, 0, 1))
+    own = jnp.transpose(spectra, (0, 2, 1)).reshape(spec_rows, block_width)
     owner_index = lax.axis_index("pairs")
     core = owner_index % 2
     chip = owner_index // 2
@@ -83,17 +85,17 @@
     partner = lax.ppermute(own, "pairs", swap)
     here = jnp.where(first_core, jnp.stack([own, partner]), jnp.stack([partner, own]))
     near = lax.ppermute(here, "pairs", ring)
-    relay = jnp.where(first_core, near[:, :, :half_seg], near[:, :, half_seg:])
+    relay = jnp.where(first_core, near[:, :half_rows], near[:, half_rows:])
     far_part = lax.ppermute(relay, "pairs", ring)
-    other = lax.ppermute(jnp.concatenate([near, far_part], axis=2), "pairs", swap)
-    other_near = other[:, :, :seg_dev]
-    other_far = other[:, :, seg_dev:]
+    other = lax.ppermute(jnp.concatenate([near, far_part], axis=1), "pairs", swap)
+    other_near = other[:, :spec_rows]
+    other_far = other[:, spec_rows:]
     next_chip = jnp.where(first_core, other_near, near)
     prev_chip = jnp.where(first_core, near, other_near)
     far_chip = jnp.where(
         first_core,
-        jnp.concatenate([far_part, other_far], axis=2),
-        jnp.concatenate([other_far, far_part], axis=2),
+        jnp.concatenate([far_part, other_far], axis=1),
+        jnp.concatenate([other_far, far_part], axis=1),
     )
     table = jnp.stack([here, next_chip, far_chip, prev_chip]).reshape(
         (pairs_count,) + own.shape
@@ -103,12 +105,13 @@
     position = ((own_pairs // 2 - chip) % chips) * 2 + own_pairs % 2
     left = jnp.take(table, position[:, 0], axis=0)
     right = jnp.take(table, position[:, 1], axis=0)
-    left6 = left.reshape(left.shape[:3] + (side, side, rows))
-    left_view = jnp.where(first_core, left6, jnp.swapaxes(left6, 3, 4))
+    left5 = left.reshape((slot_count, spec_rows, side, side, rows))
+    left_view = jnp.where(first_core, left5, jnp.swapaxes(left5, 2, 3))
+    packed_rows = spec_rows * side * rows // block_width
 
     def rows_for(pos):
-        picked = lax.dynamic_index_in_dim(left_view, pos, axis=4, keepdims=False)
-        return picked.reshape(picked.shape[:3] + (side * rows,))
+        picked = lax.dynamic_index_in_dim(left_view, pos, axis=3, keepdims=False)
+        return picked.reshape((slot_count, packed_rows, block_width))
 
     def gather_perm(d):
         perm = []
@@ -137,34 +140,33 @@
         return perm
 
     axes = ("pairs", "z", "y")
-    pieces = [jnp.concatenate([right, rows_for(gather_pos)], axis=-1)]
+    pieces = [jnp.concatenate([right, rows_for(gather_pos)], axis=1)]
     for d in range(1, side):
-        message = jnp.concatenate([right, rows_for((gather_pos + d) % side)], axis=-1)
+        message = jnp.concatenate([right, rows_for((gather_pos + d) % side)], axis=1)
         pieces.append(lax.ppermute(message, axes, gather_perm(d)))
     gathered = jnp.stack(pieces)
-    right_all = gathered[..., :block_width]
-    left_all = gathered[..., block_width:]
-    lr = left_all[:, :, :FREQS]
-    li = left_all[:, :, FREQS:]
-    rr = right_all[:, :, :FREQS]
-    ri = right_all[:, :, FREQS:]
-    lhs = jnp.stack([lr, li], axis=0)
-    rhs_real = jnp.stack([rr, ri], axis=0)
-    rhs_imag = jnp.stack([ri, -rr], axis=0)
-    rhs = jnp.stack([rhs_real, rhs_imag], axis=-2)
+    right_all = gathered[:, :, :spec_rows].reshape(
+        (side, slot_count, seg_dev, 2, FREQS, block_width)
+    )
+    left_all = gathered[:, :, spec_rows:].reshape(
+        (side, slot_count, seg_dev, 2, FREQS, side * rows)
+    )
+    right_swapped = jnp.stack([right_all[:, :, :, 1], -right_all[:, :, :, 0]], axis=3)
+    rhs = jnp.concatenate([right_all, right_swapped], axis=-1)
     partial_value = jnp.einsum(
-        "cakfsm,cakfspj->kfmpj", lhs, rhs, preferred_element_type=jnp.float32
+        "akscfm,akscfn->kfmn", left_all, rhs, preferred_element_type=jnp.float32
     )
-    partial_value = partial_value.reshape(
-        (slot_count, FREQS, side, rows, 2, block_width)
-    )
+    partial_value = partial_value.reshape((slot_count, FREQS, side, rows, 2, block_width))
     partial_value = jnp.transpose(partial_value, (2, 0, 4, 1, 3, 5)).astype(jnp.bfloat16)
+    chunk_rows = slot_count * 2 * FREQS * rows
+    partial_value = partial_value.reshape((side, chunk_rows, block_width))
     stacked = lax.dynamic_index_in_dim(partial_value, reduce_pos, 0, keepdims=False).astype(
         jnp.float32
     )
     for e in range(1, side):
         chunk = lax.dynamic_index_in_dim(partial_value, (reduce_pos + e) % side, 0, keepdims=False)
         stacked = stacked + lax.ppermute(chunk, axes, reduce_perm(e)).astype(jnp.float32)
+    stacked = stacked.reshape((slot_count, 2, FREQS, rows, block_width))
     lag_weights = lag_table(seg_dev * side * side).reshape(2, FREQS, LAGS)
     correlation = jnp.einsum(
         "kpfrj,pft->krjt",

time: 64.2 us -> 58.8 us (0.916)
  waiting for transfers between devices: 31.6 us -> 23.3 us
  local copies, waits for them, and re-layouts: 4.12 us -> 8.94 us
  other arithmetic: 4.65 us -> 1.94 us
    ppermute x3, waiting for transfers between devices: 11.4 us -> 5.45 us  [shards(): pieces.append(lax.ppermute(message, axes, gather_perm(d)))]
    reshape x5 -> x6, local copies, waits for them, and re-layouts: 0.89 us -> 4.08 us  [the longest x4 3.22 us: rows_for(): return picked.reshape((slot_count, packed_rows, block_width))]
    ppermute x3, waiting for transfers between devices: 7.1 us -> 4.72 us  [shards(): lax.ppermute(chunk, axes, reduce_perm(e)).astype(jnp.float32)]
    dynamic_slice x1 -> x5, local copies, waits for them, and re-layouts: 0.27 us -> 2.18 us  [rows_for(): picked = lax.dynamic_index_in_dim(left_view, pos, axis=3, keepdims=False)]
    another operation x2, other arithmetic: 1.98 us -> 0.17 us  [shards(): gathered = jnp.stack(pieces)]
    another operation x6 -> x2, other arithmetic: 1.27 us -> 0.09 us  [the longest x2 0.96 us: shards(): rhs = jnp.stack([rhs_real, rhs_imag], axis=-2)]
where the time goes in v3:
time: 58.8 us; the launch traced here: 58.6 us
  waiting for transfers between devices  23.3 us (40%)
  starting transfers between devices  14.8 us (25%)
  matrix products  9.36 us (16%)
  local copies, waits for them, and re-layouts  8.94 us (15%)
  other arithmetic  1.94 us (3%)
    ppermute x3, starting transfers between devices, shards(): lax.ppermute(chunk, axes, reduce_perm(e)).astype(jnp.float32)  6.58 us
    ppermute x3, starting transfers between devices, shards(): pieces.append(lax.ppermute(message, axes, gather_perm(d)))  5.98 us
    ppermute x1, waiting for transfers between devices, shards(): far_part = lax.ppermute(relay, 'pairs', ring)  5.46 us
    ppermute x3, waiting for transfers between devices, shards(): pieces.append(lax.ppermute(message, axes, gather_perm(d)))  5.45 us
    ppermute x1, waiting for transfers between devices, shards(): near = lax.ppermute(here, 'pairs', ring)  5.29 us
    dot_general x1, matrix products, shards(): jnp.dot(records[0], band_table(), preferred_element_type=jnp.float32)  5 us
    ppermute x3, waiting for transfers between devices, shards(): lax.ppermute(chunk, axes, reduce_perm(e)).astype(jnp.float32)  4.72 us
    reshape x4, local copies, waits for them, and re-layouts, rows_for(): return picked.reshape((slot_count, packed_rows, block_width))  3.22 us
  transfers between devices with their start and end apart: 10, of which 8 were waited for; matrix products, arithmetic and copies ran while one was open for 3% of the time, Pallas kernels for 0%

profile of v3, /device:TPU:0, one launch (start us, length us, event | category | flops | bytes accessed | tf_op | source)
XLA Modules:
  0.0 58.6 jit_solution(8084749973409190378)
XLA Ops:
  0.0 0.0 copy-start
  0.0 5.0 %fusion.16 = f32[6,128,64]{1,2,0:T(8,128)S(1)} fusion(bf16[4096,64,1]{0,1,2:T(8,128)(2,1)} %constant.172, bf16[1,6,128,4096]{3,2,1,0:T(8,128)(2,1)} %param.6), kind=kOutput, calls=%fused_computation.16 | convolution fusion | flops 402653184 | bytes 7012352 | tf_op jit(solution)/shard_map/dot_general | solution.py:70
  5.1 0.1 multiply_convert_fusion.1
  5.2 0.1 collective-permute-start
  5.3 0.0 copy-done
  5.3 0.2 fusion.35
  5.5 0.2 slice_reduce_fusion.1
  5.7 0.8 %collective-permute-done = bf16[384,128]{1,0:T(8,128)(2,1)S(1)} collective-permute-done((bf16[384,128]{1,0:T(8,128)(2,1)S(1)}, bf16[384,128]{1,0:T(8,128)(2,1)S(1)}, u32[]{:S(2)}, u32[]{:S(2)}) %collective-permute-start) | collective-permute-done | bytes 98336 | tf_op jit(solution)/shard_map/ppermute | solution.py:85
  6.6 1.6 %collective-permute-start.1 = (bf16[2,384,128]{2,1,0:T(8,128)(2,1)S(1)}, bf16[2,384,128]{2,1,0:T(8,128)(2,1)S(1)}, u32[]{:S(2)}, u32[]{:S(2)}) collective-permute-start(bf16[2,384,128]{2,1,0:T(8,128)(2,1)S(1)} %maximum_select_fusion.1), channel_id=1, source_target_pairs={{0,32},{32,64},{64,96},{96,0},{16,112},{48,16},{80,48},{112,80},{1... | collective-permute-start | bytes 589832 | tf_op jit(solution)/shard_map/ppermute | solution.py:87
  8.2 5.3 %collective-permute-done.1 = bf16[2,384,128]{2,1,0:T(8,128)(2,1)S(1)} collective-permute-done((bf16[2,384,128]{2,1,0:T(8,128)(2,1)S(1)}, bf16[2,384,128]{2,1,0:T(8,128)(2,1)S(1)}, u32[]{:S(2)}, u32[]{:S(2)}) %collective-permute-start.1) | collective-permute-done | bytes 196640 | tf_op jit(solution)/shard_map/ppermute | solution.py:87
  13.5 0.4 collective-permute-start.2
  14.0 5.5 %collective-permute-done.2 = bf16[2,192,128]{2,1,0:T(8,128)(2,1)S(1)} collective-permute-done((bf16[2,192,128]{2,1,0:T(8,128)(2,1)S(1)}, bf16[2,192,128]{2,1,0:T(8,128)(2,1)S(1)}, u32[]{:S(2)}, u32[]{:S(2)}) %collective-permute-start.2) | collective-permute-done | bytes 98336 | tf_op jit(solution)/shard_map/ppermute | solution.py:89
  19.5 0.1 collective-permute-start.3
  19.6 1.5 %collective-permute-done.3 = bf16[2,576,128]{2,1,0:T(8,128)(2,1)S(1)} collective-permute-done((bf16[2,576,128]{2,1,0:T(8,128)(2,1)S(1)}, bf16[2,576,128]{2,1,0:T(8,128)(2,1)S(1)}, u32[]{:S(2)}, u32[]{:S(2)}) %collective-permute-start.3) | collective-permute-done | bytes 294944 | tf_op jit(solution)/shard_map/ppermute | solution.py:90
  21.1 0.1 maximum_select_fusion.2
  21.2 0.1 pad_maximum_fusion.3
  21.3 0.6 gather_fusion.1
  21.9 0.1 broadcast_select_fusion
  22.0 0.2 copy.17
  22.3 0.5 copy.19
  22.8 0.8 %reshape.185 = bf16[2,96,128]{2,1,0:T(8,128)(2,1)S(1)} reshape(bf16[2,384,4,1,8]{4,2,1,0,3:T(4,128)(2,1)S(1)} %copy.19) | data formatting | bytes 98304 | tf_op jit(solution)/shard_map/reshape | solution.py:114
  23.6 0.5 copy.20
  24.2 0.8 %reshape.186 = bf16[2,96,128]{2,1,0:T(8,128)(2,1)S(1)} reshape(bf16[2,384,4,1,8]{4,2,1,0,3:T(4,128)(2,1)S(1)} %copy.20) | data formatting | bytes 98304 | tf_op jit(solution)/shard_map/reshape | solution.py:114
  25.0 0.5 copy.21
  25.5 0.8 %reshape.187 = bf16[2,96,128]{2,1,0:T(8,128)(2,1)S(1)} reshape(bf16[2,384,4,1,8]{4,2,1,0,3:T(4,128)(2,1)S(1)} %copy.21) | data formatting | bytes 98304 | tf_op jit(solution)/shard_map/reshape | solution.py:114
  26.3 0.5 copy.22
  26.9 0.8 %reshape.188 = bf16[2,96,128]{2,1,0:T(8,128)(2,1)S(1)} reshape(bf16[2,384,4,1,8]{4,2,1,0,3:T(4,128)(2,1)S(1)} %copy.22) | data formatting | bytes 98304 | tf_op jit(solution)/shard_map/reshape | solution.py:114
  27.7 0.6 gather_fusion
  28.3 0.1 broadcast_select_fusion.1
  28.4 0.1 maximum_bitcast_fusion
  28.5 1.7 %collective-permute-start.4 = (bf16[2,480,128]{2,1,0:T(8,128)(2,1)S(1)}, bf16[2,480,128]{2,1,0:T(8,128)(2,1)S(1)}, u32[]{:S(2)}, u32[]{:S(2)}) collective-permute-start(bf16[2,480,128]{2,1,0:T(8,128)(2,1)S(1)} %get-tuple-element.20), channel_id=1, source_target_pairs={{0,1},{1,2},{2,3},{3,0},{4,5},{5,6},{6,7},{7,4},{8,9},{9,10},{10,1... | collective-permute-start | bytes 737288 | tf_op jit(solution)/shard_map/ppermute | solution.py:146
  30.2 2.9 %collective-permute-start.5 = (bf16[2,480,128]{2,1,0:T(8,128)(2,1)S(1)}, bf16[2,480,128]{2,1,0:T(8,128)(2,1)S(1)}, u32[]{:S(2)}, u32[]{:S(2)}) collective-permute-start(bf16[2,480,128]{2,1,0:T(8,128)(2,1)S(1)} %get-tuple-element.21), channel_id=1, source_target_pairs={{0,2},{1,3},{2,0},{3,1},{4,6},{5,7},{6,4},{7,5},{8,10},{9,11},{10,... | collective-permute-start | bytes 737288 | tf_op jit(solution)/shard_map/ppermute | solution.py:146
  33.1 1.3 %collective-permute-start.6 = (bf16[2,480,128]{2,1,0:T(8,128)(2,1)S(1)}, bf16[2,480,128]{2,1,0:T(8,128)(2,1)S(1)}, u32[]{:S(2)}, u32[]{:S(2)}) collective-permute-start(bf16[2,480,128]{2,1,0:T(8,128)(2,1)S(1)} %get-tuple-element.22), channel_id=1, source_target_pairs={{0,3},{1,0},{2,1},{3,2},{4,7},{5,4},{6,5},{7,6},{8,11},{9,8},{10,9... | collective-permute-start | bytes 737288 | tf_op jit(solution)/shard_map/ppermute | solution.py:146
  34.5 1.5 %collective-permute-done.4 = bf16[2,480,128]{2,1,0:T(8,128)(2,1)S(1)} collective-permute-done((bf16[2,480,128]{2,1,0:T(8,128)(2,1)S(1)}, bf16[2,480,128]{2,1,0:T(8,128)(2,1)S(1)}, u32[]{:S(2)}, u32[]{:S(2)}) %collective-permute-start.4) | collective-permute-done | bytes 245792 | tf_op jit(solution)/shard_map/ppermute | solution.py:146
  36.0 4.0 %collective-permute-done.5 = bf16[2,480,128]{2,1,0:T(8,128)(2,1)S(1)} collective-permute-done((bf16[2,480,128]{2,1,0:T(8,128)(2,1)S(1)}, bf16[2,480,128]{2,1,0:T(8,128)(2,1)S(1)}, u32[]{:S(2)}, u32[]{:S(2)}) %collective-permute-start.5) | collective-permute-done | bytes 245792 | tf_op jit(solution)/shard_map/ppermute | solution.py:146
  39.9 0.0 collective-permute-done.6
  40.0 0.1 pad_maximum_fusion
  40.0 0.3 reshape.189
  40.3 0.5 copy.25
  40.9 0.2 fusion.42
  41.1 1.7 %fusion.11 = bf16[2,32,4,8,2,128]{5,3,4,2,1,0:T(8,128)(2,1)S(1)} fusion(bf16[4,2,6,1,32,128]{5,2,3,0,4,1:T(8,128)(2,1)S(1)} %get-tuple-element.16, bf16[4,2,6,1,32,128]{5,2,3,0,4,1:T(8,128)(2,1)S(1)} %get-tuple-element.15, bf16[4,2,6,2,32,128]{5,2,3,0,4,1:T(8,128)(2,1)S(1)} %copy.25, bf16[4,2,6,2,32,32]{5,4,3,2,1,0:T(8,128)(2,1)S(1)} %reshape.189), kind=kOutput, calls=%fused_computation.13 | convolution fusion | flops 55574528 | bytes 2818048 | tf_op jit(solution)/shard_map/akscfm,akscfn->kfmn/dot_general | solution.py:156
  42.8 0.0 copy-start.1
  42.8 0.3 copy.27
  43.1 0.1 dynamic-slice_bitcast_fusion.2
  43.2 2.0 %collective-permute-start.7 = (bf16[1024,128]{1,0:T(8,128)(2,1)S(1)}, bf16[1024,128]{1,0:T(8,128)(2,1)S(1)}, u32[]{:S(2)}, u32[]{:S(2)}) collective-permute-start(bf16[1024,128]{1,0:T(8,128)(2,1)S(1)} %get-tuple-element.12), channel_id=1, source_target_pairs={{0,4},{1,5},{2,6},{3,7},{4,8},{5,9},{6,10},{7,11},{8,12},{9,13},{1... | collective-permute-start | bytes 786440 | tf_op jit(solution)/shard_map/ppermute | solution.py:168
  45.2 3.6 %collective-permute-start.8 = (bf16[1024,128]{1,0:T(8,128)(2,1)S(1)}, bf16[1024,128]{1,0:T(8,128)(2,1)S(1)}, u32[]{:S(2)}, u32[]{:S(2)}) collective-permute-start(bf16[1024,128]{1,0:T(8,128)(2,1)S(1)} %get-tuple-element.14), channel_id=1, source_target_pairs={{0,8},{1,9},{2,10},{3,11},{4,12},{5,13},{6,14},{7,15},{8,0},{9,1},... | collective-permute-start | bytes 786440 | tf_op jit(solution)/shard_map/ppermute | solution.py:168
  48.8 1.0 %collective-permute-start.9 = (bf16[1024,128]{1,0:T(8,128)(2,1)S(1)}, bf16[1024,128]{1,0:T(8,128)(2,1)S(1)}, u32[]{:S(2)}, u32[]{:S(2)}) collective-permute-start(bf16[1024,128]{1,0:T(8,128)(2,1)S(1)} %get-tuple-element.13), channel_id=1, source_target_pairs={{0,12},{1,13},{2,14},{3,15},{4,0},{5,1},{6,2},{7,3},{8,4},{9,5},{1... | collective-permute-start | bytes 786440 | tf_op jit(solution)/shard_map/ppermute | solution.py:168
  49.8 0.2 fusion.34
  49.9 0.0 copy-done.1
  49.9 0.6 %dynamic_slice.42 = s32[1]{0:T(128)} dynamic-slice(s32[8]{0:T(128)S(1)} %copy-done.1, s32[]{:T(128)S(6)} %select_n.166), dynamic_slice_sizes={1} | dynamic-slice | bytes 12 | tf_op jit(solution)/shard_map/dynamic_slice | solution.py:104
  50.5 0.6 %compare_convert_fusion = f32[2]{0:T(128)S(1)} fusion(s32[]{:T(128)} %bitcast.39), kind=kLoop, calls=%fused_computation.88 | loop fusion | flops 4 | bytes 12 | tf_op jit(solution)/shard_map/convert_element_type | solution.py:178
  51.2 0.5 collective-permute-done.7
  51.6 4.3 %collective-permute-done.8 = bf16[1024,128]{1,0:T(8,128)(2,1)S(1)} collective-permute-done((bf16[1024,128]{1,0:T(8,128)(2,1)S(1)}, bf16[1024,128]{1,0:T(8,128)(2,1)S(1)}, u32[]{:S(2)}, u32[]{:S(2)}) %collective-permute-start.8) | collective-permute-done | bytes 262176 | tf_op jit(solution)/shard_map/ppermute | solution.py:168
  55.9 0.0 collective-permute-done.9
  55.9 0.1 fusion.21
  56.0 2.6 %fusion.15 = bf16[1,2,8,128,128]{4,3,2,1,0:T(8,128)(2,1)} fusion(f32[2,32,128,1,1]{2,1,0,4,3:T(8,128)S(1)} %bitcast.103, f32[2,2,32,8,128]{4,3,2,1,0:T(8,128)S(1)} %bitcast.87, f32[2]{0:T(128)S(1)} %compare_convert_fusion), kind=kOutput, calls=%fused_computation.15 | convolution fusion | flops 201850880 | bytes 1081352 | tf_op jit(solution)/shard_map/kpfrj,pft->krjt/dot_general | solution.py:171
  (21 shorter events, 0.3 us)
Async XLA Ops:
  0.0 5.3 %copy-start = (s32[8,2,2]{0,2,1:T(2,128)S(1)}, s32[8,2,2]{0,2,1:T(2,128)}, u32[]{:S(2)}) copy-start(s32[8,2,2]{0,2,1:T(2,128)} %param.7) | copy-start | bytes 388
  5.2 1.4 %collective-permute-start = (bf16[384,128]{1,0:T(8,128)(2,1)S(1)}, bf16[384,128]{1,0:T(8,128)(2,1)S(1)}, u32[]{:S(2)}, u32[]{:S(2)}) collective-permute-start(bf16[384,128]{1,0:T(8,128)(2,1)S(1)} %bitcast.96), channel_id=1, source_target_pairs={{0,16},{16,0},{32,48},{48,32},{64,80},{80,64},{96,112},{112,96},{1... | collective-permute-start | bytes 294920 | tf_op jit(solution)/shard_map/ppermute | solution.py:85
  6.6 6.9 %collective-permute-start.1 = (bf16[2,384,128]{2,1,0:T(8,128)(2,1)S(1)}, bf16[2,384,128]{2,1,0:T(8,128)(2,1)S(1)}, u32[]{:S(2)}, u32[]{:S(2)}) collective-permute-start(bf16[2,384,128]{2,1,0:T(8,128)(2,1)S(1)} %maximum_select_fusion.1), channel_id=1, source_target_pairs={{0,32},{32,64},{64,96},{96,0},{16,112},{48,16},{80,48},{112,80},{1... | collective-permute-start | bytes 589832 | tf_op jit(solution)/shard_map/ppermute | solution.py:87
  13.5 5.9 %collective-permute-start.2 = (bf16[2,192,128]{2,1,0:T(8,128)(2,1)S(1)}, bf16[2,192,128]{2,1,0:T(8,128)(2,1)S(1)}, u32[]{:S(2)}, u32[]{:S(2)}) collective-permute-start(bf16[2,192,128]{2,1,0:T(8,128)(2,1)S(1)} %slice_select_fusion), channel_id=1, source_target_pairs={{0,32},{32,64},{64,96},{96,0},{16,112},{48,16},{80,48},{112,80},{1... | collective-permute-start | bytes 294920 | tf_op jit(solution)/shard_map/ppermute | solution.py:89
  19.5 1.7 %collective-permute-start.3 = (bf16[2,576,128]{2,1,0:T(8,128)(2,1)S(1)}, bf16[2,576,128]{2,1,0:T(8,128)(2,1)S(1)}, u32[]{:S(2)}, u32[]{:S(2)}) collective-permute-start(bf16[2,576,128]{2,1,0:T(8,128)(2,1)S(1)} %pad_maximum_fusion.4), channel_id=1, source_target_pairs={{0,16},{16,0},{32,48},{48,32},{64,80},{80,64},{96,112},{112,96},{1... | collective-permute-start | bytes 884744 | tf_op jit(solution)/shard_map/ppermute | solution.py:90
  28.5 7.5 %collective-permute-start.4 = (bf16[2,480,128]{2,1,0:T(8,128)(2,1)S(1)}, bf16[2,480,128]{2,1,0:T(8,128)(2,1)S(1)}, u32[]{:S(2)}, u32[]{:S(2)}) collective-permute-start(bf16[2,480,128]{2,1,0:T(8,128)(2,1)S(1)} %get-tuple-element.20), channel_id=1, source_target_pairs={{0,1},{1,2},{2,3},{3,0},{4,5},{5,6},{6,7},{7,4},{8,9},{9,10},{10,1... | collective-permute-start | bytes 737288 | tf_op jit(solution)/shard_map/ppermute | solution.py:146
  30.2 9.7 %collective-permute-start.5 = (bf16[2,480,128]{2,1,0:T(8,128)(2,1)S(1)}, bf16[2,480,128]{2,1,0:T(8,128)(2,1)S(1)}, u32[]{:S(2)}, u32[]{:S(2)}) collective-permute-start(bf16[2,480,128]{2,1,0:T(8,128)(2,1)S(1)} %get-tuple-element.21), channel_id=1, source_target_pairs={{0,2},{1,3},{2,0},{3,1},{4,6},{5,7},{6,4},{7,5},{8,10},{9,11},{10,... | collective-permute-start | bytes 737288 | tf_op jit(solution)/shard_map/ppermute | solution.py:146
  33.1 6.8 %collective-permute-start.6 = (bf16[2,480,128]{2,1,0:T(8,128)(2,1)S(1)}, bf16[2,480,128]{2,1,0:T(8,128)(2,1)S(1)}, u32[]{:S(2)}, u32[]{:S(2)}) collective-permute-start(bf16[2,480,128]{2,1,0:T(8,128)(2,1)S(1)} %get-tuple-element.22), channel_id=1, source_target_pairs={{0,3},{1,0},{2,1},{3,2},{4,7},{5,4},{6,5},{7,6},{8,11},{9,8},{10,9... | collective-permute-start | bytes 737288 | tf_op jit(solution)/shard_map/ppermute | solution.py:146
  42.8 7.1 %copy-start.1 = (s32[8]{0:T(128)S(1)}, s32[8]{0:T(128)}, u32[]{:S(2)}) copy-start(s32[8]{0:T(128)} %param.8) | copy-start | bytes 100
  43.2 8.5 %collective-permute-start.7 = (bf16[1024,128]{1,0:T(8,128)(2,1)S(1)}, bf16[1024,128]{1,0:T(8,128)(2,1)S(1)}, u32[]{:S(2)}, u32[]{:S(2)}) collective-permute-start(bf16[1024,128]{1,0:T(8,128)(2,1)S(1)} %get-tuple-element.12), channel_id=1, source_target_pairs={{0,4},{1,5},{2,6},{3,7},{4,8},{5,9},{6,10},{7,11},{8,12},{9,13},{1... | collective-permute-start | bytes 786440 | tf_op jit(solution)/shard_map/ppermute | solution.py:168
  45.2 10.7 %collective-permute-start.8 = (bf16[1024,128]{1,0:T(8,128)(2,1)S(1)}, bf16[1024,128]{1,0:T(8,128)(2,1)S(1)}, u32[]{:S(2)}, u32[]{:S(2)}) collective-permute-start(bf16[1024,128]{1,0:T(8,128)(2,1)S(1)} %get-tuple-element.14), channel_id=1, source_target_pairs={{0,8},{1,9},{2,10},{3,11},{4,12},{5,13},{6,14},{7,15},{8,0},{9,1},... | collective-permute-start | bytes 786440 | tf_op jit(solution)/shard_map/ppermute | solution.py:168
  48.8 7.2 %collective-permute-start.9 = (bf16[1024,128]{1,0:T(8,128)(2,1)S(1)}, bf16[1024,128]{1,0:T(8,128)(2,1)S(1)}, u32[]{:S(2)}, u32[]{:S(2)}) collective-permute-start(bf16[1024,128]{1,0:T(8,128)(2,1)S(1)} %get-tuple-element.13), channel_id=1, source_target_pairs={{0,12},{1,13},{2,14},{3,15},{4,0},{5,1},{6,2},{7,3},{8,4},{9,5},{1... | collective-permute-start | bytes 786440 | tf_op jit(solution)/shard_map/ppermute | solution.py:168

commit v4 on v3

--- a/solution.py
+++ b/solution.py
@@ -79,27 +79,19 @@
     reduce_pos = jnp.where(first_core, z_index, y_index)
 
     swap = [(p, p ^ 1) for p in range(pairs_count)]
-    ring = [(2 * x, 2 * ((x + 1) % chips)) for x in range(chips)] + [
-        (2 * x + 1, 2 * ((x - 1) % chips) + 1) for x in range(chips)
-    ]
+    chip_up = [(p, 2 * ((p // 2 + 1) % chips) + p % 2) for p in range(pairs_count)]
+    chip_down = [(p, 2 * ((p // 2 - 1) % chips) + p % 2) for p in range(pairs_count)]
     partner = lax.ppermute(own, "pairs", swap)
-    here = jnp.where(first_core, jnp.stack([own, partner]), jnp.stack([partner, own]))
-    near = lax.ppermute(here, "pairs", ring)
-    relay = jnp.where(first_core, near[:, :half_rows], near[:, half_rows:])
-    far_part = lax.ppermute(relay, "pairs", ring)
-    other = lax.ppermute(jnp.concatenate([near, far_part], axis=1), "pairs", swap)
-    other_near = other[:, :spec_rows]
-    other_far = other[:, spec_rows:]
-    next_chip = jnp.where(first_core, other_near, near)
-    prev_chip = jnp.where(first_core, near, other_near)
-    far_chip = jnp.where(
-        first_core,
-        jnp.concatenate([far_part, other_far], axis=1),
-        jnp.concatenate([other_far, far_part], axis=1),
-    )
-    table = jnp.stack([here, next_chip, far_chip, prev_chip]).reshape(
-        (pairs_count,) + own.shape
-    )
+    from_below = lax.ppermute(own, "pairs", chip_up)
+    from_above = lax.ppermute(own, "pairs", chip_down)
+    far_low = lax.ppermute(from_below[:half_rows], "pairs", chip_up)
+    far_high = lax.ppermute(from_above[half_rows:], "pairs", chip_down)
+    mine = jnp.stack([own, from_above, jnp.concatenate([far_low, far_high]), from_below])
+    theirs = lax.ppermute(mine[1:], "pairs", swap)
+    theirs = jnp.concatenate([partner[None], theirs])
+    table = jnp.where(
+        first_core, jnp.stack([mine, theirs], axis=1), jnp.stack([theirs, mine], axis=1)
+    ).reshape((pairs_count,) + own.shape)
     own_pairs = lax.dynamic_index_in_dim(pair_list, owner_index, 0, keepdims=False)
     live_slots = jnp.arange(slot_count, dtype=jnp.int32) < pair_count[owner_index]
     position = ((own_pairs // 2 - chip) % chips) * 2 + own_pairs % 2
@@ -108,64 +100,103 @@
     left5 = left.reshape((slot_count, spec_rows, side, side, rows))
     left_view = jnp.where(first_core, left5, jnp.swapaxes(left5, 2, 3))
     packed_rows = spec_rows * side * rows // block_width
+    packs = jnp.transpose(left_view, (3, 0, 1, 2, 4)).reshape(
+        (side, slot_count, packed_rows, block_width)
+    )
 
     def rows_for(pos):
-        picked = lax.dynamic_index_in_dim(left_view, pos, axis=3, keepdims=False)
-        return picked.reshape((slot_count, packed_rows, block_width))
-
-    def gather_perm(d):
+        return lax.dynamic_index_in_dim(packs, pos % side, 0, keepdims=False)
+
+    def axis_perm(d, gather):
         perm = []
         for p in range(pairs_count):
+            along_y = (p % 2 == 0) == gather
             for z in range(side):
                 for y in range(side):
                     src = (p * side + z) * side + y
-                    if p % 2 == 0:
+                    if along_y:
                         dst = (p * side + z) * side + (y + d) % side
                     else:
                         dst = (p * side + (z + d) % side) * side + y
                     perm.append((src, dst))
         return perm
 
-    def reduce_perm(e):
-        perm = []
-        for p in range(pairs_count):
-            for z in range(side):
-                for y in range(side):
-                    src = (p * side + z) * side + y
-                    if p % 2 == 0:
-                        dst = (p * side + (z + e) % side) * side + y
-                    else:
-                        dst = (p * side + z) * side + (y + e) % side
-                    perm.append((src, dst))
-        return perm
-
     axes = ("pairs", "z", "y")
-    pieces = [jnp.concatenate([right, rows_for(gather_pos)], axis=1)]
-    for d in range(1, side):
-        message = jnp.concatenate([right, rows_for((gather_pos + d) % side)], axis=1)
-        pieces.append(lax.ppermute(message, axes, gather_perm(d)))
-    gathered = jnp.stack(pieces)
-    right_all = gathered[:, :, :spec_rows].reshape(
-        (side, slot_count, seg_dev, 2, FREQS, block_width)
-    )
-    left_all = gathered[:, :, spec_rows:].reshape(
-        (side, slot_count, seg_dev, 2, FREQS, side * rows)
-    )
+    half_pack = packed_rows // 2
+    half_spec = spec_rows // 2
+    up_msg = jnp.concatenate(
+        [right, rows_for(gather_pos + 1), rows_for(gather_pos + 2)[:, :half_pack]], axis=1
+    )
+    down_msg = jnp.concatenate(
+        [right, rows_for(gather_pos - 1), rows_for(gather_pos + 2)[:, half_pack:]], axis=1
+    )
+    from_lower = lax.ppermute(up_msg, axes, axis_perm(1, True))
+    from_upper = lax.ppermute(down_msg, axes, axis_perm(-1, True))
+    relay_at = spec_rows + packed_rows
+    up_msg2 = jnp.concatenate([from_lower[:, :half_spec], from_lower[:, relay_at:]], axis=1)
+    down_msg2 = jnp.concatenate([from_upper[:, half_spec:spec_rows], from_upper[:, relay_at:]], axis=1)
+    far_lower = lax.ppermute(up_msg2, axes, axis_perm(1, True))
+    far_upper = lax.ppermute(down_msg2, axes, axis_perm(-1, True))
+    far_right = jnp.concatenate([far_lower[:, :half_spec], far_upper[:, :half_spec]], axis=1)
+    far_left = jnp.concatenate([far_lower[:, half_spec:], far_upper[:, half_spec:]], axis=1)
+    right_all = jnp.stack(
+        [right, from_lower[:, :spec_rows], from_upper[:, :spec_rows], far_right]
+    )
+    left_all = jnp.stack(
+        [
+            rows_for(gather_pos),
+            from_lower[:, spec_rows:relay_at],
+            from_upper[:, spec_rows:relay_at],
+            far_left,
+        ]
+    )
+    right_all = right_all.reshape((side, slot_count, seg_dev, 2, FREQS, block_width))
+    left_all = left_all.reshape((side, slot_count, seg_dev, 2, FREQS, side * rows))
     right_swapped = jnp.stack([right_all[:, :, :, 1], -right_all[:, :, :, 0]], axis=3)
     rhs = jnp.concatenate([right_all, right_swapped], axis=-1)
     partial_value = jnp.einsum(
         "akscfm,akscfn->kfmn", left_all, rhs, preferred_element_type=jnp.float32
     )
     partial_value = partial_value.reshape((slot_count, FREQS, side, rows, 2, block_width))
-    partial_value = jnp.transpose(partial_value, (2, 0, 4, 1, 3, 5)).astype(jnp.bfloat16)
+    partial_value = jnp.transpose(partial_value, (2, 0, 4, 1, 3, 5))
     chunk_rows = slot_count * 2 * FREQS * rows
+    half_chunk = chunk_rows // 2
     partial_value = partial_value.reshape((side, chunk_rows, block_width))
-    stacked = lax.dynamic_index_in_dim(partial_value, reduce_pos, 0, keepdims=False).astype(
-        jnp.float32
-    )
-    for e in range(1, side):
-        chunk = lax.dynamic_index_in_dim(partial_value, (reduce_pos + e) % side, 0, keepdims=False)
-        stacked = stacked + lax.ppermute(chunk, axes, reduce_perm(e)).astype(jnp.float32)
+    partial_bf = partial_value.astype(jnp.bfloat16)
+
+    def chunk_at(pos, values):
+        return lax.dynamic_index_in_dim(values, pos % side, 0, keepdims=False)
+
+    up_msg = jnp.concatenate(
+        [chunk_at(reduce_pos + 1, partial_bf)[half_chunk:], chunk_at(reduce_pos + 2, partial_bf)[:half_chunk]]
+    )
+    down_msg = jnp.concatenate(
+        [chunk_at(reduce_pos - 1, partial_bf)[:half_chunk], chunk_at(reduce_pos + 2, partial_bf)[half_chunk:]]
+    )
+    from_lower = lax.ppermute(up_msg, axes, axis_perm(1, False))
+    from_upper = lax.ppermute(down_msg, axes, axis_perm(-1, False))
+    up_msg2 = (
+        chunk_at(reduce_pos + 1, partial_value)[:half_chunk]
+        + from_lower[half_chunk:].astype(jnp.float32)
+    ).astype(jnp.bfloat16)
+    down_msg2 = (
+        chunk_at(reduce_pos - 1, partial_value)[half_chunk:]
+        + from_upper[half_chunk:].astype(jnp.float32)
+    ).astype(jnp.bfloat16)
+    far_lower = lax.ppermute(up_msg2, axes, axis_perm(1, False))
+    far_upper = lax.ppermute(down_msg2, axes, axis_perm(-1, False))
+    own_chunk = chunk_at(reduce_pos, partial_value)
+    low_half = (
+        own_chunk[:half_chunk]
+        + from_upper[:half_chunk].astype(jnp.float32)
+        + far_lower.astype(jnp.float32)
+    )
+    high_half = (
+        own_chunk[half_chunk:]
+        + from_lower[:half_chunk].astype(jnp.float32)
+        + far_upper.astype(jnp.float32)
+    )
+    stacked = jnp.concatenate([low_half, high_half])
     stacked = stacked.reshape((slot_count, 2, FREQS, rows, block_width))
     lag_weights = lag_table(seg_dev * side * side).reshape(2, FREQS, LAGS)
     correlation = jnp.einsum(

time: 58.8 us -> 66.9 us (1.14); the launches traced: 58.6 us -> 65.9 us
  starting transfers between devices: 14.8 us -> 18.9 us
  local copies, waits for them, and re-layouts: 8.94 us -> 10.9 us
  waiting for transfers between devices: 23.3 us -> 24.2 us
    ppermute x9 -> x13, starting transfers between devices: 14.7 us -> 18.9 us  [the longest x1 2.94 us: shards(): far_high = lax.ppermute(from_above[half_rows:], 'pairs', chip_down)]
    dynamic_slice x5 -> x1, local copies, waits for them, and re-layouts: 2.18 us -> 0.03 us  [rows_for(): return lax.dynamic_index_in_dim(packs, pos % side, 0, keepdims=False)]
    transpose x0 -> x1, local copies, waits for them, and re-layouts: none -> 1.91 us  [shards(): jnp.transpose(left_view, (3, 0, 1, 2, 4))]
    ppermute x9 -> x13, waiting for transfers between devices: 22.4 us -> 24.2 us  [the longest x1 5.7 us: shards(): far_lower = lax.ppermute(up_msg2, axes, axis_perm(1, False))]
    another operation x0 -> x9, local copies, waits for them, and re-layouts: none -> 1.24 us  [the longest x8 1.08 us: shards(): jnp.stack([rows_for(gather_pos), from_lower[:, spec_rows:relay_at], from_...]
    gather x1, local copies, waits for them, and re-layouts: 0.59 us -> 1.72 us  [shards(): right = jnp.take(table, position[:, 1], axis=0)]
    ppermute x1, waiting for transfers between devices: 0.83 us -> 0.01 us  [shards(): partner = lax.ppermute(own, 'pairs', swap)]
    reshape x6 -> x2, local copies, waits for them, and re-layouts: 4.08 us -> 3.61 us  [the longest x1 3.4 us: shards(): jnp.transpose(left_view, (3, 0, 1, 2, 4))]
  transfers between devices with their start and end apart: 10 -> 14, of which waited for: 8 -> 9; matrix products, arithmetic and copies ran while one was open for 3% -> 5% of each run, Pallas kernels for 0% -> 0%
where the time goes in v4:
time: 66.9 us; the launch traced here: 65.9 us
  waiting for transfers between devices  24.2 us (36%)
  starting transfers between devices  18.9 us (28%)
  local copies, waits for them, and re-layouts  10.9 us (16%)
  matrix products  9.4 us (14%)
  other arithmetic  2.04 us (3%)
    ppermute x1, waiting for transfers between devices, shards(): far_lower = lax.ppermute(up_msg2, axes, axis_perm(1, False))  5.7 us
    dot_general x1, matrix products, shards(): jnp.dot(records[0], band_table(), preferred_element_type=jnp.float32)  5 us
    ppermute x1, waiting for transfers between devices, shards(): from_lower = lax.ppermute(up_msg, axes, axis_perm(1, True))  4 us
    ppermute x1, waiting for transfers between devices, shards(): far_upper = lax.ppermute(down_msg2, axes, axis_perm(-1, False))  3.49 us
    reshape x1, local copies, waits for them, and re-layouts, shards(): jnp.transpose(left_view, (3, 0, 1, 2, 4))  3.4 us
    ppermute x1, waiting for transfers between devices, shards(): from_lower = lax.ppermute(up_msg, axes, axis_perm(1, False))  3.33 us
    ppermute x1, starting transfers between devices, shards(): far_high = lax.ppermute(from_above[half_rows:], 'pairs', chip_down)  2.94 us
    ppermute x1, starting transfers between devices, shards(): far_upper = lax.ppermute(down_msg2, axes, axis_perm(-1, True))  2.86 us
  transfers between devices with their start and end apart: 14, of which 9 were waited for; matrix products, arithmetic and copies ran while one was open for 5% of the time, Pallas kernels for 0%

profile of v4, /device:TPU:0, one launch (start us, length us, event | category | flops | bytes accessed | tf_op | source)
XLA Modules:
  0.0 65.9 jit_solution(13159419897714073420)
XLA Ops:
  0.0 5.0 %fusion.14 = f32[6,128,64]{1,2,0:T(8,128)S(1)} fusion(bf16[4096,64,1]{0,1,2:T(8,128)(2,1)} %constant.199, bf16[1,6,128,4096]{3,2,1,0:T(8,128)(2,1)} %param.6), kind=kOutput, calls=%fused_computation.15 | convolution fusion | flops 402653184 | bytes 7012352 | tf_op jit(solution)/shard_map/dot_general | solution.py:70
  5.1 0.1 multiply_convert_fusion.1
  5.2 1.6 %collective-permute-start.1 = (bf16[384,128]{1,0:T(8,128)(2,1)S(1)}, bf16[384,128]{1,0:T(8,128)(2,1)S(1)}, u32[]{:S(2)}, u32[]{:S(2)}) collective-permute-start(bf16[384,128]{1,0:T(8,128)(2,1)S(1)} %bitcast.119), channel_id=1, source_target_pairs={{0,32},{16,48},{32,64},{48,80},{64,96},{80,112},{96,0},{112,16},{1... | collective-permute-start | bytes 294920 | tf_op jit(solution)/shard_map/ppermute | solution.py:85
  6.8 1.7 %collective-permute-start = (bf16[384,128]{1,0:T(8,128)(2,1)S(1)}, bf16[384,128]{1,0:T(8,128)(2,1)S(1)}, u32[]{:S(2)}, u32[]{:S(2)}) collective-permute-start(bf16[384,128]{1,0:T(8,128)(2,1)S(1)} %bitcast.120), channel_id=1, source_target_pairs={{0,96},{16,112},{32,0},{48,16},{64,32},{80,48},{96,64},{112,80},{1... | collective-permute-start | bytes 294920 | tf_op jit(solution)/shard_map/ppermute | solution.py:86
  8.5 0.0 collective-permute-start.4
  8.5 0.2 fusion.48
  8.7 0.2 slice_reduce_fusion.1
  8.9 2.1 %collective-permute-done.1 = bf16[384,128]{1,0:T(8,128)(2,1)S(1)} collective-permute-done((bf16[384,128]{1,0:T(8,128)(2,1)S(1)}, bf16[384,128]{1,0:T(8,128)(2,1)S(1)}, u32[]{:S(2)}, u32[]{:S(2)}) %collective-permute-start.1) | collective-permute-done | bytes 98336 | tf_op jit(solution)/shard_map/ppermute | solution.py:85
  11.1 0.4 collective-permute-start.2
  11.4 0.0 collective-permute-done
  11.4 2.9 %collective-permute-start.3 = (bf16[192,128]{1,0:T(8,128)(2,1)S(1)}, bf16[192,128]{1,0:T(8,128)(2,1)S(1)}, u32[]{:S(2)}, u32[]{:S(2)}) collective-permute-start(bf16[192,128]{1,0:T(8,128)(2,1)S(1)} %slice.194), channel_id=1, source_target_pairs={{0,96},{16,112},{32,0},{48,16},{64,32},{80,48},{96,64},{112,80},{1... | collective-permute-start | bytes 147464 | tf_op jit(solution)/shard_map/ppermute | solution.py:88
  14.4 2.0 %collective-permute-done.2 = bf16[192,128]{1,0:T(8,128)(2,1)S(1)} collective-permute-done((bf16[192,128]{1,0:T(8,128)(2,1)S(1)}, bf16[192,128]{1,0:T(8,128)(2,1)S(1)}, u32[]{:S(2)}, u32[]{:S(2)}) %collective-permute-start.2) | collective-permute-done | bytes 49184 | tf_op jit(solution)/shard_map/ppermute | solution.py:87
  16.4 0.0 collective-permute-done.3
  16.4 0.1 collective-permute-start.5
  16.5 0.1 maximum_bitcast_fusion
  16.6 0.0 collective-permute-done.4
  16.6 1.5 %collective-permute-done.5 = bf16[3,384,128]{2,1,0:T(8,128)(2,1)S(1)} collective-permute-done((bf16[3,384,128]{2,1,0:T(8,128)(2,1)S(1)}, bf16[3,384,128]{2,1,0:T(8,128)(2,1)S(1)}, u32[]{:S(2)}, u32[]{:S(2)}) %collective-permute-start.5) | collective-permute-done | bytes 294944 | tf_op jit(solution)/shard_map/ppermute | solution.py:90
  18.1 0.1 maximum_select_fusion
  18.2 0.6 gather_fusion
  18.8 0.1 broadcast_select_fusion.1
  18.9 0.2 copy.6
  19.1 0.0 copy-done.1
  19.1 1.9 %copy.8 = bf16[4,2,384,4,8]{4,3,2,1,0:T(4,128)(2,1)S(1)} copy(bf16[4,2,384,4,8]{2,4,0,3,1:T(8,128)(2,1)S(1)} %fusion.35) | data formatting | bytes 393216 | tf_op jit(solution)/shard_map/transpose | solution.py:103
  21.1 3.4 %reshape.77 = bf16[4,2,96,128]{3,2,1,0:T(8,128)(2,1)S(1)} reshape(bf16[4,2,384,4,8]{4,3,2,1,0:T(4,128)(2,1)S(1)} %copy.8) | data formatting | bytes 393216 | tf_op jit(solution)/shard_map/reshape | solution.py:103
  24.5 1.7 %gather_fusion.1 = bf16[2,384,128]{2,1,0:T(8,128)(2,1)S(1)} fusion(bf16[8,384,128]{2,1,0:T(8,128)(2,1)} %bitcast.110, s32[1024]{0:T(1024)S(1)} %pad_clamp_fusion), kind=kCustom, calls=%fused_computation.1.clone | custom fusion | bytes 393224 | tf_op jit(solution)/shard_map/jit(_take)/gather | solution.py:99
  26.2 0.1 broadcast_select_fusion
  26.3 0.1 fusion.26
  26.4 1.7 %collective-permute-start.6 = (bf16[2,528,128]{2,1,0:T(8,128)(2,1)S(1)}, bf16[2,528,128]{2,1,0:T(8,128)(2,1)S(1)}, u32[]{:S(2)}, u32[]{:S(2)}) collective-permute-start(bf16[2,528,128]{2,1,0:T(8,128)(2,1)S(1)} %get-tuple-element.25), channel_id=1, source_target_pairs={{0,1},{1,2},{2,3},{3,0},{4,5},{5,6},{6,7},{7,4},{8,9},{9,10},{10,1... | collective-permute-start | bytes 811016 | tf_op jit(solution)/shard_map/ppermute | solution.py:133
  28.1 1.6 %collective-permute-start.7 = (bf16[2,528,128]{2,1,0:T(8,128)(2,1)S(1)}, bf16[2,528,128]{2,1,0:T(8,128)(2,1)S(1)}, u32[]{:S(2)}, u32[]{:S(2)}) collective-permute-start(bf16[2,528,128]{2,1,0:T(8,128)(2,1)S(1)} %get-tuple-element.24), channel_id=1, source_target_pairs={{0,3},{1,0},{2,1},{3,2},{4,7},{5,4},{6,5},{7,6},{8,11},{9,8},{10,9... | collective-permute-start | bytes 811016 | tf_op jit(solution)/shard_map/ppermute | solution.py:134
  29.7 0.1 stack.71
  29.9 0.1 copy.9
  30.0 0.1 copy_dynamic-update-slice_fusion.3
  30.1 4.0 %collective-permute-done.6 = bf16[2,528,128]{2,1,0:T(8,128)(2,1)S(1)} collective-permute-done((bf16[2,528,128]{2,1,0:T(8,128)(2,1)S(1)}, bf16[2,528,128]{2,1,0:T(8,128)(2,1)S(1)}, u32[]{:S(2)}, u32[]{:S(2)}) %collective-permute-start.6) | collective-permute-done | bytes 270368 | tf_op jit(solution)/shard_map/ppermute | solution.py:133
  34.2 0.5 collective-permute-start.8
  34.7 0.0 collective-permute-done.7
  34.8 2.9 %collective-permute-start.9 = (bf16[2,240,128]{2,1,0:T(8,128)(2,1)S(1)}, bf16[2,240,128]{2,1,0:T(8,128)(2,1)S(1)}, u32[]{:S(2)}, u32[]{:S(2)}) collective-permute-start(bf16[2,240,128]{2,1,0:T(8,128)(2,1)S(1)} %pad_maximum_fusion.8), channel_id=1, source_target_pairs={{0,3},{1,0},{2,1},{3,2},{4,7},{5,4},{6,5},{7,6},{8,11},{9,8},{10,9... | collective-permute-start | bytes 368648 | tf_op jit(solution)/shard_map/ppermute | solution.py:139
  37.6 0.1 stack.72
  37.8 0.1 copy.10
  37.9 0.1 stack.73
  38.1 0.1 copy.11
  38.2 0.2 copy_dynamic-update-slice_fusion.2
  38.4 0.2 copy_dynamic-update-slice_fusion.1
  38.6 1.8 %collective-permute-done.8 = bf16[2,240,128]{2,1,0:T(8,128)(2,1)S(1)} collective-permute-done((bf16[2,240,128]{2,1,0:T(8,128)(2,1)S(1)}, bf16[2,240,128]{2,1,0:T(8,128)(2,1)S(1)}, u32[]{:S(2)}, u32[]{:S(2)}) %collective-permute-start.8) | collective-permute-done | bytes 122912 | tf_op jit(solution)/shard_map/ppermute | solution.py:138
  40.4 0.1 stack.74
  40.5 0.1 copy.12
  40.7 0.2 copy_dynamic-update-slice_fusion
  40.9 0.2 fusion.55
  41.1 1.8 %fusion.8 = f32[2,32,4,8,2,128]{5,3,4,2,1,0:T(8,128)S(1)} fusion(bf16[4,2,6,1,32,128]{5,2,3,0,4,1:T(8,128)(2,1)S(1)} %get-tuple-element.19, bf16[4,2,6,1,32,128]{5,2,3,0,4,1:T(8,128)(2,1)S(1)} %get-tuple-element.18, bf16[4,2,6,2,32,128]{5,2,3,0,4,1:T(8,128)(2,1)S(1)} %copy_dynamic-update-slice_fusion, bf16[1,2,6,2,32,32]{5,2,3,0,4,1:T(8,128)(2,1)S(1)} %copy.12, ...), kind=kOutput, calls=%fused_computation.10 | convolution fusion | flops 55345152 | bytes 3866624 | tf_op jit(solution)/shard_map/akscfm,akscfn->kfmn/dot_general | solution.py:157
  42.9 0.2 copy.17
  43.1 0.0 copy-start.2
  43.1 0.1 bitcast_convert_fusion
  43.3 2.1 %collective-permute-start.11 = (bf16[1024,128]{1,0:T(8,128)(2,1)S(1)}, bf16[1024,128]{1,0:T(8,128)(2,1)S(1)}, u32[]{:S(2)}, u32[]{:S(2)}) collective-permute-start(bf16[1024,128]{1,0:T(8,128)(2,1)S(1)} %pad_maximum_fusion.5), channel_id=1, source_target_pairs={{0,4},{1,5},{2,6},{3,7},{4,8},{5,9},{6,10},{7,11},{8,12},{9,13},{1... | collective-permute-start | bytes 786440 | tf_op jit(solution)/shard_map/ppermute | solution.py:176
  45.4 0.6 dynamic_slice.53
  46.0 2.5 %collective-permute-start.10 = (bf16[1024,128]{1,0:T(8,128)(2,1)S(1)}, bf16[1024,128]{1,0:T(8,128)(2,1)S(1)}, u32[]{:S(2)}, u32[]{:S(2)}) collective-permute-start(bf16[1024,128]{1,0:T(8,128)(2,1)S(1)} %pad_maximum_fusion.4), channel_id=1, source_target_pairs={{0,12},{1,13},{2,14},{3,15},{4,0},{5,1},{6,2},{7,3},{8,4},{9,5},{1... | collective-permute-start | bytes 786440 | tf_op jit(solution)/shard_map/ppermute | solution.py:177
  48.5 3.3 %collective-permute-done.11 = bf16[1024,128]{1,0:T(8,128)(2,1)S(1)} collective-permute-done((bf16[1024,128]{1,0:T(8,128)(2,1)S(1)}, bf16[1024,128]{1,0:T(8,128)(2,1)S(1)}, u32[]{:S(2)}, u32[]{:S(2)}) %collective-permute-start.11) | collective-permute-done | bytes 262176 | tf_op jit(solution)/shard_map/ppermute | solution.py:176
  51.9 0.1 collective-permute-start.12
  52.0 0.2 fusion.47
  52.1 0.3 collective-permute-done.10
  52.4 5.7 %collective-permute-done.12 = bf16[512,128]{1,0:T(8,128)(2,1)S(1)} collective-permute-done((bf16[512,128]{1,0:T(8,128)(2,1)S(1)}, bf16[512,128]{1,0:T(8,128)(2,1)S(1)}, u32[]{:S(2)}, u32[]{:S(2)}) %collective-permute-start.12) | collective-permute-done | bytes 131104 | tf_op jit(solution)/shard_map/ppermute | solution.py:186
  58.1 0.1 fusion.34
  58.2 0.9 %collective-permute-start.13 = (bf16[512,128]{1,0:T(8,128)(2,1)S(1)}, bf16[512,128]{1,0:T(8,128)(2,1)S(1)}, u32[]{:S(2)}, u32[]{:S(2)}) collective-permute-start(bf16[512,128]{1,0:T(8,128)(2,1)S(1)} %get-tuple-element.13), channel_id=1, source_target_pairs={{0,12},{1,13},{2,14},{3,15},{4,0},{5,1},{6,2},{7,3},{8,4},{9,5},{1... | collective-permute-start | bytes 393224 | tf_op jit(solution)/shard_map/ppermute | solution.py:187
  59.1 0.6 compare_convert_fusion
  59.8 3.5 %collective-permute-done.13 = bf16[512,128]{1,0:T(8,128)(2,1)S(1)} collective-permute-done((bf16[512,128]{1,0:T(8,128)(2,1)S(1)}, bf16[512,128]{1,0:T(8,128)(2,1)S(1)}, u32[]{:S(2)}, u32[]{:S(2)}) %collective-permute-start.13) | collective-permute-done | bytes 131104 | tf_op jit(solution)/shard_map/ppermute | solution.py:187
  63.3 2.6 %fusion.13 = bf16[1,2,8,128,128]{4,3,2,1,0:T(8,128)(2,1)} fusion(f32[2,32,128,1,1]{2,1,0,4,3:T(8,128)S(1)} %bitcast.123, f32[2,2,32,8,128]{4,3,2,1,0:T(8,128)S(1)} %bitcast.107, f32[2]{0:T(128)S(1)} %compare_convert_fusion), kind=kOutput, calls=%fused_computation.14 | convolution fusion | flops 201850880 | bytes 1081352 | tf_op jit(solution)/shard_map/kpfrj,pft->krjt/dot_general | solution.py:202
  (47 shorter events, 0.6 us)
Async XLA Ops:
  0.0 8.5 %copy-start = (s32[8,2,2]{0,2,1:T(2,128)S(1)}, s32[8,2,2]{0,2,1:T(2,128)}, u32[]{:S(2)}) copy-start(s32[8,2,2]{0,2,1:T(2,128)} %param.7) | copy-start | bytes 388
  5.2 5.9 %collective-permute-start.1 = (bf16[384,128]{1,0:T(8,128)(2,1)S(1)}, bf16[384,128]{1,0:T(8,128)(2,1)S(1)}, u32[]{:S(2)}, u32[]{:S(2)}) collective-permute-start(bf16[384,128]{1,0:T(8,128)(2,1)S(1)} %bitcast.119), channel_id=1, source_target_pairs={{0,32},{16,48},{32,64},{48,80},{64,96},{80,112},{96,0},{112,16},{1... | collective-permute-start | bytes 294920 | tf_op jit(solution)/shard_map/ppermute | solution.py:85
  6.8 4.6 %collective-permute-start = (bf16[384,128]{1,0:T(8,128)(2,1)S(1)}, bf16[384,128]{1,0:T(8,128)(2,1)S(1)}, u32[]{:S(2)}, u32[]{:S(2)}) collective-permute-start(bf16[384,128]{1,0:T(8,128)(2,1)S(1)} %bitcast.120), channel_id=1, source_target_pairs={{0,96},{16,112},{32,0},{48,16},{64,32},{80,48},{96,64},{112,80},{1... | collective-permute-start | bytes 294920 | tf_op jit(solution)/shard_map/ppermute | solution.py:86
  8.5 8.1 %collective-permute-start.4 = (bf16[384,128]{1,0:T(8,128)(2,1)S(1)}, bf16[384,128]{1,0:T(8,128)(2,1)S(1)}, u32[]{:S(2)}, u32[]{:S(2)}) collective-permute-start(bf16[384,128]{1,0:T(8,128)(2,1)S(1)} %bitcast.121), channel_id=1, source_target_pairs={{0,16},{16,0},{32,48},{48,32},{64,80},{80,64},{96,112},{112,96},{1... | collective-permute-start | bytes 294920 | tf_op jit(solution)/shard_map/ppermute | solution.py:84
  11.1 5.3 %collective-permute-start.2 = (bf16[192,128]{1,0:T(8,128)(2,1)S(1)}, bf16[192,128]{1,0:T(8,128)(2,1)S(1)}, u32[]{:S(2)}, u32[]{:S(2)}) collective-permute-start(bf16[192,128]{1,0:T(8,128)(2,1)S(1)} %slice.193), channel_id=1, source_target_pairs={{0,32},{16,48},{32,64},{48,80},{64,96},{80,112},{96,0},{112,16},{1... | collective-permute-start | bytes 147464 | tf_op jit(solution)/shard_map/ppermute | solution.py:87
  11.4 4.9 %collective-permute-start.3 = (bf16[192,128]{1,0:T(8,128)(2,1)S(1)}, bf16[192,128]{1,0:T(8,128)(2,1)S(1)}, u32[]{:S(2)}, u32[]{:S(2)}) collective-permute-start(bf16[192,128]{1,0:T(8,128)(2,1)S(1)} %slice.194), channel_id=1, source_target_pairs={{0,96},{16,112},{32,0},{48,16},{64,32},{80,48},{96,64},{112,80},{1... | collective-permute-start | bytes 147464 | tf_op jit(solution)/shard_map/ppermute | solution.py:88
  16.4 1.7 %collective-permute-start.5 = (bf16[3,384,128]{2,1,0:T(8,128)(2,1)S(1)}, bf16[3,384,128]{2,1,0:T(8,128)(2,1)S(1)}, u32[]{:S(2)}, u32[]{:S(2)}) collective-permute-start(bf16[3,384,128]{2,1,0:T(8,128)(2,1)S(1)} %pad_maximum_fusion.1), channel_id=1, source_target_pairs={{0,16},{16,0},{32,48},{48,32},{64,80},{80,64},{96,112},{112,96},{1... | collective-permute-start | bytes 884744 | tf_op jit(solution)/shard_map/ppermute | solution.py:90
  18.2 0.9 %copy-start.1 = (bf16[4,2,384,128]{3,2,1,0:T(8,128)(2,1)}, bf16[4,2,384,128]{3,2,1,0:T(8,128)(2,1)S(1)}, u32[]{:S(2)}) copy-start(bf16[4,2,384,128]{3,2,1,0:T(8,128)(2,1)S(1)} %maximum_select_fusion) | copy-start | bytes 2359300
  26.4 7.7 %collective-permute-start.6 = (bf16[2,528,128]{2,1,0:T(8,128)(2,1)S(1)}, bf16[2,528,128]{2,1,0:T(8,128)(2,1)S(1)}, u32[]{:S(2)}, u32[]{:S(2)}) collective-permute-start(bf16[2,528,128]{2,1,0:T(8,128)(2,1)S(1)} %get-tuple-element.25), channel_id=1, source_target_pairs={{0,1},{1,2},{2,3},{3,0},{4,5},{5,6},{6,7},{7,4},{8,9},{9,10},{10,1... | collective-permute-start | bytes 811016 | tf_op jit(solution)/shard_map/ppermute | solution.py:133
  28.1 6.6 %collective-permute-start.7 = (bf16[2,528,128]{2,1,0:T(8,128)(2,1)S(1)}, bf16[2,528,128]{2,1,0:T(8,128)(2,1)S(1)}, u32[]{:S(2)}, u32[]{:S(2)}) collective-permute-start(bf16[2,528,128]{2,1,0:T(8,128)(2,1)S(1)} %get-tuple-element.24), channel_id=1, source_target_pairs={{0,3},{1,0},{2,1},{3,2},{4,7},{5,4},{6,5},{7,6},{8,11},{9,8},{10,9... | collective-permute-start | bytes 811016 | tf_op jit(solution)/shard_map/ppermute | solution.py:134
  34.2 6.2 %collective-permute-start.8 = (bf16[2,240,128]{2,1,0:T(8,128)(2,1)S(1)}, bf16[2,240,128]{2,1,0:T(8,128)(2,1)S(1)}, u32[]{:S(2)}, u32[]{:S(2)}) collective-permute-start(bf16[2,240,128]{2,1,0:T(8,128)(2,1)S(1)} %pad_maximum_fusion.7), channel_id=1, source_target_pairs={{0,1},{1,2},{2,3},{3,0},{4,5},{5,6},{6,7},{7,4},{8,9},{9,10},{10,1... | collective-permute-start | bytes 368648 | tf_op jit(solution)/shard_map/ppermute | solution.py:138
  34.8 5.6 %collective-permute-start.9 = (bf16[2,240,128]{2,1,0:T(8,128)(2,1)S(1)}, bf16[2,240,128]{2,1,0:T(8,128)(2,1)S(1)}, u32[]{:S(2)}, u32[]{:S(2)}) collective-permute-start(bf16[2,240,128]{2,1,0:T(8,128)(2,1)S(1)} %pad_maximum_fusion.8), channel_id=1, source_target_pairs={{0,3},{1,0},{2,1},{3,2},{4,7},{5,4},{6,5},{7,6},{8,11},{9,8},{10,9... | collective-permute-start | bytes 368648 | tf_op jit(solution)/shard_map/ppermute | solution.py:139
  43.1 2.3 %copy-start.2 = (s32[8]{0:T(128)S(1)}, s32[8]{0:T(128)}, u32[]{:S(2)}) copy-start(s32[8]{0:T(128)} %param.8) | copy-start | bytes 100
  43.3 8.5 %collective-permute-start.11 = (bf16[1024,128]{1,0:T(8,128)(2,1)S(1)}, bf16[1024,128]{1,0:T(8,128)(2,1)S(1)}, u32[]{:S(2)}, u32[]{:S(2)}) collective-permute-start(bf16[1024,128]{1,0:T(8,128)(2,1)S(1)} %pad_maximum_fusion.5), channel_id=1, source_target_pairs={{0,4},{1,5},{2,6},{3,7},{4,8},{5,9},{6,10},{7,11},{8,12},{9,13},{1... | collective-permute-start | bytes 786440 | tf_op jit(solution)/shard_map/ppermute | solution.py:176
  46.0 6.4 %collective-permute-start.10 = (bf16[1024,128]{1,0:T(8,128)(2,1)S(1)}, bf16[1024,128]{1,0:T(8,128)(2,1)S(1)}, u32[]{:S(2)}, u32[]{:S(2)}) collective-permute-start(bf16[1024,128]{1,0:T(8,128)(2,1)S(1)} %pad_maximum_fusion.4), channel_id=1, source_target_pairs={{0,12},{1,13},{2,14},{3,15},{4,0},{5,1},{6,2},{7,3},{8,4},{9,5},{1... | collective-permute-start | bytes 786440 | tf_op jit(solution)/shard_map/ppermute | solution.py:177
  51.9 6.2 %collective-permute-start.12 = (bf16[512,128]{1,0:T(8,128)(2,1)S(1)}, bf16[512,128]{1,0:T(8,128)(2,1)S(1)}, u32[]{:S(2)}, u32[]{:S(2)}) collective-permute-start(bf16[512,128]{1,0:T(8,128)(2,1)S(1)} %fusion.32), channel_id=1, source_target_pairs={{0,4},{1,5},{2,6},{3,7},{4,8},{5,9},{6,10},{7,11},{8,12},{9,13},{1... | collective-permute-start | bytes 393224 | tf_op jit(solution)/shard_map/ppermute | solution.py:186
  58.2 5.0 %collective-permute-start.13 = (bf16[512,128]{1,0:T(8,128)(2,1)S(1)}, bf16[512,128]{1,0:T(8,128)(2,1)S(1)}, u32[]{:S(2)}, u32[]{:S(2)}) collective-permute-start(bf16[512,128]{1,0:T(8,128)(2,1)S(1)} %get-tuple-element.13), channel_id=1, source_target_pairs={{0,12},{1,13},{2,14},{3,15},{4,0},{5,1},{6,2},{7,3},{8,4},{9,5},{1... | collective-permute-start | bytes 393224 | tf_op jit(solution)/shard_map/ppermute | solution.py:187

commit v5 on v3

--- a/solution.py
+++ b/solution.py
@@ -79,39 +79,34 @@
     reduce_pos = jnp.where(first_core, z_index, y_index)
 
     swap = [(p, p ^ 1) for p in range(pairs_count)]
-    ring = [(2 * x, 2 * ((x + 1) % chips)) for x in range(chips)] + [
-        (2 * x + 1, 2 * ((x - 1) % chips) + 1) for x in range(chips)
-    ]
+
+    def chip_shift(d):
+        return [(p, 2 * ((p // 2 + d) % chips) + p % 2) for p in range(pairs_count)]
+
     partner = lax.ppermute(own, "pairs", swap)
-    here = jnp.where(first_core, jnp.stack([own, partner]), jnp.stack([partner, own]))
-    near = lax.ppermute(here, "pairs", ring)
-    relay = jnp.where(first_core, near[:, :half_rows], near[:, half_rows:])
-    far_part = lax.ppermute(relay, "pairs", ring)
-    other = lax.ppermute(jnp.concatenate([near, far_part], axis=1), "pairs", swap)
-    other_near = other[:, :spec_rows]
-    other_far = other[:, spec_rows:]
-    next_chip = jnp.where(first_core, other_near, near)
-    prev_chip = jnp.where(first_core, near, other_near)
-    far_chip = jnp.where(
-        first_core,
-        jnp.concatenate([far_part, other_far], axis=1),
-        jnp.concatenate([other_far, far_part], axis=1),
-    )
-    table = jnp.stack([here, next_chip, far_chip, prev_chip]).reshape(
-        (pairs_count,) + own.shape
-    )
+    from_below = lax.ppermute(own, "pairs", chip_shift(1))
+    from_above = lax.ppermute(own, "pairs", chip_shift(-1))
+    from_far = lax.ppermute(own, "pairs", chip_shift(2))
+    mine = jnp.stack([own, from_above, from_far, from_below])
+    theirs = lax.ppermute(mine[1:], "pairs", swap)
+    theirs = jnp.concatenate([partner[None], theirs])
+    table = jnp.where(
+        first_core, jnp.stack([mine, theirs], axis=1), jnp.stack([theirs, mine], axis=1)
+    ).reshape((pairs_count,) + own.shape)
     own_pairs = lax.dynamic_index_in_dim(pair_list, owner_index, 0, keepdims=False)
     live_slots = jnp.arange(slot_count, dtype=jnp.int32) < pair_count[owner_index]
     position = ((own_pairs // 2 - chip) % chips) * 2 + own_pairs % 2
     left = jnp.take(table, position[:, 0], axis=0)
     right = jnp.take(table, position[:, 1], axis=0)
-    left5 = left.reshape((slot_count, spec_rows, side, side, rows))
-    left_view = jnp.where(first_core, left5, jnp.swapaxes(left5, 2, 3))
+    left_t = jnp.transpose(left, (0, 2, 1)).reshape((slot_count, side, side, rows, spec_rows))
+    left_t = jnp.where(first_core, jnp.swapaxes(left_t, 1, 2), left_t)
     packed_rows = spec_rows * side * rows // block_width
+    packs = jnp.transpose(left_t, (1, 0, 2, 3, 4)).reshape(
+        (side, slot_count, packed_rows, block_width)
+    )
 
     def rows_for(pos):
-        picked = lax.dynamic_index_in_dim(left_view, pos, axis=3, keepdims=False)
-        return picked.reshape((slot_count, packed_rows, block_width))
+        return lax.dynamic_index_in_dim(packs, pos, 0, keepdims=False)
 
     def gather_perm(d):
         perm = []
@@ -148,9 +143,8 @@
     right_all = gathered[:, :, :spec_rows].reshape(
         (side, slot_count, seg_dev, 2, FREQS, block_width)
     )
-    left_all = gathered[:, :, spec_rows:].reshape(
-        (side, slot_count, seg_dev, 2, FREQS, side * rows)
-    )
+    left_all = gathered[:, :, spec_rows:].reshape((side, slot_count, side * rows, seg_dev, 2, FREQS))
+    left_all = jnp.transpose(left_all, (0, 1, 3, 4, 5, 2))
     right_swapped = jnp.stack([right_all[:, :, :, 1], -right_all[:, :, :, 0]], axis=3)
     rhs = jnp.concatenate([right_all, right_swapped], axis=-1)
     partial_value = jnp.einsum(

time: 58.8 us -> 53.1 us (0.903)
  waiting for transfers between devices: 23.3 us -> 19.7 us
  local copies, waits for them, and re-layouts: 8.94 us -> 5.55 us
  starting transfers between devices: 14.8 us -> 16.6 us
    ppermute x3 -> x4, waiting for transfers between devices: 12.3 us -> 7.17 us  [the longest x1 2.66 us: shards(): from_far = lax.ppermute(own, 'pairs', chip_shift(2))]
    reshape x4 -> x1, local copies, waits for them, and re-layouts: 3.22 us -> 0.1 us  [shards(): jnp.transpose(left_t, (1, 0, 2, 3, 4))]
    ppermute x3 -> x4, starting transfers between devices: 2.16 us -> 4.68 us  [the longest x1 2.91 us: shards(): from_above = lax.ppermute(own, 'pairs', chip_shift(-1))]
    ppermute x3, waiting for transfers between devices: 4.72 us -> 7.1 us  [shards(): lax.ppermute(chunk, axes, reduce_perm(e)).astype(jnp.float32)]
    dynamic_slice x5 -> x0, local copies, waits for them, and re-layouts: 2.18 us -> none  [rows_for(): picked = lax.dynamic_index_in_dim(left_view, pos, axis=3, keepdims=False)]
    reshape x1 -> x2, local copies, waits for them, and re-layouts: 0.32 us -> 2.22 us  [shards(): gathered[:, :, spec_rows:]]
    ppermute x1, waiting for transfers between devices: 0.83 us -> 0.01 us  [shards(): partner = lax.ppermute(own, 'pairs', swap)]
    ppermute x3, starting transfers between devices: 6.58 us -> 5.97 us  [shards(): lax.ppermute(chunk, axes, reduce_perm(e)).astype(jnp.float32)]
  transfers between devices with their start and end apart: 10 -> 11, of which waited for: 8 -> 8; matrix products, arithmetic and copies ran while one was open for 3% -> 4% of each run, Pallas kernels for 0% -> 0%
where the time goes in v5:
time: 53.1 us; the launch traced here: 52.9 us
  waiting for transfers between devices  19.7 us (37%)
  starting transfers between devices  16.6 us (31%)
  matrix products  8.93 us (17%)
  local copies, waits for them, and re-layouts  5.55 us (10%)
  other arithmetic  1.88 us (4%)
    ppermute x3, waiting for transfers between devices, shards(): lax.ppermute(chunk, axes, reduce_perm(e)).astype(jnp.float32)  7.1 us
    ppermute x3, starting transfers between devices, shards(): lax.ppermute(chunk, axes, reduce_perm(e)).astype(jnp.float32)  5.97 us
    ppermute x3, starting transfers between devices, shards(): pieces.append(lax.ppermute(message, axes, gather_perm(d)))  5.9 us
    ppermute x3, waiting for transfers between devices, shards(): pieces.append(lax.ppermute(message, axes, gather_perm(d)))  5.45 us
    dot_general x1, matrix products, shards(): jnp.dot(records[0], band_table(), preferred_element_type=jnp.float32)  5 us
    ppermute x1, starting transfers between devices, shards(): from_above = lax.ppermute(own, 'pairs', chip_shift(-1))  2.91 us
    ppermute x1, waiting for transfers between devices, shards(): from_far = lax.ppermute(own, 'pairs', chip_shift(2))  2.66 us
    dot_general x1, matrix products, shards(): jnp.einsum('kpfrj,pft->krjt', stacked, lag_weights, precision=lax.Precisi...  2.61 us
  transfers between devices with their start and end apart: 11, of which 8 were waited for; matrix products, arithmetic and copies ran while one was open for 4% of the time, Pallas kernels for 0%

profile of v5, /device:TPU:0, one launch (start us, length us, event | category | flops | bytes accessed | tf_op | source)
XLA Modules:
  0.0 52.9 jit_solution(2108136144638046033)
XLA Ops:
  0.0 0.0 copy-start
  0.0 5.0 %fusion.16 = f32[6,128,64]{1,2,0:T(8,128)S(1)} fusion(bf16[4096,64,1]{0,1,2:T(8,128)(2,1)} %constant.172, bf16[1,6,128,4096]{3,2,1,0:T(8,128)(2,1)} %param.6), kind=kOutput, calls=%fused_computation.16 | convolution fusion | flops 402653184 | bytes 7012352 | tf_op jit(solution)/shard_map/dot_general | solution.py:70
  5.1 0.1 multiply_convert_fusion.1
  5.2 2.9 %collective-permute-start = (bf16[384,128]{1,0:T(8,128)(2,1)S(1)}, bf16[384,128]{1,0:T(8,128)(2,1)S(1)}, u32[]{:S(2)}, u32[]{:S(2)}) collective-permute-start(bf16[384,128]{1,0:T(8,128)(2,1)S(1)} %bitcast.121), channel_id=1, source_target_pairs={{0,96},{16,112},{32,0},{48,16},{64,32},{80,48},{96,64},{112,80},{1... | collective-permute-start | bytes 294920 | tf_op jit(solution)/shard_map/ppermute | solution.py:88
  8.1 0.8 %collective-permute-start.1 = (bf16[384,128]{1,0:T(8,128)(2,1)S(1)}, bf16[384,128]{1,0:T(8,128)(2,1)S(1)}, u32[]{:S(2)}, u32[]{:S(2)}) collective-permute-start(bf16[384,128]{1,0:T(8,128)(2,1)S(1)} %bitcast.122), channel_id=1, source_target_pairs={{0,64},{16,80},{32,96},{48,112},{64,0},{80,16},{96,32},{112,48},{1... | collective-permute-start | bytes 294920 | tf_op jit(solution)/shard_map/ppermute | solution.py:89
  8.9 0.9 %collective-permute-start.2 = (bf16[384,128]{1,0:T(8,128)(2,1)S(1)}, bf16[384,128]{1,0:T(8,128)(2,1)S(1)}, u32[]{:S(2)}, u32[]{:S(2)}) collective-permute-start(bf16[384,128]{1,0:T(8,128)(2,1)S(1)} %bitcast.123), channel_id=1, source_target_pairs={{0,32},{16,48},{32,64},{48,80},{64,96},{80,112},{96,0},{112,16},{1... | collective-permute-start | bytes 294920 | tf_op jit(solution)/shard_map/ppermute | solution.py:87
  9.8 0.0 collective-permute-start.3
  9.8 0.0 copy-done
  9.8 0.2 fusion.36
  10.0 0.2 slice_reduce_fusion.1
  10.3 2.0 %collective-permute-done = bf16[384,128]{1,0:T(8,128)(2,1)S(1)} collective-permute-done((bf16[384,128]{1,0:T(8,128)(2,1)S(1)}, bf16[384,128]{1,0:T(8,128)(2,1)S(1)}, u32[]{:S(2)}, u32[]{:S(2)}) %collective-permute-start) | collective-permute-done | bytes 98336 | tf_op jit(solution)/shard_map/ppermute | solution.py:88
  12.3 2.7 %collective-permute-done.1 = bf16[384,128]{1,0:T(8,128)(2,1)S(1)} collective-permute-done((bf16[384,128]{1,0:T(8,128)(2,1)S(1)}, bf16[384,128]{1,0:T(8,128)(2,1)S(1)}, u32[]{:S(2)}, u32[]{:S(2)}) %collective-permute-start.1) | collective-permute-done | bytes 98336 | tf_op jit(solution)/shard_map/ppermute | solution.py:89
  14.9 1.0 %collective-permute-done.2 = bf16[384,128]{1,0:T(8,128)(2,1)S(1)} collective-permute-done((bf16[384,128]{1,0:T(8,128)(2,1)S(1)}, bf16[384,128]{1,0:T(8,128)(2,1)S(1)}, u32[]{:S(2)}, u32[]{:S(2)}) %collective-permute-start.2) | collective-permute-done | bytes 98336 | tf_op jit(solution)/shard_map/ppermute | solution.py:87
  16.0 0.1 collective-permute-start.4
  16.1 0.1 maximum_bitcast_fusion
  16.2 0.0 collective-permute-done.3
  16.2 1.5 %collective-permute-done.4 = bf16[3,384,128]{2,1,0:T(8,128)(2,1)S(1)} collective-permute-done((bf16[3,384,128]{2,1,0:T(8,128)(2,1)S(1)}, bf16[3,384,128]{2,1,0:T(8,128)(2,1)S(1)}, u32[]{:S(2)}, u32[]{:S(2)}) %collective-permute-start.4) | collective-permute-done | bytes 294944 | tf_op jit(solution)/shard_map/ppermute | solution.py:91
  17.7 0.1 maximum_select_fusion
  17.8 0.6 %gather_fusion.1 = bf16[2,384,128]{2,1,0:T(8,128)(2,1)S(1)} fusion(bf16[8,384,128]{2,1,0:T(8,128)(2,1)S(1)} %bitcast.106, s32[1024]{0:T(1024)S(1)} %pad_clamp_fusion), kind=kCustom, calls=%fused_computation.1.clone | custom fusion | bytes 393224 | tf_op jit(solution)/shard_map/jit(_take)/gather | solution.py:99
  18.4 0.1 select_bitcast_fusion
  18.5 0.2 copy.6
  18.7 0.1 reshape.59
  18.8 0.6 %gather_fusion = bf16[2,384,128]{2,1,0:T(8,128)(2,1)S(1)} fusion(bf16[8,384,128]{2,1,0:T(8,128)(2,1)S(1)} %bitcast.107, s32[1024]{0:T(1024)S(1)} %pad_clamp_fusion.1), kind=kCustom, calls=%fused_computation.clone | custom fusion | bytes 393224 | tf_op jit(solution)/shard_map/jit(_take)/gather | solution.py:100
  19.4 0.1 broadcast_select_fusion
  19.5 0.1 maximum_bitcast_fusion.2
  19.6 1.6 %collective-permute-start.5 = (bf16[2,480,128]{2,1,0:T(8,128)(2,1)S(1)}, bf16[2,480,128]{2,1,0:T(8,128)(2,1)S(1)}, u32[]{:S(2)}, u32[]{:S(2)}) collective-permute-start(bf16[2,480,128]{2,1,0:T(8,128)(2,1)S(1)} %get-tuple-element.18), channel_id=1, source_target_pairs={{0,1},{1,2},{2,3},{3,0},{4,5},{5,6},{6,7},{7,4},{8,9},{9,10},{10,1... | collective-permute-start | bytes 737288 | tf_op jit(solution)/shard_map/ppermute | solution.py:141
  21.3 2.9 %collective-permute-start.6 = (bf16[2,480,128]{2,1,0:T(8,128)(2,1)S(1)}, bf16[2,480,128]{2,1,0:T(8,128)(2,1)S(1)}, u32[]{:S(2)}, u32[]{:S(2)}) collective-permute-start(bf16[2,480,128]{2,1,0:T(8,128)(2,1)S(1)} %get-tuple-element.19), channel_id=1, source_target_pairs={{0,2},{1,3},{2,0},{3,1},{4,6},{5,7},{6,4},{7,5},{8,10},{9,11},{10,... | collective-permute-start | bytes 737288 | tf_op jit(solution)/shard_map/ppermute | solution.py:141
  24.2 1.3 %collective-permute-start.7 = (bf16[2,480,128]{2,1,0:T(8,128)(2,1)S(1)}, bf16[2,480,128]{2,1,0:T(8,128)(2,1)S(1)}, u32[]{:S(2)}, u32[]{:S(2)}) collective-permute-start(bf16[2,480,128]{2,1,0:T(8,128)(2,1)S(1)} %get-tuple-element.20), channel_id=1, source_target_pairs={{0,3},{1,0},{2,1},{3,2},{4,7},{5,4},{6,5},{7,6},{8,11},{9,8},{10,9... | collective-permute-start | bytes 737288 | tf_op jit(solution)/shard_map/ppermute | solution.py:141
  25.5 1.6 %collective-permute-done.5 = bf16[2,480,128]{2,1,0:T(8,128)(2,1)S(1)} collective-permute-done((bf16[2,480,128]{2,1,0:T(8,128)(2,1)S(1)}, bf16[2,480,128]{2,1,0:T(8,128)(2,1)S(1)}, u32[]{:S(2)}, u32[]{:S(2)}) %collective-permute-start.5) | collective-permute-done | bytes 245792 | tf_op jit(solution)/shard_map/ppermute | solution.py:141
  27.1 3.9 %collective-permute-done.6 = bf16[2,480,128]{2,1,0:T(8,128)(2,1)S(1)} collective-permute-done((bf16[2,480,128]{2,1,0:T(8,128)(2,1)S(1)}, bf16[2,480,128]{2,1,0:T(8,128)(2,1)S(1)}, u32[]{:S(2)}, u32[]{:S(2)}) %collective-permute-start.6) | collective-permute-done | bytes 245792 | tf_op jit(solution)/shard_map/ppermute | solution.py:141
  31.0 0.0 collective-permute-done.7
  31.0 0.1 pad_maximum_fusion
  31.1 0.3 reshape.60
  31.4 1.9 %copy.12 = bf16[4,2,32,6,2,32]{2,3,4,0,5,1:T(8,128)(2,1)S(1)} copy(bf16[4,2,32,6,2,32]{5,4,3,2,1,0:T(2,128)(2,1)S(1)} %reshape.60) | data formatting | bytes 393216 | tf_op jit(solution)/shard_map/reshape | solution.py:146
  33.3 0.5 %copy.15 = bf16[4,2,6,2,32,128]{5,2,3,0,4,1:T(8,128)(2,1)S(1)} copy(bf16[4,2,6,2,32,128]{5,4,3,2,1,0:T(8,128)(2,1)S(1)} %bitcast.104) | data formatting | bytes 1572864 | tf_op jit(solution)/shard_map/reshape | solution.py:143
  33.8 0.2 fusion.43
  34.0 1.3 %fusion.11 = bf16[2,32,4,8,2,128]{5,3,4,2,1,0:T(8,128)(2,1)S(1)} fusion(bf16[4,2,6,1,32,128]{5,2,3,0,4,1:T(8,128)(2,1)S(1)} %get-tuple-element.16, bf16[4,2,6,1,32,128]{5,2,3,0,4,1:T(8,128)(2,1)S(1)} %get-tuple-element.15, bf16[4,2,6,2,32,128]{5,2,3,0,4,1:T(8,128)(2,1)S(1)} %copy.15, bf16[4,2,32,6,2,32]{2,3,4,0,5,1:T(8,128)(2,1)S(1)} %copy.12), kind=kOutput, calls=%fused_computation.13 | convolution fusion | flops 55574528 | bytes 2818048 | tf_op jit(solution)/shard_map/akscfm,akscfn->kfmn/dot_general | solution.py:150
  35.3 0.0 copy-start.1
  35.4 0.3 copy.16
  35.6 0.1 dynamic-slice_bitcast_fusion.2
  35.7 4.1 %collective-permute-start.10 = (bf16[1024,128]{1,0:T(8,128)(2,1)S(1)}, bf16[1024,128]{1,0:T(8,128)(2,1)S(1)}, u32[]{:S(2)}, u32[]{:S(2)}) collective-permute-start(bf16[1024,128]{1,0:T(8,128)(2,1)S(1)} %get-tuple-element.13), channel_id=1, source_target_pairs={{0,12},{1,13},{2,14},{3,15},{4,0},{5,1},{6,2},{7,3},{8,4},{9,5},{1... | collective-permute-start | bytes 786440 | tf_op jit(solution)/shard_map/ppermute | solution.py:162
  39.8 0.0 collective-permute-start.8
  39.8 1.9 %collective-permute-start.9 = (bf16[1024,128]{1,0:T(8,128)(2,1)S(1)}, bf16[1024,128]{1,0:T(8,128)(2,1)S(1)}, u32[]{:S(2)}, u32[]{:S(2)}) collective-permute-start(bf16[1024,128]{1,0:T(8,128)(2,1)S(1)} %get-tuple-element.14), channel_id=1, source_target_pairs={{0,8},{1,9},{2,10},{3,11},{4,12},{5,13},{6,14},{7,15},{8,0},{9,1},... | collective-permute-start | bytes 786440 | tf_op jit(solution)/shard_map/ppermute | solution.py:162
  41.7 0.2 fusion.35
  41.8 0.0 copy-done.1
  41.8 0.6 %dynamic_slice.42 = s32[1]{0:T(128)} dynamic-slice(s32[8]{0:T(128)S(1)} %copy-done.1, s32[]{:T(128)S(6)} %select_n.126), dynamic_slice_sizes={1} | dynamic-slice | bytes 12 | tf_op jit(solution)/shard_map/dynamic_slice | solution.py:97
  42.4 0.6 %compare_convert_fusion = f32[2]{0:T(128)S(1)} fusion(s32[]{:T(128)} %bitcast.44), kind=kLoop, calls=%fused_computation.84 | loop fusion | flops 4 | bytes 12 | tf_op jit(solution)/shard_map/convert_element_type | solution.py:172
  43.1 0.6 %collective-permute-done.10 = bf16[1024,128]{1,0:T(8,128)(2,1)S(1)} collective-permute-done((bf16[1024,128]{1,0:T(8,128)(2,1)S(1)}, bf16[1024,128]{1,0:T(8,128)(2,1)S(1)}, u32[]{:S(2)}, u32[]{:S(2)}) %collective-permute-start.10) | collective-permute-done | bytes 262176 | tf_op jit(solution)/shard_map/ppermute | solution.py:162
  43.7 6.5 %collective-permute-done.8 = bf16[1024,128]{1,0:T(8,128)(2,1)S(1)} collective-permute-done((bf16[1024,128]{1,0:T(8,128)(2,1)S(1)}, bf16[1024,128]{1,0:T(8,128)(2,1)S(1)}, u32[]{:S(2)}, u32[]{:S(2)}) %collective-permute-start.8) | collective-permute-done | bytes 262176 | tf_op jit(solution)/shard_map/ppermute | solution.py:162
  50.2 0.0 collective-permute-done.9
  50.2 0.1 fusion.21
  50.3 2.6 %fusion.15 = bf16[1,2,8,128,128]{4,3,2,1,0:T(8,128)(2,1)} fusion(f32[2,32,128,1,1]{2,1,0,4,3:T(8,128)S(1)} %bitcast.126, f32[2,2,32,8,128]{4,3,2,1,0:T(8,128)S(1)} %bitcast.105, f32[2]{0:T(128)S(1)} %compare_convert_fusion), kind=kOutput, calls=%fused_computation.15 | convolution fusion | flops 201850880 | bytes 1081352 | tf_op jit(solution)/shard_map/kpfrj,pft->krjt/dot_general | solution.py:165
  (17 shorter events, 0.3 us)
Async XLA Ops:
  0.0 9.8 %copy-start = (s32[8,2,2]{0,2,1:T(2,128)S(1)}, s32[8,2,2]{0,2,1:T(2,128)}, u32[]{:S(2)}) copy-start(s32[8,2,2]{0,2,1:T(2,128)} %param.7) | copy-start | bytes 388
  5.2 7.1 %collective-permute-start = (bf16[384,128]{1,0:T(8,128)(2,1)S(1)}, bf16[384,128]{1,0:T(8,128)(2,1)S(1)}, u32[]{:S(2)}, u32[]{:S(2)}) collective-permute-start(bf16[384,128]{1,0:T(8,128)(2,1)S(1)} %bitcast.121), channel_id=1, source_target_pairs={{0,96},{16,112},{32,0},{48,16},{64,32},{80,48},{96,64},{112,80},{1... | collective-permute-start | bytes 294920 | tf_op jit(solution)/shard_map/ppermute | solution.py:88
  8.1 6.9 %collective-permute-start.1 = (bf16[384,128]{1,0:T(8,128)(2,1)S(1)}, bf16[384,128]{1,0:T(8,128)(2,1)S(1)}, u32[]{:S(2)}, u32[]{:S(2)}) collective-permute-start(bf16[384,128]{1,0:T(8,128)(2,1)S(1)} %bitcast.122), channel_id=1, source_target_pairs={{0,64},{16,80},{32,96},{48,112},{64,0},{80,16},{96,32},{112,48},{1... | collective-permute-start | bytes 294920 | tf_op jit(solution)/shard_map/ppermute | solution.py:89
  8.9 7.1 %collective-permute-start.2 = (bf16[384,128]{1,0:T(8,128)(2,1)S(1)}, bf16[384,128]{1,0:T(8,128)(2,1)S(1)}, u32[]{:S(2)}, u32[]{:S(2)}) collective-permute-start(bf16[384,128]{1,0:T(8,128)(2,1)S(1)} %bitcast.123), channel_id=1, source_target_pairs={{0,32},{16,48},{32,64},{48,80},{64,96},{80,112},{96,0},{112,16},{1... | collective-permute-start | bytes 294920 | tf_op jit(solution)/shard_map/ppermute | solution.py:87
  9.8 6.4 %collective-permute-start.3 = (bf16[384,128]{1,0:T(8,128)(2,1)S(1)}, bf16[384,128]{1,0:T(8,128)(2,1)S(1)}, u32[]{:S(2)}, u32[]{:S(2)}) collective-permute-start(bf16[384,128]{1,0:T(8,128)(2,1)S(1)} %bitcast.124), channel_id=1, source_target_pairs={{0,16},{16,0},{32,48},{48,32},{64,80},{80,64},{96,112},{112,96},{1... | collective-permute-start | bytes 294920 | tf_op jit(solution)/shard_map/ppermute | solution.py:86
  16.0 1.7 %collective-permute-start.4 = (bf16[3,384,128]{2,1,0:T(8,128)(2,1)S(1)}, bf16[3,384,128]{2,1,0:T(8,128)(2,1)S(1)}, u32[]{:S(2)}, u32[]{:S(2)}) collective-permute-start(bf16[3,384,128]{2,1,0:T(8,128)(2,1)S(1)} %pad_maximum_fusion.3), channel_id=1, source_target_pairs={{0,16},{16,0},{32,48},{48,32},{64,80},{80,64},{96,112},{112,96},{1... | collective-permute-start | bytes 884744 | tf_op jit(solution)/shard_map/ppermute | solution.py:91
  19.6 7.5 %collective-permute-start.5 = (bf16[2,480,128]{2,1,0:T(8,128)(2,1)S(1)}, bf16[2,480,128]{2,1,0:T(8,128)(2,1)S(1)}, u32[]{:S(2)}, u32[]{:S(2)}) collective-permute-start(bf16[2,480,128]{2,1,0:T(8,128)(2,1)S(1)} %get-tuple-element.18), channel_id=1, source_target_pairs={{0,1},{1,2},{2,3},{3,0},{4,5},{5,6},{6,7},{7,4},{8,9},{9,10},{10,1... | collective-permute-start | bytes 737288 | tf_op jit(solution)/shard_map/ppermute | solution.py:141
  21.3 9.7 %collective-permute-start.6 = (bf16[2,480,128]{2,1,0:T(8,128)(2,1)S(1)}, bf16[2,480,128]{2,1,0:T(8,128)(2,1)S(1)}, u32[]{:S(2)}, u32[]{:S(2)}) collective-permute-start(bf16[2,480,128]{2,1,0:T(8,128)(2,1)S(1)} %get-tuple-element.19), channel_id=1, source_target_pairs={{0,2},{1,3},{2,0},{3,1},{4,6},{5,7},{6,4},{7,5},{8,10},{9,11},{10,... | collective-permute-start | bytes 737288 | tf_op jit(solution)/shard_map/ppermute | solution.py:141
  24.2 6.8 %collective-permute-start.7 = (bf16[2,480,128]{2,1,0:T(8,128)(2,1)S(1)}, bf16[2,480,128]{2,1,0:T(8,128)(2,1)S(1)}, u32[]{:S(2)}, u32[]{:S(2)}) collective-permute-start(bf16[2,480,128]{2,1,0:T(8,128)(2,1)S(1)} %get-tuple-element.20), channel_id=1, source_target_pairs={{0,3},{1,0},{2,1},{3,2},{4,7},{5,4},{6,5},{7,6},{8,11},{9,8},{10,9... | collective-permute-start | bytes 737288 | tf_op jit(solution)/shard_map/ppermute | solution.py:141
  35.3 6.5 %copy-start.1 = (s32[8]{0:T(128)S(1)}, s32[8]{0:T(128)}, u32[]{:S(2)}) copy-start(s32[8]{0:T(128)} %param.8) | copy-start | bytes 100
  35.7 8.0 %collective-permute-start.10 = (bf16[1024,128]{1,0:T(8,128)(2,1)S(1)}, bf16[1024,128]{1,0:T(8,128)(2,1)S(1)}, u32[]{:S(2)}, u32[]{:S(2)}) collective-permute-start(bf16[1024,128]{1,0:T(8,128)(2,1)S(1)} %get-tuple-element.13), channel_id=1, source_target_pairs={{0,12},{1,13},{2,14},{3,15},{4,0},{5,1},{6,2},{7,3},{8,4},{9,5},{1... | collective-permute-start | bytes 786440 | tf_op jit(solution)/shard_map/ppermute | solution.py:162
  39.8 10.4 %collective-permute-start.8 = (bf16[1024,128]{1,0:T(8,128)(2,1)S(1)}, bf16[1024,128]{1,0:T(8,128)(2,1)S(1)}, u32[]{:S(2)}, u32[]{:S(2)}) collective-permute-start(bf16[1024,128]{1,0:T(8,128)(2,1)S(1)} %get-tuple-element.12), channel_id=1, source_target_pairs={{0,4},{1,5},{2,6},{3,7},{4,8},{5,9},{6,10},{7,11},{8,12},{9,13},{1... | collective-permute-start | bytes 786440 | tf_op jit(solution)/shard_map/ppermute | solution.py:162
  39.8 10.4 %collective-permute-start.9 = (bf16[1024,128]{1,0:T(8,128)(2,1)S(1)}, bf16[1024,128]{1,0:T(8,128)(2,1)S(1)}, u32[]{:S(2)}, u32[]{:S(2)}) collective-permute-start(bf16[1024,128]{1,0:T(8,128)(2,1)S(1)} %get-tuple-element.14), channel_id=1, source_target_pairs={{0,8},{1,9},{2,10},{3,11},{4,12},{5,13},{6,14},{7,15},{8,0},{9,1},... | collective-permute-start | bytes 786440 | tf_op jit(solution)/shard_map/ppermute | solution.py:162

commit v6 on v5

--- a/solution.py
+++ b/solution.py
@@ -5,6 +5,7 @@
 import ml_dtypes
 import numpy as np
 from jax import lax
+from jax.experimental import pallas as pl
 from jax.sharding import Mesh
 from jax.sharding import PartitionSpec as P
 
@@ -36,6 +37,31 @@
     return jnp.concatenate([jnp.cos(phase), -jnp.sin(phase)], axis=0) * (
         1.0 / math.sqrt(segments * FREQS)
     )
+
+
+def project_kernel(x_ref, table_ref, out_ref):
+    out_ref[...] = jnp.dot(x_ref[...], table_ref[...], preferred_element_type=jnp.float32)
+
+
+def band_project(samples):
+    count = samples.shape[0]
+    tile = 128
+    width = 2 * FREQS
+    return pl.pallas_call(
+        project_kernel,
+        out_shape=jax.ShapeDtypeStruct((count, width), jnp.float32),
+        grid=(count // tile,),
+        in_specs=[
+            pl.BlockSpec((tile, NSAMP), lambda i: (i, 0)),
+            pl.BlockSpec((NSAMP, width), lambda i: (0, 0)),
+        ],
+        out_specs=pl.BlockSpec((tile, width), lambda i: (i, 0)),
+        cost_estimate=pl.CostEstimate(
+            flops=2 * count * NSAMP * width,
+            transcendentals=0,
+            bytes_accessed=count * NSAMP * 2 + NSAMP * width * 2 + count * width * 4,
+        ),
+    )(samples, band_table())
 
 
 def whiten(spectra):
@@ -67,7 +93,8 @@
     width = 2 * FREQS
     spec_rows = seg_dev * width
     half_rows = spec_rows // 2
-    spectra = whiten(jnp.dot(records[0], band_table(), preferred_element_type=jnp.float32))
+    samples = records[0].reshape(seg_dev * block_width, NSAMP)
+    spectra = whiten(band_project(samples)).reshape(seg_dev, block_width, 2 * FREQS)
     own = jnp.transpose(spectra, (0, 2, 1)).reshape(spec_rows, block_width)
     owner_index = lax.axis_index("pairs")
     core = owner_index % 2
@@ -166,7 +193,7 @@
         "kpfrj,pft->krjt",
         stacked,
         lag_weights,
-        precision=lax.Precision.HIGHEST,
+        precision=lax.Precision.HIGH,
         preferred_element_type=jnp.float32,
     )
     masked = correlation * live_slots.astype(jnp.float32)[:, None, None, None]

time: 53.1 us -> 57.6 us (1.085)
  Pallas kernels: 0 us -> 6.72 us
  matrix products: 8.93 us -> 3.11 us
  other arithmetic: 1.88 us -> 5.03 us
    pallas_call x0 -> x1, Pallas kernels: none -> 6.72 us  [band_project(): pl.pallas_call(project_kernel, out_shape=jax.ShapeDtypeStruct((count, wid...]
    dot_general x1 -> x0, matrix products: 5 us -> none  [shards(): jnp.dot(records[0], band_table(), preferred_element_type=jnp.float32)]
    another operation x2, other arithmetic: 0.09 us -> 1.75 us
    reduce_sum x1, other arithmetic: 0.03 us -> 1.46 us  [whiten(): jnp.mean(power_bins, axis=-1, keepdims=True)]
    dot_general x1, matrix products: 2.61 us -> 1.8 us  [shards(): jnp.einsum('kpfrj,pft->krjt', stacked, lag_weights, precision=lax.Precisi...]
  transfers between devices with their start and end apart: 11 -> 11, of which waited for: 8 -> 8; matrix products, arithmetic and copies ran while one was open for 4% -> 3% of each run, Pallas kernels for 0% -> 0%
where the time goes in v6:
time: 57.6 us; the launch traced here: 57.4 us
  waiting for transfers between devices  19.7 us (34%)
  starting transfers between devices  16.6 us (29%)
  Pallas kernels  6.72 us (12%)
  local copies, waits for them, and re-layouts  5.9 us (10%)
  other arithmetic  5.03 us (9%)
  matrix products  3.11 us (5%)
    ppermute x3, waiting for transfers between devices, shards(): lax.ppermute(chunk, axes, reduce_perm(e)).astype(jnp.float32)  7.11 us
    pallas_call x1, Pallas kernels, band_project(): pl.pallas_call(project_kernel, out_shape=jax.ShapeDtypeStruct((count, wid...  6.72 us
    ppermute x3, starting transfers between devices, shards(): lax.ppermute(chunk, axes, reduce_perm(e)).astype(jnp.float32)  5.97 us
    ppermute x3, starting transfers between devices, shards(): pieces.append(lax.ppermute(message, axes, gather_perm(d)))  5.89 us
    ppermute x3, waiting for transfers between devices, shards(): pieces.append(lax.ppermute(message, axes, gather_perm(d)))  5.45 us
    ppermute x1, starting transfers between devices, shards(): from_above = lax.ppermute(own, 'pairs', chip_shift(-1))  2.91 us
    ppermute x1, waiting for transfers between devices, shards(): from_far = lax.ppermute(own, 'pairs', chip_shift(2))  2.66 us
    reshape x2, local copies, waits for them, and re-layouts, shards(): gathered[:, :, spec_rows:]  2.24 us
  transfers between devices with their start and end apart: 11, of which 8 were waited for; matrix products, arithmetic and copies ran while one was open for 3% of the time, Pallas kernels for 0%

profile of v6, /device:TPU:0, one launch (start us, length us, event | category | flops | bytes accessed | tf_op | source)
XLA Modules:
  0.0 57.4 jit_solution(14288798494404798072)
XLA Ops:
  0.0 0.0 copy-start
  0.0 6.7 %shard_map.46 = f32[768,64]{1,0:T(8,128)} custom-call(bf16[768,4096]{1,0:T(8,128)(2,1)} %bitcast.96, bf16[4096,64]{1,0:T(8,128)(2,1)} %constant.168.clone.table_ref), custom_call_target="tpu_custom_call" | custom-call | flops 402653184 | bytes 7012352 | tf_op jit(solution)/shard_map/pallas_call | solution.py:50
  6.7 0.0 copy-start.1
  6.7 1.5 %fusion.28 = (f32[768]{0:T(1024)S(1)}, f32[768,32]{1,0:T(8,128)S(1)}) fusion(f32[768,64]{1,0:T(8,128)} %shard_map.46), kind=kLoop, calls=%fused_computation.86 | loop fusion | flops 97536 | bytes 297984 | tf_op jit(solution)/shard_map/reduce_sum | solution.py:80
  8.2 1.6 %multiply_convert_fusion.1 = (bf16[768,32]{1,0:T(8,128)(2,1)S(1)}, f32[768,32]{1,0:T(8,128)S(1)}) fusion(f32[768,64]{1,0:T(8,128)} %shard_map.46, f32[768]{0:T(1024)S(1)} %broadcast_multiply_fusion, f32[768,32]{1,0:T(8,128)S(1)} %get-tuple-element.11), kind=kLoop, calls=%fused_computation.27 | loop fusion | flops 221184 | bytes 347136 | tf_op jit(solution)/shard_map/convert.4
  9.8 0.0 copy-done.1
  9.8 0.2 multiply_convert_fusion
  10.0 0.1 copy.16
  10.1 0.1 copy.15
  10.3 2.9 %collective-permute-start = (bf16[384,128]{1,0:T(8,128)(2,1)S(1)}, bf16[384,128]{1,0:T(8,128)(2,1)S(1)}, u32[]{:S(2)}, u32[]{:S(2)}) collective-permute-start(bf16[384,128]{1,0:T(8,128)(2,1)S(1)} %bitcast.118), channel_id=1, source_target_pairs={{0,96},{16,112},{32,0},{48,16},{64,32},{80,48},{96,64},{112,80},{1... | collective-permute-start | bytes 294920 | tf_op jit(solution)/shard_map/ppermute | solution.py:115
  13.2 0.8 %collective-permute-start.1 = (bf16[384,128]{1,0:T(8,128)(2,1)S(1)}, bf16[384,128]{1,0:T(8,128)(2,1)S(1)}, u32[]{:S(2)}, u32[]{:S(2)}) collective-permute-start(bf16[384,128]{1,0:T(8,128)(2,1)S(1)} %bitcast.119), channel_id=1, source_target_pairs={{0,64},{16,80},{32,96},{48,112},{64,0},{80,16},{96,32},{112,48},{1... | collective-permute-start | bytes 294920 | tf_op jit(solution)/shard_map/ppermute | solution.py:116
  14.0 0.9 %collective-permute-start.2 = (bf16[384,128]{1,0:T(8,128)(2,1)S(1)}, bf16[384,128]{1,0:T(8,128)(2,1)S(1)}, u32[]{:S(2)}, u32[]{:S(2)}) collective-permute-start(bf16[384,128]{1,0:T(8,128)(2,1)S(1)} %bitcast.120), channel_id=1, source_target_pairs={{0,32},{16,48},{32,64},{48,80},{64,96},{80,112},{96,0},{112,16},{1... | collective-permute-start | bytes 294920 | tf_op jit(solution)/shard_map/ppermute | solution.py:114
  14.9 0.0 collective-permute-start.3
  14.9 0.0 copy-done
  14.9 0.2 fusion.23
  15.1 0.2 slice_reduce_fusion.1
  15.3 2.0 %collective-permute-done = bf16[384,128]{1,0:T(8,128)(2,1)S(1)} collective-permute-done((bf16[384,128]{1,0:T(8,128)(2,1)S(1)}, bf16[384,128]{1,0:T(8,128)(2,1)S(1)}, u32[]{:S(2)}, u32[]{:S(2)}) %collective-permute-start) | collective-permute-done | bytes 98336 | tf_op jit(solution)/shard_map/ppermute | solution.py:115
  17.4 2.7 %collective-permute-done.1 = bf16[384,128]{1,0:T(8,128)(2,1)S(1)} collective-permute-done((bf16[384,128]{1,0:T(8,128)(2,1)S(1)}, bf16[384,128]{1,0:T(8,128)(2,1)S(1)}, u32[]{:S(2)}, u32[]{:S(2)}) %collective-permute-start.1) | collective-permute-done | bytes 98336 | tf_op jit(solution)/shard_map/ppermute | solution.py:116
  20.0 1.0 %collective-permute-done.2 = bf16[384,128]{1,0:T(8,128)(2,1)S(1)} collective-permute-done((bf16[384,128]{1,0:T(8,128)(2,1)S(1)}, bf16[384,128]{1,0:T(8,128)(2,1)S(1)}, u32[]{:S(2)}, u32[]{:S(2)}) %collective-permute-start.2) | collective-permute-done | bytes 98336 | tf_op jit(solution)/shard_map/ppermute | solution.py:114
  21.1 0.1 collective-permute-start.4
  21.2 0.1 maximum_bitcast_fusion
  21.2 0.0 collective-permute-done.3
  21.3 1.5 %collective-permute-done.4 = bf16[3,384,128]{2,1,0:T(8,128)(2,1)S(1)} collective-permute-done((bf16[3,384,128]{2,1,0:T(8,128)(2,1)S(1)}, bf16[3,384,128]{2,1,0:T(8,128)(2,1)S(1)}, u32[]{:S(2)}, u32[]{:S(2)}) %collective-permute-start.4) | collective-permute-done | bytes 294944 | tf_op jit(solution)/shard_map/ppermute | solution.py:118
  22.8 0.1 maximum_select_fusion
  22.9 0.1 copy.17
  23.0 0.6 %gather_fusion.1 = bf16[2,384,128]{2,1,0:T(8,128)(2,1)S(1)} fusion(bf16[8,384,128]{2,1,0:T(8,128)(2,1)S(1)} %bitcast.101, s32[1024]{0:T(1024)S(1)} %pad_clamp_fusion), kind=kCustom, calls=%fused_computation.1.clone | custom fusion | bytes 393224 | tf_op jit(solution)/shard_map/jit(_take)/gather | solution.py:126
  23.6 0.1 select_bitcast_fusion
  23.7 0.2 copy.18
  23.9 0.1 reshape.64
  24.0 0.6 %gather_fusion = bf16[2,384,128]{2,1,0:T(8,128)(2,1)S(1)} fusion(bf16[8,384,128]{2,1,0:T(8,128)(2,1)S(1)} %bitcast.102, s32[1024]{0:T(1024)S(1)} %pad_clamp_fusion.1), kind=kCustom, calls=%fused_computation.clone | custom fusion | bytes 393224 | tf_op jit(solution)/shard_map/jit(_take)/gather | solution.py:127
  24.6 0.1 broadcast_select_fusion
  24.7 0.1 maximum_bitcast_fusion.2
  24.8 1.6 %collective-permute-start.5 = (bf16[2,480,128]{2,1,0:T(8,128)(2,1)S(1)}, bf16[2,480,128]{2,1,0:T(8,128)(2,1)S(1)}, u32[]{:S(2)}, u32[]{:S(2)}) collective-permute-start(bf16[2,480,128]{2,1,0:T(8,128)(2,1)S(1)} %get-tuple-element.18), channel_id=1, source_target_pairs={{0,1},{1,2},{2,3},{3,0},{4,5},{5,6},{6,7},{7,4},{8,9},{9,10},{10,1... | collective-permute-start | bytes 737288 | tf_op jit(solution)/shard_map/ppermute | solution.py:168
  26.5 2.9 %collective-permute-start.6 = (bf16[2,480,128]{2,1,0:T(8,128)(2,1)S(1)}, bf16[2,480,128]{2,1,0:T(8,128)(2,1)S(1)}, u32[]{:S(2)}, u32[]{:S(2)}) collective-permute-start(bf16[2,480,128]{2,1,0:T(8,128)(2,1)S(1)} %get-tuple-element.19), channel_id=1, source_target_pairs={{0,2},{1,3},{2,0},{3,1},{4,6},{5,7},{6,4},{7,5},{8,10},{9,11},{10,... | collective-permute-start | bytes 737288 | tf_op jit(solution)/shard_map/ppermute | solution.py:168
  29.4 1.3 %collective-permute-start.7 = (bf16[2,480,128]{2,1,0:T(8,128)(2,1)S(1)}, bf16[2,480,128]{2,1,0:T(8,128)(2,1)S(1)}, u32[]{:S(2)}, u32[]{:S(2)}) collective-permute-start(bf16[2,480,128]{2,1,0:T(8,128)(2,1)S(1)} %get-tuple-element.20), channel_id=1, source_target_pairs={{0,3},{1,0},{2,1},{3,2},{4,7},{5,4},{6,5},{7,6},{8,11},{9,8},{10,9... | collective-permute-start | bytes 737288 | tf_op jit(solution)/shard_map/ppermute | solution.py:168
  30.7 1.6 %collective-permute-done.5 = bf16[2,480,128]{2,1,0:T(8,128)(2,1)S(1)} collective-permute-done((bf16[2,480,128]{2,1,0:T(8,128)(2,1)S(1)}, bf16[2,480,128]{2,1,0:T(8,128)(2,1)S(1)}, u32[]{:S(2)}, u32[]{:S(2)}) %collective-permute-start.5) | collective-permute-done | bytes 245792 | tf_op jit(solution)/shard_map/ppermute | solution.py:168
  32.3 3.9 %collective-permute-done.6 = bf16[2,480,128]{2,1,0:T(8,128)(2,1)S(1)} collective-permute-done((bf16[2,480,128]{2,1,0:T(8,128)(2,1)S(1)}, bf16[2,480,128]{2,1,0:T(8,128)(2,1)S(1)}, u32[]{:S(2)}, u32[]{:S(2)}) %collective-permute-start.6) | collective-permute-done | bytes 245792 | tf_op jit(solution)/shard_map/ppermute | solution.py:168
  36.2 0.0 collective-permute-done.7
  36.2 0.1 pad_maximum_fusion
  36.3 0.3 reshape.65
  36.6 1.9 %copy.24 = bf16[4,2,32,6,2,32]{2,3,4,0,5,1:T(8,128)(2,1)S(1)} copy(bf16[4,2,32,6,2,32]{5,4,3,2,1,0:T(2,128)(2,1)S(1)} %reshape.65) | data formatting | bytes 393216 | tf_op jit(solution)/shard_map/reshape | solution.py:173
  38.5 0.5 copy.27
  39.1 0.2 fusion.29
  39.3 1.3 %fusion.9 = bf16[2,32,4,8,2,128]{5,3,4,2,1,0:T(8,128)(2,1)S(1)} fusion(bf16[4,2,6,1,32,128]{5,2,3,0,4,1:T(8,128)(2,1)S(1)} %get-tuple-element.16, bf16[4,2,6,1,32,128]{5,2,3,0,4,1:T(8,128)(2,1)S(1)} %get-tuple-element.15, bf16[4,2,6,2,32,128]{5,2,3,0,4,1:T(8,128)(2,1)S(1)} %copy.27, bf16[4,2,32,6,2,32]{2,3,4,0,5,1:T(8,128)(2,1)S(1)} %copy.24), kind=kOutput, calls=%fused_computation.11 | convolution fusion | flops 55574528 | bytes 2818048 | tf_op jit(solution)/shard_map/akscfm,akscfn->kfmn/dot_general | solution.py:177
  40.6 0.0 copy-start.2
  40.6 0.3 copy.28
  40.9 0.1 dynamic-slice_bitcast_fusion.2
  40.9 4.1 %collective-permute-start.10 = (bf16[1024,128]{1,0:T(8,128)(2,1)S(1)}, bf16[1024,128]{1,0:T(8,128)(2,1)S(1)}, u32[]{:S(2)}, u32[]{:S(2)}) collective-permute-start(bf16[1024,128]{1,0:T(8,128)(2,1)S(1)} %get-tuple-element.13), channel_id=1, source_target_pairs={{0,12},{1,13},{2,14},{3,15},{4,0},{5,1},{6,2},{7,3},{8,4},{9,5},{1... | collective-permute-start | bytes 786440 | tf_op jit(solution)/shard_map/ppermute | solution.py:189
  45.0 0.0 collective-permute-start.8
  45.0 1.9 %collective-permute-start.9 = (bf16[1024,128]{1,0:T(8,128)(2,1)S(1)}, bf16[1024,128]{1,0:T(8,128)(2,1)S(1)}, u32[]{:S(2)}, u32[]{:S(2)}) collective-permute-start(bf16[1024,128]{1,0:T(8,128)(2,1)S(1)} %get-tuple-element.14), channel_id=1, source_target_pairs={{0,8},{1,9},{2,10},{3,11},{4,12},{5,13},{6,14},{7,15},{8,0},{9,1},... | collective-permute-start | bytes 786440 | tf_op jit(solution)/shard_map/ppermute | solution.py:189
  46.9 0.2 fusion.22
  47.0 0.0 copy-done.2
  47.1 0.6 %dynamic_slice.42 = s32[1]{0:T(128)} dynamic-slice(s32[8]{0:T(128)S(1)} %copy-done.2, s32[]{:T(128)S(6)} %select_n.126), dynamic_slice_sizes={1} | dynamic-slice | bytes 12 | tf_op jit(solution)/shard_map/dynamic_slice | solution.py:124
  47.6 0.6 %compare_convert_fusion = f32[2]{0:T(128)S(1)} fusion(s32[]{:T(128)} %bitcast.44), kind=kLoop, calls=%fused_computation.71 | loop fusion | flops 4 | bytes 12 | tf_op jit(solution)/shard_map/convert_element_type | solution.py:199
  48.3 0.6 %collective-permute-done.10 = bf16[1024,128]{1,0:T(8,128)(2,1)S(1)} collective-permute-done((bf16[1024,128]{1,0:T(8,128)(2,1)S(1)}, bf16[1024,128]{1,0:T(8,128)(2,1)S(1)}, u32[]{:S(2)}, u32[]{:S(2)}) %collective-permute-start.10) | collective-permute-done | bytes 262176 | tf_op jit(solution)/shard_map/ppermute | solution.py:189
  48.9 6.5 %collective-permute-done.8 = bf16[1024,128]{1,0:T(8,128)(2,1)S(1)} collective-permute-done((bf16[1024,128]{1,0:T(8,128)(2,1)S(1)}, bf16[1024,128]{1,0:T(8,128)(2,1)S(1)}, u32[]{:S(2)}, u32[]{:S(2)}) %collective-permute-start.8) | collective-permute-done | bytes 262176 | tf_op jit(solution)/shard_map/ppermute | solution.py:189
  55.4 0.0 collective-permute-done.9
  55.4 0.1 fusion.16
  55.5 1.8 %fusion.13 = bf16[1,2,8,128,128]{4,3,2,1,0:T(8,128)(2,1)} fusion(f32[2,32,128,1,1]{2,1,0,4,3:T(8,128)S(1)} %bitcast.123, f32[2,2,32,8,128]{4,3,2,1,0:T(8,128)S(1)} %bitcast.100, f32[2]{0:T(128)S(1)} %compare_convert_fusion), kind=kOutput, calls=%fused_computation.13 | convolution fusion | flops 101187584 | bytes 1081352 | tf_op jit(solution)/shard_map/kpfrj,pft->krjt/dot_general | solution.py:192
  (15 shorter events, 0.2 us)
Async XLA Ops:
  0.0 14.9 %copy-start = (s32[8,2,2]{0,2,1:T(2,128)S(1)}, s32[8,2,2]{0,2,1:T(2,128)}, u32[]{:S(2)}) copy-start(s32[8,2,2]{0,2,1:T(2,128)} %param.7) | copy-start | bytes 388
  6.7 3.1 %copy-start.1 = (f32[768,64]{1,0:T(8,128)S(1)}, f32[768,64]{1,0:T(8,128)}, u32[]{:S(2)}) copy-start(f32[768,64]{1,0:T(8,128)} %shard_map.46) | copy-start | bytes 589828
  10.3 7.1 %collective-permute-start = (bf16[384,128]{1,0:T(8,128)(2,1)S(1)}, bf16[384,128]{1,0:T(8,128)(2,1)S(1)}, u32[]{:S(2)}, u32[]{:S(2)}) collective-permute-start(bf16[384,128]{1,0:T(8,128)(2,1)S(1)} %bitcast.118), channel_id=1, source_target_pairs={{0,96},{16,112},{32,0},{48,16},{64,32},{80,48},{96,64},{112,80},{1... | collective-permute-start | bytes 294920 | tf_op jit(solution)/shard_map/ppermute | solution.py:115
  13.2 6.9 %collective-permute-start.1 = (bf16[384,128]{1,0:T(8,128)(2,1)S(1)}, bf16[384,128]{1,0:T(8,128)(2,1)S(1)}, u32[]{:S(2)}, u32[]{:S(2)}) collective-permute-start(bf16[384,128]{1,0:T(8,128)(2,1)S(1)} %bitcast.119), channel_id=1, source_target_pairs={{0,64},{16,80},{32,96},{48,112},{64,0},{80,16},{96,32},{112,48},{1... | collective-permute-start | bytes 294920 | tf_op jit(solution)/shard_map/ppermute | solution.py:116
  14.0 7.1 %collective-permute-start.2 = (bf16[384,128]{1,0:T(8,128)(2,1)S(1)}, bf16[384,128]{1,0:T(8,128)(2,1)S(1)}, u32[]{:S(2)}, u32[]{:S(2)}) collective-permute-start(bf16[384,128]{1,0:T(8,128)(2,1)S(1)} %bitcast.120), channel_id=1, source_target_pairs={{0,32},{16,48},{32,64},{48,80},{64,96},{80,112},{96,0},{112,16},{1... | collective-permute-start | bytes 294920 | tf_op jit(solution)/shard_map/ppermute | solution.py:114
  14.9 6.4 %collective-permute-start.3 = (bf16[384,128]{1,0:T(8,128)(2,1)S(1)}, bf16[384,128]{1,0:T(8,128)(2,1)S(1)}, u32[]{:S(2)}, u32[]{:S(2)}) collective-permute-start(bf16[384,128]{1,0:T(8,128)(2,1)S(1)} %bitcast.121), channel_id=1, source_target_pairs={{0,16},{16,0},{32,48},{48,32},{64,80},{80,64},{96,112},{112,96},{1... | collective-permute-start | bytes 294920 | tf_op jit(solution)/shard_map/ppermute | solution.py:113
  21.1 1.7 %collective-permute-start.4 = (bf16[3,384,128]{2,1,0:T(8,128)(2,1)S(1)}, bf16[3,384,128]{2,1,0:T(8,128)(2,1)S(1)}, u32[]{:S(2)}, u32[]{:S(2)}) collective-permute-start(bf16[3,384,128]{2,1,0:T(8,128)(2,1)S(1)} %pad_maximum_fusion.3), channel_id=1, source_target_pairs={{0,16},{16,0},{32,48},{48,32},{64,80},{80,64},{96,112},{112,96},{1... | collective-permute-start | bytes 884744 | tf_op jit(solution)/shard_map/ppermute | solution.py:118
  24.8 7.5 %collective-permute-start.5 = (bf16[2,480,128]{2,1,0:T(8,128)(2,1)S(1)}, bf16[2,480,128]{2,1,0:T(8,128)(2,1)S(1)}, u32[]{:S(2)}, u32[]{:S(2)}) collective-permute-start(bf16[2,480,128]{2,1,0:T(8,128)(2,1)S(1)} %get-tuple-element.18), channel_id=1, source_target_pairs={{0,1},{1,2},{2,3},{3,0},{4,5},{5,6},{6,7},{7,4},{8,9},{9,10},{10,1... | collective-permute-start | bytes 737288 | tf_op jit(solution)/shard_map/ppermute | solution.py:168
  26.5 9.7 %collective-permute-start.6 = (bf16[2,480,128]{2,1,0:T(8,128)(2,1)S(1)}, bf16[2,480,128]{2,1,0:T(8,128)(2,1)S(1)}, u32[]{:S(2)}, u32[]{:S(2)}) collective-permute-start(bf16[2,480,128]{2,1,0:T(8,128)(2,1)S(1)} %get-tuple-element.19), channel_id=1, source_target_pairs={{0,2},{1,3},{2,0},{3,1},{4,6},{5,7},{6,4},{7,5},{8,10},{9,11},{10,... | collective-permute-start | bytes 737288 | tf_op jit(solution)/shard_map/ppermute | solution.py:168
  29.4 6.8 %collective-permute-start.7 = (bf16[2,480,128]{2,1,0:T(8,128)(2,1)S(1)}, bf16[2,480,128]{2,1,0:T(8,128)(2,1)S(1)}, u32[]{:S(2)}, u32[]{:S(2)}) collective-permute-start(bf16[2,480,128]{2,1,0:T(8,128)(2,1)S(1)} %get-tuple-element.20), channel_id=1, source_target_pairs={{0,3},{1,0},{2,1},{3,2},{4,7},{5,4},{6,5},{7,6},{8,11},{9,8},{10,9... | collective-permute-start | bytes 737288 | tf_op jit(solution)/shard_map/ppermute | solution.py:168
  40.6 6.5 %copy-start.2 = (s32[8]{0:T(128)S(1)}, s32[8]{0:T(128)}, u32[]{:S(2)}) copy-start(s32[8]{0:T(128)} %param.8) | copy-start | bytes 100
  40.9 8.0 %collective-permute-start.10 = (bf16[1024,128]{1,0:T(8,128)(2,1)S(1)}, bf16[1024,128]{1,0:T(8,128)(2,1)S(1)}, u32[]{:S(2)}, u32[]{:S(2)}) collective-permute-start(bf16[1024,128]{1,0:T(8,128)(2,1)S(1)} %get-tuple-element.13), channel_id=1, source_target_pairs={{0,12},{1,13},{2,14},{3,15},{4,0},{5,1},{6,2},{7,3},{8,4},{9,5},{1... | collective-permute-start | bytes 786440 | tf_op jit(solution)/shard_map/ppermute | solution.py:189
  45.0 10.4 %collective-permute-start.8 = (bf16[1024,128]{1,0:T(8,128)(2,1)S(1)}, bf16[1024,128]{1,0:T(8,128)(2,1)S(1)}, u32[]{:S(2)}, u32[]{:S(2)}) collective-permute-start(bf16[1024,128]{1,0:T(8,128)(2,1)S(1)} %get-tuple-element.12), channel_id=1, source_target_pairs={{0,4},{1,5},{2,6},{3,7},{4,8},{5,9},{6,10},{7,11},{8,12},{9,13},{1... | collective-permute-start | bytes 786440 | tf_op jit(solution)/shard_map/ppermute | solution.py:189
  45.0 10.4 %collective-permute-start.9 = (bf16[1024,128]{1,0:T(8,128)(2,1)S(1)}, bf16[1024,128]{1,0:T(8,128)(2,1)S(1)}, u32[]{:S(2)}, u32[]{:S(2)}) collective-permute-start(bf16[1024,128]{1,0:T(8,128)(2,1)S(1)} %get-tuple-element.14), channel_id=1, source_target_pairs={{0,8},{1,9},{2,10},{3,11},{4,12},{5,13},{6,14},{7,15},{8,0},{9,1},... | collective-permute-start | bytes 786440 | tf_op jit(solution)/shard_map/ppermute | solution.py:189

commit v7 on v5

--- a/solution.py
+++ b/solution.py
@@ -5,6 +5,7 @@
 import ml_dtypes
 import numpy as np
 from jax import lax
+from jax.experimental.layout import Layout, with_layout_constraint
 from jax.sharding import Mesh
 from jax.sharding import PartitionSpec as P
 
@@ -67,7 +68,11 @@
     width = 2 * FREQS
     spec_rows = seg_dev * width
     half_rows = spec_rows // 2
-    spectra = whiten(jnp.dot(records[0], band_table(), preferred_element_type=jnp.float32))
+    samples = records[0].reshape(seg_dev * block_width, NSAMP)
+    projected = with_layout_constraint(
+        jnp.dot(samples, band_table(), preferred_element_type=jnp.float32), Layout((0, 1))
+    )
+    spectra = whiten(projected).reshape(seg_dev, block_width, 2 * FREQS)
     own = jnp.transpose(spectra, (0, 2, 1)).reshape(spec_rows, block_width)
     owner_index = lax.axis_index("pairs")
     core = owner_index % 2
@@ -166,7 +171,7 @@
         "kpfrj,pft->krjt",
         stacked,
         lag_weights,
-        precision=lax.Precision.HIGHEST,
+        precision=lax.Precision.HIGH,
         preferred_element_type=jnp.float32,
     )
     masked = correlation * live_slots.astype(jnp.float32)[:, None, None, None]

time: 53.1 us -> 52.2 us (0.983)
  waiting for transfers between devices: 19.7 us -> 17.8 us
  other arithmetic: 1.88 us -> 2.87 us
  matrix products: 8.93 us -> 8.01 us
  starting transfers between devices: 16.6 us -> 17.2 us
    ppermute x1, starting transfers between devices: 2.91 us -> 1.67 us  [shards(): from_above = lax.ppermute(own, 'pairs', chip_shift(-1))]
    ppermute x1, starting transfers between devices: 0.8 us -> 1.89 us  [shards(): from_far = lax.ppermute(own, 'pairs', chip_shift(2))]
    ppermute x1, waiting for transfers between devices: 2.01 us -> 1.06 us  [shards(): from_above = lax.ppermute(own, 'pairs', chip_shift(-1))]
    dot_general x1, matrix products: 2.61 us -> 1.8 us  [shards(): jnp.einsum('kpfrj,pft->krjt', stacked, lag_weights, precision=lax.Precisi...]
    ppermute x1, waiting for transfers between devices: 1.01 us -> 0.21 us  [shards(): from_below = lax.ppermute(own, 'pairs', chip_shift(1))]
    ppermute x1, starting transfers between devices: 0.88 us -> 1.64 us  [shards(): from_below = lax.ppermute(own, 'pairs', chip_shift(1))]
    another operation x2, other arithmetic: 0.09 us -> 0.75 us
where the time goes in v7:
time: 52.2 us; the launch traced here: 52.1 us
  waiting for transfers between devices  17.8 us (34%)
  starting transfers between devices  17.2 us (33%)
  matrix products  8.01 us (15%)
  local copies, waits for them, and re-layouts  5.86 us (11%)
  other arithmetic  2.87 us (5%)
    ppermute x3, waiting for transfers between devices, shards(): lax.ppermute(chunk, axes, reduce_perm(e)).astype(jnp.float32)  7.14 us
    ppermute x3, starting transfers between devices, shards(): pieces.append(lax.ppermute(message, axes, gather_perm(d)))  5.98 us
    ppermute x3, starting transfers between devices, shards(): lax.ppermute(chunk, axes, reduce_perm(e)).astype(jnp.float32)  5.97 us
    ppermute x3, waiting for transfers between devices, shards(): pieces.append(lax.ppermute(message, axes, gather_perm(d)))  5.45 us
    dot_general x1, matrix products, shards(): jnp.dot(samples, band_table(), preferred_element_type=jnp.float32)  4.89 us
    ppermute x1, waiting for transfers between devices, shards(): from_far = lax.ppermute(own, 'pairs', chip_shift(2))  2.47 us
    reshape x2, local copies, waits for them, and re-layouts, shards(): gathered[:, :, spec_rows:]  2.22 us
    ppermute x1, starting transfers between devices, shards(): from_far = lax.ppermute(own, 'pairs', chip_shift(2))  1.89 us
  transfers between devices with their start and end apart: 11, of which 8 were waited for; matrix products, arithmetic and copies ran while one was open for 4% of the time, Pallas kernels for 0%

profile of v7, /device:TPU:0, one launch (start us, length us, event | category | flops | bytes accessed | tf_op | source)
XLA Modules:
  0.0 52.1 jit_solution(17586200218588833371)
XLA Ops:
  0.0 0.0 copy-start
  0.0 4.9 %convolution_bitcast_fusion.1 = f32[768,64]{1,0:T(8,128)S(1)} fusion(bf16[768,4096]{1,0:T(8,128)(2,1)} %bitcast.128, bf16[4096,64]{1,0:T(8,128)(2,1)} %constant.168.clone), kind=kOutput, calls=%fused_computation.14 | convolution fusion | flops 402653184 | bytes 7012352 | tf_op jit(solution)/shard_map/dot_general | solution.py:73
  4.9 0.3 fusion.28
  5.2 0.6 %multiply_convert_fusion.1 = (bf16[768,32]{1,0:T(8,128)(2,1)S(1)}, f32[768,32]{1,0:T(8,128)S(1)}) fusion(f32[768,64]{1,0:T(8,128)S(1)} %convolution_bitcast_fusion.1, f32[768]{0:T(1024)S(1)} %broadcast_multiply_fusion, f32[768,32]{1,0:T(8,128)S(1)} %get-tuple-element.11), kind=kLoop, calls=%fused_computation.28 | loop fusion | flops 221184 | bytes 347136 | tf_op jit(solution)/shard_map/convert.4
  5.8 0.2 multiply_convert_fusion
  6.0 0.1 copy.16
  6.1 0.1 copy.15
  6.2 1.6 %collective-permute-start.2 = (bf16[384,128]{1,0:T(8,128)(2,1)S(1)}, bf16[384,128]{1,0:T(8,128)(2,1)S(1)}, u32[]{:S(2)}, u32[]{:S(2)}) collective-permute-start(bf16[384,128]{1,0:T(8,128)(2,1)S(1)} %bitcast.121), channel_id=1, source_target_pairs={{0,32},{16,48},{32,64},{48,80},{64,96},{80,112},{96,0},{112,16},{1... | collective-permute-start | bytes 294920 | tf_op jit(solution)/shard_map/ppermute | solution.py:92
  7.9 1.7 %collective-permute-start = (bf16[384,128]{1,0:T(8,128)(2,1)S(1)}, bf16[384,128]{1,0:T(8,128)(2,1)S(1)}, u32[]{:S(2)}, u32[]{:S(2)}) collective-permute-start(bf16[384,128]{1,0:T(8,128)(2,1)S(1)} %bitcast.122), channel_id=1, source_target_pairs={{0,96},{16,112},{32,0},{48,16},{64,32},{80,48},{96,64},{112,80},{1... | collective-permute-start | bytes 294920 | tf_op jit(solution)/shard_map/ppermute | solution.py:93
  9.6 1.9 %collective-permute-start.1 = (bf16[384,128]{1,0:T(8,128)(2,1)S(1)}, bf16[384,128]{1,0:T(8,128)(2,1)S(1)}, u32[]{:S(2)}, u32[]{:S(2)}) collective-permute-start(bf16[384,128]{1,0:T(8,128)(2,1)S(1)} %bitcast.123), channel_id=1, source_target_pairs={{0,64},{16,80},{32,96},{48,112},{64,0},{80,16},{96,32},{112,48},{1... | collective-permute-start | bytes 294920 | tf_op jit(solution)/shard_map/ppermute | solution.py:94
  11.4 0.0 collective-permute-start.3
  11.4 0.0 copy-done
  11.5 0.2 fusion.23
  11.7 0.2 slice_reduce_fusion.1
  11.9 0.2 collective-permute-done.2
  12.1 1.1 %collective-permute-done = bf16[384,128]{1,0:T(8,128)(2,1)S(1)} collective-permute-done((bf16[384,128]{1,0:T(8,128)(2,1)S(1)}, bf16[384,128]{1,0:T(8,128)(2,1)S(1)}, u32[]{:S(2)}, u32[]{:S(2)}) %collective-permute-start) | collective-permute-done | bytes 98336 | tf_op jit(solution)/shard_map/ppermute | solution.py:93
  13.2 2.5 %collective-permute-done.1 = bf16[384,128]{1,0:T(8,128)(2,1)S(1)} collective-permute-done((bf16[384,128]{1,0:T(8,128)(2,1)S(1)}, bf16[384,128]{1,0:T(8,128)(2,1)S(1)}, u32[]{:S(2)}, u32[]{:S(2)}) %collective-permute-start.1) | collective-permute-done | bytes 98336 | tf_op jit(solution)/shard_map/ppermute | solution.py:94
  15.7 0.1 collective-permute-start.4
  15.8 0.1 maximum_bitcast_fusion
  15.9 0.0 collective-permute-done.3
  15.9 1.5 %collective-permute-done.4 = bf16[3,384,128]{2,1,0:T(8,128)(2,1)S(1)} collective-permute-done((bf16[3,384,128]{2,1,0:T(8,128)(2,1)S(1)}, bf16[3,384,128]{2,1,0:T(8,128)(2,1)S(1)}, u32[]{:S(2)}, u32[]{:S(2)}) %collective-permute-start.4) | collective-permute-done | bytes 294944 | tf_op jit(solution)/shard_map/ppermute | solution.py:96
  17.4 0.1 maximum_select_fusion
  17.6 0.1 copy.17
  17.6 0.6 %gather_fusion.1 = bf16[2,384,128]{2,1,0:T(8,128)(2,1)S(1)} fusion(bf16[8,384,128]{2,1,0:T(8,128)(2,1)S(1)} %bitcast.104, s32[1024]{0:T(1024)S(1)} %pad_clamp_fusion), kind=kCustom, calls=%fused_computation.1.clone | custom fusion | bytes 393224 | tf_op jit(solution)/shard_map/jit(_take)/gather | solution.py:104
  18.2 0.1 select_bitcast_fusion
  18.3 0.2 copy.18
  18.5 0.1 reshape.64
  18.6 0.6 %gather_fusion = bf16[2,384,128]{2,1,0:T(8,128)(2,1)S(1)} fusion(bf16[8,384,128]{2,1,0:T(8,128)(2,1)S(1)} %bitcast.105, s32[1024]{0:T(1024)S(1)} %pad_clamp_fusion.1), kind=kCustom, calls=%fused_computation.clone | custom fusion | bytes 393224 | tf_op jit(solution)/shard_map/jit(_take)/gather | solution.py:105
  19.2 0.1 broadcast_select_fusion
  19.3 0.1 maximum_bitcast_fusion.2
  19.5 1.7 %collective-permute-start.5 = (bf16[2,480,128]{2,1,0:T(8,128)(2,1)S(1)}, bf16[2,480,128]{2,1,0:T(8,128)(2,1)S(1)}, u32[]{:S(2)}, u32[]{:S(2)}) collective-permute-start(bf16[2,480,128]{2,1,0:T(8,128)(2,1)S(1)} %get-tuple-element.18), channel_id=1, source_target_pairs={{0,1},{1,2},{2,3},{3,0},{4,5},{5,6},{6,7},{7,4},{8,9},{9,10},{10,1... | collective-permute-start | bytes 737288 | tf_op jit(solution)/shard_map/ppermute | solution.py:146
  21.2 2.9 %collective-permute-start.6 = (bf16[2,480,128]{2,1,0:T(8,128)(2,1)S(1)}, bf16[2,480,128]{2,1,0:T(8,128)(2,1)S(1)}, u32[]{:S(2)}, u32[]{:S(2)}) collective-permute-start(bf16[2,480,128]{2,1,0:T(8,128)(2,1)S(1)} %get-tuple-element.19), channel_id=1, source_target_pairs={{0,2},{1,3},{2,0},{3,1},{4,6},{5,7},{6,4},{7,5},{8,10},{9,11},{10,... | collective-permute-start | bytes 737288 | tf_op jit(solution)/shard_map/ppermute | solution.py:146
  24.1 1.3 %collective-permute-start.7 = (bf16[2,480,128]{2,1,0:T(8,128)(2,1)S(1)}, bf16[2,480,128]{2,1,0:T(8,128)(2,1)S(1)}, u32[]{:S(2)}, u32[]{:S(2)}) collective-permute-start(bf16[2,480,128]{2,1,0:T(8,128)(2,1)S(1)} %get-tuple-element.20), channel_id=1, source_target_pairs={{0,3},{1,0},{2,1},{3,2},{4,7},{5,4},{6,5},{7,6},{8,11},{9,8},{10,9... | collective-permute-start | bytes 737288 | tf_op jit(solution)/shard_map/ppermute | solution.py:146
  25.5 1.5 %collective-permute-done.5 = bf16[2,480,128]{2,1,0:T(8,128)(2,1)S(1)} collective-permute-done((bf16[2,480,128]{2,1,0:T(8,128)(2,1)S(1)}, bf16[2,480,128]{2,1,0:T(8,128)(2,1)S(1)}, u32[]{:S(2)}, u32[]{:S(2)}) %collective-permute-start.5) | collective-permute-done | bytes 245792 | tf_op jit(solution)/shard_map/ppermute | solution.py:146
  26.9 4.0 %collective-permute-done.6 = bf16[2,480,128]{2,1,0:T(8,128)(2,1)S(1)} collective-permute-done((bf16[2,480,128]{2,1,0:T(8,128)(2,1)S(1)}, bf16[2,480,128]{2,1,0:T(8,128)(2,1)S(1)}, u32[]{:S(2)}, u32[]{:S(2)}) %collective-permute-start.6) | collective-permute-done | bytes 245792 | tf_op jit(solution)/shard_map/ppermute | solution.py:146
  30.9 0.0 collective-permute-done.7
  30.9 0.1 pad_maximum_fusion
  31.0 0.3 reshape.65
  31.3 1.9 %copy.24 = bf16[4,2,32,6,2,32]{2,3,4,0,5,1:T(8,128)(2,1)S(1)} copy(bf16[4,2,32,6,2,32]{5,4,3,2,1,0:T(2,128)(2,1)S(1)} %reshape.65) | data formatting | bytes 393216 | tf_op jit(solution)/shard_map/reshape | solution.py:151
  33.2 0.5 %copy.27 = bf16[4,2,6,2,32,128]{5,2,3,0,4,1:T(8,128)(2,1)S(1)} copy(bf16[4,2,6,2,32,128]{5,4,3,2,1,0:T(8,128)(2,1)S(1)} %bitcast.102) | data formatting | bytes 1572864 | tf_op jit(solution)/shard_map/reshape | solution.py:148
  33.8 0.2 fusion.29
  33.9 1.3 %fusion.9 = bf16[2,32,4,8,2,128]{5,3,4,2,1,0:T(8,128)(2,1)S(1)} fusion(bf16[4,2,6,1,32,128]{5,2,3,0,4,1:T(8,128)(2,1)S(1)} %get-tuple-element.16, bf16[4,2,6,1,32,128]{5,2,3,0,4,1:T(8,128)(2,1)S(1)} %get-tuple-element.15, bf16[4,2,6,2,32,128]{5,2,3,0,4,1:T(8,128)(2,1)S(1)} %copy.27, bf16[4,2,32,6,2,32]{2,3,4,0,5,1:T(8,128)(2,1)S(1)} %copy.24), kind=kOutput, calls=%fused_computation.11 | convolution fusion | flops 55574528 | bytes 2818048 | tf_op jit(solution)/shard_map/akscfm,akscfn->kfmn/dot_general | solution.py:155
  35.3 0.0 copy-start.1
  35.3 0.3 copy.28
  35.6 0.1 dynamic-slice_bitcast_fusion.2
  35.6 4.1 %collective-permute-start.10 = (bf16[1024,128]{1,0:T(8,128)(2,1)S(1)}, bf16[1024,128]{1,0:T(8,128)(2,1)S(1)}, u32[]{:S(2)}, u32[]{:S(2)}) collective-permute-start(bf16[1024,128]{1,0:T(8,128)(2,1)S(1)} %get-tuple-element.13), channel_id=1, source_target_pairs={{0,12},{1,13},{2,14},{3,15},{4,0},{5,1},{6,2},{7,3},{8,4},{9,5},{1... | collective-permute-start | bytes 786440 | tf_op jit(solution)/shard_map/ppermute | solution.py:167
  39.8 0.0 collective-permute-start.8
  39.8 1.8 %collective-permute-start.9 = (bf16[1024,128]{1,0:T(8,128)(2,1)S(1)}, bf16[1024,128]{1,0:T(8,128)(2,1)S(1)}, u32[]{:S(2)}, u32[]{:S(2)}) collective-permute-start(bf16[1024,128]{1,0:T(8,128)(2,1)S(1)} %get-tuple-element.14), channel_id=1, source_target_pairs={{0,8},{1,9},{2,10},{3,11},{4,12},{5,13},{6,14},{7,15},{8,0},{9,1},... | collective-permute-start | bytes 786440 | tf_op jit(solution)/shard_map/ppermute | solution.py:167
  41.6 0.2 fusion.22
  41.7 0.0 copy-done.1
  41.8 0.6 %dynamic_slice.42 = s32[1]{0:T(128)} dynamic-slice(s32[8]{0:T(128)S(1)} %copy-done.1, s32[]{:T(128)S(6)} %select_n.126), dynamic_slice_sizes={1} | dynamic-slice | bytes 12 | tf_op jit(solution)/shard_map/dynamic_slice | solution.py:102
  42.3 0.6 %compare_convert_fusion = f32[2]{0:T(128)S(1)} fusion(s32[]{:T(128)} %bitcast.45), kind=kLoop, calls=%fused_computation.72 | loop fusion | flops 4 | bytes 12 | tf_op jit(solution)/shard_map/convert_element_type | solution.py:177
  43.0 0.6 %collective-permute-done.10 = bf16[1024,128]{1,0:T(8,128)(2,1)S(1)} collective-permute-done((bf16[1024,128]{1,0:T(8,128)(2,1)S(1)}, bf16[1024,128]{1,0:T(8,128)(2,1)S(1)}, u32[]{:S(2)}, u32[]{:S(2)}) %collective-permute-start.10) | collective-permute-done | bytes 262176 | tf_op jit(solution)/shard_map/ppermute | solution.py:167
  43.7 6.5 %collective-permute-done.8 = bf16[1024,128]{1,0:T(8,128)(2,1)S(1)} collective-permute-done((bf16[1024,128]{1,0:T(8,128)(2,1)S(1)}, bf16[1024,128]{1,0:T(8,128)(2,1)S(1)}, u32[]{:S(2)}, u32[]{:S(2)}) %collective-permute-start.8) | collective-permute-done | bytes 262176 | tf_op jit(solution)/shard_map/ppermute | solution.py:167
  50.2 0.0 collective-permute-done.9
  50.2 0.1 fusion.16
  50.3 1.8 %fusion.13 = bf16[1,2,8,128,128]{4,3,2,1,0:T(8,128)(2,1)} fusion(f32[2,32,128,1,1]{2,1,0,4,3:T(8,128)S(1)} %bitcast.126, f32[2,2,32,8,128]{4,3,2,1,0:T(8,128)S(1)} %bitcast.103, f32[2]{0:T(128)S(1)} %compare_convert_fusion), kind=kOutput, calls=%fused_computation.13 | convolution fusion | flops 101187584 | bytes 1081352 | tf_op jit(solution)/shard_map/kpfrj,pft->krjt/dot_general | solution.py:170
  (15 shorter events, 0.2 us)
Async XLA Ops:
  0.0 11.5 %copy-start = (s32[8,2,2]{0,2,1:T(2,128)S(1)}, s32[8,2,2]{0,2,1:T(2,128)}, u32[]{:S(2)}) copy-start(s32[8,2,2]{0,2,1:T(2,128)} %param.7) | copy-start | bytes 388
  6.2 5.9 %collective-permute-start.2 = (bf16[384,128]{1,0:T(8,128)(2,1)S(1)}, bf16[384,128]{1,0:T(8,128)(2,1)S(1)}, u32[]{:S(2)}, u32[]{:S(2)}) collective-permute-start(bf16[384,128]{1,0:T(8,128)(2,1)S(1)} %bitcast.121), channel_id=1, source_target_pairs={{0,32},{16,48},{32,64},{48,80},{64,96},{80,112},{96,0},{112,16},{1... | collective-permute-start | bytes 294920 | tf_op jit(solution)/shard_map/ppermute | solution.py:92
  7.9 5.3 %collective-permute-start = (bf16[384,128]{1,0:T(8,128)(2,1)S(1)}, bf16[384,128]{1,0:T(8,128)(2,1)S(1)}, u32[]{:S(2)}, u32[]{:S(2)}) collective-permute-start(bf16[384,128]{1,0:T(8,128)(2,1)S(1)} %bitcast.122), channel_id=1, source_target_pairs={{0,96},{16,112},{32,0},{48,16},{64,32},{80,48},{96,64},{112,80},{1... | collective-permute-start | bytes 294920 | tf_op jit(solution)/shard_map/ppermute | solution.py:93
  9.6 6.1 %collective-permute-start.1 = (bf16[384,128]{1,0:T(8,128)(2,1)S(1)}, bf16[384,128]{1,0:T(8,128)(2,1)S(1)}, u32[]{:S(2)}, u32[]{:S(2)}) collective-permute-start(bf16[384,128]{1,0:T(8,128)(2,1)S(1)} %bitcast.123), channel_id=1, source_target_pairs={{0,64},{16,80},{32,96},{48,112},{64,0},{80,16},{96,32},{112,48},{1... | collective-permute-start | bytes 294920 | tf_op jit(solution)/shard_map/ppermute | solution.py:94
  11.4 4.4 %collective-permute-start.3 = (bf16[384,128]{1,0:T(8,128)(2,1)S(1)}, bf16[384,128]{1,0:T(8,128)(2,1)S(1)}, u32[]{:S(2)}, u32[]{:S(2)}) collective-permute-start(bf16[384,128]{1,0:T(8,128)(2,1)S(1)} %bitcast.124), channel_id=1, source_target_pairs={{0,16},{16,0},{32,48},{48,32},{64,80},{80,64},{96,112},{112,96},{1... | collective-permute-start | bytes 294920 | tf_op jit(solution)/shard_map/ppermute | solution.py:91
  15.7 1.7 %collective-permute-start.4 = (bf16[3,384,128]{2,1,0:T(8,128)(2,1)S(1)}, bf16[3,384,128]{2,1,0:T(8,128)(2,1)S(1)}, u32[]{:S(2)}, u32[]{:S(2)}) collective-permute-start(bf16[3,384,128]{2,1,0:T(8,128)(2,1)S(1)} %pad_maximum_fusion.3), channel_id=1, source_target_pairs={{0,16},{16,0},{32,48},{48,32},{64,80},{80,64},{96,112},{112,96},{1... | collective-permute-start | bytes 884744 | tf_op jit(solution)/shard_map/ppermute | solution.py:96
  19.5 7.5 %collective-permute-start.5 = (bf16[2,480,128]{2,1,0:T(8,128)(2,1)S(1)}, bf16[2,480,128]{2,1,0:T(8,128)(2,1)S(1)}, u32[]{:S(2)}, u32[]{:S(2)}) collective-permute-start(bf16[2,480,128]{2,1,0:T(8,128)(2,1)S(1)} %get-tuple-element.18), channel_id=1, source_target_pairs={{0,1},{1,2},{2,3},{3,0},{4,5},{5,6},{6,7},{7,4},{8,9},{9,10},{10,1... | collective-permute-start | bytes 737288 | tf_op jit(solution)/shard_map/ppermute | solution.py:146
  21.2 9.7 %collective-permute-start.6 = (bf16[2,480,128]{2,1,0:T(8,128)(2,1)S(1)}, bf16[2,480,128]{2,1,0:T(8,128)(2,1)S(1)}, u32[]{:S(2)}, u32[]{:S(2)}) collective-permute-start(bf16[2,480,128]{2,1,0:T(8,128)(2,1)S(1)} %get-tuple-element.19), channel_id=1, source_target_pairs={{0,2},{1,3},{2,0},{3,1},{4,6},{5,7},{6,4},{7,5},{8,10},{9,11},{10,... | collective-permute-start | bytes 737288 | tf_op jit(solution)/shard_map/ppermute | solution.py:146
  24.1 6.8 %collective-permute-start.7 = (bf16[2,480,128]{2,1,0:T(8,128)(2,1)S(1)}, bf16[2,480,128]{2,1,0:T(8,128)(2,1)S(1)}, u32[]{:S(2)}, u32[]{:S(2)}) collective-permute-start(bf16[2,480,128]{2,1,0:T(8,128)(2,1)S(1)} %get-tuple-element.20), channel_id=1, source_target_pairs={{0,3},{1,0},{2,1},{3,2},{4,7},{5,4},{6,5},{7,6},{8,11},{9,8},{10,9... | collective-permute-start | bytes 737288 | tf_op jit(solution)/shard_map/ppermute | solution.py:146
  35.3 6.5 %copy-start.1 = (s32[8]{0:T(128)S(1)}, s32[8]{0:T(128)}, u32[]{:S(2)}) copy-start(s32[8]{0:T(128)} %param.8) | copy-start | bytes 100
  35.6 8.0 %collective-permute-start.10 = (bf16[1024,128]{1,0:T(8,128)(2,1)S(1)}, bf16[1024,128]{1,0:T(8,128)(2,1)S(1)}, u32[]{:S(2)}, u32[]{:S(2)}) collective-permute-start(bf16[1024,128]{1,0:T(8,128)(2,1)S(1)} %get-tuple-element.13), channel_id=1, source_target_pairs={{0,12},{1,13},{2,14},{3,15},{4,0},{5,1},{6,2},{7,3},{8,4},{9,5},{1... | collective-permute-start | bytes 786440 | tf_op jit(solution)/shard_map/ppermute | solution.py:167
  39.8 10.4 %collective-permute-start.8 = (bf16[1024,128]{1,0:T(8,128)(2,1)S(1)}, bf16[1024,128]{1,0:T(8,128)(2,1)S(1)}, u32[]{:S(2)}, u32[]{:S(2)}) collective-permute-start(bf16[1024,128]{1,0:T(8,128)(2,1)S(1)} %get-tuple-element.12), channel_id=1, source_target_pairs={{0,4},{1,5},{2,6},{3,7},{4,8},{5,9},{6,10},{7,11},{8,12},{9,13},{1... | collective-permute-start | bytes 786440 | tf_op jit(solution)/shard_map/ppermute | solution.py:167
  39.8 10.4 %collective-permute-start.9 = (bf16[1024,128]{1,0:T(8,128)(2,1)S(1)}, bf16[1024,128]{1,0:T(8,128)(2,1)S(1)}, u32[]{:S(2)}, u32[]{:S(2)}) collective-permute-start(bf16[1024,128]{1,0:T(8,128)(2,1)S(1)} %get-tuple-element.14), channel_id=1, source_target_pairs={{0,8},{1,9},{2,10},{3,11},{4,12},{5,13},{6,14},{7,15},{8,0},{9,1},... | collective-permute-start | bytes 786440 | tf_op jit(solution)/shard_map/ppermute | solution.py:167

commit v8 on v7

--- a/solution.py
+++ b/solution.py
@@ -101,8 +101,12 @@
     own_pairs = lax.dynamic_index_in_dim(pair_list, owner_index, 0, keepdims=False)
     live_slots = jnp.arange(slot_count, dtype=jnp.int32) < pair_count[owner_index]
     position = ((own_pairs // 2 - chip) % chips) * 2 + own_pairs % 2
-    left = jnp.take(table, position[:, 0], axis=0)
-    right = jnp.take(table, position[:, 1], axis=0)
+    left = jnp.stack(
+        [lax.dynamic_index_in_dim(table, position[k, 0], 0, keepdims=False) for k in range(slot_count)]
+    )
+    right = jnp.stack(
+        [lax.dynamic_index_in_dim(table, position[k, 1], 0, keepdims=False) for k in range(slot_count)]
+    )
     left_t = jnp.transpose(left, (0, 2, 1)).reshape((slot_count, side, side, rows, spec_rows))
     left_t = jnp.where(first_core, jnp.swapaxes(left_t, 1, 2), left_t)
     packed_rows = spec_rows * side * rows // block_width
@@ -171,7 +175,7 @@
         "kpfrj,pft->krjt",
         stacked,
         lag_weights,
-        precision=lax.Precision.HIGH,
+        precision=lax.Precision.DEFAULT,
         preferred_element_type=jnp.float32,
     )
     masked = correlation * live_slots.astype(jnp.float32)[:, None, None, None]

time: 52.2 us -> 57.2 us (1.096)
  between operations: 0.31 us -> 7.88 us
  waiting for transfers between devices: 17.8 us -> 16.6 us
  matrix products: 8.01 us -> 7.35 us
  local copies, waits for them, and re-layouts: 5.86 us -> 5.21 us
    ppermute x1, waiting for transfers between devices: 1.48 us -> 0.01 us  [shards(): theirs = lax.ppermute(mine[1:], 'pairs', swap)]
    gather x2 -> x0, local copies, waits for them, and re-layouts: 1.17 us -> none  [the longest x1 0.59 us: shards(): left = jnp.take(table, position[:, 0], axis=0)]
    dot_general x1, matrix products: 1.8 us -> 1.14 us  [shards(): jnp.einsum('kpfrj,pft->krjt', stacked, lag_weights, precision=lax.Precisi...]
  transfers between devices with their start and end apart: 11 -> 11, of which waited for: 8 -> 7; matrix products, arithmetic and copies ran while one was open for 4% -> 4% of each run, Pallas kernels for 0% -> 0%
where the time goes in v8:
time: 57.2 us; the launch traced here: 57 us
  starting transfers between devices  17.2 us (30%)
  waiting for transfers between devices  16.6 us (29%)
  between operations  7.88 us (14%)
  matrix products  7.35 us (13%)
  local copies, waits for them, and re-layouts  5.21 us (9%)
  other arithmetic  2.71 us (5%)
    ppermute x3, waiting for transfers between devices, shards(): lax.ppermute(chunk, axes, reduce_perm(e)).astype(jnp.float32)  7.14 us
    ppermute x3, starting transfers between devices, shards(): pieces.append(lax.ppermute(message, axes, gather_perm(d)))  5.98 us
    ppermute x3, starting transfers between devices, shards(): lax.ppermute(chunk, axes, reduce_perm(e)).astype(jnp.float32)  5.97 us
    ppermute x3, waiting for transfers between devices, shards(): pieces.append(lax.ppermute(message, axes, gather_perm(d)))  5.45 us
    dot_general x1, matrix products, shards(): jnp.dot(samples, band_table(), preferred_element_type=jnp.float32)  4.89 us
    ppermute x1, waiting for transfers between devices, shards(): from_far = lax.ppermute(own, 'pairs', chip_shift(2))  2.47 us
    reshape x2, local copies, waits for them, and re-layouts, shards(): gathered[:, :, spec_rows:]  2.22 us
    ppermute x1, starting transfers between devices, shards(): from_far = lax.ppermute(own, 'pairs', chip_shift(2))  1.89 us
  transfers between devices with their start and end apart: 11, of which 7 were waited for; matrix products, arithmetic and copies ran while one was open for 4% of the time, Pallas kernels for 0%

profile of v8, /device:TPU:0, one launch (start us, length us, event | category | flops | bytes accessed | tf_op | source)
XLA Modules:
  0.0 57.0 jit_solution(470094161661966939)
XLA Ops:
  0.0 0.0 copy-start
  0.0 4.9 %convolution_bitcast_fusion.1 = f32[768,64]{1,0:T(8,128)S(1)} fusion(bf16[768,4096]{1,0:T(8,128)(2,1)} %bitcast.131, bf16[4096,64]{1,0:T(8,128)(2,1)} %constant.168.clone), kind=kOutput, calls=%fused_computation.12 | convolution fusion | flops 402653184 | bytes 7012352 | tf_op jit(solution)/shard_map/dot_general | solution.py:73
  4.9 0.3 fusion.28
  5.2 0.6 %multiply_convert_fusion.1 = (bf16[768,32]{1,0:T(8,128)(2,1)S(1)}, f32[768,32]{1,0:T(8,128)S(1)}) fusion(f32[768,64]{1,0:T(8,128)S(1)} %convolution_bitcast_fusion.1, f32[768]{0:T(1024)S(1)} %broadcast_multiply_fusion, f32[768,32]{1,0:T(8,128)S(1)} %get-tuple-element.8), kind=kLoop, calls=%fused_computation.26 | loop fusion | flops 221184 | bytes 347136 | tf_op jit(solution)/shard_map/convert.4
  5.8 0.2 multiply_convert_fusion
  6.0 0.1 copy.23
  6.1 0.1 copy.22
  6.2 1.6 %collective-permute-start.2 = (bf16[384,128]{1,0:T(8,128)(2,1)S(1)}, bf16[384,128]{1,0:T(8,128)(2,1)S(1)}, u32[]{:S(2)}, u32[]{:S(2)}) collective-permute-start(bf16[384,128]{1,0:T(8,128)(2,1)S(1)} %bitcast.123), channel_id=1, source_target_pairs={{0,32},{16,48},{32,64},{48,80},{64,96},{80,112},{96,0},{112,16},{1... | collective-permute-start | bytes 294920 | tf_op jit(solution)/shard_map/ppermute | solution.py:92
  7.9 1.7 %collective-permute-start = (bf16[384,128]{1,0:T(8,128)(2,1)S(1)}, bf16[384,128]{1,0:T(8,128)(2,1)S(1)}, u32[]{:S(2)}, u32[]{:S(2)}) collective-permute-start(bf16[384,128]{1,0:T(8,128)(2,1)S(1)} %bitcast.124), channel_id=1, source_target_pairs={{0,96},{16,112},{32,0},{48,16},{64,32},{80,48},{96,64},{112,80},{1... | collective-permute-start | bytes 294920 | tf_op jit(solution)/shard_map/ppermute | solution.py:93
  9.6 1.9 %collective-permute-start.1 = (bf16[384,128]{1,0:T(8,128)(2,1)S(1)}, bf16[384,128]{1,0:T(8,128)(2,1)S(1)}, u32[]{:S(2)}, u32[]{:S(2)}) collective-permute-start(bf16[384,128]{1,0:T(8,128)(2,1)S(1)} %bitcast.125), channel_id=1, source_target_pairs={{0,64},{16,80},{32,96},{48,112},{64,0},{80,16},{96,32},{112,48},{1... | collective-permute-start | bytes 294920 | tf_op jit(solution)/shard_map/ppermute | solution.py:94
  11.4 0.0 collective-permute-start.3
  11.4 0.0 copy-done
  11.5 0.2 fusion.23
  11.7 0.5 collective-permute-done.2
  12.1 1.1 %collective-permute-done = bf16[384,128]{1,0:T(8,128)(2,1)S(1)} collective-permute-done((bf16[384,128]{1,0:T(8,128)(2,1)S(1)}, bf16[384,128]{1,0:T(8,128)(2,1)S(1)}, u32[]{:S(2)}, u32[]{:S(2)}) %collective-permute-start) | collective-permute-done | bytes 98336 | tf_op jit(solution)/shard_map/ppermute | solution.py:93
  13.2 2.5 %collective-permute-done.1 = bf16[384,128]{1,0:T(8,128)(2,1)S(1)} collective-permute-done((bf16[384,128]{1,0:T(8,128)(2,1)S(1)}, bf16[384,128]{1,0:T(8,128)(2,1)S(1)}, u32[]{:S(2)}, u32[]{:S(2)}) %collective-permute-start.1) | collective-permute-done | bytes 98336 | tf_op jit(solution)/shard_map/ppermute | solution.py:94
  15.7 0.1 collective-permute-start.4
  15.9 0.7 %fusion.30 = (s32[1,1]{1,0:T(1,128)}, s32[1,1]{1,0:T(1,128)}, s32[1,1]{1,0:T(1,128)}, s32[1,1]{1,0:T(1,128)}) fusion(s32[2,2]{1,0:T(2,128)S(1)} %fusion.25), kind=kLoop, calls=%fused_computation.83 | loop fusion | bytes 32 | tf_op jit(solution)/shard_map/slice | solution.py:108
  24.1 0.1 maximum_bitcast_fusion
  24.2 0.0 collective-permute-done.3
  24.2 0.0 collective-permute-done.4
  24.2 0.1 maximum_select_fusion
  24.4 0.1 copy.24
  24.5 0.2 copy.25
  24.7 0.1 reshape.68
  24.9 0.1 maximum_bitcast_fusion.2
  25.0 1.7 %collective-permute-start.5 = (bf16[2,480,128]{2,1,0:T(8,128)(2,1)S(1)}, bf16[2,480,128]{2,1,0:T(8,128)(2,1)S(1)}, u32[]{:S(2)}, u32[]{:S(2)}) collective-permute-start(bf16[2,480,128]{2,1,0:T(8,128)(2,1)S(1)} %get-tuple-element.19), channel_id=1, source_target_pairs={{0,1},{1,2},{2,3},{3,0},{4,5},{5,6},{6,7},{7,4},{8,9},{9,10},{10,1... | collective-permute-start | bytes 737288 | tf_op jit(solution)/shard_map/ppermute | solution.py:150
  26.7 2.9 %collective-permute-start.6 = (bf16[2,480,128]{2,1,0:T(8,128)(2,1)S(1)}, bf16[2,480,128]{2,1,0:T(8,128)(2,1)S(1)}, u32[]{:S(2)}, u32[]{:S(2)}) collective-permute-start(bf16[2,480,128]{2,1,0:T(8,128)(2,1)S(1)} %get-tuple-element.20), channel_id=1, source_target_pairs={{0,2},{1,3},{2,0},{3,1},{4,6},{5,7},{6,4},{7,5},{8,10},{9,11},{10,... | collective-permute-start | bytes 737288 | tf_op jit(solution)/shard_map/ppermute | solution.py:150
  29.6 1.3 %collective-permute-start.7 = (bf16[2,480,128]{2,1,0:T(8,128)(2,1)S(1)}, bf16[2,480,128]{2,1,0:T(8,128)(2,1)S(1)}, u32[]{:S(2)}, u32[]{:S(2)}) collective-permute-start(bf16[2,480,128]{2,1,0:T(8,128)(2,1)S(1)} %get-tuple-element.21), channel_id=1, source_target_pairs={{0,3},{1,0},{2,1},{3,2},{4,7},{5,4},{6,5},{7,6},{8,11},{9,8},{10,9... | collective-permute-start | bytes 737288 | tf_op jit(solution)/shard_map/ppermute | solution.py:150
  31.0 1.5 %collective-permute-done.5 = bf16[2,480,128]{2,1,0:T(8,128)(2,1)S(1)} collective-permute-done((bf16[2,480,128]{2,1,0:T(8,128)(2,1)S(1)}, bf16[2,480,128]{2,1,0:T(8,128)(2,1)S(1)}, u32[]{:S(2)}, u32[]{:S(2)}) %collective-permute-start.5) | collective-permute-done | bytes 245792 | tf_op jit(solution)/shard_map/ppermute | solution.py:150
  32.5 4.0 %collective-permute-done.6 = bf16[2,480,128]{2,1,0:T(8,128)(2,1)S(1)} collective-permute-done((bf16[2,480,128]{2,1,0:T(8,128)(2,1)S(1)}, bf16[2,480,128]{2,1,0:T(8,128)(2,1)S(1)}, u32[]{:S(2)}, u32[]{:S(2)}) %collective-permute-start.6) | collective-permute-done | bytes 245792 | tf_op jit(solution)/shard_map/ppermute | solution.py:150
  36.4 0.0 collective-permute-done.7
  36.5 0.1 pad_maximum_fusion
  36.5 0.3 reshape.60
  36.8 1.9 %copy.28 = bf16[4,2,32,6,2,32]{2,3,4,0,5,1:T(8,128)(2,1)S(1)} copy(bf16[4,2,32,6,2,32]{5,4,3,2,1,0:T(2,128)(2,1)S(1)} %reshape.60) | data formatting | bytes 393216 | tf_op jit(solution)/shard_map/reshape | solution.py:155
  38.7 0.5 copy.31
  39.3 0.2 fusion.29
  39.5 1.3 %fusion.9 = bf16[2,32,4,8,2,128]{5,3,4,2,1,0:T(8,128)(2,1)S(1)} fusion(bf16[4,2,6,1,32,128]{5,2,3,0,4,1:T(8,128)(2,1)S(1)} %get-tuple-element.13, bf16[4,2,6,1,32,128]{5,2,3,0,4,1:T(8,128)(2,1)S(1)} %get-tuple-element.12, bf16[4,2,6,2,32,128]{5,2,3,0,4,1:T(8,128)(2,1)S(1)} %copy.31, bf16[4,2,32,6,2,32]{2,3,4,0,5,1:T(8,128)(2,1)S(1)} %copy.28), kind=kOutput, calls=%fused_computation.9 | convolution fusion | flops 55574528 | bytes 2818048 | tf_op jit(solution)/shard_map/akscfm,akscfn->kfmn/dot_general | solution.py:159
  40.8 0.0 copy-start.1
  40.8 0.3 copy.32
  41.1 0.1 dynamic-slice_bitcast_fusion.2
  41.2 4.1 %collective-permute-start.10 = (bf16[1024,128]{1,0:T(8,128)(2,1)S(1)}, bf16[1024,128]{1,0:T(8,128)(2,1)S(1)}, u32[]{:S(2)}, u32[]{:S(2)}) collective-permute-start(bf16[1024,128]{1,0:T(8,128)(2,1)S(1)} %get-tuple-element.10), channel_id=1, source_target_pairs={{0,12},{1,13},{2,14},{3,15},{4,0},{5,1},{6,2},{7,3},{8,4},{9,5},{1... | collective-permute-start | bytes 786440 | tf_op jit(solution)/shard_map/ppermute | solution.py:171
  45.3 0.0 collective-permute-start.8
  45.3 1.8 %collective-permute-start.9 = (bf16[1024,128]{1,0:T(8,128)(2,1)S(1)}, bf16[1024,128]{1,0:T(8,128)(2,1)S(1)}, u32[]{:S(2)}, u32[]{:S(2)}) collective-permute-start(bf16[1024,128]{1,0:T(8,128)(2,1)S(1)} %get-tuple-element.11), channel_id=1, source_target_pairs={{0,8},{1,9},{2,10},{3,11},{4,12},{5,13},{6,14},{7,15},{8,0},{9,1},... | collective-permute-start | bytes 786440 | tf_op jit(solution)/shard_map/ppermute | solution.py:171
  47.1 0.2 fusion.22
  47.3 0.0 copy-done.1
  47.3 0.6 %dynamic_slice.59 = s32[1]{0:T(128)} dynamic-slice(s32[8]{0:T(128)S(1)} %copy-done.1, s32[]{:T(128)S(6)} %select_n.132), dynamic_slice_sizes={1} | dynamic-slice | bytes 12 | tf_op jit(solution)/shard_map/dynamic_slice | solution.py:102
  47.9 0.6 %compare_convert_fusion = f32[2]{0:T(128)S(1)} fusion(s32[]{:T(128)} %bitcast.49), kind=kLoop, calls=%fused_computation.68 | loop fusion | flops 4 | bytes 12 | tf_op jit(solution)/shard_map/convert_element_type | solution.py:181
  48.5 0.6 %collective-permute-done.10 = bf16[1024,128]{1,0:T(8,128)(2,1)S(1)} collective-permute-done((bf16[1024,128]{1,0:T(8,128)(2,1)S(1)}, bf16[1024,128]{1,0:T(8,128)(2,1)S(1)}, u32[]{:S(2)}, u32[]{:S(2)}) %collective-permute-start.10) | collective-permute-done | bytes 262176 | tf_op jit(solution)/shard_map/ppermute | solution.py:171
  49.2 6.5 %collective-permute-done.8 = bf16[1024,128]{1,0:T(8,128)(2,1)S(1)} collective-permute-done((bf16[1024,128]{1,0:T(8,128)(2,1)S(1)}, bf16[1024,128]{1,0:T(8,128)(2,1)S(1)}, u32[]{:S(2)}, u32[]{:S(2)}) %collective-permute-start.8) | collective-permute-done | bytes 262176 | tf_op jit(solution)/shard_map/ppermute | solution.py:171
  55.7 0.0 collective-permute-done.9
  55.7 0.1 fusion.16
  55.8 1.1 %fusion.13 = bf16[1,2,8,128,128]{4,3,2,1,0:T(8,128)(2,1)} fusion(bf16[2,32,128,1,1]{2,1,0,4,3:T(8,128)(2,1)S(1)} %bitcast.130, bf16[2,2,32,8,128]{4,3,2,1,0:T(8,128)(2,1)S(1)} %bitcast.128, f32[2]{0:T(128)S(1)} %compare_convert_fusion), kind=kOutput, calls=%fused_computation.11 | convolution fusion | flops 34078720 | bytes 802824 | tf_op jit(solution)/shard_map/kpfrj,pft->krjt/dot_general | solution.py:174
  (13 shorter events, 0.3 us)
Async XLA Ops:
  0.0 11.5 %copy-start = (s32[8,2,2]{0,2,1:T(2,128)S(1)}, s32[8,2,2]{0,2,1:T(2,128)}, u32[]{:S(2)}) copy-start(s32[8,2,2]{0,2,1:T(2,128)} %param.5) | copy-start | bytes 388
  6.2 5.9 %collective-permute-start.2 = (bf16[384,128]{1,0:T(8,128)(2,1)S(1)}, bf16[384,128]{1,0:T(8,128)(2,1)S(1)}, u32[]{:S(2)}, u32[]{:S(2)}) collective-permute-start(bf16[384,128]{1,0:T(8,128)(2,1)S(1)} %bitcast.123), channel_id=1, source_target_pairs={{0,32},{16,48},{32,64},{48,80},{64,96},{80,112},{96,0},{112,16},{1... | collective-permute-start | bytes 294920 | tf_op jit(solution)/shard_map/ppermute | solution.py:92
  7.9 5.3 %collective-permute-start = (bf16[384,128]{1,0:T(8,128)(2,1)S(1)}, bf16[384,128]{1,0:T(8,128)(2,1)S(1)}, u32[]{:S(2)}, u32[]{:S(2)}) collective-permute-start(bf16[384,128]{1,0:T(8,128)(2,1)S(1)} %bitcast.124), channel_id=1, source_target_pairs={{0,96},{16,112},{32,0},{48,16},{64,32},{80,48},{96,64},{112,80},{1... | collective-permute-start | bytes 294920 | tf_op jit(solution)/shard_map/ppermute | solution.py:93
  9.6 6.1 %collective-permute-start.1 = (bf16[384,128]{1,0:T(8,128)(2,1)S(1)}, bf16[384,128]{1,0:T(8,128)(2,1)S(1)}, u32[]{:S(2)}, u32[]{:S(2)}) collective-permute-start(bf16[384,128]{1,0:T(8,128)(2,1)S(1)} %bitcast.125), channel_id=1, source_target_pairs={{0,64},{16,80},{32,96},{48,112},{64,0},{80,16},{96,32},{112,48},{1... | collective-permute-start | bytes 294920 | tf_op jit(solution)/shard_map/ppermute | solution.py:94
  11.4 12.7 %collective-permute-start.3 = (bf16[384,128]{1,0:T(8,128)(2,1)S(1)}, bf16[384,128]{1,0:T(8,128)(2,1)S(1)}, u32[]{:S(2)}, u32[]{:S(2)}) collective-permute-start(bf16[384,128]{1,0:T(8,128)(2,1)S(1)} %bitcast.126), channel_id=1, source_target_pairs={{0,16},{16,0},{32,48},{48,32},{64,80},{80,64},{96,112},{112,96},{1... | collective-permute-start | bytes 294920 | tf_op jit(solution)/shard_map/ppermute | solution.py:91
  15.7 8.5 %collective-permute-start.4 = (bf16[3,384,128]{2,1,0:T(8,128)(2,1)S(1)}, bf16[3,384,128]{2,1,0:T(8,128)(2,1)S(1)}, u32[]{:S(2)}, u32[]{:S(2)}) collective-permute-start(bf16[3,384,128]{2,1,0:T(8,128)(2,1)S(1)} %pad_maximum_fusion.3), channel_id=1, source_target_pairs={{0,16},{16,0},{32,48},{48,32},{64,80},{80,64},{96,112},{112,96},{1... | collective-permute-start | bytes 884744 | tf_op jit(solution)/shard_map/ppermute | solution.py:96
  25.0 7.5 %collective-permute-start.5 = (bf16[2,480,128]{2,1,0:T(8,128)(2,1)S(1)}, bf16[2,480,128]{2,1,0:T(8,128)(2,1)S(1)}, u32[]{:S(2)}, u32[]{:S(2)}) collective-permute-start(bf16[2,480,128]{2,1,0:T(8,128)(2,1)S(1)} %get-tuple-element.19), channel_id=1, source_target_pairs={{0,1},{1,2},{2,3},{3,0},{4,5},{5,6},{6,7},{7,4},{8,9},{9,10},{10,1... | collective-permute-start | bytes 737288 | tf_op jit(solution)/shard_map/ppermute | solution.py:150
  26.7 9.7 %collective-permute-start.6 = (bf16[2,480,128]{2,1,0:T(8,128)(2,1)S(1)}, bf16[2,480,128]{2,1,0:T(8,128)(2,1)S(1)}, u32[]{:S(2)}, u32[]{:S(2)}) collective-permute-start(bf16[2,480,128]{2,1,0:T(8,128)(2,1)S(1)} %get-tuple-element.20), channel_id=1, source_target_pairs={{0,2},{1,3},{2,0},{3,1},{4,6},{5,7},{6,4},{7,5},{8,10},{9,11},{10,... | collective-permute-start | bytes 737288 | tf_op jit(solution)/shard_map/ppermute | solution.py:150
  29.6 6.8 %collective-permute-start.7 = (bf16[2,480,128]{2,1,0:T(8,128)(2,1)S(1)}, bf16[2,480,128]{2,1,0:T(8,128)(2,1)S(1)}, u32[]{:S(2)}, u32[]{:S(2)}) collective-permute-start(bf16[2,480,128]{2,1,0:T(8,128)(2,1)S(1)} %get-tuple-element.21), channel_id=1, source_target_pairs={{0,3},{1,0},{2,1},{3,2},{4,7},{5,4},{6,5},{7,6},{8,11},{9,8},{10,9... | collective-permute-start | bytes 737288 | tf_op jit(solution)/shard_map/ppermute | solution.py:150
  40.8 6.5 %copy-start.1 = (s32[8]{0:T(128)S(1)}, s32[8]{0:T(128)}, u32[]{:S(2)}) copy-start(s32[8]{0:T(128)} %param.6) | copy-start | bytes 100
  41.2 8.0 %collective-permute-start.10 = (bf16[1024,128]{1,0:T(8,128)(2,1)S(1)}, bf16[1024,128]{1,0:T(8,128)(2,1)S(1)}, u32[]{:S(2)}, u32[]{:S(2)}) collective-permute-start(bf16[1024,128]{1,0:T(8,128)(2,1)S(1)} %get-tuple-element.10), channel_id=1, source_target_pairs={{0,12},{1,13},{2,14},{3,15},{4,0},{5,1},{6,2},{7,3},{8,4},{9,5},{1... | collective-permute-start | bytes 786440 | tf_op jit(solution)/shard_map/ppermute | solution.py:171
  45.3 10.4 %collective-permute-start.8 = (bf16[1024,128]{1,0:T(8,128)(2,1)S(1)}, bf16[1024,128]{1,0:T(8,128)(2,1)S(1)}, u32[]{:S(2)}, u32[]{:S(2)}) collective-permute-start(bf16[1024,128]{1,0:T(8,128)(2,1)S(1)} %get-tuple-element.9), channel_id=1, source_target_pairs={{0,4},{1,5},{2,6},{3,7},{4,8},{5,9},{6,10},{7,11},{8,12},{9,13},{1... | collective-permute-start | bytes 786440 | tf_op jit(solution)/shard_map/ppermute | solution.py:171
  45.3 10.4 %collective-permute-start.9 = (bf16[1024,128]{1,0:T(8,128)(2,1)S(1)}, bf16[1024,128]{1,0:T(8,128)(2,1)S(1)}, u32[]{:S(2)}, u32[]{:S(2)}) collective-permute-start(bf16[1024,128]{1,0:T(8,128)(2,1)S(1)} %get-tuple-element.11), channel_id=1, source_target_pairs={{0,8},{1,9},{2,10},{3,11},{4,12},{5,13},{6,14},{7,15},{8,0},{9,1},... | collective-permute-start | bytes 786440 | tf_op jit(solution)/shard_map/ppermute | solution.py:171

commit v9 on v7

--- a/solution.py
+++ b/solution.py
@@ -171,7 +171,7 @@
         "kpfrj,pft->krjt",
         stacked,
         lag_weights,
-        precision=lax.Precision.HIGH,
+        precision=lax.Precision.DEFAULT,
         preferred_element_type=jnp.float32,
     )
     masked = correlation * live_slots.astype(jnp.float32)[:, None, None, None]

time: 52.2 us -> 51.5 us (0.987)
  matrix products: 8.01 us -> 7.34 us
    dot_general x1, matrix products: 1.8 us -> 1.13 us  [shards(): jnp.einsum('kpfrj,pft->krjt', stacked, lag_weights, precision=lax.Precisi...]
where the time goes in v9:
time: 51.5 us; the launch traced here: 51.4 us
  waiting for transfers between devices  17.8 us (35%)
  starting transfers between devices  17.2 us (33%)
  matrix products  7.34 us (14%)
  local copies, waits for them, and re-layouts  5.86 us (11%)
  other arithmetic  2.89 us (6%)
    ppermute x3, waiting for transfers between devices, shards(): lax.ppermute(chunk, axes, reduce_perm(e)).astype(jnp.float32)  7.14 us
    ppermute x3, starting transfers between devices, shards(): pieces.append(lax.ppermute(message, axes, gather_perm(d)))  5.98 us
    ppermute x3, starting transfers between devices, shards(): lax.ppermute(chunk, axes, reduce_perm(e)).astype(jnp.float32)  5.97 us
    ppermute x3, waiting for transfers between devices, shards(): pieces.append(lax.ppermute(message, axes, gather_perm(d)))  5.45 us
    dot_general x1, matrix products, shards(): jnp.dot(samples, band_table(), preferred_element_type=jnp.float32)  4.89 us
    ppermute x1, waiting for transfers between devices, shards(): from_far = lax.ppermute(own, 'pairs', chip_shift(2))  2.47 us
    reshape x2, local copies, waits for them, and re-layouts, shards(): gathered[:, :, spec_rows:]  2.22 us
    ppermute x1, starting transfers between devices, shards(): from_far = lax.ppermute(own, 'pairs', chip_shift(2))  1.89 us
  transfers between devices with their start and end apart: 11, of which 8 were waited for; matrix products, arithmetic and copies ran while one was open for 4% of the time, Pallas kernels for 0%

profile of v9, /device:TPU:0, one launch (start us, length us, event | category | flops | bytes accessed | tf_op | source)
XLA Modules:
  0.0 51.4 jit_solution(18345564383954038686)
XLA Ops:
  0.0 0.0 copy-start
  0.0 4.9 %convolution_bitcast_fusion.1 = f32[768,64]{1,0:T(8,128)S(1)} fusion(bf16[768,4096]{1,0:T(8,128)(2,1)} %bitcast.128, bf16[4096,64]{1,0:T(8,128)(2,1)} %constant.168.clone), kind=kOutput, calls=%fused_computation.14 | convolution fusion | flops 402653184 | bytes 7012352 | tf_op jit(solution)/shard_map/dot_general | solution.py:73
  4.9 0.3 fusion.28
  5.2 0.6 %multiply_convert_fusion.1 = (bf16[768,32]{1,0:T(8,128)(2,1)S(1)}, f32[768,32]{1,0:T(8,128)S(1)}) fusion(f32[768,64]{1,0:T(8,128)S(1)} %convolution_bitcast_fusion.1, f32[768]{0:T(1024)S(1)} %broadcast_multiply_fusion, f32[768,32]{1,0:T(8,128)S(1)} %get-tuple-element.11), kind=kLoop, calls=%fused_computation.28 | loop fusion | flops 221184 | bytes 347136 | tf_op jit(solution)/shard_map/convert.4
  5.8 0.2 multiply_convert_fusion
  6.0 0.1 copy.16
  6.1 0.1 copy.15
  6.2 1.6 %collective-permute-start.2 = (bf16[384,128]{1,0:T(8,128)(2,1)S(1)}, bf16[384,128]{1,0:T(8,128)(2,1)S(1)}, u32[]{:S(2)}, u32[]{:S(2)}) collective-permute-start(bf16[384,128]{1,0:T(8,128)(2,1)S(1)} %bitcast.120), channel_id=1, source_target_pairs={{0,32},{16,48},{32,64},{48,80},{64,96},{80,112},{96,0},{112,16},{1... | collective-permute-start | bytes 294920 | tf_op jit(solution)/shard_map/ppermute | solution.py:92
  7.9 1.7 %collective-permute-start = (bf16[384,128]{1,0:T(8,128)(2,1)S(1)}, bf16[384,128]{1,0:T(8,128)(2,1)S(1)}, u32[]{:S(2)}, u32[]{:S(2)}) collective-permute-start(bf16[384,128]{1,0:T(8,128)(2,1)S(1)} %bitcast.121), channel_id=1, source_target_pairs={{0,96},{16,112},{32,0},{48,16},{64,32},{80,48},{96,64},{112,80},{1... | collective-permute-start | bytes 294920 | tf_op jit(solution)/shard_map/ppermute | solution.py:93
  9.6 1.9 %collective-permute-start.1 = (bf16[384,128]{1,0:T(8,128)(2,1)S(1)}, bf16[384,128]{1,0:T(8,128)(2,1)S(1)}, u32[]{:S(2)}, u32[]{:S(2)}) collective-permute-start(bf16[384,128]{1,0:T(8,128)(2,1)S(1)} %bitcast.122), channel_id=1, source_target_pairs={{0,64},{16,80},{32,96},{48,112},{64,0},{80,16},{96,32},{112,48},{1... | collective-permute-start | bytes 294920 | tf_op jit(solution)/shard_map/ppermute | solution.py:94
  11.4 0.0 collective-permute-start.3
  11.4 0.0 copy-done
  11.5 0.2 fusion.23
  11.7 0.2 slice_reduce_fusion.1
  11.9 0.2 collective-permute-done.2
  12.1 1.1 %collective-permute-done = bf16[384,128]{1,0:T(8,128)(2,1)S(1)} collective-permute-done((bf16[384,128]{1,0:T(8,128)(2,1)S(1)}, bf16[384,128]{1,0:T(8,128)(2,1)S(1)}, u32[]{:S(2)}, u32[]{:S(2)}) %collective-permute-start) | collective-permute-done | bytes 98336 | tf_op jit(solution)/shard_map/ppermute | solution.py:93
  13.2 2.5 %collective-permute-done.1 = bf16[384,128]{1,0:T(8,128)(2,1)S(1)} collective-permute-done((bf16[384,128]{1,0:T(8,128)(2,1)S(1)}, bf16[384,128]{1,0:T(8,128)(2,1)S(1)}, u32[]{:S(2)}, u32[]{:S(2)}) %collective-permute-start.1) | collective-permute-done | bytes 98336 | tf_op jit(solution)/shard_map/ppermute | solution.py:94
  15.7 0.1 collective-permute-start.4
  15.8 0.1 maximum_bitcast_fusion
  15.9 0.0 collective-permute-done.3
  15.9 1.5 %collective-permute-done.4 = bf16[3,384,128]{2,1,0:T(8,128)(2,1)S(1)} collective-permute-done((bf16[3,384,128]{2,1,0:T(8,128)(2,1)S(1)}, bf16[3,384,128]{2,1,0:T(8,128)(2,1)S(1)}, u32[]{:S(2)}, u32[]{:S(2)}) %collective-permute-start.4) | collective-permute-done | bytes 294944 | tf_op jit(solution)/shard_map/ppermute | solution.py:96
  17.4 0.1 maximum_select_fusion
  17.6 0.1 copy.17
  17.6 0.6 %gather_fusion.1 = bf16[2,384,128]{2,1,0:T(8,128)(2,1)S(1)} fusion(bf16[8,384,128]{2,1,0:T(8,128)(2,1)S(1)} %bitcast.103, s32[1024]{0:T(1024)S(1)} %pad_clamp_fusion), kind=kCustom, calls=%fused_computation.1.clone | custom fusion | bytes 393224 | tf_op jit(solution)/shard_map/jit(_take)/gather | solution.py:104
  18.2 0.1 select_bitcast_fusion
  18.3 0.2 copy.18
  18.5 0.1 reshape.64
  18.6 0.6 %gather_fusion = bf16[2,384,128]{2,1,0:T(8,128)(2,1)S(1)} fusion(bf16[8,384,128]{2,1,0:T(8,128)(2,1)S(1)} %bitcast.104, s32[1024]{0:T(1024)S(1)} %pad_clamp_fusion.1), kind=kCustom, calls=%fused_computation.clone | custom fusion | bytes 393224 | tf_op jit(solution)/shard_map/jit(_take)/gather | solution.py:105
  19.2 0.1 broadcast_select_fusion
  19.3 0.1 maximum_bitcast_fusion.2
  19.5 1.7 %collective-permute-start.5 = (bf16[2,480,128]{2,1,0:T(8,128)(2,1)S(1)}, bf16[2,480,128]{2,1,0:T(8,128)(2,1)S(1)}, u32[]{:S(2)}, u32[]{:S(2)}) collective-permute-start(bf16[2,480,128]{2,1,0:T(8,128)(2,1)S(1)} %get-tuple-element.18), channel_id=1, source_target_pairs={{0,1},{1,2},{2,3},{3,0},{4,5},{5,6},{6,7},{7,4},{8,9},{9,10},{10,1... | collective-permute-start | bytes 737288 | tf_op jit(solution)/shard_map/ppermute | solution.py:146
  21.2 2.9 %collective-permute-start.6 = (bf16[2,480,128]{2,1,0:T(8,128)(2,1)S(1)}, bf16[2,480,128]{2,1,0:T(8,128)(2,1)S(1)}, u32[]{:S(2)}, u32[]{:S(2)}) collective-permute-start(bf16[2,480,128]{2,1,0:T(8,128)(2,1)S(1)} %get-tuple-element.19), channel_id=1, source_target_pairs={{0,2},{1,3},{2,0},{3,1},{4,6},{5,7},{6,4},{7,5},{8,10},{9,11},{10,... | collective-permute-start | bytes 737288 | tf_op jit(solution)/shard_map/ppermute | solution.py:146
  24.1 1.3 %collective-permute-start.7 = (bf16[2,480,128]{2,1,0:T(8,128)(2,1)S(1)}, bf16[2,480,128]{2,1,0:T(8,128)(2,1)S(1)}, u32[]{:S(2)}, u32[]{:S(2)}) collective-permute-start(bf16[2,480,128]{2,1,0:T(8,128)(2,1)S(1)} %get-tuple-element.20), channel_id=1, source_target_pairs={{0,3},{1,0},{2,1},{3,2},{4,7},{5,4},{6,5},{7,6},{8,11},{9,8},{10,9... | collective-permute-start | bytes 737288 | tf_op jit(solution)/shard_map/ppermute | solution.py:146
  25.5 1.5 %collective-permute-done.5 = bf16[2,480,128]{2,1,0:T(8,128)(2,1)S(1)} collective-permute-done((bf16[2,480,128]{2,1,0:T(8,128)(2,1)S(1)}, bf16[2,480,128]{2,1,0:T(8,128)(2,1)S(1)}, u32[]{:S(2)}, u32[]{:S(2)}) %collective-permute-start.5) | collective-permute-done | bytes 245792 | tf_op jit(solution)/shard_map/ppermute | solution.py:146
  26.9 4.0 %collective-permute-done.6 = bf16[2,480,128]{2,1,0:T(8,128)(2,1)S(1)} collective-permute-done((bf16[2,480,128]{2,1,0:T(8,128)(2,1)S(1)}, bf16[2,480,128]{2,1,0:T(8,128)(2,1)S(1)}, u32[]{:S(2)}, u32[]{:S(2)}) %collective-permute-start.6) | collective-permute-done | bytes 245792 | tf_op jit(solution)/shard_map/ppermute | solution.py:146
  30.9 0.0 collective-permute-done.7
  30.9 0.1 pad_maximum_fusion
  31.0 0.3 reshape.65
  31.3 1.9 %copy.24 = bf16[4,2,32,6,2,32]{2,3,4,0,5,1:T(8,128)(2,1)S(1)} copy(bf16[4,2,32,6,2,32]{5,4,3,2,1,0:T(2,128)(2,1)S(1)} %reshape.65) | data formatting | bytes 393216 | tf_op jit(solution)/shard_map/reshape | solution.py:151
  33.2 0.5 %copy.27 = bf16[4,2,6,2,32,128]{5,2,3,0,4,1:T(8,128)(2,1)S(1)} copy(bf16[4,2,6,2,32,128]{5,4,3,2,1,0:T(8,128)(2,1)S(1)} %bitcast.102) | data formatting | bytes 1572864 | tf_op jit(solution)/shard_map/reshape | solution.py:148
  33.8 0.2 fusion.29
  33.9 1.3 %fusion.9 = bf16[2,32,4,8,2,128]{5,3,4,2,1,0:T(8,128)(2,1)S(1)} fusion(bf16[4,2,6,1,32,128]{5,2,3,0,4,1:T(8,128)(2,1)S(1)} %get-tuple-element.16, bf16[4,2,6,1,32,128]{5,2,3,0,4,1:T(8,128)(2,1)S(1)} %get-tuple-element.15, bf16[4,2,6,2,32,128]{5,2,3,0,4,1:T(8,128)(2,1)S(1)} %copy.27, bf16[4,2,32,6,2,32]{2,3,4,0,5,1:T(8,128)(2,1)S(1)} %copy.24), kind=kOutput, calls=%fused_computation.11 | convolution fusion | flops 55574528 | bytes 2818048 | tf_op jit(solution)/shard_map/akscfm,akscfn->kfmn/dot_general | solution.py:155
  35.3 0.0 copy-start.1
  35.3 0.3 copy.28
  35.6 0.1 dynamic-slice_bitcast_fusion.2
  35.6 4.1 %collective-permute-start.10 = (bf16[1024,128]{1,0:T(8,128)(2,1)S(1)}, bf16[1024,128]{1,0:T(8,128)(2,1)S(1)}, u32[]{:S(2)}, u32[]{:S(2)}) collective-permute-start(bf16[1024,128]{1,0:T(8,128)(2,1)S(1)} %get-tuple-element.13), channel_id=1, source_target_pairs={{0,12},{1,13},{2,14},{3,15},{4,0},{5,1},{6,2},{7,3},{8,4},{9,5},{1... | collective-permute-start | bytes 786440 | tf_op jit(solution)/shard_map/ppermute | solution.py:167
  39.8 0.0 collective-permute-start.8
  39.8 1.8 %collective-permute-start.9 = (bf16[1024,128]{1,0:T(8,128)(2,1)S(1)}, bf16[1024,128]{1,0:T(8,128)(2,1)S(1)}, u32[]{:S(2)}, u32[]{:S(2)}) collective-permute-start(bf16[1024,128]{1,0:T(8,128)(2,1)S(1)} %get-tuple-element.14), channel_id=1, source_target_pairs={{0,8},{1,9},{2,10},{3,11},{4,12},{5,13},{6,14},{7,15},{8,0},{9,1},... | collective-permute-start | bytes 786440 | tf_op jit(solution)/shard_map/ppermute | solution.py:167
  41.6 0.2 fusion.22
  41.7 0.0 copy-done.1
  41.8 0.6 %dynamic_slice.42 = s32[1]{0:T(128)} dynamic-slice(s32[8]{0:T(128)S(1)} %copy-done.1, s32[]{:T(128)S(6)} %select_n.126), dynamic_slice_sizes={1} | dynamic-slice | bytes 12 | tf_op jit(solution)/shard_map/dynamic_slice | solution.py:102
  42.3 0.6 %compare_convert_fusion = f32[2]{0:T(128)S(1)} fusion(s32[]{:T(128)} %bitcast.45), kind=kLoop, calls=%fused_computation.72 | loop fusion | flops 4 | bytes 12 | tf_op jit(solution)/shard_map/convert_element_type | solution.py:177
  43.0 0.6 %collective-permute-done.10 = bf16[1024,128]{1,0:T(8,128)(2,1)S(1)} collective-permute-done((bf16[1024,128]{1,0:T(8,128)(2,1)S(1)}, bf16[1024,128]{1,0:T(8,128)(2,1)S(1)}, u32[]{:S(2)}, u32[]{:S(2)}) %collective-permute-start.10) | collective-permute-done | bytes 262176 | tf_op jit(solution)/shard_map/ppermute | solution.py:167
  43.7 6.5 %collective-permute-done.8 = bf16[1024,128]{1,0:T(8,128)(2,1)S(1)} collective-permute-done((bf16[1024,128]{1,0:T(8,128)(2,1)S(1)}, bf16[1024,128]{1,0:T(8,128)(2,1)S(1)}, u32[]{:S(2)}, u32[]{:S(2)}) %collective-permute-start.8) | collective-permute-done | bytes 262176 | tf_op jit(solution)/shard_map/ppermute | solution.py:167
  50.2 0.0 collective-permute-done.9
  50.2 0.1 fusion.16
  50.3 1.1 %fusion.13 = bf16[1,2,8,128,128]{4,3,2,1,0:T(8,128)(2,1)} fusion(bf16[2,32,128,1,1]{2,1,0,4,3:T(8,128)(2,1)S(1)} %bitcast.127, bf16[2,2,32,8,128]{4,3,2,1,0:T(8,128)(2,1)S(1)} %bitcast.125, f32[2]{0:T(128)S(1)} %compare_convert_fusion), kind=kOutput, calls=%fused_computation.13 | convolution fusion | flops 34078720 | bytes 802824 | tf_op jit(solution)/shard_map/kpfrj,pft->krjt/dot_general | solution.py:170
  (15 shorter events, 0.2 us)
Async XLA Ops:
  0.0 11.5 %copy-start = (s32[8,2,2]{0,2,1:T(2,128)S(1)}, s32[8,2,2]{0,2,1:T(2,128)}, u32[]{:S(2)}) copy-start(s32[8,2,2]{0,2,1:T(2,128)} %param.7) | copy-start | bytes 388
  6.2 5.9 %collective-permute-start.2 = (bf16[384,128]{1,0:T(8,128)(2,1)S(1)}, bf16[384,128]{1,0:T(8,128)(2,1)S(1)}, u32[]{:S(2)}, u32[]{:S(2)}) collective-permute-start(bf16[384,128]{1,0:T(8,128)(2,1)S(1)} %bitcast.120), channel_id=1, source_target_pairs={{0,32},{16,48},{32,64},{48,80},{64,96},{80,112},{96,0},{112,16},{1... | collective-permute-start | bytes 294920 | tf_op jit(solution)/shard_map/ppermute | solution.py:92
  7.9 5.3 %collective-permute-start = (bf16[384,128]{1,0:T(8,128)(2,1)S(1)}, bf16[384,128]{1,0:T(8,128)(2,1)S(1)}, u32[]{:S(2)}, u32[]{:S(2)}) collective-permute-start(bf16[384,128]{1,0:T(8,128)(2,1)S(1)} %bitcast.121), channel_id=1, source_target_pairs={{0,96},{16,112},{32,0},{48,16},{64,32},{80,48},{96,64},{112,80},{1... | collective-permute-start | bytes 294920 | tf_op jit(solution)/shard_map/ppermute | solution.py:93
  9.6 6.1 %collective-permute-start.1 = (bf16[384,128]{1,0:T(8,128)(2,1)S(1)}, bf16[384,128]{1,0:T(8,128)(2,1)S(1)}, u32[]{:S(2)}, u32[]{:S(2)}) collective-permute-start(bf16[384,128]{1,0:T(8,128)(2,1)S(1)} %bitcast.122), channel_id=1, source_target_pairs={{0,64},{16,80},{32,96},{48,112},{64,0},{80,16},{96,32},{112,48},{1... | collective-permute-start | bytes 294920 | tf_op jit(solution)/shard_map/ppermute | solution.py:94
  11.4 4.4 %collective-permute-start.3 = (bf16[384,128]{1,0:T(8,128)(2,1)S(1)}, bf16[384,128]{1,0:T(8,128)(2,1)S(1)}, u32[]{:S(2)}, u32[]{:S(2)}) collective-permute-start(bf16[384,128]{1,0:T(8,128)(2,1)S(1)} %bitcast.123), channel_id=1, source_target_pairs={{0,16},{16,0},{32,48},{48,32},{64,80},{80,64},{96,112},{112,96},{1... | collective-permute-start | bytes 294920 | tf_op jit(solution)/shard_map/ppermute | solution.py:91
  15.7 1.7 %collective-permute-start.4 = (bf16[3,384,128]{2,1,0:T(8,128)(2,1)S(1)}, bf16[3,384,128]{2,1,0:T(8,128)(2,1)S(1)}, u32[]{:S(2)}, u32[]{:S(2)}) collective-permute-start(bf16[3,384,128]{2,1,0:T(8,128)(2,1)S(1)} %pad_maximum_fusion.3), channel_id=1, source_target_pairs={{0,16},{16,0},{32,48},{48,32},{64,80},{80,64},{96,112},{112,96},{1... | collective-permute-start | bytes 884744 | tf_op jit(solution)/shard_map/ppermute | solution.py:96
  19.5 7.5 %collective-permute-start.5 = (bf16[2,480,128]{2,1,0:T(8,128)(2,1)S(1)}, bf16[2,480,128]{2,1,0:T(8,128)(2,1)S(1)}, u32[]{:S(2)}, u32[]{:S(2)}) collective-permute-start(bf16[2,480,128]{2,1,0:T(8,128)(2,1)S(1)} %get-tuple-element.18), channel_id=1, source_target_pairs={{0,1},{1,2},{2,3},{3,0},{4,5},{5,6},{6,7},{7,4},{8,9},{9,10},{10,1... | collective-permute-start | bytes 737288 | tf_op jit(solution)/shard_map/ppermute | solution.py:146
  21.2 9.7 %collective-permute-start.6 = (bf16[2,480,128]{2,1,0:T(8,128)(2,1)S(1)}, bf16[2,480,128]{2,1,0:T(8,128)(2,1)S(1)}, u32[]{:S(2)}, u32[]{:S(2)}) collective-permute-start(bf16[2,480,128]{2,1,0:T(8,128)(2,1)S(1)} %get-tuple-element.19), channel_id=1, source_target_pairs={{0,2},{1,3},{2,0},{3,1},{4,6},{5,7},{6,4},{7,5},{8,10},{9,11},{10,... | collective-permute-start | bytes 737288 | tf_op jit(solution)/shard_map/ppermute | solution.py:146
  24.1 6.8 %collective-permute-start.7 = (bf16[2,480,128]{2,1,0:T(8,128)(2,1)S(1)}, bf16[2,480,128]{2,1,0:T(8,128)(2,1)S(1)}, u32[]{:S(2)}, u32[]{:S(2)}) collective-permute-start(bf16[2,480,128]{2,1,0:T(8,128)(2,1)S(1)} %get-tuple-element.20), channel_id=1, source_target_pairs={{0,3},{1,0},{2,1},{3,2},{4,7},{5,4},{6,5},{7,6},{8,11},{9,8},{10,9... | collective-permute-start | bytes 737288 | tf_op jit(solution)/shard_map/ppermute | solution.py:146
  35.3 6.5 %copy-start.1 = (s32[8]{0:T(128)S(1)}, s32[8]{0:T(128)}, u32[]{:S(2)}) copy-start(s32[8]{0:T(128)} %param.8) | copy-start | bytes 100
  35.6 8.0 %collective-permute-start.10 = (bf16[1024,128]{1,0:T(8,128)(2,1)S(1)}, bf16[1024,128]{1,0:T(8,128)(2,1)S(1)}, u32[]{:S(2)}, u32[]{:S(2)}) collective-permute-start(bf16[1024,128]{1,0:T(8,128)(2,1)S(1)} %get-tuple-element.13), channel_id=1, source_target_pairs={{0,12},{1,13},{2,14},{3,15},{4,0},{5,1},{6,2},{7,3},{8,4},{9,5},{1... | collective-permute-start | bytes 786440 | tf_op jit(solution)/shard_map/ppermute | solution.py:167
  39.8 10.4 %collective-permute-start.8 = (bf16[1024,128]{1,0:T(8,128)(2,1)S(1)}, bf16[1024,128]{1,0:T(8,128)(2,1)S(1)}, u32[]{:S(2)}, u32[]{:S(2)}) collective-permute-start(bf16[1024,128]{1,0:T(8,128)(2,1)S(1)} %get-tuple-element.12), channel_id=1, source_target_pairs={{0,4},{1,5},{2,6},{3,7},{4,8},{5,9},{6,10},{7,11},{8,12},{9,13},{1... | collective-permute-start | bytes 786440 | tf_op jit(solution)/shard_map/ppermute | solution.py:167
  39.8 10.4 %collective-permute-start.9 = (bf16[1024,128]{1,0:T(8,128)(2,1)S(1)}, bf16[1024,128]{1,0:T(8,128)(2,1)S(1)}, u32[]{:S(2)}, u32[]{:S(2)}) collective-permute-start(bf16[1024,128]{1,0:T(8,128)(2,1)S(1)} %get-tuple-element.14), channel_id=1, source_target_pairs={{0,8},{1,9},{2,10},{3,11},{4,12},{5,13},{6,14},{7,15},{8,0},{9,1},... | collective-permute-start | bytes 786440 | tf_op jit(solution)/shard_map/ppermute | solution.py:167

commit v10 on v9

--- a/solution.py
+++ b/solution.py
@@ -141,7 +141,7 @@
 
     axes = ("pairs", "z", "y")
     pieces = [jnp.concatenate([right, rows_for(gather_pos)], axis=1)]
-    for d in range(1, side):
+    for d in sorted(range(1, side), key=lambda step: -min(step, side - step)):
         message = jnp.concatenate([right, rows_for((gather_pos + d) % side)], axis=1)
         pieces.append(lax.ppermute(message, axes, gather_perm(d)))
     gathered = jnp.stack(pieces)
@@ -162,7 +162,7 @@
     stacked = lax.dynamic_index_in_dim(partial_value, reduce_pos, 0, keepdims=False).astype(
         jnp.float32
     )
-    for e in range(1, side):
+    for e in sorted(range(1, side), key=lambda step: -min(step, side - step)):
         chunk = lax.dynamic_index_in_dim(partial_value, (reduce_pos + e) % side, 0, keepdims=False)
         stacked = stacked + lax.ppermute(chunk, axes, reduce_perm(e)).astype(jnp.float32)
     stacked = stacked.reshape((slot_count, 2, FREQS, rows, block_width))

time: 51.5 us -> 51 us (level)
  waiting for transfers between devices: 17.8 us -> 17.2 us
    ppermute x3, waiting for transfers between devices: 5.45 us -> 4.23 us  [shards(): pieces.append(lax.ppermute(message, axes, gather_perm(d)))]
    ppermute x3, starting transfers between devices: 5.98 us -> 6.59 us  [shards(): pieces.append(lax.ppermute(message, axes, gather_perm(d)))]
    ppermute x3, waiting for transfers between devices: 7.14 us -> 7.75 us  [shards(): lax.ppermute(chunk, axes, reduce_perm(e)).astype(jnp.float32)]
    ppermute x3, starting transfers between devices: 5.97 us -> 5.36 us  [shards(): lax.ppermute(chunk, axes, reduce_perm(e)).astype(jnp.float32)]
  transfers between devices with their start and end apart: 11 -> 11, of which waited for: 8 -> 10; matrix products, arithmetic and copies ran while one was open for 4% -> 4% of each run, Pallas kernels for 0% -> 0%
where the time goes in v10:
time: 51 us; the launch traced here: 50.8 us
  starting transfers between devices  17.2 us (34%)
  waiting for transfers between devices  17.2 us (34%)
  matrix products  7.35 us (14%)
  local copies, waits for them, and re-layouts  5.86 us (11%)
  other arithmetic  2.89 us (6%)
    ppermute x3, waiting for transfers between devices, shards(): lax.ppermute(chunk, axes, reduce_perm(e)).astype(jnp.float32)  7.75 us
    ppermute x3, starting transfers between devices, shards(): pieces.append(lax.ppermute(message, axes, gather_perm(d)))  6.59 us
    ppermute x3, starting transfers between devices, shards(): lax.ppermute(chunk, axes, reduce_perm(e)).astype(jnp.float32)  5.36 us
    dot_general x1, matrix products, shards(): jnp.dot(samples, band_table(), preferred_element_type=jnp.float32)  4.89 us
    ppermute x3, waiting for transfers between devices, shards(): pieces.append(lax.ppermute(message, axes, gather_perm(d)))  4.23 us
    ppermute x1, waiting for transfers between devices, shards(): from_far = lax.ppermute(own, 'pairs', chip_shift(2))  2.47 us
    reshape x2, local copies, waits for them, and re-layouts, shards(): gathered[:, :, spec_rows:]  2.22 us
    ppermute x1, starting transfers between devices, shards(): from_far = lax.ppermute(own, 'pairs', chip_shift(2))  1.89 us
  transfers between devices with their start and end apart: 11, of which 10 were waited for; matrix products, arithmetic and copies ran while one was open for 4% of the time, Pallas kernels for 0%

profile of v10, /device:TPU:0, one launch (start us, length us, event | category | flops | bytes accessed | tf_op | source)
XLA Modules:
  0.0 50.8 jit_solution(7866909189468317085)
XLA Ops:
  0.0 0.0 copy-start
  0.0 4.9 %convolution_bitcast_fusion.1 = f32[768,64]{1,0:T(8,128)S(1)} fusion(bf16[768,4096]{1,0:T(8,128)(2,1)} %bitcast.128, bf16[4096,64]{1,0:T(8,128)(2,1)} %constant.168.clone), kind=kOutput, calls=%fused_computation.14 | convolution fusion | flops 402653184 | bytes 7012352 | tf_op jit(solution)/shard_map/dot_general | solution.py:73
  4.9 0.3 fusion.28
  5.2 0.6 %multiply_convert_fusion.1 = (bf16[768,32]{1,0:T(8,128)(2,1)S(1)}, f32[768,32]{1,0:T(8,128)S(1)}) fusion(f32[768,64]{1,0:T(8,128)S(1)} %convolution_bitcast_fusion.1, f32[768]{0:T(1024)S(1)} %broadcast_multiply_fusion, f32[768,32]{1,0:T(8,128)S(1)} %get-tuple-element.11), kind=kLoop, calls=%fused_computation.28 | loop fusion | flops 221184 | bytes 347136 | tf_op jit(solution)/shard_map/convert.4
  5.8 0.2 multiply_convert_fusion
  6.0 0.1 copy.16
  6.1 0.1 copy.15
  6.2 1.6 %collective-permute-start.2 = (bf16[384,128]{1,0:T(8,128)(2,1)S(1)}, bf16[384,128]{1,0:T(8,128)(2,1)S(1)}, u32[]{:S(2)}, u32[]{:S(2)}) collective-permute-start(bf16[384,128]{1,0:T(8,128)(2,1)S(1)} %bitcast.120), channel_id=1, source_target_pairs={{0,32},{16,48},{32,64},{48,80},{64,96},{80,112},{96,0},{112,16},{1... | collective-permute-start | bytes 294920 | tf_op jit(solution)/shard_map/ppermute | solution.py:92
  7.9 1.7 %collective-permute-start = (bf16[384,128]{1,0:T(8,128)(2,1)S(1)}, bf16[384,128]{1,0:T(8,128)(2,1)S(1)}, u32[]{:S(2)}, u32[]{:S(2)}) collective-permute-start(bf16[384,128]{1,0:T(8,128)(2,1)S(1)} %bitcast.121), channel_id=1, source_target_pairs={{0,96},{16,112},{32,0},{48,16},{64,32},{80,48},{96,64},{112,80},{1... | collective-permute-start | bytes 294920 | tf_op jit(solution)/shard_map/ppermute | solution.py:93
  9.6 1.9 %collective-permute-start.1 = (bf16[384,128]{1,0:T(8,128)(2,1)S(1)}, bf16[384,128]{1,0:T(8,128)(2,1)S(1)}, u32[]{:S(2)}, u32[]{:S(2)}) collective-permute-start(bf16[384,128]{1,0:T(8,128)(2,1)S(1)} %bitcast.122), channel_id=1, source_target_pairs={{0,64},{16,80},{32,96},{48,112},{64,0},{80,16},{96,32},{112,48},{1... | collective-permute-start | bytes 294920 | tf_op jit(solution)/shard_map/ppermute | solution.py:94
  11.4 0.0 collective-permute-start.3
  11.4 0.0 copy-done
  11.5 0.2 fusion.23
  11.7 0.2 slice_reduce_fusion.1
  11.9 0.2 collective-permute-done.2
  12.1 1.1 %collective-permute-done = bf16[384,128]{1,0:T(8,128)(2,1)S(1)} collective-permute-done((bf16[384,128]{1,0:T(8,128)(2,1)S(1)}, bf16[384,128]{1,0:T(8,128)(2,1)S(1)}, u32[]{:S(2)}, u32[]{:S(2)}) %collective-permute-start) | collective-permute-done | bytes 98336 | tf_op jit(solution)/shard_map/ppermute | solution.py:93
  13.2 2.5 %collective-permute-done.1 = bf16[384,128]{1,0:T(8,128)(2,1)S(1)} collective-permute-done((bf16[384,128]{1,0:T(8,128)(2,1)S(1)}, bf16[384,128]{1,0:T(8,128)(2,1)S(1)}, u32[]{:S(2)}, u32[]{:S(2)}) %collective-permute-start.1) | collective-permute-done | bytes 98336 | tf_op jit(solution)/shard_map/ppermute | solution.py:94
  15.7 0.1 collective-permute-start.4
  15.8 0.1 maximum_bitcast_fusion
  15.9 0.0 collective-permute-done.3
  15.9 1.5 %collective-permute-done.4 = bf16[3,384,128]{2,1,0:T(8,128)(2,1)S(1)} collective-permute-done((bf16[3,384,128]{2,1,0:T(8,128)(2,1)S(1)}, bf16[3,384,128]{2,1,0:T(8,128)(2,1)S(1)}, u32[]{:S(2)}, u32[]{:S(2)}) %collective-permute-start.4) | collective-permute-done | bytes 294944 | tf_op jit(solution)/shard_map/ppermute | solution.py:96
  17.4 0.1 maximum_select_fusion
  17.6 0.1 copy.17
  17.6 0.6 %gather_fusion.1 = bf16[2,384,128]{2,1,0:T(8,128)(2,1)S(1)} fusion(bf16[8,384,128]{2,1,0:T(8,128)(2,1)S(1)} %bitcast.103, s32[1024]{0:T(1024)S(1)} %pad_clamp_fusion), kind=kCustom, calls=%fused_computation.1.clone | custom fusion | bytes 393224 | tf_op jit(solution)/shard_map/jit(_take)/gather | solution.py:104
  18.2 0.1 select_bitcast_fusion
  18.3 0.2 copy.18
  18.5 0.1 reshape.64
  18.6 0.6 %gather_fusion = bf16[2,384,128]{2,1,0:T(8,128)(2,1)S(1)} fusion(bf16[8,384,128]{2,1,0:T(8,128)(2,1)S(1)} %bitcast.104, s32[1024]{0:T(1024)S(1)} %pad_clamp_fusion.1), kind=kCustom, calls=%fused_computation.clone | custom fusion | bytes 393224 | tf_op jit(solution)/shard_map/jit(_take)/gather | solution.py:105
  19.2 0.1 broadcast_select_fusion
  19.3 0.1 maximum_bitcast_fusion.2
  19.5 3.4 %collective-permute-start.5 = (bf16[2,480,128]{2,1,0:T(8,128)(2,1)S(1)}, bf16[2,480,128]{2,1,0:T(8,128)(2,1)S(1)}, u32[]{:S(2)}, u32[]{:S(2)}) collective-permute-start(bf16[2,480,128]{2,1,0:T(8,128)(2,1)S(1)} %get-tuple-element.18), channel_id=1, source_target_pairs={{0,2},{1,3},{2,0},{3,1},{4,6},{5,7},{6,4},{7,5},{8,10},{9,11},{10,... | collective-permute-start | bytes 737288 | tf_op jit(solution)/shard_map/ppermute | solution.py:146
  22.8 0.7 %collective-permute-start.6 = (bf16[2,480,128]{2,1,0:T(8,128)(2,1)S(1)}, bf16[2,480,128]{2,1,0:T(8,128)(2,1)S(1)}, u32[]{:S(2)}, u32[]{:S(2)}) collective-permute-start(bf16[2,480,128]{2,1,0:T(8,128)(2,1)S(1)} %get-tuple-element.19), channel_id=1, source_target_pairs={{0,1},{1,2},{2,3},{3,0},{4,5},{5,6},{6,7},{7,4},{8,9},{9,10},{10,1... | collective-permute-start | bytes 737288 | tf_op jit(solution)/shard_map/ppermute | solution.py:146
  23.5 2.6 %collective-permute-start.7 = (bf16[2,480,128]{2,1,0:T(8,128)(2,1)S(1)}, bf16[2,480,128]{2,1,0:T(8,128)(2,1)S(1)}, u32[]{:S(2)}, u32[]{:S(2)}) collective-permute-start(bf16[2,480,128]{2,1,0:T(8,128)(2,1)S(1)} %get-tuple-element.20), channel_id=1, source_target_pairs={{0,3},{1,0},{2,1},{3,2},{4,7},{5,4},{6,5},{7,6},{8,11},{9,8},{10,9... | collective-permute-start | bytes 737288 | tf_op jit(solution)/shard_map/ppermute | solution.py:146
  26.1 1.2 %collective-permute-done.5 = bf16[2,480,128]{2,1,0:T(8,128)(2,1)S(1)} collective-permute-done((bf16[2,480,128]{2,1,0:T(8,128)(2,1)S(1)}, bf16[2,480,128]{2,1,0:T(8,128)(2,1)S(1)}, u32[]{:S(2)}, u32[]{:S(2)}) %collective-permute-start.5) | collective-permute-done | bytes 245792 | tf_op jit(solution)/shard_map/ppermute | solution.py:146
  27.2 3.0 %collective-permute-done.6 = bf16[2,480,128]{2,1,0:T(8,128)(2,1)S(1)} collective-permute-done((bf16[2,480,128]{2,1,0:T(8,128)(2,1)S(1)}, bf16[2,480,128]{2,1,0:T(8,128)(2,1)S(1)}, u32[]{:S(2)}, u32[]{:S(2)}) %collective-permute-start.6) | collective-permute-done | bytes 245792 | tf_op jit(solution)/shard_map/ppermute | solution.py:146
  30.2 0.1 collective-permute-done.7
  30.3 0.1 pad_maximum_fusion
  30.4 0.3 reshape.65
  30.7 1.9 %copy.24 = bf16[4,2,32,6,2,32]{2,3,4,0,5,1:T(8,128)(2,1)S(1)} copy(bf16[4,2,32,6,2,32]{5,4,3,2,1,0:T(2,128)(2,1)S(1)} %reshape.65) | data formatting | bytes 393216 | tf_op jit(solution)/shard_map/reshape | solution.py:151
  32.6 0.5 %copy.27 = bf16[4,2,6,2,32,128]{5,2,3,0,4,1:T(8,128)(2,1)S(1)} copy(bf16[4,2,6,2,32,128]{5,4,3,2,1,0:T(8,128)(2,1)S(1)} %bitcast.102) | data formatting | bytes 1572864 | tf_op jit(solution)/shard_map/reshape | solution.py:148
  33.2 0.2 fusion.29
  33.3 1.3 %fusion.9 = bf16[2,32,4,8,2,128]{5,3,4,2,1,0:T(8,128)(2,1)S(1)} fusion(bf16[4,2,6,1,32,128]{5,2,3,0,4,1:T(8,128)(2,1)S(1)} %get-tuple-element.16, bf16[4,2,6,1,32,128]{5,2,3,0,4,1:T(8,128)(2,1)S(1)} %get-tuple-element.15, bf16[4,2,6,2,32,128]{5,2,3,0,4,1:T(8,128)(2,1)S(1)} %copy.27, bf16[4,2,32,6,2,32]{2,3,4,0,5,1:T(8,128)(2,1)S(1)} %copy.24), kind=kOutput, calls=%fused_computation.11 | convolution fusion | flops 55574528 | bytes 2818048 | tf_op jit(solution)/shard_map/akscfm,akscfn->kfmn/dot_general | solution.py:155
  34.7 0.0 copy-start.1
  34.7 0.3 copy.28
  35.0 0.1 dynamic-slice_bitcast_fusion.2
  35.0 4.1 %collective-permute-start.10 = (bf16[1024,128]{1,0:T(8,128)(2,1)S(1)}, bf16[1024,128]{1,0:T(8,128)(2,1)S(1)}, u32[]{:S(2)}, u32[]{:S(2)}) collective-permute-start(bf16[1024,128]{1,0:T(8,128)(2,1)S(1)} %get-tuple-element.13), channel_id=1, source_target_pairs={{0,12},{1,13},{2,14},{3,15},{4,0},{5,1},{6,2},{7,3},{8,4},{9,5},{1... | collective-permute-start | bytes 786440 | tf_op jit(solution)/shard_map/ppermute | solution.py:167
  39.2 0.0 collective-permute-start.8
  39.2 1.2 %collective-permute-start.9 = (bf16[1024,128]{1,0:T(8,128)(2,1)S(1)}, bf16[1024,128]{1,0:T(8,128)(2,1)S(1)}, u32[]{:S(2)}, u32[]{:S(2)}) collective-permute-start(bf16[1024,128]{1,0:T(8,128)(2,1)S(1)} %get-tuple-element.14), channel_id=1, source_target_pairs={{0,4},{1,5},{2,6},{3,7},{4,8},{5,9},{6,10},{7,11},{8,12},{9,13},{1... | collective-permute-start | bytes 786440 | tf_op jit(solution)/shard_map/ppermute | solution.py:167
  40.4 0.2 fusion.22
  40.5 0.0 copy-done.1
  40.6 0.6 %dynamic_slice.42 = s32[1]{0:T(128)} dynamic-slice(s32[8]{0:T(128)S(1)} %copy-done.1, s32[]{:T(128)S(6)} %select_n.126), dynamic_slice_sizes={1} | dynamic-slice | bytes 12 | tf_op jit(solution)/shard_map/dynamic_slice | solution.py:102
  41.1 0.6 %compare_convert_fusion = f32[2]{0:T(128)S(1)} fusion(s32[]{:T(128)} %bitcast.45), kind=kLoop, calls=%fused_computation.72 | loop fusion | flops 4 | bytes 12 | tf_op jit(solution)/shard_map/convert_element_type | solution.py:177
  41.8 4.1 %collective-permute-done.10 = bf16[1024,128]{1,0:T(8,128)(2,1)S(1)} collective-permute-done((bf16[1024,128]{1,0:T(8,128)(2,1)S(1)}, bf16[1024,128]{1,0:T(8,128)(2,1)S(1)}, u32[]{:S(2)}, u32[]{:S(2)}) %collective-permute-start.10) | collective-permute-done | bytes 262176 | tf_op jit(solution)/shard_map/ppermute | solution.py:167
  45.9 1.3 %collective-permute-done.8 = bf16[1024,128]{1,0:T(8,128)(2,1)S(1)} collective-permute-done((bf16[1024,128]{1,0:T(8,128)(2,1)S(1)}, bf16[1024,128]{1,0:T(8,128)(2,1)S(1)}, u32[]{:S(2)}, u32[]{:S(2)}) %collective-permute-start.8) | collective-permute-done | bytes 262176 | tf_op jit(solution)/shard_map/ppermute | solution.py:167
  47.1 2.4 %collective-permute-done.9 = bf16[1024,128]{1,0:T(8,128)(2,1)S(1)} collective-permute-done((bf16[1024,128]{1,0:T(8,128)(2,1)S(1)}, bf16[1024,128]{1,0:T(8,128)(2,1)S(1)}, u32[]{:S(2)}, u32[]{:S(2)}) %collective-permute-start.9) | collective-permute-done | bytes 262176 | tf_op jit(solution)/shard_map/ppermute | solution.py:167
  49.6 0.1 fusion.16
  49.7 1.1 %fusion.13 = bf16[1,2,8,128,128]{4,3,2,1,0:T(8,128)(2,1)} fusion(bf16[2,32,128,1,1]{2,1,0,4,3:T(8,128)(2,1)S(1)} %bitcast.127, bf16[2,2,32,8,128]{4,3,2,1,0:T(8,128)(2,1)S(1)} %bitcast.125, f32[2]{0:T(128)S(1)} %compare_convert_fusion), kind=kOutput, calls=%fused_computation.13 | convolution fusion | flops 34078720 | bytes 802824 | tf_op jit(solution)/shard_map/kpfrj,pft->krjt/dot_general | solution.py:170
  (15 shorter events, 0.2 us)
Async XLA Ops:
  0.0 11.5 %copy-start = (s32[8,2,2]{0,2,1:T(2,128)S(1)}, s32[8,2,2]{0,2,1:T(2,128)}, u32[]{:S(2)}) copy-start(s32[8,2,2]{0,2,1:T(2,128)} %param.7) | copy-start | bytes 388
  6.2 5.9 %collective-permute-start.2 = (bf16[384,128]{1,0:T(8,128)(2,1)S(1)}, bf16[384,128]{1,0:T(8,128)(2,1)S(1)}, u32[]{:S(2)}, u32[]{:S(2)}) collective-permute-start(bf16[384,128]{1,0:T(8,128)(2,1)S(1)} %bitcast.120), channel_id=1, source_target_pairs={{0,32},{16,48},{32,64},{48,80},{64,96},{80,112},{96,0},{112,16},{1... | collective-permute-start | bytes 294920 | tf_op jit(solution)/shard_map/ppermute | solution.py:92
  7.9 5.3 %collective-permute-start = (bf16[384,128]{1,0:T(8,128)(2,1)S(1)}, bf16[384,128]{1,0:T(8,128)(2,1)S(1)}, u32[]{:S(2)}, u32[]{:S(2)}) collective-permute-start(bf16[384,128]{1,0:T(8,128)(2,1)S(1)} %bitcast.121), channel_id=1, source_target_pairs={{0,96},{16,112},{32,0},{48,16},{64,32},{80,48},{96,64},{112,80},{1... | collective-permute-start | bytes 294920 | tf_op jit(solution)/shard_map/ppermute | solution.py:93
  9.6 6.1 %collective-permute-start.1 = (bf16[384,128]{1,0:T(8,128)(2,1)S(1)}, bf16[384,128]{1,0:T(8,128)(2,1)S(1)}, u32[]{:S(2)}, u32[]{:S(2)}) collective-permute-start(bf16[384,128]{1,0:T(8,128)(2,1)S(1)} %bitcast.122), channel_id=1, source_target_pairs={{0,64},{16,80},{32,96},{48,112},{64,0},{80,16},{96,32},{112,48},{1... | collective-permute-start | bytes 294920 | tf_op jit(solution)/shard_map/ppermute | solution.py:94
  11.4 4.4 %collective-permute-start.3 = (bf16[384,128]{1,0:T(8,128)(2,1)S(1)}, bf16[384,128]{1,0:T(8,128)(2,1)S(1)}, u32[]{:S(2)}, u32[]{:S(2)}) collective-permute-start(bf16[384,128]{1,0:T(8,128)(2,1)S(1)} %bitcast.123), channel_id=1, source_target_pairs={{0,16},{16,0},{32,48},{48,32},{64,80},{80,64},{96,112},{112,96},{1... | collective-permute-start | bytes 294920 | tf_op jit(solution)/shard_map/ppermute | solution.py:91
  15.7 1.7 %collective-permute-start.4 = (bf16[3,384,128]{2,1,0:T(8,128)(2,1)S(1)}, bf16[3,384,128]{2,1,0:T(8,128)(2,1)S(1)}, u32[]{:S(2)}, u32[]{:S(2)}) collective-permute-start(bf16[3,384,128]{2,1,0:T(8,128)(2,1)S(1)} %pad_maximum_fusion.3), channel_id=1, source_target_pairs={{0,16},{16,0},{32,48},{48,32},{64,80},{80,64},{96,112},{112,96},{1... | collective-permute-start | bytes 884744 | tf_op jit(solution)/shard_map/ppermute | solution.py:96
  19.5 7.8 %collective-permute-start.5 = (bf16[2,480,128]{2,1,0:T(8,128)(2,1)S(1)}, bf16[2,480,128]{2,1,0:T(8,128)(2,1)S(1)}, u32[]{:S(2)}, u32[]{:S(2)}) collective-permute-start(bf16[2,480,128]{2,1,0:T(8,128)(2,1)S(1)} %get-tuple-element.18), channel_id=1, source_target_pairs={{0,2},{1,3},{2,0},{3,1},{4,6},{5,7},{6,4},{7,5},{8,10},{9,11},{10,... | collective-permute-start | bytes 737288 | tf_op jit(solution)/shard_map/ppermute | solution.py:146
  22.8 7.4 %collective-permute-start.6 = (bf16[2,480,128]{2,1,0:T(8,128)(2,1)S(1)}, bf16[2,480,128]{2,1,0:T(8,128)(2,1)S(1)}, u32[]{:S(2)}, u32[]{:S(2)}) collective-permute-start(bf16[2,480,128]{2,1,0:T(8,128)(2,1)S(1)} %get-tuple-element.19), channel_id=1, source_target_pairs={{0,1},{1,2},{2,3},{3,0},{4,5},{5,6},{6,7},{7,4},{8,9},{9,10},{10,1... | collective-permute-start | bytes 737288 | tf_op jit(solution)/shard_map/ppermute | solution.py:146
  23.5 6.8 %collective-permute-start.7 = (bf16[2,480,128]{2,1,0:T(8,128)(2,1)S(1)}, bf16[2,480,128]{2,1,0:T(8,128)(2,1)S(1)}, u32[]{:S(2)}, u32[]{:S(2)}) collective-permute-start(bf16[2,480,128]{2,1,0:T(8,128)(2,1)S(1)} %get-tuple-element.20), channel_id=1, source_target_pairs={{0,3},{1,0},{2,1},{3,2},{4,7},{5,4},{6,5},{7,6},{8,11},{9,8},{10,9... | collective-permute-start | bytes 737288 | tf_op jit(solution)/shard_map/ppermute | solution.py:146
  34.7 5.9 %copy-start.1 = (s32[8]{0:T(128)S(1)}, s32[8]{0:T(128)}, u32[]{:S(2)}) copy-start(s32[8]{0:T(128)} %param.8) | copy-start | bytes 100
  35.0 10.8 %collective-permute-start.10 = (bf16[1024,128]{1,0:T(8,128)(2,1)S(1)}, bf16[1024,128]{1,0:T(8,128)(2,1)S(1)}, u32[]{:S(2)}, u32[]{:S(2)}) collective-permute-start(bf16[1024,128]{1,0:T(8,128)(2,1)S(1)} %get-tuple-element.13), channel_id=1, source_target_pairs={{0,12},{1,13},{2,14},{3,15},{4,0},{5,1},{6,2},{7,3},{8,4},{9,5},{1... | collective-permute-start | bytes 786440 | tf_op jit(solution)/shard_map/ppermute | solution.py:167
  39.2 8.0 %collective-permute-start.8 = (bf16[1024,128]{1,0:T(8,128)(2,1)S(1)}, bf16[1024,128]{1,0:T(8,128)(2,1)S(1)}, u32[]{:S(2)}, u32[]{:S(2)}) collective-permute-start(bf16[1024,128]{1,0:T(8,128)(2,1)S(1)} %get-tuple-element.12), channel_id=1, source_target_pairs={{0,8},{1,9},{2,10},{3,11},{4,12},{5,13},{6,14},{7,15},{8,0},{9,1},... | collective-permute-start | bytes 786440 | tf_op jit(solution)/shard_map/ppermute | solution.py:167
  39.2 10.4 %collective-permute-start.9 = (bf16[1024,128]{1,0:T(8,128)(2,1)S(1)}, bf16[1024,128]{1,0:T(8,128)(2,1)S(1)}, u32[]{:S(2)}, u32[]{:S(2)}) collective-permute-start(bf16[1024,128]{1,0:T(8,128)(2,1)S(1)} %get-tuple-element.14), channel_id=1, source_target_pairs={{0,4},{1,5},{2,6},{3,7},{4,8},{5,9},{6,10},{7,11},{8,12},{9,13},{1... | collective-permute-start | bytes 786440 | tf_op jit(solution)/shard_map/ppermute | solution.py:167

commit v11 on v10

--- a/solution.py
+++ b/solution.py
@@ -144,16 +144,19 @@
     for d in sorted(range(1, side), key=lambda step: -min(step, side - step)):
         message = jnp.concatenate([right, rows_for((gather_pos + d) % side)], axis=1)
         pieces.append(lax.ppermute(message, axes, gather_perm(d)))
-    gathered = jnp.stack(pieces)
-    right_all = gathered[:, :, :spec_rows].reshape(
-        (side, slot_count, seg_dev, 2, FREQS, block_width)
-    )
-    left_all = gathered[:, :, spec_rows:].reshape((side, slot_count, side * rows, seg_dev, 2, FREQS))
-    left_all = jnp.transpose(left_all, (0, 1, 3, 4, 5, 2))
+    left_pieces = []
+    right_pieces = []
+    for piece in pieces:
+        left_piece = piece[:, spec_rows:].reshape((slot_count, side * rows, seg_dev, 2, FREQS))
+        left_pieces.append(jnp.transpose(left_piece, (0, 4, 3, 2, 1)))
+        right_piece = piece[:, :spec_rows].reshape((slot_count, seg_dev, 2, FREQS, block_width))
+        right_pieces.append(jnp.transpose(right_piece, (0, 3, 2, 1, 4)))
+    left_all = jnp.stack(left_pieces, axis=2)
+    right_all = jnp.stack(right_pieces, axis=2)
     right_swapped = jnp.stack([right_all[:, :, :, 1], -right_all[:, :, :, 0]], axis=3)
     rhs = jnp.concatenate([right_all, right_swapped], axis=-1)
     partial_value = jnp.einsum(
-        "akscfm,akscfn->kfmn", left_all, rhs, preferred_element_type=jnp.float32
+        "kfacsm,kfacsn->kfmn", left_all, rhs, preferred_element_type=jnp.float32
     )
     partial_value = partial_value.reshape((slot_count, FREQS, side, rows, 2, block_width))
     partial_value = jnp.transpose(partial_value, (2, 0, 4, 1, 3, 5)).astype(jnp.bfloat16)

time: 51 us -> 52.8 us (1.035)
  waiting for transfers between devices: 17.2 us -> 20.1 us
  starting transfers between devices: 17.2 us -> 16 us
  local copies, waits for them, and re-layouts: 5.86 us -> 5.29 us
    ppermute x3, waiting for transfers between devices: 4.23 us -> 7.12 us  [shards(): pieces.append(lax.ppermute(message, axes, gather_perm(d)))]
    ppermute x3, starting transfers between devices: 6.59 us -> 5.37 us  [shards(): pieces.append(lax.ppermute(message, axes, gather_perm(d)))]
    reshape x3 -> x12, local copies, waits for them, and re-layouts: 2.76 us -> 2.13 us  [the longest x8 1.57 us: shards(): piece[:, spec_rows:].reshape((slot_count, side * rows, seg_dev, 2, FREQS))]
  transfers between devices with their start and end apart: 11 -> 11, of which waited for: 10 -> 9; matrix products, arithmetic and copies ran while one was open for 4% -> 5% of each run, Pallas kernels for 0% -> 0%
where the time goes in v11:
time: 52.8 us; the launch traced here: 52.6 us
  waiting for transfers between devices  20.1 us (38%)
  starting transfers between devices  16 us (30%)
  matrix products  7.81 us (15%)
  local copies, waits for them, and re-layouts  5.29 us (10%)
  other arithmetic  3.05 us (6%)
    ppermute x3, waiting for transfers between devices, shards(): lax.ppermute(chunk, axes, reduce_perm(e)).astype(jnp.float32)  7.75 us
    ppermute x3, waiting for transfers between devices, shards(): pieces.append(lax.ppermute(message, axes, gather_perm(d)))  7.12 us
    ppermute x3, starting transfers between devices, shards(): pieces.append(lax.ppermute(message, axes, gather_perm(d)))  5.37 us
    ppermute x3, starting transfers between devices, shards(): lax.ppermute(chunk, axes, reduce_perm(e)).astype(jnp.float32)  5.36 us
    dot_general x1, matrix products, shards(): jnp.dot(samples, band_table(), preferred_element_type=jnp.float32)  4.89 us
    ppermute x1, waiting for transfers between devices, shards(): from_far = lax.ppermute(own, 'pairs', chip_shift(2))  2.47 us
    ppermute x1, starting transfers between devices, shards(): from_far = lax.ppermute(own, 'pairs', chip_shift(2))  1.89 us
    dot_general x1, matrix products, shards(): jnp.einsum('kfacsm,kfacsn->kfmn', left_all, rhs, preferred_element_type=j...  1.79 us
  transfers between devices with their start and end apart: 11, of which 9 were waited for; matrix products, arithmetic and copies ran while one was open for 5% of the time, Pallas kernels for 0%

profile of v11, /device:TPU:0, one launch (start us, length us, event | category | flops | bytes accessed | tf_op | source)
XLA Modules:
  0.0 52.6 jit_solution(4379291387024595364)
XLA Ops:
  0.0 4.9 %convolution_bitcast_fusion.1 = f32[768,64]{1,0:T(8,128)S(1)} fusion(bf16[768,4096]{1,0:T(8,128)(2,1)} %bitcast.162, bf16[4096,64]{1,0:T(8,128)(2,1)} %constant.168.clone), kind=kOutput, calls=%fused_computation.20 | convolution fusion | flops 402653184 | bytes 7012352 | tf_op jit(solution)/shard_map/dot_general | solution.py:73
  4.9 0.3 fusion.40
  5.2 0.6 %multiply_convert_fusion.1 = (bf16[768,32]{1,0:T(8,128)(2,1)S(1)}, f32[768,32]{1,0:T(8,128)S(1)}) fusion(f32[768,64]{1,0:T(8,128)S(1)} %convolution_bitcast_fusion.1, f32[768]{0:T(1024)S(1)} %broadcast_multiply_fusion, f32[768,32]{1,0:T(8,128)S(1)} %get-tuple-element.11), kind=kLoop, calls=%fused_computation.38 | loop fusion | flops 221184 | bytes 347136 | tf_op jit(solution)/shard_map/convert.4
  5.8 0.2 multiply_convert_fusion
  6.0 0.1 copy.22
  6.1 0.1 copy.21
  6.2 1.6 %collective-permute-start.2 = (bf16[384,128]{1,0:T(8,128)(2,1)S(1)}, bf16[384,128]{1,0:T(8,128)(2,1)S(1)}, u32[]{:S(2)}, u32[]{:S(2)}) collective-permute-start(bf16[384,128]{1,0:T(8,128)(2,1)S(1)} %bitcast.150), channel_id=1, source_target_pairs={{0,32},{16,48},{32,64},{48,80},{64,96},{80,112},{96,0},{112,16},{1... | collective-permute-start | bytes 294920 | tf_op jit(solution)/shard_map/ppermute | solution.py:92
  7.9 1.7 %collective-permute-start = (bf16[384,128]{1,0:T(8,128)(2,1)S(1)}, bf16[384,128]{1,0:T(8,128)(2,1)S(1)}, u32[]{:S(2)}, u32[]{:S(2)}) collective-permute-start(bf16[384,128]{1,0:T(8,128)(2,1)S(1)} %bitcast.151), channel_id=1, source_target_pairs={{0,96},{16,112},{32,0},{48,16},{64,32},{80,48},{96,64},{112,80},{1... | collective-permute-start | bytes 294920 | tf_op jit(solution)/shard_map/ppermute | solution.py:93
  9.6 1.9 %collective-permute-start.1 = (bf16[384,128]{1,0:T(8,128)(2,1)S(1)}, bf16[384,128]{1,0:T(8,128)(2,1)S(1)}, u32[]{:S(2)}, u32[]{:S(2)}) collective-permute-start(bf16[384,128]{1,0:T(8,128)(2,1)S(1)} %bitcast.152), channel_id=1, source_target_pairs={{0,64},{16,80},{32,96},{48,112},{64,0},{80,16},{96,32},{112,48},{1... | collective-permute-start | bytes 294920 | tf_op jit(solution)/shard_map/ppermute | solution.py:94
  11.4 0.0 collective-permute-start.3
  11.4 0.0 copy-done
  11.5 0.2 fusion.35
  11.7 0.2 slice_reduce_fusion
  11.9 0.2 collective-permute-done.2
  12.1 1.1 %collective-permute-done = bf16[384,128]{1,0:T(8,128)(2,1)S(1)} collective-permute-done((bf16[384,128]{1,0:T(8,128)(2,1)S(1)}, bf16[384,128]{1,0:T(8,128)(2,1)S(1)}, u32[]{:S(2)}, u32[]{:S(2)}) %collective-permute-start) | collective-permute-done | bytes 98336 | tf_op jit(solution)/shard_map/ppermute | solution.py:93
  13.2 2.5 %collective-permute-done.1 = bf16[384,128]{1,0:T(8,128)(2,1)S(1)} collective-permute-done((bf16[384,128]{1,0:T(8,128)(2,1)S(1)}, bf16[384,128]{1,0:T(8,128)(2,1)S(1)}, u32[]{:S(2)}, u32[]{:S(2)}) %collective-permute-start.1) | collective-permute-done | bytes 98336 | tf_op jit(solution)/shard_map/ppermute | solution.py:94
  15.7 0.1 collective-permute-start.4
  15.8 0.1 maximum_bitcast_fusion
  15.9 0.0 collective-permute-done.3
  15.9 1.5 %collective-permute-done.4 = bf16[3,384,128]{2,1,0:T(8,128)(2,1)S(1)} collective-permute-done((bf16[3,384,128]{2,1,0:T(8,128)(2,1)S(1)}, bf16[3,384,128]{2,1,0:T(8,128)(2,1)S(1)}, u32[]{:S(2)}, u32[]{:S(2)}) %collective-permute-start.4) | collective-permute-done | bytes 294944 | tf_op jit(solution)/shard_map/ppermute | solution.py:96
  17.4 0.1 maximum_select_fusion
  17.6 0.1 copy.23
  17.6 0.6 %gather_fusion = bf16[2,384,128]{2,1,0:T(8,128)(2,1)S(1)} fusion(bf16[8,384,128]{2,1,0:T(8,128)(2,1)S(1)} %bitcast.127, s32[1024]{0:T(1024)S(1)} %pad_clamp_fusion.1), kind=kCustom, calls=%fused_computation.clone | custom fusion | bytes 393224 | tf_op jit(solution)/shard_map/jit(_take)/gather | solution.py:104
  18.2 0.1 select_bitcast_fusion
  18.3 0.2 copy.24
  18.5 0.1 reshape.83
  18.6 0.6 %gather_fusion.1 = bf16[2,384,128]{2,1,0:T(8,128)(2,1)S(1)} fusion(bf16[8,384,128]{2,1,0:T(8,128)(2,1)S(1)} %bitcast.128, s32[1024]{0:T(1024)S(1)} %pad_clamp_fusion), kind=kCustom, calls=%fused_computation.1.clone | custom fusion | bytes 393224 | tf_op jit(solution)/shard_map/jit(_take)/gather | solution.py:105
  19.2 0.1 broadcast_select_fusion
  19.3 0.1 pad_maximum_fusion.2
  19.4 3.2 %collective-permute-start.7 = (bf16[2,480,128]{2,1,0:T(8,128)(2,1)S(1)}, bf16[2,480,128]{2,1,0:T(8,128)(2,1)S(1)}, u32[]{:S(2)}, u32[]{:S(2)}) collective-permute-start(bf16[2,480,128]{2,1,0:T(8,128)(2,1)S(1)} %get-tuple-element.23), channel_id=1, source_target_pairs={{0,3},{1,0},{2,1},{3,2},{4,7},{5,4},{6,5},{7,6},{8,11},{9,8},{10,9... | collective-permute-start | bytes 737288 | tf_op jit(solution)/shard_map/ppermute | solution.py:146
  22.6 0.0 collective-permute-start.6
  22.6 2.2 %collective-permute-start.5 = (bf16[2,480,128]{2,1,0:T(8,128)(2,1)S(1)}, bf16[2,480,128]{2,1,0:T(8,128)(2,1)S(1)}, u32[]{:S(2)}, u32[]{:S(2)}) collective-permute-start(bf16[2,480,128]{2,1,0:T(8,128)(2,1)S(1)} %get-tuple-element.21), channel_id=1, source_target_pairs={{0,2},{1,3},{2,0},{3,1},{4,6},{5,7},{6,4},{7,5},{8,10},{9,11},{10,... | collective-permute-start | bytes 737288 | tf_op jit(solution)/shard_map/ppermute | solution.py:146
  24.8 0.1 copy.57
  25.0 0.1 reshape.84
  25.1 0.3 copy.27
  25.4 1.0 %collective-permute-done.7 = bf16[2,480,128]{2,1,0:T(8,128)(2,1)S(1)} collective-permute-done((bf16[2,480,128]{2,1,0:T(8,128)(2,1)S(1)}, bf16[2,480,128]{2,1,0:T(8,128)(2,1)S(1)}, u32[]{:S(2)}, u32[]{:S(2)}) %collective-permute-start.7) | collective-permute-done | bytes 245792 | tf_op jit(solution)/shard_map/ppermute | solution.py:146
  26.3 0.1 copy.54
  26.5 6.2 %collective-permute-done.6 = bf16[2,480,128]{2,1,0:T(8,128)(2,1)S(1)} collective-permute-done((bf16[2,480,128]{2,1,0:T(8,128)(2,1)S(1)}, bf16[2,480,128]{2,1,0:T(8,128)(2,1)S(1)}, u32[]{:S(2)}, u32[]{:S(2)}) %collective-permute-start.6) | collective-permute-done | bytes 245792 | tf_op jit(solution)/shard_map/ppermute | solution.py:146
  32.7 0.1 copy.55
  32.8 0.0 collective-permute-done.5
  32.8 0.1 copy.56
  33.0 0.3 pad_maximum_fusion
  33.2 0.2 fusion.41
  33.4 0.1 reshape.85
  33.6 0.3 copy.29
  33.9 0.1 reshape.86
  34.0 0.3 copy.31
  34.3 0.1 reshape.87
  34.4 0.3 copy.33
  34.7 0.0 copy-start.1
  34.7 1.8 %fusion.15 = bf16[2,32,4,8,2,128]{5,3,4,2,1,0:T(8,128)(2,1)S(1)} fusion(bf16[2,32,4,1,6,128]{5,4,3,2,1,0:T(8,128)(2,1)S(1)} %get-tuple-element.16, bf16[2,32,4,1,6,128]{5,4,3,2,1,0:T(8,128)(2,1)S(1)} %get-tuple-element.15, bf16[2,32,1,2,6,128]{5,4,3,2,1,0:T(8,128)(2,1)S(1)} %bitcast.133, bf16[2,32,1,2,6,128]{5,4,3,2,1,0:T(8,128)(2,1)S(1)} %bitcast.135, ...), kind=kOutput, calls=%fused_computation.17 | convolution fusion | flops 60588032 | bytes 2818048 | tf_op jit(solution)/shard_map/kfacsm,kfacsn->kfmn/dot_general | solution.py:158
  36.5 0.3 copy.38
  36.8 0.1 dynamic-slice_bitcast_fusion.2
  36.8 4.1 %collective-permute-start.10 = (bf16[1024,128]{1,0:T(8,128)(2,1)S(1)}, bf16[1024,128]{1,0:T(8,128)(2,1)S(1)}, u32[]{:S(2)}, u32[]{:S(2)}) collective-permute-start(bf16[1024,128]{1,0:T(8,128)(2,1)S(1)} %get-tuple-element.13), channel_id=1, source_target_pairs={{0,12},{1,13},{2,14},{3,15},{4,0},{5,1},{6,2},{7,3},{8,4},{9,5},{1... | collective-permute-start | bytes 786440 | tf_op jit(solution)/shard_map/ppermute | solution.py:170
  41.0 0.0 collective-permute-start.8
  41.0 1.2 %collective-permute-start.9 = (bf16[1024,128]{1,0:T(8,128)(2,1)S(1)}, bf16[1024,128]{1,0:T(8,128)(2,1)S(1)}, u32[]{:S(2)}, u32[]{:S(2)}) collective-permute-start(bf16[1024,128]{1,0:T(8,128)(2,1)S(1)} %get-tuple-element.14), channel_id=1, source_target_pairs={{0,4},{1,5},{2,6},{3,7},{4,8},{5,9},{6,10},{7,11},{8,12},{9,13},{1... | collective-permute-start | bytes 786440 | tf_op jit(solution)/shard_map/ppermute | solution.py:170
  42.2 0.2 fusion.34
  42.4 0.6 %dynamic_slice.42 = s32[1]{0:T(128)} dynamic-slice(s32[8]{0:T(128)S(1)} %copy-done.1, s32[]{:T(128)S(6)} %select_n.127), dynamic_slice_sizes={1} | dynamic-slice | bytes 12 | tf_op jit(solution)/shard_map/dynamic_slice | solution.py:102
  43.0 0.6 %compare_convert_fusion = f32[2]{0:T(128)S(1)} fusion(s32[]{:T(128)} %bitcast.58), kind=kLoop, calls=%fused_computation.84 | loop fusion | flops 4 | bytes 12 | tf_op jit(solution)/shard_map/convert_element_type | solution.py:180
  43.6 4.1 %collective-permute-done.10 = bf16[1024,128]{1,0:T(8,128)(2,1)S(1)} collective-permute-done((bf16[1024,128]{1,0:T(8,128)(2,1)S(1)}, bf16[1024,128]{1,0:T(8,128)(2,1)S(1)}, u32[]{:S(2)}, u32[]{:S(2)}) %collective-permute-start.10) | collective-permute-done | bytes 262176 | tf_op jit(solution)/shard_map/ppermute | solution.py:170
  47.7 1.3 %collective-permute-done.8 = bf16[1024,128]{1,0:T(8,128)(2,1)S(1)} collective-permute-done((bf16[1024,128]{1,0:T(8,128)(2,1)S(1)}, bf16[1024,128]{1,0:T(8,128)(2,1)S(1)}, u32[]{:S(2)}, u32[]{:S(2)}) %collective-permute-start.8) | collective-permute-done | bytes 262176 | tf_op jit(solution)/shard_map/ppermute | solution.py:170
  49.0 2.4 %collective-permute-done.9 = bf16[1024,128]{1,0:T(8,128)(2,1)S(1)} collective-permute-done((bf16[1024,128]{1,0:T(8,128)(2,1)S(1)}, bf16[1024,128]{1,0:T(8,128)(2,1)S(1)}, u32[]{:S(2)}, u32[]{:S(2)}) %collective-permute-start.9) | collective-permute-done | bytes 262176 | tf_op jit(solution)/shard_map/ppermute | solution.py:170
  51.4 0.1 fusion.28
  51.5 1.1 %fusion.19 = bf16[1,2,8,128,128]{4,3,2,1,0:T(8,128)(2,1)} fusion(bf16[2,32,128,1,1]{2,1,0,4,3:T(8,128)(2,1)S(1)} %bitcast.161, bf16[2,2,32,8,128]{4,3,2,1,0:T(8,128)(2,1)S(1)} %bitcast.155, f32[2]{0:T(128)S(1)} %compare_convert_fusion), kind=kOutput, calls=%fused_computation.19 | convolution fusion | flops 34078720 | bytes 802824 | tf_op jit(solution)/shard_map/kpfrj,pft->krjt/dot_general | solution.py:173
  (22 shorter events, 0.3 us)
Async XLA Ops:
  0.0 11.5 %copy-start = (s32[8,2,2]{0,2,1:T(2,128)S(1)}, s32[8,2,2]{0,2,1:T(2,128)}, u32[]{:S(2)}) copy-start(s32[8,2,2]{0,2,1:T(2,128)} %param.7) | copy-start | bytes 388
  6.2 5.9 %collective-permute-start.2 = (bf16[384,128]{1,0:T(8,128)(2,1)S(1)}, bf16[384,128]{1,0:T(8,128)(2,1)S(1)}, u32[]{:S(2)}, u32[]{:S(2)}) collective-permute-start(bf16[384,128]{1,0:T(8,128)(2,1)S(1)} %bitcast.150), channel_id=1, source_target_pairs={{0,32},{16,48},{32,64},{48,80},{64,96},{80,112},{96,0},{112,16},{1... | collective-permute-start | bytes 294920 | tf_op jit(solution)/shard_map/ppermute | solution.py:92
  7.9 5.3 %collective-permute-start = (bf16[384,128]{1,0:T(8,128)(2,1)S(1)}, bf16[384,128]{1,0:T(8,128)(2,1)S(1)}, u32[]{:S(2)}, u32[]{:S(2)}) collective-permute-start(bf16[384,128]{1,0:T(8,128)(2,1)S(1)} %bitcast.151), channel_id=1, source_target_pairs={{0,96},{16,112},{32,0},{48,16},{64,32},{80,48},{96,64},{112,80},{1... | collective-permute-start | bytes 294920 | tf_op jit(solution)/shard_map/ppermute | solution.py:93
  9.6 6.1 %collective-permute-start.1 = (bf16[384,128]{1,0:T(8,128)(2,1)S(1)}, bf16[384,128]{1,0:T(8,128)(2,1)S(1)}, u32[]{:S(2)}, u32[]{:S(2)}) collective-permute-start(bf16[384,128]{1,0:T(8,128)(2,1)S(1)} %bitcast.152), channel_id=1, source_target_pairs={{0,64},{16,80},{32,96},{48,112},{64,0},{80,16},{96,32},{112,48},{1... | collective-permute-start | bytes 294920 | tf_op jit(solution)/shard_map/ppermute | solution.py:94
  11.4 4.4 %collective-permute-start.3 = (bf16[384,128]{1,0:T(8,128)(2,1)S(1)}, bf16[384,128]{1,0:T(8,128)(2,1)S(1)}, u32[]{:S(2)}, u32[]{:S(2)}) collective-permute-start(bf16[384,128]{1,0:T(8,128)(2,1)S(1)} %bitcast.153), channel_id=1, source_target_pairs={{0,16},{16,0},{32,48},{48,32},{64,80},{80,64},{96,112},{112,96},{1... | collective-permute-start | bytes 294920 | tf_op jit(solution)/shard_map/ppermute | solution.py:91
  15.7 1.7 %collective-permute-start.4 = (bf16[3,384,128]{2,1,0:T(8,128)(2,1)S(1)}, bf16[3,384,128]{2,1,0:T(8,128)(2,1)S(1)}, u32[]{:S(2)}, u32[]{:S(2)}) collective-permute-start(bf16[3,384,128]{2,1,0:T(8,128)(2,1)S(1)} %pad_maximum_fusion.1), channel_id=1, source_target_pairs={{0,16},{16,0},{32,48},{48,32},{64,80},{80,64},{96,112},{112,96},{1... | collective-permute-start | bytes 884744 | tf_op jit(solution)/shard_map/ppermute | solution.py:96
  19.4 6.9 %collective-permute-start.7 = (bf16[2,480,128]{2,1,0:T(8,128)(2,1)S(1)}, bf16[2,480,128]{2,1,0:T(8,128)(2,1)S(1)}, u32[]{:S(2)}, u32[]{:S(2)}) collective-permute-start(bf16[2,480,128]{2,1,0:T(8,128)(2,1)S(1)} %get-tuple-element.23), channel_id=1, source_target_pairs={{0,3},{1,0},{2,1},{3,2},{4,7},{5,4},{6,5},{7,6},{8,11},{9,8},{10,9... | collective-permute-start | bytes 737288 | tf_op jit(solution)/shard_map/ppermute | solution.py:146
  22.6 10.0 %collective-permute-start.6 = (bf16[2,480,128]{2,1,0:T(8,128)(2,1)S(1)}, bf16[2,480,128]{2,1,0:T(8,128)(2,1)S(1)}, u32[]{:S(2)}, u32[]{:S(2)}) collective-permute-start(bf16[2,480,128]{2,1,0:T(8,128)(2,1)S(1)} %get-tuple-element.22), channel_id=1, source_target_pairs={{0,1},{1,2},{2,3},{3,0},{4,5},{5,6},{6,7},{7,4},{8,9},{9,10},{10,1... | collective-permute-start | bytes 737288 | tf_op jit(solution)/shard_map/ppermute | solution.py:146
  22.6 10.2 %collective-permute-start.5 = (bf16[2,480,128]{2,1,0:T(8,128)(2,1)S(1)}, bf16[2,480,128]{2,1,0:T(8,128)(2,1)S(1)}, u32[]{:S(2)}, u32[]{:S(2)}) collective-permute-start(bf16[2,480,128]{2,1,0:T(8,128)(2,1)S(1)} %get-tuple-element.21), channel_id=1, source_target_pairs={{0,2},{1,3},{2,0},{3,1},{4,6},{5,7},{6,4},{7,5},{8,10},{9,11},{10,... | collective-permute-start | bytes 737288 | tf_op jit(solution)/shard_map/ppermute | solution.py:146
  34.7 7.7 %copy-start.1 = (s32[8]{0:T(128)S(1)}, s32[8]{0:T(128)}, u32[]{:S(2)}) copy-start(s32[8]{0:T(128)} %param.8) | copy-start | bytes 100
  36.8 10.8 %collective-permute-start.10 = (bf16[1024,128]{1,0:T(8,128)(2,1)S(1)}, bf16[1024,128]{1,0:T(8,128)(2,1)S(1)}, u32[]{:S(2)}, u32[]{:S(2)}) collective-permute-start(bf16[1024,128]{1,0:T(8,128)(2,1)S(1)} %get-tuple-element.13), channel_id=1, source_target_pairs={{0,12},{1,13},{2,14},{3,15},{4,0},{5,1},{6,2},{7,3},{8,4},{9,5},{1... | collective-permute-start | bytes 786440 | tf_op jit(solution)/shard_map/ppermute | solution.py:170
  41.0 8.0 %collective-permute-start.8 = (bf16[1024,128]{1,0:T(8,128)(2,1)S(1)}, bf16[1024,128]{1,0:T(8,128)(2,1)S(1)}, u32[]{:S(2)}, u32[]{:S(2)}) collective-permute-start(bf16[1024,128]{1,0:T(8,128)(2,1)S(1)} %get-tuple-element.12), channel_id=1, source_target_pairs={{0,8},{1,9},{2,10},{3,11},{4,12},{5,13},{6,14},{7,15},{8,0},{9,1},... | collective-permute-start | bytes 786440 | tf_op jit(solution)/shard_map/ppermute | solution.py:170
  41.0 10.4 %collective-permute-start.9 = (bf16[1024,128]{1,0:T(8,128)(2,1)S(1)}, bf16[1024,128]{1,0:T(8,128)(2,1)S(1)}, u32[]{:S(2)}, u32[]{:S(2)}) collective-permute-start(bf16[1024,128]{1,0:T(8,128)(2,1)S(1)} %get-tuple-element.14), channel_id=1, source_target_pairs={{0,4},{1,5},{2,6},{3,7},{4,8},{5,9},{6,10},{7,11},{8,12},{9,13},{1... | collective-permute-start | bytes 786440 | tf_op jit(solution)/shard_map/ppermute | solution.py:170

commit v12 on v10

--- a/solution.py
+++ b/solution.py
@@ -101,8 +101,9 @@
     own_pairs = lax.dynamic_index_in_dim(pair_list, owner_index, 0, keepdims=False)
     live_slots = jnp.arange(slot_count, dtype=jnp.int32) < pair_count[owner_index]
     position = ((own_pairs // 2 - chip) % chips) * 2 + own_pairs % 2
-    left = jnp.take(table, position[:, 0], axis=0)
-    right = jnp.take(table, position[:, 1], axis=0)
+    chosen = jnp.take(table, position.T.reshape(-1), axis=0)
+    left = chosen[:slot_count]
+    right = chosen[slot_count:]
     left_t = jnp.transpose(left, (0, 2, 1)).reshape((slot_count, side, side, rows, spec_rows))
     left_t = jnp.where(first_core, jnp.swapaxes(left_t, 1, 2), left_t)
     packed_rows = spec_rows * side * rows // block_width

time: 51 us -> 50.4 us (0.988); the launches traced: 50.8 us -> 49.7 us
  waiting for transfers between devices: 17.2 us -> 15.4 us
  starting transfers between devices: 17.2 us -> 18.4 us
    ppermute x1, waiting for transfers between devices: 2.47 us -> 0.01 us  [shards(): from_far = lax.ppermute(own, 'pairs', chip_shift(2))]
    ppermute x1, waiting for transfers between devices: 0.21 us -> 2.05 us  [shards(): from_below = lax.ppermute(own, 'pairs', chip_shift(1))]
    ppermute x1, starting transfers between devices: 1.89 us -> 3.18 us  [shards(): from_far = lax.ppermute(own, 'pairs', chip_shift(2))]
    ppermute x1, waiting for transfers between devices: 1.06 us -> 0.01 us  [shards(): from_above = lax.ppermute(own, 'pairs', chip_shift(-1))]
    ppermute x1, starting transfers between devices: 1.64 us -> 0.6 us  [shards(): from_below = lax.ppermute(own, 'pairs', chip_shift(1))]
    ppermute x1, starting transfers between devices: 1.67 us -> 2.64 us  [shards(): from_above = lax.ppermute(own, 'pairs', chip_shift(-1))]
    gather x2 -> x1, local copies, waits for them, and re-layouts: 1.17 us -> 0.62 us  [shards(): chosen = jnp.take(table, position.T.reshape(-1), axis=0)]
  transfers between devices with their start and end apart: 11 -> 11, of which waited for: 10 -> 8; matrix products, arithmetic and copies ran while one was open for 4% -> 4% of each run, Pallas kernels for 0% -> 0%
where the time goes in v12:
time: 50.4 us; the launch traced here: 49.7 us
  starting transfers between devices  18.4 us (37%)
  waiting for transfers between devices  15.4 us (31%)
  matrix products  7.34 us (15%)
  local copies, waits for them, and re-layouts  5.42 us (11%)
  other arithmetic  2.81 us (6%)
    ppermute x3, waiting for transfers between devices, shards(): lax.ppermute(chunk, axes, reduce_perm(e)).astype(jnp.float32)  7.67 us
    ppermute x3, starting transfers between devices, shards(): pieces.append(lax.ppermute(message, axes, gather_perm(d)))  6.51 us
    ppermute x3, starting transfers between devices, shards(): lax.ppermute(chunk, axes, reduce_perm(e)).astype(jnp.float32)  5.41 us
    dot_general x1, matrix products, shards(): jnp.dot(samples, band_table(), preferred_element_type=jnp.float32)  4.89 us
    ppermute x3, waiting for transfers between devices, shards(): pieces.append(lax.ppermute(message, axes, gather_perm(d)))  4.23 us
    ppermute x1, starting transfers between devices, shards(): from_far = lax.ppermute(own, 'pairs', chip_shift(2))  3.18 us
    ppermute x1, starting transfers between devices, shards(): from_above = lax.ppermute(own, 'pairs', chip_shift(-1))  2.64 us
    reshape x2, local copies, waits for them, and re-layouts, shards(): gathered[:, :, spec_rows:]  2.22 us
  transfers between devices with their start and end apart: 11, of which 8 were waited for; matrix products, arithmetic and copies ran while one was open for 4% of the time, Pallas kernels for 0%

profile of v12, /device:TPU:0, one launch (start us, length us, event | category | flops | bytes accessed | tf_op | source)
XLA Modules:
  0.0 49.7 jit_solution(3517414710185049295)
XLA Ops:
  0.0 0.0 copy-start
  0.0 4.9 %convolution_bitcast_fusion.1 = f32[768,64]{1,0:T(8,128)S(1)} fusion(bf16[768,4096]{1,0:T(8,128)(2,1)} %bitcast.131, bf16[4096,64]{1,0:T(8,128)(2,1)} %constant.172.clone), kind=kOutput, calls=%fused_computation.13 | convolution fusion | flops 402653184 | bytes 7012352 | tf_op jit(solution)/shard_map/dot_general | solution.py:73
  4.9 0.3 fusion.30
  5.2 0.6 %multiply_convert_fusion.1 = (bf16[768,32]{1,0:T(8,128)(2,1)S(1)}, f32[768,32]{1,0:T(8,128)S(1)}) fusion(f32[768,64]{1,0:T(8,128)S(1)} %convolution_bitcast_fusion.1, f32[768]{0:T(1024)S(1)} %broadcast_multiply_fusion, f32[768,32]{1,0:T(8,128)S(1)} %get-tuple-element.8), kind=kLoop, calls=%fused_computation.27 | loop fusion | flops 221184 | bytes 347136 | tf_op jit(solution)/shard_map/convert.4
  5.8 0.2 multiply_convert_fusion
  6.0 0.1 copy.28
  6.1 0.1 copy.27
  6.2 3.2 %collective-permute-start.1 = (bf16[384,128]{1,0:T(8,128)(2,1)S(1)}, bf16[384,128]{1,0:T(8,128)(2,1)S(1)}, u32[]{:S(2)}, u32[]{:S(2)}) collective-permute-start(bf16[384,128]{1,0:T(8,128)(2,1)S(1)} %bitcast.123), channel_id=1, source_target_pairs={{0,64},{16,80},{32,96},{48,112},{64,0},{80,16},{96,32},{112,48},{1... | collective-permute-start | bytes 294920 | tf_op jit(solution)/shard_map/ppermute | solution.py:94
  9.4 0.6 %collective-permute-start.2 = (bf16[384,128]{1,0:T(8,128)(2,1)S(1)}, bf16[384,128]{1,0:T(8,128)(2,1)S(1)}, u32[]{:S(2)}, u32[]{:S(2)}) collective-permute-start(bf16[384,128]{1,0:T(8,128)(2,1)S(1)} %bitcast.124), channel_id=1, source_target_pairs={{0,32},{16,48},{32,64},{48,80},{64,96},{80,112},{96,0},{112,16},{1... | collective-permute-start | bytes 294920 | tf_op jit(solution)/shard_map/ppermute | solution.py:92
  10.0 2.6 %collective-permute-start = (bf16[384,128]{1,0:T(8,128)(2,1)S(1)}, bf16[384,128]{1,0:T(8,128)(2,1)S(1)}, u32[]{:S(2)}, u32[]{:S(2)}) collective-permute-start(bf16[384,128]{1,0:T(8,128)(2,1)S(1)} %bitcast.125), channel_id=1, source_target_pairs={{0,96},{16,112},{32,0},{48,16},{64,32},{80,48},{96,64},{112,80},{1... | collective-permute-start | bytes 294920 | tf_op jit(solution)/shard_map/ppermute | solution.py:93
  12.7 0.0 collective-permute-start.3
  12.7 0.0 copy-done
  12.7 0.2 fusion.23
  12.9 0.1 copy.26
  13.0 0.1 reshape.98
  13.1 0.1 reshape.96
  13.2 0.0 collective-permute-done.1
  13.2 2.1 %collective-permute-done.2 = bf16[384,128]{1,0:T(8,128)(2,1)S(1)} collective-permute-done((bf16[384,128]{1,0:T(8,128)(2,1)S(1)}, bf16[384,128]{1,0:T(8,128)(2,1)S(1)}, u32[]{:S(2)}, u32[]{:S(2)}) %collective-permute-start.2) | collective-permute-done | bytes 98336 | tf_op jit(solution)/shard_map/ppermute | solution.py:92
  15.3 0.0 collective-permute-done
  15.3 0.1 collective-permute-start.4
  15.4 0.1 maximum_bitcast_fusion
  15.5 0.0 collective-permute-done.3
  15.5 1.5 %collective-permute-done.4 = bf16[3,384,128]{2,1,0:T(8,128)(2,1)S(1)} collective-permute-done((bf16[3,384,128]{2,1,0:T(8,128)(2,1)S(1)}, bf16[3,384,128]{2,1,0:T(8,128)(2,1)S(1)}, u32[]{:S(2)}, u32[]{:S(2)}) %collective-permute-start.4) | collective-permute-done | bytes 294944 | tf_op jit(solution)/shard_map/ppermute | solution.py:96
  17.0 0.1 maximum_select_fusion
  17.1 0.1 copy.29
  17.2 0.6 %gather_fusion = bf16[4,384,128]{2,1,0:T(8,128)(2,1)S(1)} fusion(bf16[8,384,128]{2,1,0:T(8,128)(2,1)S(1)} %bitcast.107, s32[1024]{0:T(1024)S(1)} %pad_clamp_fusion), kind=kCustom, calls=%fused_computation | custom fusion | bytes 786448 | tf_op jit(solution)/shard_map/jit(_take)/gather | solution.py:104
  17.8 0.1 broadcast_select_fusion
  18.0 0.2 copy.31
  18.2 0.1 reshape.117
  18.3 0.1 maximum_bitcast_fusion.2
  18.5 3.3 %collective-permute-start.5 = (bf16[2,480,128]{2,1,0:T(8,128)(2,1)S(1)}, bf16[2,480,128]{2,1,0:T(8,128)(2,1)S(1)}, u32[]{:S(2)}, u32[]{:S(2)}) collective-permute-start(bf16[2,480,128]{2,1,0:T(8,128)(2,1)S(1)} %get-tuple-element.17), channel_id=1, source_target_pairs={{0,2},{1,3},{2,0},{3,1},{4,6},{5,7},{6,4},{7,5},{8,10},{9,11},{10,... | collective-permute-start | bytes 737288 | tf_op jit(solution)/shard_map/ppermute | solution.py:147
  21.7 0.7 %collective-permute-start.6 = (bf16[2,480,128]{2,1,0:T(8,128)(2,1)S(1)}, bf16[2,480,128]{2,1,0:T(8,128)(2,1)S(1)}, u32[]{:S(2)}, u32[]{:S(2)}) collective-permute-start(bf16[2,480,128]{2,1,0:T(8,128)(2,1)S(1)} %get-tuple-element.18), channel_id=1, source_target_pairs={{0,1},{1,2},{2,3},{3,0},{4,5},{5,6},{6,7},{7,4},{8,9},{9,10},{10,1... | collective-permute-start | bytes 737288 | tf_op jit(solution)/shard_map/ppermute | solution.py:147
  22.4 2.6 %collective-permute-start.7 = (bf16[2,480,128]{2,1,0:T(8,128)(2,1)S(1)}, bf16[2,480,128]{2,1,0:T(8,128)(2,1)S(1)}, u32[]{:S(2)}, u32[]{:S(2)}) collective-permute-start(bf16[2,480,128]{2,1,0:T(8,128)(2,1)S(1)} %get-tuple-element.19), channel_id=1, source_target_pairs={{0,3},{1,0},{2,1},{3,2},{4,7},{5,4},{6,5},{7,6},{8,11},{9,8},{10,9... | collective-permute-start | bytes 737288 | tf_op jit(solution)/shard_map/ppermute | solution.py:147
  25.0 1.3 %collective-permute-done.5 = bf16[2,480,128]{2,1,0:T(8,128)(2,1)S(1)} collective-permute-done((bf16[2,480,128]{2,1,0:T(8,128)(2,1)S(1)}, bf16[2,480,128]{2,1,0:T(8,128)(2,1)S(1)}, u32[]{:S(2)}, u32[]{:S(2)}) %collective-permute-start.5) | collective-permute-done | bytes 245792 | tf_op jit(solution)/shard_map/ppermute | solution.py:147
  26.2 2.9 %collective-permute-done.6 = bf16[2,480,128]{2,1,0:T(8,128)(2,1)S(1)} collective-permute-done((bf16[2,480,128]{2,1,0:T(8,128)(2,1)S(1)}, bf16[2,480,128]{2,1,0:T(8,128)(2,1)S(1)}, u32[]{:S(2)}, u32[]{:S(2)}) %collective-permute-start.6) | collective-permute-done | bytes 245792 | tf_op jit(solution)/shard_map/ppermute | solution.py:147
  29.1 0.1 collective-permute-done.7
  29.2 0.1 pad_maximum_fusion
  29.3 0.3 reshape.101
  29.6 1.9 %copy.34 = bf16[4,2,32,6,2,32]{2,3,4,0,5,1:T(8,128)(2,1)S(1)} copy(bf16[4,2,32,6,2,32]{5,4,3,2,1,0:T(2,128)(2,1)S(1)} %reshape.101) | data formatting | bytes 393216 | tf_op jit(solution)/shard_map/reshape | solution.py:152
  31.5 0.5 %copy.37 = bf16[4,2,6,2,32,128]{5,2,3,0,4,1:T(8,128)(2,1)S(1)} copy(bf16[4,2,6,2,32,128]{5,4,3,2,1,0:T(8,128)(2,1)S(1)} %bitcast.106) | data formatting | bytes 1572864 | tf_op jit(solution)/shard_map/reshape | solution.py:149
  32.1 0.2 fusion.31
  32.3 1.3 %fusion.9 = bf16[2,32,4,8,2,128]{5,3,4,2,1,0:T(8,128)(2,1)S(1)} fusion(bf16[4,2,6,1,32,128]{5,2,3,0,4,1:T(8,128)(2,1)S(1)} %get-tuple-element.13, bf16[4,2,6,1,32,128]{5,2,3,0,4,1:T(8,128)(2,1)S(1)} %get-tuple-element.12, bf16[4,2,6,2,32,128]{5,2,3,0,4,1:T(8,128)(2,1)S(1)} %copy.37, bf16[4,2,32,6,2,32]{2,3,4,0,5,1:T(8,128)(2,1)S(1)} %copy.34), kind=kOutput, calls=%fused_computation.10 | convolution fusion | flops 55574528 | bytes 2818048 | tf_op jit(solution)/shard_map/akscfm,akscfn->kfmn/dot_general | solution.py:156
  33.6 0.0 copy-start.1
  33.6 0.3 copy.38
  33.9 0.1 dynamic-slice_bitcast_fusion.2
  33.9 4.1 %collective-permute-start.10 = (bf16[1024,128]{1,0:T(8,128)(2,1)S(1)}, bf16[1024,128]{1,0:T(8,128)(2,1)S(1)}, u32[]{:S(2)}, u32[]{:S(2)}) collective-permute-start(bf16[1024,128]{1,0:T(8,128)(2,1)S(1)} %get-tuple-element.10), channel_id=1, source_target_pairs={{0,12},{1,13},{2,14},{3,15},{4,0},{5,1},{6,2},{7,3},{8,4},{9,5},{1... | collective-permute-start | bytes 786440 | tf_op jit(solution)/shard_map/ppermute | solution.py:168
  38.0 0.0 collective-permute-start.8
  38.0 1.3 %collective-permute-start.9 = (bf16[1024,128]{1,0:T(8,128)(2,1)S(1)}, bf16[1024,128]{1,0:T(8,128)(2,1)S(1)}, u32[]{:S(2)}, u32[]{:S(2)}) collective-permute-start(bf16[1024,128]{1,0:T(8,128)(2,1)S(1)} %get-tuple-element.11), channel_id=1, source_target_pairs={{0,4},{1,5},{2,6},{3,7},{4,8},{5,9},{6,10},{7,11},{8,12},{9,13},{1... | collective-permute-start | bytes 786440 | tf_op jit(solution)/shard_map/ppermute | solution.py:168
  39.3 0.2 fusion.22
  39.5 0.0 copy-done.1
  39.5 0.6 %dynamic_slice.42 = s32[1]{0:T(128)} dynamic-slice(s32[8]{0:T(128)S(1)} %copy-done.1, s32[]{:T(128)S(6)} %select_n.135), dynamic_slice_sizes={1} | dynamic-slice | bytes 12 | tf_op jit(solution)/shard_map/dynamic_slice | solution.py:102
  40.1 0.6 %compare_convert_fusion = f32[2]{0:T(128)S(1)} fusion(s32[]{:T(128)} %bitcast.47), kind=kLoop, calls=%fused_computation.68 | loop fusion | flops 4 | bytes 12 | tf_op jit(solution)/shard_map/convert_element_type | solution.py:178
  40.8 4.0 %collective-permute-done.10 = bf16[1024,128]{1,0:T(8,128)(2,1)S(1)} collective-permute-done((bf16[1024,128]{1,0:T(8,128)(2,1)S(1)}, bf16[1024,128]{1,0:T(8,128)(2,1)S(1)}, u32[]{:S(2)}, u32[]{:S(2)}) %collective-permute-start.10) | collective-permute-done | bytes 262176 | tf_op jit(solution)/shard_map/ppermute | solution.py:168
  44.7 1.3 %collective-permute-done.8 = bf16[1024,128]{1,0:T(8,128)(2,1)S(1)} collective-permute-done((bf16[1024,128]{1,0:T(8,128)(2,1)S(1)}, bf16[1024,128]{1,0:T(8,128)(2,1)S(1)}, u32[]{:S(2)}, u32[]{:S(2)}) %collective-permute-start.8) | collective-permute-done | bytes 262176 | tf_op jit(solution)/shard_map/ppermute | solution.py:168
  46.0 2.4 %collective-permute-done.9 = bf16[1024,128]{1,0:T(8,128)(2,1)S(1)} collective-permute-done((bf16[1024,128]{1,0:T(8,128)(2,1)S(1)}, bf16[1024,128]{1,0:T(8,128)(2,1)S(1)}, u32[]{:S(2)}, u32[]{:S(2)}) %collective-permute-start.9) | collective-permute-done | bytes 262176 | tf_op jit(solution)/shard_map/ppermute | solution.py:168
  48.4 0.1 fusion.16
  48.6 1.1 %fusion.13 = bf16[1,2,8,128,128]{4,3,2,1,0:T(8,128)(2,1)} fusion(bf16[2,32,128,1,1]{2,1,0,4,3:T(8,128)(2,1)S(1)} %bitcast.130, bf16[2,2,32,8,128]{4,3,2,1,0:T(8,128)(2,1)S(1)} %bitcast.128, f32[2]{0:T(128)S(1)} %compare_convert_fusion), kind=kOutput, calls=%fused_computation.12 | convolution fusion | flops 34078720 | bytes 802824 | tf_op jit(solution)/shard_map/kpfrj,pft->krjt/dot_general | solution.py:171
  (15 shorter events, 0.2 us)
Async XLA Ops:
  0.0 12.7 %copy-start = (s32[8,2,2]{0,2,1:T(2,128)S(1)}, s32[8,2,2]{0,2,1:T(2,128)}, u32[]{:S(2)}) copy-start(s32[8,2,2]{0,2,1:T(2,128)} %param.5) | copy-start | bytes 388
  6.2 6.9 %collective-permute-start.1 = (bf16[384,128]{1,0:T(8,128)(2,1)S(1)}, bf16[384,128]{1,0:T(8,128)(2,1)S(1)}, u32[]{:S(2)}, u32[]{:S(2)}) collective-permute-start(bf16[384,128]{1,0:T(8,128)(2,1)S(1)} %bitcast.123), channel_id=1, source_target_pairs={{0,64},{16,80},{32,96},{48,112},{64,0},{80,16},{96,32},{112,48},{1... | collective-permute-start | bytes 294920 | tf_op jit(solution)/shard_map/ppermute | solution.py:94
  9.4 5.8 %collective-permute-start.2 = (bf16[384,128]{1,0:T(8,128)(2,1)S(1)}, bf16[384,128]{1,0:T(8,128)(2,1)S(1)}, u32[]{:S(2)}, u32[]{:S(2)}) collective-permute-start(bf16[384,128]{1,0:T(8,128)(2,1)S(1)} %bitcast.124), channel_id=1, source_target_pairs={{0,32},{16,48},{32,64},{48,80},{64,96},{80,112},{96,0},{112,16},{1... | collective-permute-start | bytes 294920 | tf_op jit(solution)/shard_map/ppermute | solution.py:92
  10.0 5.2 %collective-permute-start = (bf16[384,128]{1,0:T(8,128)(2,1)S(1)}, bf16[384,128]{1,0:T(8,128)(2,1)S(1)}, u32[]{:S(2)}, u32[]{:S(2)}) collective-permute-start(bf16[384,128]{1,0:T(8,128)(2,1)S(1)} %bitcast.125), channel_id=1, source_target_pairs={{0,96},{16,112},{32,0},{48,16},{64,32},{80,48},{96,64},{112,80},{1... | collective-permute-start | bytes 294920 | tf_op jit(solution)/shard_map/ppermute | solution.py:93
  12.7 2.8 %collective-permute-start.3 = (bf16[384,128]{1,0:T(8,128)(2,1)S(1)}, bf16[384,128]{1,0:T(8,128)(2,1)S(1)}, u32[]{:S(2)}, u32[]{:S(2)}) collective-permute-start(bf16[384,128]{1,0:T(8,128)(2,1)S(1)} %bitcast.126), channel_id=1, source_target_pairs={{0,16},{16,0},{32,48},{48,32},{64,80},{80,64},{96,112},{112,96},{1... | collective-permute-start | bytes 294920 | tf_op jit(solution)/shard_map/ppermute | solution.py:91
  15.3 1.7 %collective-permute-start.4 = (bf16[3,384,128]{2,1,0:T(8,128)(2,1)S(1)}, bf16[3,384,128]{2,1,0:T(8,128)(2,1)S(1)}, u32[]{:S(2)}, u32[]{:S(2)}) collective-permute-start(bf16[3,384,128]{2,1,0:T(8,128)(2,1)S(1)} %pad_maximum_fusion.3), channel_id=1, source_target_pairs={{0,16},{16,0},{32,48},{48,32},{64,80},{80,64},{96,112},{112,96},{1... | collective-permute-start | bytes 884744 | tf_op jit(solution)/shard_map/ppermute | solution.py:96
  18.5 7.8 %collective-permute-start.5 = (bf16[2,480,128]{2,1,0:T(8,128)(2,1)S(1)}, bf16[2,480,128]{2,1,0:T(8,128)(2,1)S(1)}, u32[]{:S(2)}, u32[]{:S(2)}) collective-permute-start(bf16[2,480,128]{2,1,0:T(8,128)(2,1)S(1)} %get-tuple-element.17), channel_id=1, source_target_pairs={{0,2},{1,3},{2,0},{3,1},{4,6},{5,7},{6,4},{7,5},{8,10},{9,11},{10,... | collective-permute-start | bytes 737288 | tf_op jit(solution)/shard_map/ppermute | solution.py:147
  21.7 7.4 %collective-permute-start.6 = (bf16[2,480,128]{2,1,0:T(8,128)(2,1)S(1)}, bf16[2,480,128]{2,1,0:T(8,128)(2,1)S(1)}, u32[]{:S(2)}, u32[]{:S(2)}) collective-permute-start(bf16[2,480,128]{2,1,0:T(8,128)(2,1)S(1)} %get-tuple-element.18), channel_id=1, source_target_pairs={{0,1},{1,2},{2,3},{3,0},{4,5},{5,6},{6,7},{7,4},{8,9},{9,10},{10,1... | collective-permute-start | bytes 737288 | tf_op jit(solution)/shard_map/ppermute | solution.py:147
  22.4 6.8 %collective-permute-start.7 = (bf16[2,480,128]{2,1,0:T(8,128)(2,1)S(1)}, bf16[2,480,128]{2,1,0:T(8,128)(2,1)S(1)}, u32[]{:S(2)}, u32[]{:S(2)}) collective-permute-start(bf16[2,480,128]{2,1,0:T(8,128)(2,1)S(1)} %get-tuple-element.19), channel_id=1, source_target_pairs={{0,3},{1,0},{2,1},{3,2},{4,7},{5,4},{6,5},{7,6},{8,11},{9,8},{10,9... | collective-permute-start | bytes 737288 | tf_op jit(solution)/shard_map/ppermute | solution.py:147
  33.6 5.9 %copy-start.1 = (s32[8]{0:T(128)S(1)}, s32[8]{0:T(128)}, u32[]{:S(2)}) copy-start(s32[8]{0:T(128)} %param.6) | copy-start | bytes 100
  33.9 10.8 %collective-permute-start.10 = (bf16[1024,128]{1,0:T(8,128)(2,1)S(1)}, bf16[1024,128]{1,0:T(8,128)(2,1)S(1)}, u32[]{:S(2)}, u32[]{:S(2)}) collective-permute-start(bf16[1024,128]{1,0:T(8,128)(2,1)S(1)} %get-tuple-element.10), channel_id=1, source_target_pairs={{0,12},{1,13},{2,14},{3,15},{4,0},{5,1},{6,2},{7,3},{8,4},{9,5},{1... | collective-permute-start | bytes 786440 | tf_op jit(solution)/shard_map/ppermute | solution.py:168
  38.0 8.0 %collective-permute-start.8 = (bf16[1024,128]{1,0:T(8,128)(2,1)S(1)}, bf16[1024,128]{1,0:T(8,128)(2,1)S(1)}, u32[]{:S(2)}, u32[]{:S(2)}) collective-permute-start(bf16[1024,128]{1,0:T(8,128)(2,1)S(1)} %get-tuple-element.9), channel_id=1, source_target_pairs={{0,8},{1,9},{2,10},{3,11},{4,12},{5,13},{6,14},{7,15},{8,0},{9,1},... | collective-permute-start | bytes 786440 | tf_op jit(solution)/shard_map/ppermute | solution.py:168
  38.0 10.4 %collective-permute-start.9 = (bf16[1024,128]{1,0:T(8,128)(2,1)S(1)}, bf16[1024,128]{1,0:T(8,128)(2,1)S(1)}, u32[]{:S(2)}, u32[]{:S(2)}) collective-permute-start(bf16[1024,128]{1,0:T(8,128)(2,1)S(1)} %get-tuple-element.11), channel_id=1, source_target_pairs={{0,4},{1,5},{2,6},{3,7},{4,8},{5,9},{6,10},{7,11},{8,12},{9,13},{1... | collective-permute-start | bytes 786440 | tf_op jit(solution)/shard_map/ppermute | solution.py:168

commit v13 on v12

--- a/solution.py
+++ b/solution.py
@@ -95,13 +95,11 @@
     mine = jnp.stack([own, from_above, from_far, from_below])
     theirs = lax.ppermute(mine[1:], "pairs", swap)
     theirs = jnp.concatenate([partner[None], theirs])
-    table = jnp.where(
-        first_core, jnp.stack([mine, theirs], axis=1), jnp.stack([theirs, mine], axis=1)
-    ).reshape((pairs_count,) + own.shape)
+    table = jnp.concatenate([mine, theirs])
     own_pairs = lax.dynamic_index_in_dim(pair_list, owner_index, 0, keepdims=False)
     live_slots = jnp.arange(slot_count, dtype=jnp.int32) < pair_count[owner_index]
-    position = ((own_pairs // 2 - chip) % chips) * 2 + own_pairs % 2
-    chosen = jnp.take(table, position.T.reshape(-1), axis=0)
+    position = (own_pairs // 2 - chip) % chips + chips * (own_pairs % 2 != core)
+    chosen = jnp.take(table, position.T.reshape(-1), axis=0, mode="clip")
     left = chosen[:slot_count]
     right = chosen[slot_count:]
     left_t = jnp.transpose(left, (0, 2, 1)).reshape((slot_count, side, side, rows, spec_rows))

time: 50.4 us -> 51.3 us (1.018); the launches traced: 49.7 us -> 51.2 us
  waiting for transfers between devices: 15.4 us -> 19.1 us
  starting transfers between devices: 18.4 us -> 16.6 us
    ppermute x1, waiting for transfers between devices: 0.01 us -> 2.66 us  [shards(): from_far = lax.ppermute(own, 'pairs', chip_shift(2))]
    ppermute x1, starting transfers between devices: 3.18 us -> 0.8 us  [shards(): from_far = lax.ppermute(own, 'pairs', chip_shift(2))]
    ppermute x1, waiting for transfers between devices: 0.01 us -> 2.03 us  [shards(): from_above = lax.ppermute(own, 'pairs', chip_shift(-1))]
    ppermute x1, waiting for transfers between devices: 2.05 us -> 1.01 us  [shards(): from_below = lax.ppermute(own, 'pairs', chip_shift(1))]
  transfers between devices with their start and end apart: 11 -> 11, of which waited for: 8 -> 10; matrix products, arithmetic and copies ran while one was open for 4% -> 4% of each run, Pallas kernels for 0% -> 0%
where the time goes in v13:
time: 51.3 us; the launch traced here: 51.2 us
  waiting for transfers between devices  19.1 us (37%)
  starting transfers between devices  16.6 us (32%)
  matrix products  7.35 us (14%)
  local copies, waits for them, and re-layouts  5.39 us (11%)
  other arithmetic  2.47 us (5%)
    ppermute x3, waiting for transfers between devices, shards(): lax.ppermute(chunk, axes, reduce_perm(e)).astype(jnp.float32)  7.7 us
    ppermute x3, starting transfers between devices, shards(): pieces.append(lax.ppermute(message, axes, gather_perm(d)))  6.51 us
    ppermute x3, starting transfers between devices, shards(): lax.ppermute(chunk, axes, reduce_perm(e)).astype(jnp.float32)  5.37 us
    dot_general x1, matrix products, shards(): jnp.dot(samples, band_table(), preferred_element_type=jnp.float32)  4.89 us
    ppermute x3, waiting for transfers between devices, shards(): pieces.append(lax.ppermute(message, axes, gather_perm(d)))  4.23 us
    ppermute x1, starting transfers between devices, shards(): from_above = lax.ppermute(own, 'pairs', chip_shift(-1))  2.91 us
    ppermute x1, waiting for transfers between devices, shards(): from_far = lax.ppermute(own, 'pairs', chip_shift(2))  2.66 us
    reshape x2, local copies, waits for them, and re-layouts, shards(): gathered[:, :, spec_rows:]  2.22 us
  transfers between devices with their start and end apart: 11, of which 10 were waited for; matrix products, arithmetic and copies ran while one was open for 4% of the time, Pallas kernels for 0%

profile of v13, /device:TPU:0, one launch (start us, length us, event | category | flops | bytes accessed | tf_op | source)
XLA Modules:
  0.0 51.2 jit_solution(4062288090395083110)
XLA Ops:
  0.0 0.0 copy-start
  0.0 4.9 %convolution_bitcast_fusion.1 = f32[768,64]{1,0:T(8,128)S(1)} fusion(bf16[768,4096]{1,0:T(8,128)(2,1)} %bitcast.123, bf16[4096,64]{1,0:T(8,128)(2,1)} %constant.159.clone), kind=kOutput, calls=%fused_computation.13 | convolution fusion | flops 402653184 | bytes 7012352 | tf_op jit(solution)/shard_map/dot_general | solution.py:73
  4.9 0.3 fusion.28
  5.2 0.6 %multiply_convert_fusion.1 = (bf16[768,32]{1,0:T(8,128)(2,1)S(1)}, f32[768,32]{1,0:T(8,128)S(1)}) fusion(f32[768,64]{1,0:T(8,128)S(1)} %convolution_bitcast_fusion.1, f32[768]{0:T(1024)S(1)} %broadcast_multiply_fusion, f32[768,32]{1,0:T(8,128)S(1)} %get-tuple-element.8), kind=kLoop, calls=%fused_computation.24 | loop fusion | flops 221184 | bytes 347136 | tf_op jit(solution)/shard_map/convert.4
  5.8 0.2 multiply_convert_fusion
  6.0 0.1 copy.9
  6.1 0.1 copy.8
  6.2 2.9 %collective-permute-start = (bf16[384,128]{1,0:T(8,128)(2,1)S(1)}, bf16[384,128]{1,0:T(8,128)(2,1)S(1)}, u32[]{:S(2)}, u32[]{:S(2)}) collective-permute-start(bf16[384,128]{1,0:T(8,128)(2,1)S(1)} %bitcast.113), channel_id=1, source_target_pairs={{0,96},{16,112},{32,0},{48,16},{64,32},{80,48},{96,64},{112,80},{1... | collective-permute-start | bytes 294920 | tf_op jit(solution)/shard_map/ppermute | solution.py:93
  9.2 0.8 %collective-permute-start.1 = (bf16[384,128]{1,0:T(8,128)(2,1)S(1)}, bf16[384,128]{1,0:T(8,128)(2,1)S(1)}, u32[]{:S(2)}, u32[]{:S(2)}) collective-permute-start(bf16[384,128]{1,0:T(8,128)(2,1)S(1)} %bitcast.114), channel_id=1, source_target_pairs={{0,64},{16,80},{32,96},{48,112},{64,0},{80,16},{96,32},{112,48},{1... | collective-permute-start | bytes 294920 | tf_op jit(solution)/shard_map/ppermute | solution.py:94
  10.0 0.9 %collective-permute-start.2 = (bf16[384,128]{1,0:T(8,128)(2,1)S(1)}, bf16[384,128]{1,0:T(8,128)(2,1)S(1)}, u32[]{:S(2)}, u32[]{:S(2)}) collective-permute-start(bf16[384,128]{1,0:T(8,128)(2,1)S(1)} %bitcast.115), channel_id=1, source_target_pairs={{0,32},{16,48},{32,64},{48,80},{64,96},{80,112},{96,0},{112,16},{1... | collective-permute-start | bytes 294920 | tf_op jit(solution)/shard_map/ppermute | solution.py:92
  10.8 0.0 collective-permute-start.3
  10.8 0.0 copy-done
  10.8 0.2 fusion.23
  11.1 0.1 copy.10
  11.2 0.1 reshape.64
  11.3 2.0 %collective-permute-done = bf16[384,128]{1,0:T(8,128)(2,1)S(1)} collective-permute-done((bf16[384,128]{1,0:T(8,128)(2,1)S(1)}, bf16[384,128]{1,0:T(8,128)(2,1)S(1)}, u32[]{:S(2)}, u32[]{:S(2)}) %collective-permute-start) | collective-permute-done | bytes 98336 | tf_op jit(solution)/shard_map/ppermute | solution.py:93
  13.3 2.7 %collective-permute-done.1 = bf16[384,128]{1,0:T(8,128)(2,1)S(1)} collective-permute-done((bf16[384,128]{1,0:T(8,128)(2,1)S(1)}, bf16[384,128]{1,0:T(8,128)(2,1)S(1)}, u32[]{:S(2)}, u32[]{:S(2)}) %collective-permute-start.1) | collective-permute-done | bytes 98336 | tf_op jit(solution)/shard_map/ppermute | solution.py:94
  16.0 1.0 %collective-permute-done.2 = bf16[384,128]{1,0:T(8,128)(2,1)S(1)} collective-permute-done((bf16[384,128]{1,0:T(8,128)(2,1)S(1)}, bf16[384,128]{1,0:T(8,128)(2,1)S(1)}, u32[]{:S(2)}, u32[]{:S(2)}) %collective-permute-start.2) | collective-permute-done | bytes 98336 | tf_op jit(solution)/shard_map/ppermute | solution.py:92
  17.1 0.1 collective-permute-start.4
  17.2 0.0 collective-permute-done.3
  17.3 1.5 %collective-permute-done.4 = bf16[3,384,128]{2,1,0:T(8,128)(2,1)S(1)} collective-permute-done((bf16[3,384,128]{2,1,0:T(8,128)(2,1)S(1)}, bf16[3,384,128]{2,1,0:T(8,128)(2,1)S(1)}, u32[]{:S(2)}, u32[]{:S(2)}) %collective-permute-start.4) | collective-permute-done | bytes 294944 | tf_op jit(solution)/shard_map/ppermute | solution.py:96
  18.8 0.6 %gather_fusion = bf16[4,384,128]{2,1,0:T(8,128)(2,1)S(1)} fusion(bf16[8,384,128]{2,1,0:T(8,128)(2,1)S(1)} %constant_dynamic-update-slice_fusion, s32[1024]{0:T(1024)S(1)} %pad_clamp_fusion), kind=kCustom, calls=%fused_computation | custom fusion | bytes 786448 | tf_op jit(solution)/shard_map/jit(_take)/gather | solution.py:102
  19.4 0.2 copy.11
  19.6 0.1 reshape.56
  19.8 0.1 maximum_bitcast_fusion
  19.9 3.3 %collective-permute-start.5 = (bf16[2,480,128]{2,1,0:T(8,128)(2,1)S(1)}, bf16[2,480,128]{2,1,0:T(8,128)(2,1)S(1)}, u32[]{:S(2)}, u32[]{:S(2)}) collective-permute-start(bf16[2,480,128]{2,1,0:T(8,128)(2,1)S(1)} %get-tuple-element.17), channel_id=1, source_target_pairs={{0,2},{1,3},{2,0},{3,1},{4,6},{5,7},{6,4},{7,5},{8,10},{9,11},{10,... | collective-permute-start | bytes 737288 | tf_op jit(solution)/shard_map/ppermute | solution.py:145
  23.2 0.7 %collective-permute-start.6 = (bf16[2,480,128]{2,1,0:T(8,128)(2,1)S(1)}, bf16[2,480,128]{2,1,0:T(8,128)(2,1)S(1)}, u32[]{:S(2)}, u32[]{:S(2)}) collective-permute-start(bf16[2,480,128]{2,1,0:T(8,128)(2,1)S(1)} %get-tuple-element.18), channel_id=1, source_target_pairs={{0,1},{1,2},{2,3},{3,0},{4,5},{5,6},{6,7},{7,4},{8,9},{9,10},{10,1... | collective-permute-start | bytes 737288 | tf_op jit(solution)/shard_map/ppermute | solution.py:145
  23.9 2.6 %collective-permute-start.7 = (bf16[2,480,128]{2,1,0:T(8,128)(2,1)S(1)}, bf16[2,480,128]{2,1,0:T(8,128)(2,1)S(1)}, u32[]{:S(2)}, u32[]{:S(2)}) collective-permute-start(bf16[2,480,128]{2,1,0:T(8,128)(2,1)S(1)} %get-tuple-element.19), channel_id=1, source_target_pairs={{0,3},{1,0},{2,1},{3,2},{4,7},{5,4},{6,5},{7,6},{8,11},{9,8},{10,9... | collective-permute-start | bytes 737288 | tf_op jit(solution)/shard_map/ppermute | solution.py:145
  26.4 1.3 %collective-permute-done.5 = bf16[2,480,128]{2,1,0:T(8,128)(2,1)S(1)} collective-permute-done((bf16[2,480,128]{2,1,0:T(8,128)(2,1)S(1)}, bf16[2,480,128]{2,1,0:T(8,128)(2,1)S(1)}, u32[]{:S(2)}, u32[]{:S(2)}) %collective-permute-start.5) | collective-permute-done | bytes 245792 | tf_op jit(solution)/shard_map/ppermute | solution.py:145
  27.7 2.9 %collective-permute-done.6 = bf16[2,480,128]{2,1,0:T(8,128)(2,1)S(1)} collective-permute-done((bf16[2,480,128]{2,1,0:T(8,128)(2,1)S(1)}, bf16[2,480,128]{2,1,0:T(8,128)(2,1)S(1)}, u32[]{:S(2)}, u32[]{:S(2)}) %collective-permute-start.6) | collective-permute-done | bytes 245792 | tf_op jit(solution)/shard_map/ppermute | solution.py:145
  30.6 0.1 collective-permute-done.7
  30.7 0.1 pad_maximum_fusion
  30.7 0.3 reshape.57
  31.1 1.9 %copy.17 = bf16[4,2,32,6,2,32]{2,3,4,0,5,1:T(8,128)(2,1)S(1)} copy(bf16[4,2,32,6,2,32]{5,4,3,2,1,0:T(2,128)(2,1)S(1)} %reshape.57) | data formatting | bytes 393216 | tf_op jit(solution)/shard_map/reshape | solution.py:150
  33.0 0.5 %copy.20 = bf16[4,2,6,2,32,128]{5,2,3,0,4,1:T(8,128)(2,1)S(1)} copy(bf16[4,2,6,2,32,128]{5,4,3,2,1,0:T(8,128)(2,1)S(1)} %bitcast.103) | data formatting | bytes 1572864 | tf_op jit(solution)/shard_map/reshape | solution.py:147
  33.5 0.2 fusion.29
  33.7 1.3 %fusion.9 = bf16[2,32,4,8,2,128]{5,3,4,2,1,0:T(8,128)(2,1)S(1)} fusion(bf16[4,2,6,1,32,128]{5,2,3,0,4,1:T(8,128)(2,1)S(1)} %get-tuple-element.13, bf16[4,2,6,1,32,128]{5,2,3,0,4,1:T(8,128)(2,1)S(1)} %get-tuple-element.12, bf16[4,2,6,2,32,128]{5,2,3,0,4,1:T(8,128)(2,1)S(1)} %copy.20, bf16[4,2,32,6,2,32]{2,3,4,0,5,1:T(8,128)(2,1)S(1)} %copy.17), kind=kOutput, calls=%fused_computation.10 | convolution fusion | flops 55574528 | bytes 2818048 | tf_op jit(solution)/shard_map/akscfm,akscfn->kfmn/dot_general | solution.py:154
  35.0 0.0 copy-start.1
  35.0 0.3 copy.21
  35.3 0.1 dynamic-slice_bitcast_fusion.2
  35.4 4.1 %collective-permute-start.10 = (bf16[1024,128]{1,0:T(8,128)(2,1)S(1)}, bf16[1024,128]{1,0:T(8,128)(2,1)S(1)}, u32[]{:S(2)}, u32[]{:S(2)}) collective-permute-start(bf16[1024,128]{1,0:T(8,128)(2,1)S(1)} %get-tuple-element.10), channel_id=1, source_target_pairs={{0,12},{1,13},{2,14},{3,15},{4,0},{5,1},{6,2},{7,3},{8,4},{9,5},{1... | collective-permute-start | bytes 786440 | tf_op jit(solution)/shard_map/ppermute | solution.py:166
  39.5 0.0 collective-permute-start.8
  39.5 1.3 %collective-permute-start.9 = (bf16[1024,128]{1,0:T(8,128)(2,1)S(1)}, bf16[1024,128]{1,0:T(8,128)(2,1)S(1)}, u32[]{:S(2)}, u32[]{:S(2)}) collective-permute-start(bf16[1024,128]{1,0:T(8,128)(2,1)S(1)} %get-tuple-element.11), channel_id=1, source_target_pairs={{0,4},{1,5},{2,6},{3,7},{4,8},{5,9},{6,10},{7,11},{8,12},{9,13},{1... | collective-permute-start | bytes 786440 | tf_op jit(solution)/shard_map/ppermute | solution.py:166
  40.8 0.2 fusion.22
  40.9 0.0 copy-done.1
  40.9 0.6 %dynamic_slice.42 = s32[1]{0:T(128)} dynamic-slice(s32[8]{0:T(128)S(1)} %copy-done.1, s32[]{:T(128)S(6)} %select_n.103), dynamic_slice_sizes={1} | dynamic-slice | bytes 12 | tf_op jit(solution)/shard_map/dynamic_slice | solution.py:100
  41.5 0.6 %compare_convert_fusion = f32[2]{0:T(128)S(1)} fusion(s32[]{:T(128)} %bitcast.43), kind=kLoop, calls=%fused_computation.68 | loop fusion | flops 4 | bytes 12 | tf_op jit(solution)/shard_map/convert_element_type | solution.py:176
  42.2 4.0 %collective-permute-done.10 = bf16[1024,128]{1,0:T(8,128)(2,1)S(1)} collective-permute-done((bf16[1024,128]{1,0:T(8,128)(2,1)S(1)}, bf16[1024,128]{1,0:T(8,128)(2,1)S(1)}, u32[]{:S(2)}, u32[]{:S(2)}) %collective-permute-start.10) | collective-permute-done | bytes 262176 | tf_op jit(solution)/shard_map/ppermute | solution.py:166
  46.2 1.3 %collective-permute-done.8 = bf16[1024,128]{1,0:T(8,128)(2,1)S(1)} collective-permute-done((bf16[1024,128]{1,0:T(8,128)(2,1)S(1)}, bf16[1024,128]{1,0:T(8,128)(2,1)S(1)}, u32[]{:S(2)}, u32[]{:S(2)}) %collective-permute-start.8) | collective-permute-done | bytes 262176 | tf_op jit(solution)/shard_map/ppermute | solution.py:166
  47.5 2.4 %collective-permute-done.9 = bf16[1024,128]{1,0:T(8,128)(2,1)S(1)} collective-permute-done((bf16[1024,128]{1,0:T(8,128)(2,1)S(1)}, bf16[1024,128]{1,0:T(8,128)(2,1)S(1)}, u32[]{:S(2)}, u32[]{:S(2)}) %collective-permute-start.9) | collective-permute-done | bytes 262176 | tf_op jit(solution)/shard_map/ppermute | solution.py:166
  49.9 0.1 fusion.16
  50.0 1.1 %fusion.13 = bf16[1,2,8,128,128]{4,3,2,1,0:T(8,128)(2,1)} fusion(bf16[2,32,128,1,1]{2,1,0,4,3:T(8,128)(2,1)S(1)} %bitcast.122, bf16[2,2,32,8,128]{4,3,2,1,0:T(8,128)(2,1)S(1)} %bitcast.121, f32[2]{0:T(128)S(1)} %compare_convert_fusion), kind=kOutput, calls=%fused_computation.12 | convolution fusion | flops 34078720 | bytes 802824 | tf_op jit(solution)/shard_map/kpfrj,pft->krjt/dot_general | solution.py:169
  (18 shorter events, 0.3 us)
Async XLA Ops:
  0.0 10.8 %copy-start = (s32[8,2,2]{0,2,1:T(2,128)S(1)}, s32[8,2,2]{0,2,1:T(2,128)}, u32[]{:S(2)}) copy-start(s32[8,2,2]{0,2,1:T(2,128)} %param.5) | copy-start | bytes 388
  6.2 7.1 %collective-permute-start = (bf16[384,128]{1,0:T(8,128)(2,1)S(1)}, bf16[384,128]{1,0:T(8,128)(2,1)S(1)}, u32[]{:S(2)}, u32[]{:S(2)}) collective-permute-start(bf16[384,128]{1,0:T(8,128)(2,1)S(1)} %bitcast.113), channel_id=1, source_target_pairs={{0,96},{16,112},{32,0},{48,16},{64,32},{80,48},{96,64},{112,80},{1... | collective-permute-start | bytes 294920 | tf_op jit(solution)/shard_map/ppermute | solution.py:93
  9.2 6.8 %collective-permute-start.1 = (bf16[384,128]{1,0:T(8,128)(2,1)S(1)}, bf16[384,128]{1,0:T(8,128)(2,1)S(1)}, u32[]{:S(2)}, u32[]{:S(2)}) collective-permute-start(bf16[384,128]{1,0:T(8,128)(2,1)S(1)} %bitcast.114), channel_id=1, source_target_pairs={{0,64},{16,80},{32,96},{48,112},{64,0},{80,16},{96,32},{112,48},{1... | collective-permute-start | bytes 294920 | tf_op jit(solution)/shard_map/ppermute | solution.py:94
  10.0 7.1 %collective-permute-start.2 = (bf16[384,128]{1,0:T(8,128)(2,1)S(1)}, bf16[384,128]{1,0:T(8,128)(2,1)S(1)}, u32[]{:S(2)}, u32[]{:S(2)}) collective-permute-start(bf16[384,128]{1,0:T(8,128)(2,1)S(1)} %bitcast.115), channel_id=1, source_target_pairs={{0,32},{16,48},{32,64},{48,80},{64,96},{80,112},{96,0},{112,16},{1... | collective-permute-start | bytes 294920 | tf_op jit(solution)/shard_map/ppermute | solution.py:92
  10.8 6.4 %collective-permute-start.3 = (bf16[384,128]{1,0:T(8,128)(2,1)S(1)}, bf16[384,128]{1,0:T(8,128)(2,1)S(1)}, u32[]{:S(2)}, u32[]{:S(2)}) collective-permute-start(bf16[384,128]{1,0:T(8,128)(2,1)S(1)} %bitcast.116), channel_id=1, source_target_pairs={{0,16},{16,0},{32,48},{48,32},{64,80},{80,64},{96,112},{112,96},{1... | collective-permute-start | bytes 294920 | tf_op jit(solution)/shard_map/ppermute | solution.py:91
  17.1 1.7 %collective-permute-start.4 = (bf16[3,384,128]{2,1,0:T(8,128)(2,1)S(1)}, bf16[3,384,128]{2,1,0:T(8,128)(2,1)S(1)}, u32[]{:S(2)}, u32[]{:S(2)}) collective-permute-start(bf16[3,384,128]{2,1,0:T(8,128)(2,1)S(1)} %pad_maximum_fusion.3), channel_id=1, source_target_pairs={{0,16},{16,0},{32,48},{48,32},{64,80},{80,64},{96,112},{112,96},{1... | collective-permute-start | bytes 884744 | tf_op jit(solution)/shard_map/ppermute | solution.py:96
  19.9 7.8 %collective-permute-start.5 = (bf16[2,480,128]{2,1,0:T(8,128)(2,1)S(1)}, bf16[2,480,128]{2,1,0:T(8,128)(2,1)S(1)}, u32[]{:S(2)}, u32[]{:S(2)}) collective-permute-start(bf16[2,480,128]{2,1,0:T(8,128)(2,1)S(1)} %get-tuple-element.17), channel_id=1, source_target_pairs={{0,2},{1,3},{2,0},{3,1},{4,6},{5,7},{6,4},{7,5},{8,10},{9,11},{10,... | collective-permute-start | bytes 737288 | tf_op jit(solution)/shard_map/ppermute | solution.py:145
  23.2 7.4 %collective-permute-start.6 = (bf16[2,480,128]{2,1,0:T(8,128)(2,1)S(1)}, bf16[2,480,128]{2,1,0:T(8,128)(2,1)S(1)}, u32[]{:S(2)}, u32[]{:S(2)}) collective-permute-start(bf16[2,480,128]{2,1,0:T(8,128)(2,1)S(1)} %get-tuple-element.18), channel_id=1, source_target_pairs={{0,1},{1,2},{2,3},{3,0},{4,5},{5,6},{6,7},{7,4},{8,9},{9,10},{10,1... | collective-permute-start | bytes 737288 | tf_op jit(solution)/shard_map/ppermute | solution.py:145
  23.9 6.8 %collective-permute-start.7 = (bf16[2,480,128]{2,1,0:T(8,128)(2,1)S(1)}, bf16[2,480,128]{2,1,0:T(8,128)(2,1)S(1)}, u32[]{:S(2)}, u32[]{:S(2)}) collective-permute-start(bf16[2,480,128]{2,1,0:T(8,128)(2,1)S(1)} %get-tuple-element.19), channel_id=1, source_target_pairs={{0,3},{1,0},{2,1},{3,2},{4,7},{5,4},{6,5},{7,6},{8,11},{9,8},{10,9... | collective-permute-start | bytes 737288 | tf_op jit(solution)/shard_map/ppermute | solution.py:145
  35.0 5.9 %copy-start.1 = (s32[8]{0:T(128)S(1)}, s32[8]{0:T(128)}, u32[]{:S(2)}) copy-start(s32[8]{0:T(128)} %param.6) | copy-start | bytes 100
  35.4 10.8 %collective-permute-start.10 = (bf16[1024,128]{1,0:T(8,128)(2,1)S(1)}, bf16[1024,128]{1,0:T(8,128)(2,1)S(1)}, u32[]{:S(2)}, u32[]{:S(2)}) collective-permute-start(bf16[1024,128]{1,0:T(8,128)(2,1)S(1)} %get-tuple-element.10), channel_id=1, source_target_pairs={{0,12},{1,13},{2,14},{3,15},{4,0},{5,1},{6,2},{7,3},{8,4},{9,5},{1... | collective-permute-start | bytes 786440 | tf_op jit(solution)/shard_map/ppermute | solution.py:166
  39.5 8.0 %collective-permute-start.8 = (bf16[1024,128]{1,0:T(8,128)(2,1)S(1)}, bf16[1024,128]{1,0:T(8,128)(2,1)S(1)}, u32[]{:S(2)}, u32[]{:S(2)}) collective-permute-start(bf16[1024,128]{1,0:T(8,128)(2,1)S(1)} %get-tuple-element.9), channel_id=1, source_target_pairs={{0,8},{1,9},{2,10},{3,11},{4,12},{5,13},{6,14},{7,15},{8,0},{9,1},... | collective-permute-start | bytes 786440 | tf_op jit(solution)/shard_map/ppermute | solution.py:166
  39.5 10.4 %collective-permute-start.9 = (bf16[1024,128]{1,0:T(8,128)(2,1)S(1)}, bf16[1024,128]{1,0:T(8,128)(2,1)S(1)}, u32[]{:S(2)}, u32[]{:S(2)}) collective-permute-start(bf16[1024,128]{1,0:T(8,128)(2,1)S(1)} %get-tuple-element.11), channel_id=1, source_target_pairs={{0,4},{1,5},{2,6},{3,7},{4,8},{5,9},{6,10},{7,11},{8,12},{9,13},{1... | collective-permute-start | bytes 786440 | tf_op jit(solution)/shard_map/ppermute | solution.py:166

commit v14 on v12

--- a/solution.py
+++ b/solution.py
@@ -5,7 +5,6 @@
 import ml_dtypes
 import numpy as np
 from jax import lax
-from jax.experimental.layout import Layout, with_layout_constraint
 from jax.sharding import Mesh
 from jax.sharding import PartitionSpec as P
 
@@ -68,11 +67,7 @@
     width = 2 * FREQS
     spec_rows = seg_dev * width
     half_rows = spec_rows // 2
-    samples = records[0].reshape(seg_dev * block_width, NSAMP)
-    projected = with_layout_constraint(
-        jnp.dot(samples, band_table(), preferred_element_type=jnp.float32), Layout((0, 1))
-    )
-    spectra = whiten(projected).reshape(seg_dev, block_width, 2 * FREQS)
+    spectra = whiten(jnp.dot(records[0], band_table(), preferred_element_type=jnp.float32))
     own = jnp.transpose(spectra, (0, 2, 1)).reshape(spec_rows, block_width)
     owner_index = lax.axis_index("pairs")
     core = owner_index % 2

time: 50.4 us -> 49.2 us (0.976)
  waiting for transfers between devices: 15.4 us -> 17.1 us
  starting transfers between devices: 18.4 us -> 17.2 us
  other arithmetic: 2.81 us -> 1.82 us
    ppermute x1, waiting for transfers between devices: 0.01 us -> 2.46 us  [shards(): from_far = lax.ppermute(own, 'pairs', chip_shift(2))]
    ppermute x1, waiting for transfers between devices: 2.05 us -> 0.17 us  [shards(): from_below = lax.ppermute(own, 'pairs', chip_shift(1))]
    ppermute x1, starting transfers between devices: 3.18 us -> 1.89 us  [shards(): from_far = lax.ppermute(own, 'pairs', chip_shift(2))]
    ppermute x1, waiting for transfers between devices: 0.01 us -> 1.07 us  [shards(): from_above = lax.ppermute(own, 'pairs', chip_shift(-1))]
    ppermute x1, starting transfers between devices: 0.6 us -> 1.64 us  [shards(): from_below = lax.ppermute(own, 'pairs', chip_shift(1))]
    ppermute x1, starting transfers between devices: 2.64 us -> 1.66 us  [shards(): from_above = lax.ppermute(own, 'pairs', chip_shift(-1))]
    another operation x2, other arithmetic: 0.75 us -> 0.09 us
  transfers between devices with their start and end apart: 11 -> 11, of which waited for: 8 -> 10; matrix products, arithmetic and copies ran while one was open for 4% -> 4% of each run, Pallas kernels for 0% -> 0%
where the time goes in v14:
time: 49.2 us; the launch traced here: 49 us
  starting transfers between devices  17.2 us (35%)
  waiting for transfers between devices  17.1 us (35%)
  matrix products  7.46 us (15%)
  local copies, waits for them, and re-layouts  5.11 us (10%)
  other arithmetic  1.82 us (4%)
    ppermute x3, waiting for transfers between devices, shards(): lax.ppermute(chunk, axes, reduce_perm(e)).astype(jnp.float32)  7.71 us
    ppermute x3, starting transfers between devices, shards(): pieces.append(lax.ppermute(message, axes, gather_perm(d)))  6.59 us
    ppermute x3, starting transfers between devices, shards(): lax.ppermute(chunk, axes, reduce_perm(e)).astype(jnp.float32)  5.36 us
    dot_general x1, matrix products, shards(): jnp.dot(records[0], band_table(), preferred_element_type=jnp.float32)  5 us
    ppermute x3, waiting for transfers between devices, shards(): pieces.append(lax.ppermute(message, axes, gather_perm(d)))  4.23 us
    ppermute x1, waiting for transfers between devices, shards(): from_far = lax.ppermute(own, 'pairs', chip_shift(2))  2.46 us
    reshape x2, local copies, waits for them, and re-layouts, shards(): gathered[:, :, spec_rows:]  2.22 us
    ppermute x1, starting transfers between devices, shards(): from_far = lax.ppermute(own, 'pairs', chip_shift(2))  1.89 us
  transfers between devices with their start and end apart: 11, of which 10 were waited for; matrix products, arithmetic and copies ran while one was open for 4% of the time, Pallas kernels for 0%

profile of v14, /device:TPU:0, one launch (start us, length us, event | category | flops | bytes accessed | tf_op | source)
XLA Modules:
  0.0 49.0 jit_solution(13709063758284935650)
XLA Ops:
  0.0 0.0 copy-start
  0.0 5.0 %fusion.16 = f32[6,128,64]{1,2,0:T(8,128)S(1)} fusion(bf16[4096,64,1]{0,1,2:T(8,128)(2,1)} %constant.176, bf16[1,6,128,4096]{3,2,1,0:T(8,128)(2,1)} %param.4), kind=kOutput, calls=%fused_computation.15 | convolution fusion | flops 402653184 | bytes 7012352 | tf_op jit(solution)/shard_map/dot_general | solution.py:70
  5.1 0.1 multiply_convert_fusion.1
  5.2 1.6 %collective-permute-start.2 = (bf16[384,128]{1,0:T(8,128)(2,1)S(1)}, bf16[384,128]{1,0:T(8,128)(2,1)S(1)}, u32[]{:S(2)}, u32[]{:S(2)}) collective-permute-start(bf16[384,128]{1,0:T(8,128)(2,1)S(1)} %bitcast.123), channel_id=1, source_target_pairs={{0,32},{16,48},{32,64},{48,80},{64,96},{80,112},{96,0},{112,16},{1... | collective-permute-start | bytes 294920 | tf_op jit(solution)/shard_map/ppermute | solution.py:87
  6.8 1.7 %collective-permute-start = (bf16[384,128]{1,0:T(8,128)(2,1)S(1)}, bf16[384,128]{1,0:T(8,128)(2,1)S(1)}, u32[]{:S(2)}, u32[]{:S(2)}) collective-permute-start(bf16[384,128]{1,0:T(8,128)(2,1)S(1)} %bitcast.124), channel_id=1, source_target_pairs={{0,96},{16,112},{32,0},{48,16},{64,32},{80,48},{96,64},{112,80},{1... | collective-permute-start | bytes 294920 | tf_op jit(solution)/shard_map/ppermute | solution.py:88
  8.5 1.9 %collective-permute-start.1 = (bf16[384,128]{1,0:T(8,128)(2,1)S(1)}, bf16[384,128]{1,0:T(8,128)(2,1)S(1)}, u32[]{:S(2)}, u32[]{:S(2)}) collective-permute-start(bf16[384,128]{1,0:T(8,128)(2,1)S(1)} %bitcast.125), channel_id=1, source_target_pairs={{0,64},{16,80},{32,96},{48,112},{64,0},{80,16},{96,32},{112,48},{1... | collective-permute-start | bytes 294920 | tf_op jit(solution)/shard_map/ppermute | solution.py:89
  10.4 0.0 collective-permute-start.3
  10.4 0.0 copy-done
  10.4 0.2 fusion.36
  10.6 0.1 copy.8
  10.7 0.1 reshape.93
  10.8 0.1 reshape.91
  10.9 0.2 collective-permute-done.2
  11.1 1.1 %collective-permute-done = bf16[384,128]{1,0:T(8,128)(2,1)S(1)} collective-permute-done((bf16[384,128]{1,0:T(8,128)(2,1)S(1)}, bf16[384,128]{1,0:T(8,128)(2,1)S(1)}, u32[]{:S(2)}, u32[]{:S(2)}) %collective-permute-start) | collective-permute-done | bytes 98336 | tf_op jit(solution)/shard_map/ppermute | solution.py:88
  12.1 2.5 %collective-permute-done.1 = bf16[384,128]{1,0:T(8,128)(2,1)S(1)} collective-permute-done((bf16[384,128]{1,0:T(8,128)(2,1)S(1)}, bf16[384,128]{1,0:T(8,128)(2,1)S(1)}, u32[]{:S(2)}, u32[]{:S(2)}) %collective-permute-start.1) | collective-permute-done | bytes 98336 | tf_op jit(solution)/shard_map/ppermute | solution.py:89
  14.6 0.1 collective-permute-start.4
  14.7 0.1 maximum_bitcast_fusion
  14.8 0.0 collective-permute-done.3
  14.8 1.5 %collective-permute-done.4 = bf16[3,384,128]{2,1,0:T(8,128)(2,1)S(1)} collective-permute-done((bf16[3,384,128]{2,1,0:T(8,128)(2,1)S(1)}, bf16[3,384,128]{2,1,0:T(8,128)(2,1)S(1)}, u32[]{:S(2)}, u32[]{:S(2)}) %collective-permute-start.4) | collective-permute-done | bytes 294944 | tf_op jit(solution)/shard_map/ppermute | solution.py:91
  16.3 0.1 maximum_select_fusion
  16.4 0.6 %gather_fusion = bf16[4,384,128]{2,1,0:T(8,128)(2,1)S(1)} fusion(bf16[8,384,128]{2,1,0:T(8,128)(2,1)S(1)} %bitcast.109, s32[1024]{0:T(1024)S(1)} %pad_clamp_fusion), kind=kCustom, calls=%fused_computation | custom fusion | bytes 786448 | tf_op jit(solution)/shard_map/jit(_take)/gather | solution.py:99
  17.1 0.1 broadcast_select_fusion
  17.2 0.2 copy.10
  17.4 0.1 reshape.113
  17.6 0.1 maximum_bitcast_fusion.2
  17.7 3.4 %collective-permute-start.5 = (bf16[2,480,128]{2,1,0:T(8,128)(2,1)S(1)}, bf16[2,480,128]{2,1,0:T(8,128)(2,1)S(1)}, u32[]{:S(2)}, u32[]{:S(2)}) collective-permute-start(bf16[2,480,128]{2,1,0:T(8,128)(2,1)S(1)} %get-tuple-element.17), channel_id=1, source_target_pairs={{0,2},{1,3},{2,0},{3,1},{4,6},{5,7},{6,4},{7,5},{8,10},{9,11},{10,... | collective-permute-start | bytes 737288 | tf_op jit(solution)/shard_map/ppermute | solution.py:142
  21.0 0.7 %collective-permute-start.6 = (bf16[2,480,128]{2,1,0:T(8,128)(2,1)S(1)}, bf16[2,480,128]{2,1,0:T(8,128)(2,1)S(1)}, u32[]{:S(2)}, u32[]{:S(2)}) collective-permute-start(bf16[2,480,128]{2,1,0:T(8,128)(2,1)S(1)} %get-tuple-element.18), channel_id=1, source_target_pairs={{0,1},{1,2},{2,3},{3,0},{4,5},{5,6},{6,7},{7,4},{8,9},{9,10},{10,1... | collective-permute-start | bytes 737288 | tf_op jit(solution)/shard_map/ppermute | solution.py:142
  21.7 2.6 %collective-permute-start.7 = (bf16[2,480,128]{2,1,0:T(8,128)(2,1)S(1)}, bf16[2,480,128]{2,1,0:T(8,128)(2,1)S(1)}, u32[]{:S(2)}, u32[]{:S(2)}) collective-permute-start(bf16[2,480,128]{2,1,0:T(8,128)(2,1)S(1)} %get-tuple-element.19), channel_id=1, source_target_pairs={{0,3},{1,0},{2,1},{3,2},{4,7},{5,4},{6,5},{7,6},{8,11},{9,8},{10,9... | collective-permute-start | bytes 737288 | tf_op jit(solution)/shard_map/ppermute | solution.py:142
  24.3 1.2 %collective-permute-done.5 = bf16[2,480,128]{2,1,0:T(8,128)(2,1)S(1)} collective-permute-done((bf16[2,480,128]{2,1,0:T(8,128)(2,1)S(1)}, bf16[2,480,128]{2,1,0:T(8,128)(2,1)S(1)}, u32[]{:S(2)}, u32[]{:S(2)}) %collective-permute-start.5) | collective-permute-done | bytes 245792 | tf_op jit(solution)/shard_map/ppermute | solution.py:142
  25.5 3.0 %collective-permute-done.6 = bf16[2,480,128]{2,1,0:T(8,128)(2,1)S(1)} collective-permute-done((bf16[2,480,128]{2,1,0:T(8,128)(2,1)S(1)}, bf16[2,480,128]{2,1,0:T(8,128)(2,1)S(1)}, u32[]{:S(2)}, u32[]{:S(2)}) %collective-permute-start.6) | collective-permute-done | bytes 245792 | tf_op jit(solution)/shard_map/ppermute | solution.py:142
  28.4 0.1 collective-permute-done.7
  28.5 0.1 pad_maximum_fusion
  28.6 0.3 reshape.96
  28.9 1.9 %copy.13 = bf16[4,2,32,6,2,32]{2,3,4,0,5,1:T(8,128)(2,1)S(1)} copy(bf16[4,2,32,6,2,32]{5,4,3,2,1,0:T(2,128)(2,1)S(1)} %reshape.96) | data formatting | bytes 393216 | tf_op jit(solution)/shard_map/reshape | solution.py:147
  30.8 0.5 %copy.16 = bf16[4,2,6,2,32,128]{5,2,3,0,4,1:T(8,128)(2,1)S(1)} copy(bf16[4,2,6,2,32,128]{5,4,3,2,1,0:T(8,128)(2,1)S(1)} %bitcast.108) | data formatting | bytes 1572864 | tf_op jit(solution)/shard_map/reshape | solution.py:144
  31.4 0.2 fusion.45
  31.6 1.3 %fusion.11 = bf16[2,32,4,8,2,128]{5,3,4,2,1,0:T(8,128)(2,1)S(1)} fusion(bf16[4,2,6,1,32,128]{5,2,3,0,4,1:T(8,128)(2,1)S(1)} %get-tuple-element.13, bf16[4,2,6,1,32,128]{5,2,3,0,4,1:T(8,128)(2,1)S(1)} %get-tuple-element.12, bf16[4,2,6,2,32,128]{5,2,3,0,4,1:T(8,128)(2,1)S(1)} %copy.16, bf16[4,2,32,6,2,32]{2,3,4,0,5,1:T(8,128)(2,1)S(1)} %copy.13), kind=kOutput, calls=%fused_computation.12 | convolution fusion | flops 55574528 | bytes 2818048 | tf_op jit(solution)/shard_map/akscfm,akscfn->kfmn/dot_general | solution.py:151
  32.9 0.0 copy-start.1
  32.9 0.3 copy.17
  33.2 0.1 dynamic-slice_bitcast_fusion.2
  33.2 4.1 %collective-permute-start.10 = (bf16[1024,128]{1,0:T(8,128)(2,1)S(1)}, bf16[1024,128]{1,0:T(8,128)(2,1)S(1)}, u32[]{:S(2)}, u32[]{:S(2)}) collective-permute-start(bf16[1024,128]{1,0:T(8,128)(2,1)S(1)} %get-tuple-element.10), channel_id=1, source_target_pairs={{0,12},{1,13},{2,14},{3,15},{4,0},{5,1},{6,2},{7,3},{8,4},{9,5},{1... | collective-permute-start | bytes 786440 | tf_op jit(solution)/shard_map/ppermute | solution.py:163
  37.3 0.0 collective-permute-start.8
  37.3 1.3 %collective-permute-start.9 = (bf16[1024,128]{1,0:T(8,128)(2,1)S(1)}, bf16[1024,128]{1,0:T(8,128)(2,1)S(1)}, u32[]{:S(2)}, u32[]{:S(2)}) collective-permute-start(bf16[1024,128]{1,0:T(8,128)(2,1)S(1)} %get-tuple-element.11), channel_id=1, source_target_pairs={{0,4},{1,5},{2,6},{3,7},{4,8},{5,9},{6,10},{7,11},{8,12},{9,13},{1... | collective-permute-start | bytes 786440 | tf_op jit(solution)/shard_map/ppermute | solution.py:163
  38.6 0.2 fusion.35
  38.8 0.0 copy-done.1
  38.8 0.6 %dynamic_slice.42 = s32[1]{0:T(128)} dynamic-slice(s32[8]{0:T(128)S(1)} %copy-done.1, s32[]{:T(128)S(6)} %select_n.135), dynamic_slice_sizes={1} | dynamic-slice | bytes 12 | tf_op jit(solution)/shard_map/dynamic_slice | solution.py:97
  39.4 0.6 %compare_convert_fusion = f32[2]{0:T(128)S(1)} fusion(s32[]{:T(128)} %bitcast.46), kind=kLoop, calls=%fused_computation.80 | loop fusion | flops 4 | bytes 12 | tf_op jit(solution)/shard_map/convert_element_type | solution.py:173
  40.0 4.0 %collective-permute-done.10 = bf16[1024,128]{1,0:T(8,128)(2,1)S(1)} collective-permute-done((bf16[1024,128]{1,0:T(8,128)(2,1)S(1)}, bf16[1024,128]{1,0:T(8,128)(2,1)S(1)}, u32[]{:S(2)}, u32[]{:S(2)}) %collective-permute-start.10) | collective-permute-done | bytes 262176 | tf_op jit(solution)/shard_map/ppermute | solution.py:163
  44.0 1.3 %collective-permute-done.8 = bf16[1024,128]{1,0:T(8,128)(2,1)S(1)} collective-permute-done((bf16[1024,128]{1,0:T(8,128)(2,1)S(1)}, bf16[1024,128]{1,0:T(8,128)(2,1)S(1)}, u32[]{:S(2)}, u32[]{:S(2)}) %collective-permute-start.8) | collective-permute-done | bytes 262176 | tf_op jit(solution)/shard_map/ppermute | solution.py:163
  45.3 2.4 %collective-permute-done.9 = bf16[1024,128]{1,0:T(8,128)(2,1)S(1)} collective-permute-done((bf16[1024,128]{1,0:T(8,128)(2,1)S(1)}, bf16[1024,128]{1,0:T(8,128)(2,1)S(1)}, u32[]{:S(2)}, u32[]{:S(2)}) %collective-permute-start.9) | collective-permute-done | bytes 262176 | tf_op jit(solution)/shard_map/ppermute | solution.py:163
  47.7 0.1 fusion.21
  47.9 1.1 %fusion.15 = bf16[1,2,8,128,128]{4,3,2,1,0:T(8,128)(2,1)} fusion(bf16[2,32,128,1,1]{2,1,0,4,3:T(8,128)(2,1)S(1)} %bitcast.130, bf16[2,2,32,8,128]{4,3,2,1,0:T(8,128)(2,1)S(1)} %bitcast.128, f32[2]{0:T(128)S(1)} %compare_convert_fusion), kind=kOutput, calls=%fused_computation.14 | convolution fusion | flops 34078720 | bytes 802824 | tf_op jit(solution)/shard_map/kpfrj,pft->krjt/dot_general | solution.py:166
  (17 shorter events, 0.3 us)
Async XLA Ops:
  0.0 10.4 %copy-start = (s32[8,2,2]{0,2,1:T(2,128)S(1)}, s32[8,2,2]{0,2,1:T(2,128)}, u32[]{:S(2)}) copy-start(s32[8,2,2]{0,2,1:T(2,128)} %param.5) | copy-start | bytes 388
  5.2 5.9 %collective-permute-start.2 = (bf16[384,128]{1,0:T(8,128)(2,1)S(1)}, bf16[384,128]{1,0:T(8,128)(2,1)S(1)}, u32[]{:S(2)}, u32[]{:S(2)}) collective-permute-start(bf16[384,128]{1,0:T(8,128)(2,1)S(1)} %bitcast.123), channel_id=1, source_target_pairs={{0,32},{16,48},{32,64},{48,80},{64,96},{80,112},{96,0},{112,16},{1... | collective-permute-start | bytes 294920 | tf_op jit(solution)/shard_map/ppermute | solution.py:87
  6.8 5.3 %collective-permute-start = (bf16[384,128]{1,0:T(8,128)(2,1)S(1)}, bf16[384,128]{1,0:T(8,128)(2,1)S(1)}, u32[]{:S(2)}, u32[]{:S(2)}) collective-permute-start(bf16[384,128]{1,0:T(8,128)(2,1)S(1)} %bitcast.124), channel_id=1, source_target_pairs={{0,96},{16,112},{32,0},{48,16},{64,32},{80,48},{96,64},{112,80},{1... | collective-permute-start | bytes 294920 | tf_op jit(solution)/shard_map/ppermute | solution.py:88
  8.5 6.1 %collective-permute-start.1 = (bf16[384,128]{1,0:T(8,128)(2,1)S(1)}, bf16[384,128]{1,0:T(8,128)(2,1)S(1)}, u32[]{:S(2)}, u32[]{:S(2)}) collective-permute-start(bf16[384,128]{1,0:T(8,128)(2,1)S(1)} %bitcast.125), channel_id=1, source_target_pairs={{0,64},{16,80},{32,96},{48,112},{64,0},{80,16},{96,32},{112,48},{1... | collective-permute-start | bytes 294920 | tf_op jit(solution)/shard_map/ppermute | solution.py:89
  10.4 4.4 %collective-permute-start.3 = (bf16[384,128]{1,0:T(8,128)(2,1)S(1)}, bf16[384,128]{1,0:T(8,128)(2,1)S(1)}, u32[]{:S(2)}, u32[]{:S(2)}) collective-permute-start(bf16[384,128]{1,0:T(8,128)(2,1)S(1)} %bitcast.126), channel_id=1, source_target_pairs={{0,16},{16,0},{32,48},{48,32},{64,80},{80,64},{96,112},{112,96},{1... | collective-permute-start | bytes 294920 | tf_op jit(solution)/shard_map/ppermute | solution.py:86
  14.6 1.7 %collective-permute-start.4 = (bf16[3,384,128]{2,1,0:T(8,128)(2,1)S(1)}, bf16[3,384,128]{2,1,0:T(8,128)(2,1)S(1)}, u32[]{:S(2)}, u32[]{:S(2)}) collective-permute-start(bf16[3,384,128]{2,1,0:T(8,128)(2,1)S(1)} %pad_maximum_fusion.3), channel_id=1, source_target_pairs={{0,16},{16,0},{32,48},{48,32},{64,80},{80,64},{96,112},{112,96},{1... | collective-permute-start | bytes 884744 | tf_op jit(solution)/shard_map/ppermute | solution.py:91
  17.7 7.8 %collective-permute-start.5 = (bf16[2,480,128]{2,1,0:T(8,128)(2,1)S(1)}, bf16[2,480,128]{2,1,0:T(8,128)(2,1)S(1)}, u32[]{:S(2)}, u32[]{:S(2)}) collective-permute-start(bf16[2,480,128]{2,1,0:T(8,128)(2,1)S(1)} %get-tuple-element.17), channel_id=1, source_target_pairs={{0,2},{1,3},{2,0},{3,1},{4,6},{5,7},{6,4},{7,5},{8,10},{9,11},{10,... | collective-permute-start | bytes 737288 | tf_op jit(solution)/shard_map/ppermute | solution.py:142
  21.0 7.4 %collective-permute-start.6 = (bf16[2,480,128]{2,1,0:T(8,128)(2,1)S(1)}, bf16[2,480,128]{2,1,0:T(8,128)(2,1)S(1)}, u32[]{:S(2)}, u32[]{:S(2)}) collective-permute-start(bf16[2,480,128]{2,1,0:T(8,128)(2,1)S(1)} %get-tuple-element.18), channel_id=1, source_target_pairs={{0,1},{1,2},{2,3},{3,0},{4,5},{5,6},{6,7},{7,4},{8,9},{9,10},{10,1... | collective-permute-start | bytes 737288 | tf_op jit(solution)/shard_map/ppermute | solution.py:142
  21.7 6.8 %collective-permute-start.7 = (bf16[2,480,128]{2,1,0:T(8,128)(2,1)S(1)}, bf16[2,480,128]{2,1,0:T(8,128)(2,1)S(1)}, u32[]{:S(2)}, u32[]{:S(2)}) collective-permute-start(bf16[2,480,128]{2,1,0:T(8,128)(2,1)S(1)} %get-tuple-element.19), channel_id=1, source_target_pairs={{0,3},{1,0},{2,1},{3,2},{4,7},{5,4},{6,5},{7,6},{8,11},{9,8},{10,9... | collective-permute-start | bytes 737288 | tf_op jit(solution)/shard_map/ppermute | solution.py:142
  32.9 5.9 %copy-start.1 = (s32[8]{0:T(128)S(1)}, s32[8]{0:T(128)}, u32[]{:S(2)}) copy-start(s32[8]{0:T(128)} %param.6) | copy-start | bytes 100
  33.2 10.8 %collective-permute-start.10 = (bf16[1024,128]{1,0:T(8,128)(2,1)S(1)}, bf16[1024,128]{1,0:T(8,128)(2,1)S(1)}, u32[]{:S(2)}, u32[]{:S(2)}) collective-permute-start(bf16[1024,128]{1,0:T(8,128)(2,1)S(1)} %get-tuple-element.10), channel_id=1, source_target_pairs={{0,12},{1,13},{2,14},{3,15},{4,0},{5,1},{6,2},{7,3},{8,4},{9,5},{1... | collective-permute-start | bytes 786440 | tf_op jit(solution)/shard_map/ppermute | solution.py:163
  37.3 8.0 %collective-permute-start.8 = (bf16[1024,128]{1,0:T(8,128)(2,1)S(1)}, bf16[1024,128]{1,0:T(8,128)(2,1)S(1)}, u32[]{:S(2)}, u32[]{:S(2)}) collective-permute-start(bf16[1024,128]{1,0:T(8,128)(2,1)S(1)} %get-tuple-element.9), channel_id=1, source_target_pairs={{0,8},{1,9},{2,10},{3,11},{4,12},{5,13},{6,14},{7,15},{8,0},{9,1},... | collective-permute-start | bytes 786440 | tf_op jit(solution)/shard_map/ppermute | solution.py:163
  37.3 10.4 %collective-permute-start.9 = (bf16[1024,128]{1,0:T(8,128)(2,1)S(1)}, bf16[1024,128]{1,0:T(8,128)(2,1)S(1)}, u32[]{:S(2)}, u32[]{:S(2)}) collective-permute-start(bf16[1024,128]{1,0:T(8,128)(2,1)S(1)} %get-tuple-element.11), channel_id=1, source_target_pairs={{0,4},{1,5},{2,6},{3,7},{4,8},{5,9},{6,10},{7,11},{8,12},{9,13},{1... | collective-permute-start | bytes 786440 | tf_op jit(solution)/shard_map/ppermute | solution.py:163

commit v15 on v13

--- a/solution.py
+++ b/solution.py
@@ -5,7 +5,6 @@
 import ml_dtypes
 import numpy as np
 from jax import lax
-from jax.experimental.layout import Layout, with_layout_constraint
 from jax.sharding import Mesh
 from jax.sharding import PartitionSpec as P
 
@@ -68,11 +67,7 @@
     width = 2 * FREQS
     spec_rows = seg_dev * width
     half_rows = spec_rows // 2
-    samples = records[0].reshape(seg_dev * block_width, NSAMP)
-    projected = with_layout_constraint(
-        jnp.dot(samples, band_table(), preferred_element_type=jnp.float32), Layout((0, 1))
-    )
-    spectra = whiten(projected).reshape(seg_dev, block_width, 2 * FREQS)
+    spectra = whiten(jnp.dot(records[0], band_table(), preferred_element_type=jnp.float32))
     own = jnp.transpose(spectra, (0, 2, 1)).reshape(spec_rows, block_width)
     owner_index = lax.axis_index("pairs")
     core = owner_index % 2

time: 51.3 us -> 50.3 us (0.981)
  other arithmetic: 2.47 us -> 1.54 us
    another operation x2, other arithmetic: 0.75 us -> 0.09 us
where the time goes in v15:
time: 50.3 us; the launch traced here: 50.1 us
  waiting for transfers between devices  19.1 us (38%)
  starting transfers between devices  16.6 us (33%)
  matrix products  7.47 us (15%)
  local copies, waits for them, and re-layouts  5.13 us (10%)
  other arithmetic  1.54 us (3%)
    ppermute x3, waiting for transfers between devices, shards(): lax.ppermute(chunk, axes, reduce_perm(e)).astype(jnp.float32)  7.7 us
    ppermute x3, starting transfers between devices, shards(): pieces.append(lax.ppermute(message, axes, gather_perm(d)))  6.51 us
    ppermute x3, starting transfers between devices, shards(): lax.ppermute(chunk, axes, reduce_perm(e)).astype(jnp.float32)  5.37 us
    dot_general x1, matrix products, shards(): jnp.dot(records[0], band_table(), preferred_element_type=jnp.float32)  5 us
    ppermute x3, waiting for transfers between devices, shards(): pieces.append(lax.ppermute(message, axes, gather_perm(d)))  4.23 us
    ppermute x1, starting transfers between devices, shards(): from_above = lax.ppermute(own, 'pairs', chip_shift(-1))  2.91 us
    ppermute x1, waiting for transfers between devices, shards(): from_far = lax.ppermute(own, 'pairs', chip_shift(2))  2.66 us
    reshape x2, local copies, waits for them, and re-layouts, shards(): gathered[:, :, spec_rows:]  2.22 us
  transfers between devices with their start and end apart: 11, of which 10 were waited for; matrix products, arithmetic and copies ran while one was open for 4% of the time, Pallas kernels for 0%

profile of v15, /device:TPU:0, one launch (start us, length us, event | category | flops | bytes accessed | tf_op | source)
XLA Modules:
  0.0 50.1 jit_solution(7409582682268911845)
XLA Ops:
  0.0 0.0 copy-start
  0.0 5.0 %fusion.16 = f32[6,128,64]{1,2,0:T(8,128)S(1)} fusion(bf16[4096,64,1]{0,1,2:T(8,128)(2,1)} %constant.163, bf16[1,6,128,4096]{3,2,1,0:T(8,128)(2,1)} %param.4), kind=kOutput, calls=%fused_computation.15 | convolution fusion | flops 402653184 | bytes 7012352 | tf_op jit(solution)/shard_map/dot_general | solution.py:70
  5.1 0.1 multiply_convert_fusion.1
  5.2 2.9 %collective-permute-start = (bf16[384,128]{1,0:T(8,128)(2,1)S(1)}, bf16[384,128]{1,0:T(8,128)(2,1)S(1)}, u32[]{:S(2)}, u32[]{:S(2)}) collective-permute-start(bf16[384,128]{1,0:T(8,128)(2,1)S(1)} %bitcast.113), channel_id=1, source_target_pairs={{0,96},{16,112},{32,0},{48,16},{64,32},{80,48},{96,64},{112,80},{1... | collective-permute-start | bytes 294920 | tf_op jit(solution)/shard_map/ppermute | solution.py:88
  8.1 0.8 %collective-permute-start.1 = (bf16[384,128]{1,0:T(8,128)(2,1)S(1)}, bf16[384,128]{1,0:T(8,128)(2,1)S(1)}, u32[]{:S(2)}, u32[]{:S(2)}) collective-permute-start(bf16[384,128]{1,0:T(8,128)(2,1)S(1)} %bitcast.114), channel_id=1, source_target_pairs={{0,64},{16,80},{32,96},{48,112},{64,0},{80,16},{96,32},{112,48},{1... | collective-permute-start | bytes 294920 | tf_op jit(solution)/shard_map/ppermute | solution.py:89
  8.9 0.9 %collective-permute-start.2 = (bf16[384,128]{1,0:T(8,128)(2,1)S(1)}, bf16[384,128]{1,0:T(8,128)(2,1)S(1)}, u32[]{:S(2)}, u32[]{:S(2)}) collective-permute-start(bf16[384,128]{1,0:T(8,128)(2,1)S(1)} %bitcast.115), channel_id=1, source_target_pairs={{0,32},{16,48},{32,64},{48,80},{64,96},{80,112},{96,0},{112,16},{1... | collective-permute-start | bytes 294920 | tf_op jit(solution)/shard_map/ppermute | solution.py:87
  9.8 0.0 collective-permute-start.3
  9.8 0.0 copy-done
  9.8 0.2 fusion.36
  10.0 0.1 copy.22
  10.1 0.1 reshape.59
  10.2 2.0 %collective-permute-done = bf16[384,128]{1,0:T(8,128)(2,1)S(1)} collective-permute-done((bf16[384,128]{1,0:T(8,128)(2,1)S(1)}, bf16[384,128]{1,0:T(8,128)(2,1)S(1)}, u32[]{:S(2)}, u32[]{:S(2)}) %collective-permute-start) | collective-permute-done | bytes 98336 | tf_op jit(solution)/shard_map/ppermute | solution.py:88
  12.3 2.7 %collective-permute-done.1 = bf16[384,128]{1,0:T(8,128)(2,1)S(1)} collective-permute-done((bf16[384,128]{1,0:T(8,128)(2,1)S(1)}, bf16[384,128]{1,0:T(8,128)(2,1)S(1)}, u32[]{:S(2)}, u32[]{:S(2)}) %collective-permute-start.1) | collective-permute-done | bytes 98336 | tf_op jit(solution)/shard_map/ppermute | solution.py:89
  14.9 1.0 %collective-permute-done.2 = bf16[384,128]{1,0:T(8,128)(2,1)S(1)} collective-permute-done((bf16[384,128]{1,0:T(8,128)(2,1)S(1)}, bf16[384,128]{1,0:T(8,128)(2,1)S(1)}, u32[]{:S(2)}, u32[]{:S(2)}) %collective-permute-start.2) | collective-permute-done | bytes 98336 | tf_op jit(solution)/shard_map/ppermute | solution.py:87
  16.0 0.1 collective-permute-start.4
  16.1 0.0 collective-permute-done.3
  16.2 1.5 %collective-permute-done.4 = bf16[3,384,128]{2,1,0:T(8,128)(2,1)S(1)} collective-permute-done((bf16[3,384,128]{2,1,0:T(8,128)(2,1)S(1)}, bf16[3,384,128]{2,1,0:T(8,128)(2,1)S(1)}, u32[]{:S(2)}, u32[]{:S(2)}) %collective-permute-start.4) | collective-permute-done | bytes 294944 | tf_op jit(solution)/shard_map/ppermute | solution.py:91
  17.7 0.6 %gather_fusion = bf16[4,384,128]{2,1,0:T(8,128)(2,1)S(1)} fusion(bf16[8,384,128]{2,1,0:T(8,128)(2,1)S(1)} %constant_dynamic-update-slice_fusion, s32[1024]{0:T(1024)S(1)} %pad_clamp_fusion), kind=kCustom, calls=%fused_computation | custom fusion | bytes 786448 | tf_op jit(solution)/shard_map/jit(_take)/gather | solution.py:97
  18.4 0.2 copy.23
  18.6 0.1 reshape.51
  18.7 0.1 maximum_bitcast_fusion
  18.8 3.3 %collective-permute-start.5 = (bf16[2,480,128]{2,1,0:T(8,128)(2,1)S(1)}, bf16[2,480,128]{2,1,0:T(8,128)(2,1)S(1)}, u32[]{:S(2)}, u32[]{:S(2)}) collective-permute-start(bf16[2,480,128]{2,1,0:T(8,128)(2,1)S(1)} %get-tuple-element.17), channel_id=1, source_target_pairs={{0,2},{1,3},{2,0},{3,1},{4,6},{5,7},{6,4},{7,5},{8,10},{9,11},{10,... | collective-permute-start | bytes 737288 | tf_op jit(solution)/shard_map/ppermute | solution.py:140
  22.1 0.7 %collective-permute-start.6 = (bf16[2,480,128]{2,1,0:T(8,128)(2,1)S(1)}, bf16[2,480,128]{2,1,0:T(8,128)(2,1)S(1)}, u32[]{:S(2)}, u32[]{:S(2)}) collective-permute-start(bf16[2,480,128]{2,1,0:T(8,128)(2,1)S(1)} %get-tuple-element.18), channel_id=1, source_target_pairs={{0,1},{1,2},{2,3},{3,0},{4,5},{5,6},{6,7},{7,4},{8,9},{9,10},{10,1... | collective-permute-start | bytes 737288 | tf_op jit(solution)/shard_map/ppermute | solution.py:140
  22.8 2.6 %collective-permute-start.7 = (bf16[2,480,128]{2,1,0:T(8,128)(2,1)S(1)}, bf16[2,480,128]{2,1,0:T(8,128)(2,1)S(1)}, u32[]{:S(2)}, u32[]{:S(2)}) collective-permute-start(bf16[2,480,128]{2,1,0:T(8,128)(2,1)S(1)} %get-tuple-element.19), channel_id=1, source_target_pairs={{0,3},{1,0},{2,1},{3,2},{4,7},{5,4},{6,5},{7,6},{8,11},{9,8},{10,9... | collective-permute-start | bytes 737288 | tf_op jit(solution)/shard_map/ppermute | solution.py:140
  25.4 1.3 %collective-permute-done.5 = bf16[2,480,128]{2,1,0:T(8,128)(2,1)S(1)} collective-permute-done((bf16[2,480,128]{2,1,0:T(8,128)(2,1)S(1)}, bf16[2,480,128]{2,1,0:T(8,128)(2,1)S(1)}, u32[]{:S(2)}, u32[]{:S(2)}) %collective-permute-start.5) | collective-permute-done | bytes 245792 | tf_op jit(solution)/shard_map/ppermute | solution.py:140
  26.6 2.9 %collective-permute-done.6 = bf16[2,480,128]{2,1,0:T(8,128)(2,1)S(1)} collective-permute-done((bf16[2,480,128]{2,1,0:T(8,128)(2,1)S(1)}, bf16[2,480,128]{2,1,0:T(8,128)(2,1)S(1)}, u32[]{:S(2)}, u32[]{:S(2)}) %collective-permute-start.6) | collective-permute-done | bytes 245792 | tf_op jit(solution)/shard_map/ppermute | solution.py:140
  29.5 0.1 collective-permute-done.7
  29.6 0.1 pad_maximum_fusion
  29.7 0.3 reshape.52
  30.0 1.9 %copy.29 = bf16[4,2,32,6,2,32]{2,3,4,0,5,1:T(8,128)(2,1)S(1)} copy(bf16[4,2,32,6,2,32]{5,4,3,2,1,0:T(2,128)(2,1)S(1)} %reshape.52) | data formatting | bytes 393216 | tf_op jit(solution)/shard_map/reshape | solution.py:145
  31.9 0.5 %copy.32 = bf16[4,2,6,2,32,128]{5,2,3,0,4,1:T(8,128)(2,1)S(1)} copy(bf16[4,2,6,2,32,128]{5,4,3,2,1,0:T(8,128)(2,1)S(1)} %bitcast.105) | data formatting | bytes 1572864 | tf_op jit(solution)/shard_map/reshape | solution.py:142
  32.5 0.2 fusion.43
  32.6 1.3 %fusion.11 = bf16[2,32,4,8,2,128]{5,3,4,2,1,0:T(8,128)(2,1)S(1)} fusion(bf16[4,2,6,1,32,128]{5,2,3,0,4,1:T(8,128)(2,1)S(1)} %get-tuple-element.13, bf16[4,2,6,1,32,128]{5,2,3,0,4,1:T(8,128)(2,1)S(1)} %get-tuple-element.12, bf16[4,2,6,2,32,128]{5,2,3,0,4,1:T(8,128)(2,1)S(1)} %copy.32, bf16[4,2,32,6,2,32]{2,3,4,0,5,1:T(8,128)(2,1)S(1)} %copy.29), kind=kOutput, calls=%fused_computation.12 | convolution fusion | flops 55574528 | bytes 2818048 | tf_op jit(solution)/shard_map/akscfm,akscfn->kfmn/dot_general | solution.py:149
  34.0 0.0 copy-start.1
  34.0 0.3 copy.33
  34.2 0.1 dynamic-slice_bitcast_fusion.2
  34.3 4.1 %collective-permute-start.10 = (bf16[1024,128]{1,0:T(8,128)(2,1)S(1)}, bf16[1024,128]{1,0:T(8,128)(2,1)S(1)}, u32[]{:S(2)}, u32[]{:S(2)}) collective-permute-start(bf16[1024,128]{1,0:T(8,128)(2,1)S(1)} %get-tuple-element.10), channel_id=1, source_target_pairs={{0,12},{1,13},{2,14},{3,15},{4,0},{5,1},{6,2},{7,3},{8,4},{9,5},{1... | collective-permute-start | bytes 786440 | tf_op jit(solution)/shard_map/ppermute | solution.py:161
  38.4 0.0 collective-permute-start.8
  38.4 1.3 %collective-permute-start.9 = (bf16[1024,128]{1,0:T(8,128)(2,1)S(1)}, bf16[1024,128]{1,0:T(8,128)(2,1)S(1)}, u32[]{:S(2)}, u32[]{:S(2)}) collective-permute-start(bf16[1024,128]{1,0:T(8,128)(2,1)S(1)} %get-tuple-element.11), channel_id=1, source_target_pairs={{0,4},{1,5},{2,6},{3,7},{4,8},{5,9},{6,10},{7,11},{8,12},{9,13},{1... | collective-permute-start | bytes 786440 | tf_op jit(solution)/shard_map/ppermute | solution.py:161
  39.7 0.2 fusion.35
  39.8 0.0 copy-done.1
  39.8 0.6 %dynamic_slice.42 = s32[1]{0:T(128)} dynamic-slice(s32[8]{0:T(128)S(1)} %copy-done.1, s32[]{:T(128)S(6)} %select_n.103), dynamic_slice_sizes={1} | dynamic-slice | bytes 12 | tf_op jit(solution)/shard_map/dynamic_slice | solution.py:95
  40.4 0.6 %compare_convert_fusion = f32[2]{0:T(128)S(1)} fusion(s32[]{:T(128)} %bitcast.42), kind=kLoop, calls=%fused_computation.80 | loop fusion | flops 4 | bytes 12 | tf_op jit(solution)/shard_map/convert_element_type | solution.py:171
  41.1 4.0 %collective-permute-done.10 = bf16[1024,128]{1,0:T(8,128)(2,1)S(1)} collective-permute-done((bf16[1024,128]{1,0:T(8,128)(2,1)S(1)}, bf16[1024,128]{1,0:T(8,128)(2,1)S(1)}, u32[]{:S(2)}, u32[]{:S(2)}) %collective-permute-start.10) | collective-permute-done | bytes 262176 | tf_op jit(solution)/shard_map/ppermute | solution.py:161
  45.1 1.3 %collective-permute-done.8 = bf16[1024,128]{1,0:T(8,128)(2,1)S(1)} collective-permute-done((bf16[1024,128]{1,0:T(8,128)(2,1)S(1)}, bf16[1024,128]{1,0:T(8,128)(2,1)S(1)}, u32[]{:S(2)}, u32[]{:S(2)}) %collective-permute-start.8) | collective-permute-done | bytes 262176 | tf_op jit(solution)/shard_map/ppermute | solution.py:161
  46.4 2.4 %collective-permute-done.9 = bf16[1024,128]{1,0:T(8,128)(2,1)S(1)} collective-permute-done((bf16[1024,128]{1,0:T(8,128)(2,1)S(1)}, bf16[1024,128]{1,0:T(8,128)(2,1)S(1)}, u32[]{:S(2)}, u32[]{:S(2)}) %collective-permute-start.9) | collective-permute-done | bytes 262176 | tf_op jit(solution)/shard_map/ppermute | solution.py:161
  48.8 0.1 fusion.21
  49.0 1.1 %fusion.15 = bf16[1,2,8,128,128]{4,3,2,1,0:T(8,128)(2,1)} fusion(bf16[2,32,128,1,1]{2,1,0,4,3:T(8,128)(2,1)S(1)} %bitcast.122, bf16[2,2,32,8,128]{4,3,2,1,0:T(8,128)(2,1)S(1)} %bitcast.121, f32[2]{0:T(128)S(1)} %compare_convert_fusion), kind=kOutput, calls=%fused_computation.14 | convolution fusion | flops 34078720 | bytes 802824 | tf_op jit(solution)/shard_map/kpfrj,pft->krjt/dot_general | solution.py:164
  (20 shorter events, 0.3 us)
Async XLA Ops:
  0.0 9.8 %copy-start = (s32[8,2,2]{0,2,1:T(2,128)S(1)}, s32[8,2,2]{0,2,1:T(2,128)}, u32[]{:S(2)}) copy-start(s32[8,2,2]{0,2,1:T(2,128)} %param.5) | copy-start | bytes 388
  5.2 7.1 %collective-permute-start = (bf16[384,128]{1,0:T(8,128)(2,1)S(1)}, bf16[384,128]{1,0:T(8,128)(2,1)S(1)}, u32[]{:S(2)}, u32[]{:S(2)}) collective-permute-start(bf16[384,128]{1,0:T(8,128)(2,1)S(1)} %bitcast.113), channel_id=1, source_target_pairs={{0,96},{16,112},{32,0},{48,16},{64,32},{80,48},{96,64},{112,80},{1... | collective-permute-start | bytes 294920 | tf_op jit(solution)/shard_map/ppermute | solution.py:88
  8.1 6.9 %collective-permute-start.1 = (bf16[384,128]{1,0:T(8,128)(2,1)S(1)}, bf16[384,128]{1,0:T(8,128)(2,1)S(1)}, u32[]{:S(2)}, u32[]{:S(2)}) collective-permute-start(bf16[384,128]{1,0:T(8,128)(2,1)S(1)} %bitcast.114), channel_id=1, source_target_pairs={{0,64},{16,80},{32,96},{48,112},{64,0},{80,16},{96,32},{112,48},{1... | collective-permute-start | bytes 294920 | tf_op jit(solution)/shard_map/ppermute | solution.py:89
  8.9 7.1 %collective-permute-start.2 = (bf16[384,128]{1,0:T(8,128)(2,1)S(1)}, bf16[384,128]{1,0:T(8,128)(2,1)S(1)}, u32[]{:S(2)}, u32[]{:S(2)}) collective-permute-start(bf16[384,128]{1,0:T(8,128)(2,1)S(1)} %bitcast.115), channel_id=1, source_target_pairs={{0,32},{16,48},{32,64},{48,80},{64,96},{80,112},{96,0},{112,16},{1... | collective-permute-start | bytes 294920 | tf_op jit(solution)/shard_map/ppermute | solution.py:87
  9.8 6.4 %collective-permute-start.3 = (bf16[384,128]{1,0:T(8,128)(2,1)S(1)}, bf16[384,128]{1,0:T(8,128)(2,1)S(1)}, u32[]{:S(2)}, u32[]{:S(2)}) collective-permute-start(bf16[384,128]{1,0:T(8,128)(2,1)S(1)} %bitcast.116), channel_id=1, source_target_pairs={{0,16},{16,0},{32,48},{48,32},{64,80},{80,64},{96,112},{112,96},{1... | collective-permute-start | bytes 294920 | tf_op jit(solution)/shard_map/ppermute | solution.py:86
  16.0 1.7 %collective-permute-start.4 = (bf16[3,384,128]{2,1,0:T(8,128)(2,1)S(1)}, bf16[3,384,128]{2,1,0:T(8,128)(2,1)S(1)}, u32[]{:S(2)}, u32[]{:S(2)}) collective-permute-start(bf16[3,384,128]{2,1,0:T(8,128)(2,1)S(1)} %pad_maximum_fusion.3), channel_id=1, source_target_pairs={{0,16},{16,0},{32,48},{48,32},{64,80},{80,64},{96,112},{112,96},{1... | collective-permute-start | bytes 884744 | tf_op jit(solution)/shard_map/ppermute | solution.py:91
  18.8 7.8 %collective-permute-start.5 = (bf16[2,480,128]{2,1,0:T(8,128)(2,1)S(1)}, bf16[2,480,128]{2,1,0:T(8,128)(2,1)S(1)}, u32[]{:S(2)}, u32[]{:S(2)}) collective-permute-start(bf16[2,480,128]{2,1,0:T(8,128)(2,1)S(1)} %get-tuple-element.17), channel_id=1, source_target_pairs={{0,2},{1,3},{2,0},{3,1},{4,6},{5,7},{6,4},{7,5},{8,10},{9,11},{10,... | collective-permute-start | bytes 737288 | tf_op jit(solution)/shard_map/ppermute | solution.py:140
  22.1 7.4 %collective-permute-start.6 = (bf16[2,480,128]{2,1,0:T(8,128)(2,1)S(1)}, bf16[2,480,128]{2,1,0:T(8,128)(2,1)S(1)}, u32[]{:S(2)}, u32[]{:S(2)}) collective-permute-start(bf16[2,480,128]{2,1,0:T(8,128)(2,1)S(1)} %get-tuple-element.18), channel_id=1, source_target_pairs={{0,1},{1,2},{2,3},{3,0},{4,5},{5,6},{6,7},{7,4},{8,9},{9,10},{10,1... | collective-permute-start | bytes 737288 | tf_op jit(solution)/shard_map/ppermute | solution.py:140
  22.8 6.8 %collective-permute-start.7 = (bf16[2,480,128]{2,1,0:T(8,128)(2,1)S(1)}, bf16[2,480,128]{2,1,0:T(8,128)(2,1)S(1)}, u32[]{:S(2)}, u32[]{:S(2)}) collective-permute-start(bf16[2,480,128]{2,1,0:T(8,128)(2,1)S(1)} %get-tuple-element.19), channel_id=1, source_target_pairs={{0,3},{1,0},{2,1},{3,2},{4,7},{5,4},{6,5},{7,6},{8,11},{9,8},{10,9... | collective-permute-start | bytes 737288 | tf_op jit(solution)/shard_map/ppermute | solution.py:140
  34.0 5.9 %copy-start.1 = (s32[8]{0:T(128)S(1)}, s32[8]{0:T(128)}, u32[]{:S(2)}) copy-start(s32[8]{0:T(128)} %param.6) | copy-start | bytes 100
  34.3 10.8 %collective-permute-start.10 = (bf16[1024,128]{1,0:T(8,128)(2,1)S(1)}, bf16[1024,128]{1,0:T(8,128)(2,1)S(1)}, u32[]{:S(2)}, u32[]{:S(2)}) collective-permute-start(bf16[1024,128]{1,0:T(8,128)(2,1)S(1)} %get-tuple-element.10), channel_id=1, source_target_pairs={{0,12},{1,13},{2,14},{3,15},{4,0},{5,1},{6,2},{7,3},{8,4},{9,5},{1... | collective-permute-start | bytes 786440 | tf_op jit(solution)/shard_map/ppermute | solution.py:161
  38.4 8.0 %collective-permute-start.8 = (bf16[1024,128]{1,0:T(8,128)(2,1)S(1)}, bf16[1024,128]{1,0:T(8,128)(2,1)S(1)}, u32[]{:S(2)}, u32[]{:S(2)}) collective-permute-start(bf16[1024,128]{1,0:T(8,128)(2,1)S(1)} %get-tuple-element.9), channel_id=1, source_target_pairs={{0,8},{1,9},{2,10},{3,11},{4,12},{5,13},{6,14},{7,15},{8,0},{9,1},... | collective-permute-start | bytes 786440 | tf_op jit(solution)/shard_map/ppermute | solution.py:161
  38.4 10.4 %collective-permute-start.9 = (bf16[1024,128]{1,0:T(8,128)(2,1)S(1)}, bf16[1024,128]{1,0:T(8,128)(2,1)S(1)}, u32[]{:S(2)}, u32[]{:S(2)}) collective-permute-start(bf16[1024,128]{1,0:T(8,128)(2,1)S(1)} %get-tuple-element.11), channel_id=1, source_target_pairs={{0,4},{1,5},{2,6},{3,7},{4,8},{5,9},{6,10},{7,11},{8,12},{9,13},{1... | collective-permute-start | bytes 786440 | tf_op jit(solution)/shard_map/ppermute | solution.py:161

commit v16 on v14

--- a/solution.py
+++ b/solution.py
@@ -88,8 +88,9 @@
     from_above = lax.ppermute(own, "pairs", chip_shift(-1))
     from_far = lax.ppermute(own, "pairs", chip_shift(2))
     mine = jnp.stack([own, from_above, from_far, from_below])
-    theirs = lax.ppermute(mine[1:], "pairs", swap)
-    theirs = jnp.concatenate([partner[None], theirs])
+    theirs_near = lax.ppermute(jnp.stack([from_above, from_below]), "pairs", swap)
+    theirs_far = lax.ppermute(from_far, "pairs", swap)
+    theirs = jnp.stack([partner, theirs_near[0], theirs_far, theirs_near[1]])
     table = jnp.where(
         first_core, jnp.stack([mine, theirs], axis=1), jnp.stack([theirs, mine], axis=1)
     ).reshape((pairs_count,) + own.shape)

time: 49.2 us -> 47 us (0.955)
  waiting for transfers between devices: 17.1 us -> 14.3 us
  starting transfers between devices: 17.2 us -> 17.9 us
    ppermute x3, waiting for transfers between devices: 7.71 us -> 5.33 us  [shards(): lax.ppermute(chunk, axes, reduce_perm(e)).astype(jnp.float32)]
    ppermute x3, starting transfers between devices: 5.36 us -> 5.97 us  [shards(): lax.ppermute(chunk, axes, reduce_perm(e)).astype(jnp.float32)]
    ppermute x1 -> x2, waiting for transfers between devices: 1.48 us -> 1.2 us  [the longest x1 1.2 us: shards(): theirs_far = lax.ppermute(from_far, 'pairs', swap)]
  transfers between devices with their start and end apart: 11 -> 12, of which waited for: 10 -> 10; matrix products, arithmetic and copies ran while one was open for 4% -> 4% of each run, Pallas kernels for 0% -> 0%
where the time goes in v16:
time: 47 us; the launch traced here: 46.9 us
  starting transfers between devices  17.9 us (38%)
  waiting for transfers between devices  14.3 us (30%)
  matrix products  7.46 us (16%)
  local copies, waits for them, and re-layouts  5.12 us (11%)
  other arithmetic  1.82 us (4%)
    ppermute x3, starting transfers between devices, shards(): pieces.append(lax.ppermute(message, axes, gather_perm(d)))  6.59 us
    ppermute x3, starting transfers between devices, shards(): lax.ppermute(chunk, axes, reduce_perm(e)).astype(jnp.float32)  5.97 us
    ppermute x3, waiting for transfers between devices, shards(): lax.ppermute(chunk, axes, reduce_perm(e)).astype(jnp.float32)  5.33 us
    dot_general x1, matrix products, shards(): jnp.dot(records[0], band_table(), preferred_element_type=jnp.float32)  5 us
    ppermute x3, waiting for transfers between devices, shards(): pieces.append(lax.ppermute(message, axes, gather_perm(d)))  4.23 us
    ppermute x1, waiting for transfers between devices, shards(): from_far = lax.ppermute(own, 'pairs', chip_shift(2))  2.33 us
    reshape x2, local copies, waits for them, and re-layouts, shards(): gathered[:, :, spec_rows:]  2.22 us
    ppermute x1, starting transfers between devices, shards(): from_far = lax.ppermute(own, 'pairs', chip_shift(2))  1.89 us
  transfers between devices with their start and end apart: 12, of which 10 were waited for; matrix products, arithmetic and copies ran while one was open for 4% of the time, Pallas kernels for 0%

profile of v16, /device:TPU:0, one launch (start us, length us, event | category | flops | bytes accessed | tf_op | source)
XLA Modules:
  0.0 46.9 jit_solution(12112957907224795751)
XLA Ops:
  0.0 0.0 copy-start
  0.0 5.0 %fusion.16 = f32[6,128,64]{1,2,0:T(8,128)S(1)} fusion(bf16[4096,64,1]{0,1,2:T(8,128)(2,1)} %constant.176, bf16[1,6,128,4096]{3,2,1,0:T(8,128)(2,1)} %param.4), kind=kOutput, calls=%fused_computation.15 | convolution fusion | flops 402653184 | bytes 7012352 | tf_op jit(solution)/shard_map/dot_general | solution.py:70
  5.1 0.1 multiply_convert_fusion.1
  5.2 1.6 %collective-permute-start.2 = (bf16[384,128]{1,0:T(8,128)(2,1)S(1)}, bf16[384,128]{1,0:T(8,128)(2,1)S(1)}, u32[]{:S(2)}, u32[]{:S(2)}) collective-permute-start(bf16[384,128]{1,0:T(8,128)(2,1)S(1)} %bitcast.118), channel_id=1, source_target_pairs={{0,32},{16,48},{32,64},{48,80},{64,96},{80,112},{96,0},{112,16},{1... | collective-permute-start | bytes 294920 | tf_op jit(solution)/shard_map/ppermute | solution.py:87
  6.8 1.7 %collective-permute-start = (bf16[384,128]{1,0:T(8,128)(2,1)S(1)}, bf16[384,128]{1,0:T(8,128)(2,1)S(1)}, u32[]{:S(2)}, u32[]{:S(2)}) collective-permute-start(bf16[384,128]{1,0:T(8,128)(2,1)S(1)} %bitcast.119), channel_id=1, source_target_pairs={{0,96},{16,112},{32,0},{48,16},{64,32},{80,48},{96,64},{112,80},{1... | collective-permute-start | bytes 294920 | tf_op jit(solution)/shard_map/ppermute | solution.py:88
  8.5 1.9 %collective-permute-start.1 = (bf16[384,128]{1,0:T(8,128)(2,1)S(1)}, bf16[384,128]{1,0:T(8,128)(2,1)S(1)}, u32[]{:S(2)}, u32[]{:S(2)}) collective-permute-start(bf16[384,128]{1,0:T(8,128)(2,1)S(1)} %bitcast.120), channel_id=1, source_target_pairs={{0,64},{16,80},{32,96},{48,112},{64,0},{80,16},{96,32},{112,48},{1... | collective-permute-start | bytes 294920 | tf_op jit(solution)/shard_map/ppermute | solution.py:89
  10.4 0.0 collective-permute-start.3
  10.4 0.0 copy-done
  10.4 0.2 fusion.36
  10.6 0.1 copy.8
  10.7 0.1 reshape.93
  10.8 0.1 reshape.91
  11.0 0.1 collective-permute-done.2
  11.1 1.1 %collective-permute-done = bf16[384,128]{1,0:T(8,128)(2,1)S(1)} collective-permute-done((bf16[384,128]{1,0:T(8,128)(2,1)S(1)}, bf16[384,128]{1,0:T(8,128)(2,1)S(1)}, u32[]{:S(2)}, u32[]{:S(2)}) %collective-permute-start) | collective-permute-done | bytes 98336 | tf_op jit(solution)/shard_map/ppermute | solution.py:88
  12.2 0.1 collective-permute-start.4
  12.3 2.3 %collective-permute-done.1 = bf16[384,128]{1,0:T(8,128)(2,1)S(1)} collective-permute-done((bf16[384,128]{1,0:T(8,128)(2,1)S(1)}, bf16[384,128]{1,0:T(8,128)(2,1)S(1)}, u32[]{:S(2)}, u32[]{:S(2)}) %collective-permute-start.1) | collective-permute-done | bytes 98336 | tf_op jit(solution)/shard_map/ppermute | solution.py:89
  14.6 0.0 collective-permute-start.5
  14.6 0.1 maximum_bitcast_fusion
  14.7 0.0 collective-permute-done.4
  14.7 0.0 collective-permute-done.3
  14.7 1.2 %collective-permute-done.5 = bf16[384,128]{1,0:T(8,128)(2,1)S(1)} collective-permute-done((bf16[384,128]{1,0:T(8,128)(2,1)S(1)}, bf16[384,128]{1,0:T(8,128)(2,1)S(1)}, u32[]{:S(2)}, u32[]{:S(2)}) %collective-permute-start.5) | collective-permute-done | bytes 98336 | tf_op jit(solution)/shard_map/ppermute | solution.py:92
  15.9 0.1 maximum_bitcast_fusion.1
  16.0 0.1 maximum_select_fusion
  16.0 0.6 %gather_fusion = bf16[4,384,128]{2,1,0:T(8,128)(2,1)S(1)} fusion(bf16[8,384,128]{2,1,0:T(8,128)(2,1)S(1)} %bitcast.110, s32[1024]{0:T(1024)S(1)} %pad_clamp_fusion), kind=kCustom, calls=%fused_computation | custom fusion | bytes 786448 | tf_op jit(solution)/shard_map/jit(_take)/gather | solution.py:100
  16.7 0.1 broadcast_select_fusion
  16.8 0.2 copy.10
  17.0 0.1 reshape.113
  17.2 0.1 maximum_bitcast_fusion.2
  17.3 3.4 %collective-permute-start.6 = (bf16[2,480,128]{2,1,0:T(8,128)(2,1)S(1)}, bf16[2,480,128]{2,1,0:T(8,128)(2,1)S(1)}, u32[]{:S(2)}, u32[]{:S(2)}) collective-permute-start(bf16[2,480,128]{2,1,0:T(8,128)(2,1)S(1)} %get-tuple-element.17), channel_id=1, source_target_pairs={{0,2},{1,3},{2,0},{3,1},{4,6},{5,7},{6,4},{7,5},{8,10},{9,11},{10,... | collective-permute-start | bytes 737288 | tf_op jit(solution)/shard_map/ppermute | solution.py:143
  20.7 0.7 %collective-permute-start.7 = (bf16[2,480,128]{2,1,0:T(8,128)(2,1)S(1)}, bf16[2,480,128]{2,1,0:T(8,128)(2,1)S(1)}, u32[]{:S(2)}, u32[]{:S(2)}) collective-permute-start(bf16[2,480,128]{2,1,0:T(8,128)(2,1)S(1)} %get-tuple-element.18), channel_id=1, source_target_pairs={{0,1},{1,2},{2,3},{3,0},{4,5},{5,6},{6,7},{7,4},{8,9},{9,10},{10,1... | collective-permute-start | bytes 737288 | tf_op jit(solution)/shard_map/ppermute | solution.py:143
  21.3 2.6 %collective-permute-start.8 = (bf16[2,480,128]{2,1,0:T(8,128)(2,1)S(1)}, bf16[2,480,128]{2,1,0:T(8,128)(2,1)S(1)}, u32[]{:S(2)}, u32[]{:S(2)}) collective-permute-start(bf16[2,480,128]{2,1,0:T(8,128)(2,1)S(1)} %get-tuple-element.19), channel_id=1, source_target_pairs={{0,3},{1,0},{2,1},{3,2},{4,7},{5,4},{6,5},{7,6},{8,11},{9,8},{10,9... | collective-permute-start | bytes 737288 | tf_op jit(solution)/shard_map/ppermute | solution.py:143
  23.9 1.2 %collective-permute-done.6 = bf16[2,480,128]{2,1,0:T(8,128)(2,1)S(1)} collective-permute-done((bf16[2,480,128]{2,1,0:T(8,128)(2,1)S(1)}, bf16[2,480,128]{2,1,0:T(8,128)(2,1)S(1)}, u32[]{:S(2)}, u32[]{:S(2)}) %collective-permute-start.6) | collective-permute-done | bytes 245792 | tf_op jit(solution)/shard_map/ppermute | solution.py:143
  25.1 3.0 %collective-permute-done.7 = bf16[2,480,128]{2,1,0:T(8,128)(2,1)S(1)} collective-permute-done((bf16[2,480,128]{2,1,0:T(8,128)(2,1)S(1)}, bf16[2,480,128]{2,1,0:T(8,128)(2,1)S(1)}, u32[]{:S(2)}, u32[]{:S(2)}) %collective-permute-start.7) | collective-permute-done | bytes 245792 | tf_op jit(solution)/shard_map/ppermute | solution.py:143
  28.1 0.1 collective-permute-done.8
  28.2 0.1 pad_maximum_fusion
  28.2 0.3 reshape.96
  28.5 1.9 %copy.13 = bf16[4,2,32,6,2,32]{2,3,4,0,5,1:T(8,128)(2,1)S(1)} copy(bf16[4,2,32,6,2,32]{5,4,3,2,1,0:T(2,128)(2,1)S(1)} %reshape.96) | data formatting | bytes 393216 | tf_op jit(solution)/shard_map/reshape | solution.py:148
  30.4 0.5 %copy.16 = bf16[4,2,6,2,32,128]{5,2,3,0,4,1:T(8,128)(2,1)S(1)} copy(bf16[4,2,6,2,32,128]{5,4,3,2,1,0:T(8,128)(2,1)S(1)} %bitcast.109) | data formatting | bytes 1572864 | tf_op jit(solution)/shard_map/reshape | solution.py:145
  31.0 0.2 fusion.45
  31.2 1.3 %fusion.11 = bf16[2,32,4,8,2,128]{5,3,4,2,1,0:T(8,128)(2,1)S(1)} fusion(bf16[4,2,6,1,32,128]{5,2,3,0,4,1:T(8,128)(2,1)S(1)} %get-tuple-element.13, bf16[4,2,6,1,32,128]{5,2,3,0,4,1:T(8,128)(2,1)S(1)} %get-tuple-element.12, bf16[4,2,6,2,32,128]{5,2,3,0,4,1:T(8,128)(2,1)S(1)} %copy.16, bf16[4,2,32,6,2,32]{2,3,4,0,5,1:T(8,128)(2,1)S(1)} %copy.13), kind=kOutput, calls=%fused_computation.12 | convolution fusion | flops 55574528 | bytes 2818048 | tf_op jit(solution)/shard_map/akscfm,akscfn->kfmn/dot_general | solution.py:152
  32.5 0.0 copy-start.1
  32.5 0.3 copy.17
  32.8 0.1 dynamic-slice_bitcast_fusion.2
  32.9 2.0 %collective-permute-start.10 = (bf16[1024,128]{1,0:T(8,128)(2,1)S(1)}, bf16[1024,128]{1,0:T(8,128)(2,1)S(1)}, u32[]{:S(2)}, u32[]{:S(2)}) collective-permute-start(bf16[1024,128]{1,0:T(8,128)(2,1)S(1)} %get-tuple-element.11), channel_id=1, source_target_pairs={{0,4},{1,5},{2,6},{3,7},{4,8},{5,9},{6,10},{7,11},{8,12},{9,13},{1... | collective-permute-start | bytes 786440 | tf_op jit(solution)/shard_map/ppermute | solution.py:164
  34.8 2.2 %collective-permute-start.11 = (bf16[1024,128]{1,0:T(8,128)(2,1)S(1)}, bf16[1024,128]{1,0:T(8,128)(2,1)S(1)}, u32[]{:S(2)}, u32[]{:S(2)}) collective-permute-start(bf16[1024,128]{1,0:T(8,128)(2,1)S(1)} %get-tuple-element.10), channel_id=1, source_target_pairs={{0,12},{1,13},{2,14},{3,15},{4,0},{5,1},{6,2},{7,3},{8,4},{9,5},{1... | collective-permute-start | bytes 786440 | tf_op jit(solution)/shard_map/ppermute | solution.py:164
  37.0 1.8 %collective-permute-start.9 = (bf16[1024,128]{1,0:T(8,128)(2,1)S(1)}, bf16[1024,128]{1,0:T(8,128)(2,1)S(1)}, u32[]{:S(2)}, u32[]{:S(2)}) collective-permute-start(bf16[1024,128]{1,0:T(8,128)(2,1)S(1)} %get-tuple-element.9), channel_id=1, source_target_pairs={{0,8},{1,9},{2,10},{3,11},{4,12},{5,13},{6,14},{7,15},{8,0},{9,1},... | collective-permute-start | bytes 786440 | tf_op jit(solution)/shard_map/ppermute | solution.py:164
  38.8 0.2 fusion.35
  39.0 0.0 copy-done.1
  39.0 0.6 %dynamic_slice.42 = s32[1]{0:T(128)} dynamic-slice(s32[8]{0:T(128)S(1)} %copy-done.1, s32[]{:T(128)S(6)} %select_n.135), dynamic_slice_sizes={1} | dynamic-slice | bytes 12 | tf_op jit(solution)/shard_map/dynamic_slice | solution.py:98
  39.6 0.6 %compare_convert_fusion = f32[2]{0:T(128)S(1)} fusion(s32[]{:T(128)} %bitcast.47), kind=kLoop, calls=%fused_computation.80 | loop fusion | flops 4 | bytes 12 | tf_op jit(solution)/shard_map/convert_element_type | solution.py:174
  40.2 1.1 %collective-permute-done.10 = bf16[1024,128]{1,0:T(8,128)(2,1)S(1)} collective-permute-done((bf16[1024,128]{1,0:T(8,128)(2,1)S(1)}, bf16[1024,128]{1,0:T(8,128)(2,1)S(1)}, u32[]{:S(2)}, u32[]{:S(2)}) %collective-permute-start.10) | collective-permute-done | bytes 262176 | tf_op jit(solution)/shard_map/ppermute | solution.py:164
  41.3 2.5 %collective-permute-done.11 = bf16[1024,128]{1,0:T(8,128)(2,1)S(1)} collective-permute-done((bf16[1024,128]{1,0:T(8,128)(2,1)S(1)}, bf16[1024,128]{1,0:T(8,128)(2,1)S(1)}, u32[]{:S(2)}, u32[]{:S(2)}) %collective-permute-start.11) | collective-permute-done | bytes 262176 | tf_op jit(solution)/shard_map/ppermute | solution.py:164
  43.8 1.8 %collective-permute-done.9 = bf16[1024,128]{1,0:T(8,128)(2,1)S(1)} collective-permute-done((bf16[1024,128]{1,0:T(8,128)(2,1)S(1)}, bf16[1024,128]{1,0:T(8,128)(2,1)S(1)}, u32[]{:S(2)}, u32[]{:S(2)}) %collective-permute-start.9) | collective-permute-done | bytes 262176 | tf_op jit(solution)/shard_map/ppermute | solution.py:164
  45.6 0.1 fusion.21
  45.7 1.1 %fusion.15 = bf16[1,2,8,128,128]{4,3,2,1,0:T(8,128)(2,1)} fusion(bf16[2,32,128,1,1]{2,1,0,4,3:T(8,128)(2,1)S(1)} %bitcast.131, bf16[2,2,32,8,128]{4,3,2,1,0:T(8,128)(2,1)S(1)} %bitcast.127, f32[2]{0:T(128)S(1)} %compare_convert_fusion), kind=kOutput, calls=%fused_computation.14 | convolution fusion | flops 34078720 | bytes 802824 | tf_op jit(solution)/shard_map/kpfrj,pft->krjt/dot_general | solution.py:167
  (17 shorter events, 0.2 us)
Async XLA Ops:
  0.0 10.4 %copy-start = (s32[8,2,2]{0,2,1:T(2,128)S(1)}, s32[8,2,2]{0,2,1:T(2,128)}, u32[]{:S(2)}) copy-start(s32[8,2,2]{0,2,1:T(2,128)} %param.5) | copy-start | bytes 388
  5.2 5.9 %collective-permute-start.2 = (bf16[384,128]{1,0:T(8,128)(2,1)S(1)}, bf16[384,128]{1,0:T(8,128)(2,1)S(1)}, u32[]{:S(2)}, u32[]{:S(2)}) collective-permute-start(bf16[384,128]{1,0:T(8,128)(2,1)S(1)} %bitcast.118), channel_id=1, source_target_pairs={{0,32},{16,48},{32,64},{48,80},{64,96},{80,112},{96,0},{112,16},{1... | collective-permute-start | bytes 294920 | tf_op jit(solution)/shard_map/ppermute | solution.py:87
  6.8 5.3 %collective-permute-start = (bf16[384,128]{1,0:T(8,128)(2,1)S(1)}, bf16[384,128]{1,0:T(8,128)(2,1)S(1)}, u32[]{:S(2)}, u32[]{:S(2)}) collective-permute-start(bf16[384,128]{1,0:T(8,128)(2,1)S(1)} %bitcast.119), channel_id=1, source_target_pairs={{0,96},{16,112},{32,0},{48,16},{64,32},{80,48},{96,64},{112,80},{1... | collective-permute-start | bytes 294920 | tf_op jit(solution)/shard_map/ppermute | solution.py:88
  8.5 6.1 %collective-permute-start.1 = (bf16[384,128]{1,0:T(8,128)(2,1)S(1)}, bf16[384,128]{1,0:T(8,128)(2,1)S(1)}, u32[]{:S(2)}, u32[]{:S(2)}) collective-permute-start(bf16[384,128]{1,0:T(8,128)(2,1)S(1)} %bitcast.120), channel_id=1, source_target_pairs={{0,64},{16,80},{32,96},{48,112},{64,0},{80,16},{96,32},{112,48},{1... | collective-permute-start | bytes 294920 | tf_op jit(solution)/shard_map/ppermute | solution.py:89
  10.4 4.3 %collective-permute-start.3 = (bf16[384,128]{1,0:T(8,128)(2,1)S(1)}, bf16[384,128]{1,0:T(8,128)(2,1)S(1)}, u32[]{:S(2)}, u32[]{:S(2)}) collective-permute-start(bf16[384,128]{1,0:T(8,128)(2,1)S(1)} %bitcast.121), channel_id=1, source_target_pairs={{0,16},{16,0},{32,48},{48,32},{64,80},{80,64},{96,112},{112,96},{1... | collective-permute-start | bytes 294920 | tf_op jit(solution)/shard_map/ppermute | solution.py:86
  12.2 2.5 %collective-permute-start.4 = (bf16[2,384,128]{2,1,0:T(8,128)(2,1)S(1)}, bf16[2,384,128]{2,1,0:T(8,128)(2,1)S(1)}, u32[]{:S(2)}, u32[]{:S(2)}) collective-permute-start(bf16[2,384,128]{2,1,0:T(8,128)(2,1)S(1)} %pad_maximum_fusion.7), channel_id=1, source_target_pairs={{0,16},{16,0},{32,48},{48,32},{64,80},{80,64},{96,112},{112,96},{1... | collective-permute-start | bytes 589832 | tf_op jit(solution)/shard_map/ppermute | solution.py:91
  14.6 1.3 %collective-permute-start.5 = (bf16[384,128]{1,0:T(8,128)(2,1)S(1)}, bf16[384,128]{1,0:T(8,128)(2,1)S(1)}, u32[]{:S(2)}, u32[]{:S(2)}) collective-permute-start(bf16[384,128]{1,0:T(8,128)(2,1)S(1)} %collective-permute-done.1), channel_id=1, source_target_pairs={{0,16},{16,0},{32,48},{48,32},{64,80},{80,64},{96,112},{112,96},{1... | collective-permute-start | bytes 294920 | tf_op jit(solution)/shard_map/ppermute | solution.py:92
  17.3 7.8 %collective-permute-start.6 = (bf16[2,480,128]{2,1,0:T(8,128)(2,1)S(1)}, bf16[2,480,128]{2,1,0:T(8,128)(2,1)S(1)}, u32[]{:S(2)}, u32[]{:S(2)}) collective-permute-start(bf16[2,480,128]{2,1,0:T(8,128)(2,1)S(1)} %get-tuple-element.17), channel_id=1, source_target_pairs={{0,2},{1,3},{2,0},{3,1},{4,6},{5,7},{6,4},{7,5},{8,10},{9,11},{10,... | collective-permute-start | bytes 737288 | tf_op jit(solution)/shard_map/ppermute | solution.py:143
  20.7 7.4 %collective-permute-start.7 = (bf16[2,480,128]{2,1,0:T(8,128)(2,1)S(1)}, bf16[2,480,128]{2,1,0:T(8,128)(2,1)S(1)}, u32[]{:S(2)}, u32[]{:S(2)}) collective-permute-start(bf16[2,480,128]{2,1,0:T(8,128)(2,1)S(1)} %get-tuple-element.18), channel_id=1, source_target_pairs={{0,1},{1,2},{2,3},{3,0},{4,5},{5,6},{6,7},{7,4},{8,9},{9,10},{10,1... | collective-permute-start | bytes 737288 | tf_op jit(solution)/shard_map/ppermute | solution.py:143
  21.3 6.8 %collective-permute-start.8 = (bf16[2,480,128]{2,1,0:T(8,128)(2,1)S(1)}, bf16[2,480,128]{2,1,0:T(8,128)(2,1)S(1)}, u32[]{:S(2)}, u32[]{:S(2)}) collective-permute-start(bf16[2,480,128]{2,1,0:T(8,128)(2,1)S(1)} %get-tuple-element.19), channel_id=1, source_target_pairs={{0,3},{1,0},{2,1},{3,2},{4,7},{5,4},{6,5},{7,6},{8,11},{9,8},{10,9... | collective-permute-start | bytes 737288 | tf_op jit(solution)/shard_map/ppermute | solution.py:143
  32.5 6.5 %copy-start.1 = (s32[8]{0:T(128)S(1)}, s32[8]{0:T(128)}, u32[]{:S(2)}) copy-start(s32[8]{0:T(128)} %param.6) | copy-start | bytes 100
  32.9 8.5 %collective-permute-start.10 = (bf16[1024,128]{1,0:T(8,128)(2,1)S(1)}, bf16[1024,128]{1,0:T(8,128)(2,1)S(1)}, u32[]{:S(2)}, u32[]{:S(2)}) collective-permute-start(bf16[1024,128]{1,0:T(8,128)(2,1)S(1)} %get-tuple-element.11), channel_id=1, source_target_pairs={{0,4},{1,5},{2,6},{3,7},{4,8},{5,9},{6,10},{7,11},{8,12},{9,13},{1... | collective-permute-start | bytes 786440 | tf_op jit(solution)/shard_map/ppermute | solution.py:164
  34.8 8.9 %collective-permute-start.11 = (bf16[1024,128]{1,0:T(8,128)(2,1)S(1)}, bf16[1024,128]{1,0:T(8,128)(2,1)S(1)}, u32[]{:S(2)}, u32[]{:S(2)}) collective-permute-start(bf16[1024,128]{1,0:T(8,128)(2,1)S(1)} %get-tuple-element.10), channel_id=1, source_target_pairs={{0,12},{1,13},{2,14},{3,15},{4,0},{5,1},{6,2},{7,3},{8,4},{9,5},{1... | collective-permute-start | bytes 786440 | tf_op jit(solution)/shard_map/ppermute | solution.py:164
  37.0 8.5 %collective-permute-start.9 = (bf16[1024,128]{1,0:T(8,128)(2,1)S(1)}, bf16[1024,128]{1,0:T(8,128)(2,1)S(1)}, u32[]{:S(2)}, u32[]{:S(2)}) collective-permute-start(bf16[1024,128]{1,0:T(8,128)(2,1)S(1)} %get-tuple-element.9), channel_id=1, source_target_pairs={{0,8},{1,9},{2,10},{3,11},{4,12},{5,13},{6,14},{7,15},{8,0},{9,1},... | collective-permute-start | bytes 786440 | tf_op jit(solution)/shard_map/ppermute | solution.py:164

commit v17 on v16

--- a/solution.py
+++ b/solution.py
@@ -83,10 +83,11 @@
     def chip_shift(d):
         return [(p, 2 * ((p // 2 + d) % chips) + p % 2) for p in range(pairs_count)]
 
+    from_far = lax.ppermute(own, "pairs", chip_shift(2))
     partner = lax.ppermute(own, "pairs", swap)
-    from_below = lax.ppermute(own, "pairs", chip_shift(1))
-    from_above = lax.ppermute(own, "pairs", chip_shift(-1))
-    from_far = lax.ppermute(own, "pairs", chip_shift(2))
+    own_near = own + jnp.zeros((), own.dtype) * partner[:1, :1]
+    from_below = lax.ppermute(own_near, "pairs", chip_shift(1))
+    from_above = lax.ppermute(own_near, "pairs", chip_shift(-1))
     mine = jnp.stack([own, from_above, from_far, from_below])
     theirs_near = lax.ppermute(jnp.stack([from_above, from_below]), "pairs", swap)
     theirs_far = lax.ppermute(from_far, "pairs", swap)

time: 47 us -> 49.3 us (1.049)
  starting transfers between devices: 17.9 us -> 19.7 us
  waiting for transfers between devices: 14.3 us -> 13.3 us
  between operations: 0.33 us -> 0.93 us
  local copies, waits for them, and re-layouts: 5.12 us -> 5.64 us
    ppermute x1, waiting for transfers between devices: 2.33 us -> 0.01 us  [shards(): from_far = lax.ppermute(own, 'pairs', chip_shift(2))]
    ppermute x2, waiting for transfers between devices: 1.18 us -> 2.82 us  [the longest x1 2.82 us: shards(): from_below = lax.ppermute(own_near, 'pairs', chip_shift(1))]
    ppermute x1, starting transfers between devices: 1.89 us -> 3.18 us  [shards(): from_far = lax.ppermute(own, 'pairs', chip_shift(2))]
    ppermute x1, waiting for transfers between devices: 1.2 us -> 0.12 us  [shards(): theirs_far = lax.ppermute(from_far, 'pairs', swap)]
    ppermute x1, waiting for transfers between devices: 0.01 us -> 0.79 us  [shards(): lax.ppermute(jnp.stack([from_above, from_below]), 'pairs', swap)]
    ppermute x1, starting transfers between devices: 0.01 us -> 0.56 us  [shards(): theirs_far = lax.ppermute(from_far, 'pairs', swap)]
    slice x0 -> x1, local copies, waits for them, and re-layouts: none -> 0.52 us  [shards(): own_near = own + jnp.zeros((), own.dtype) * partner[:1, :1]]
  transfers between devices with their start and end apart: 12 -> 12, of which waited for: 10 -> 9; matrix products, arithmetic and copies ran while one was open for 4% -> 5% of each run, Pallas kernels for 0% -> 0%
where the time goes in v17:
time: 49.3 us; the launch traced here: 48.9 us
  starting transfers between devices  19.7 us (40%)
  waiting for transfers between devices  13.3 us (27%)
  matrix products  7.46 us (15%)
  local copies, waits for them, and re-layouts  5.64 us (11%)
  other arithmetic  1.84 us (4%)
  between operations  0.93 us (2%)
    ppermute x3, starting transfers between devices, shards(): pieces.append(lax.ppermute(message, axes, gather_perm(d)))  6.51 us
    ppermute x3, starting transfers between devices, shards(): lax.ppermute(chunk, axes, reduce_perm(e)).astype(jnp.float32)  5.97 us
    ppermute x3, waiting for transfers between devices, shards(): lax.ppermute(chunk, axes, reduce_perm(e)).astype(jnp.float32)  5.32 us
    dot_general x1, matrix products, shards(): jnp.dot(records[0], band_table(), preferred_element_type=jnp.float32)  5 us
    ppermute x3, waiting for transfers between devices, shards(): pieces.append(lax.ppermute(message, axes, gather_perm(d)))  4.23 us
    ppermute x1, starting transfers between devices, shards(): from_far = lax.ppermute(own, 'pairs', chip_shift(2))  3.18 us
    ppermute x1, waiting for transfers between devices, shards(): from_below = lax.ppermute(own_near, 'pairs', chip_shift(1))  2.82 us
    ppermute x1, starting transfers between devices, shards(): from_above = lax.ppermute(own_near, 'pairs', chip_shift(-1))  2.64 us
  transfers between devices with their start and end apart: 12, of which 9 were waited for; matrix products, arithmetic and copies ran while one was open for 5% of the time, Pallas kernels for 0%

profile of v17, /device:TPU:0, one launch (start us, length us, event | category | flops | bytes accessed | tf_op | source)
XLA Modules:
  0.0 48.9 jit_solution(15800547823476285820)
XLA Ops:
  0.0 0.0 copy-start
  0.0 5.0 %fusion.16 = f32[6,128,64]{1,2,0:T(8,128)S(1)} fusion(bf16[4096,64,1]{0,1,2:T(8,128)(2,1)} %constant.178, bf16[1,6,128,4096]{3,2,1,0:T(8,128)(2,1)} %param.4), kind=kOutput, calls=%fused_computation.15 | convolution fusion | flops 402653184 | bytes 7012352 | tf_op jit(solution)/shard_map/dot_general | solution.py:70
  5.1 0.1 multiply_convert_fusion.1
  5.2 0.1 collective-permute-start
  5.3 3.2 %collective-permute-start.2 = (bf16[384,128]{1,0:T(8,128)(2,1)S(1)}, bf16[384,128]{1,0:T(8,128)(2,1)S(1)}, u32[]{:S(2)}, u32[]{:S(2)}) collective-permute-start(bf16[384,128]{1,0:T(8,128)(2,1)S(1)} %bitcast.120), channel_id=1, source_target_pairs={{0,64},{16,80},{32,96},{48,112},{64,0},{80,16},{96,32},{112,48},{1... | collective-permute-start | bytes 294920 | tf_op jit(solution)/shard_map/ppermute | solution.py:86
  8.4 0.0 copy-done
  8.4 0.2 fusion.36
  8.7 0.1 copy.8
  8.8 0.1 reshape.93
  8.9 0.1 reshape.91
  9.0 0.0 collective-permute-done
  9.0 0.5 %slice.65 = bf16[1,1]{1,0:T(2,128)(2,1)} slice(bf16[384,128]{1,0:T(8,128)(2,1)S(1)} %collective-permute-done), slice={[0:1], [0:1]} | slice | bytes 4 | tf_op jit(solution)/shard_map/slice | solution.py:88
  10.2 0.7 %collective-permute-start.3 = (bf16[384,128]{1,0:T(8,128)(2,1)S(1)}, bf16[384,128]{1,0:T(8,128)(2,1)S(1)}, u32[]{:S(2)}, u32[]{:S(2)}) collective-permute-start(bf16[384,128]{1,0:T(8,128)(2,1)S(1)} %broadcast_add_fusion), channel_id=1, source_target_pairs={{0,32},{16,48},{32,64},{48,80},{64,96},{80,112},{96,0},{112,16},{1... | collective-permute-start | bytes 294920 | tf_op jit(solution)/shard_map/ppermute | solution.py:89
  10.8 2.6 %collective-permute-start.1 = (bf16[384,128]{1,0:T(8,128)(2,1)S(1)}, bf16[384,128]{1,0:T(8,128)(2,1)S(1)}, u32[]{:S(2)}, u32[]{:S(2)}) collective-permute-start(bf16[384,128]{1,0:T(8,128)(2,1)S(1)} %broadcast_add_fusion), channel_id=1, source_target_pairs={{0,96},{16,112},{32,0},{48,16},{64,32},{80,48},{96,64},{112,80},{1... | collective-permute-start | bytes 294920 | tf_op jit(solution)/shard_map/ppermute | solution.py:90
  13.5 2.8 %collective-permute-done.3 = bf16[384,128]{1,0:T(8,128)(2,1)S(1)} collective-permute-done((bf16[384,128]{1,0:T(8,128)(2,1)S(1)}, bf16[384,128]{1,0:T(8,128)(2,1)S(1)}, u32[]{:S(2)}, u32[]{:S(2)}) %collective-permute-start.3) | collective-permute-done | bytes 98336 | tf_op jit(solution)/shard_map/ppermute | solution.py:89
  16.3 0.0 collective-permute-done.1
  16.3 0.1 collective-permute-start.4
  16.4 0.0 collective-permute-done.2
  16.4 0.6 %collective-permute-start.5 = (bf16[384,128]{1,0:T(8,128)(2,1)S(1)}, bf16[384,128]{1,0:T(8,128)(2,1)S(1)}, u32[]{:S(2)}, u32[]{:S(2)}) collective-permute-start(bf16[384,128]{1,0:T(8,128)(2,1)S(1)} %collective-permute-done.2), channel_id=1, source_target_pairs={{0,16},{16,0},{32,48},{48,32},{64,80},{80,64},{96,112},{112,96},{1... | collective-permute-start | bytes 294920 | tf_op jit(solution)/shard_map/ppermute | solution.py:93
  17.0 0.1 maximum_bitcast_fusion
  17.1 0.8 %collective-permute-done.4 = bf16[2,384,128]{2,1,0:T(8,128)(2,1)S(1)} collective-permute-done((bf16[2,384,128]{2,1,0:T(8,128)(2,1)S(1)}, bf16[2,384,128]{2,1,0:T(8,128)(2,1)S(1)}, u32[]{:S(2)}, u32[]{:S(2)}) %collective-permute-start.4) | collective-permute-done | bytes 196640 | tf_op jit(solution)/shard_map/ppermute | solution.py:92
  17.9 0.1 collective-permute-done.5
  18.0 0.1 maximum_bitcast_fusion.1
  18.0 0.1 maximum_select_fusion
  18.1 0.6 %gather_fusion = bf16[4,384,128]{2,1,0:T(8,128)(2,1)S(1)} fusion(bf16[8,384,128]{2,1,0:T(8,128)(2,1)S(1)} %bitcast.112, s32[1024]{0:T(1024)S(1)} %pad_clamp_fusion), kind=kCustom, calls=%fused_computation | custom fusion | bytes 786448 | tf_op jit(solution)/shard_map/jit(_take)/gather | solution.py:101
  18.8 0.1 broadcast_select_fusion
  18.9 0.2 copy.10
  19.1 0.1 reshape.113
  19.3 0.1 maximum_bitcast_fusion.2
  19.4 3.3 %collective-permute-start.6 = (bf16[2,480,128]{2,1,0:T(8,128)(2,1)S(1)}, bf16[2,480,128]{2,1,0:T(8,128)(2,1)S(1)}, u32[]{:S(2)}, u32[]{:S(2)}) collective-permute-start(bf16[2,480,128]{2,1,0:T(8,128)(2,1)S(1)} %get-tuple-element.17), channel_id=1, source_target_pairs={{0,2},{1,3},{2,0},{3,1},{4,6},{5,7},{6,4},{7,5},{8,10},{9,11},{10,... | collective-permute-start | bytes 737288 | tf_op jit(solution)/shard_map/ppermute | solution.py:144
  22.7 0.7 %collective-permute-start.7 = (bf16[2,480,128]{2,1,0:T(8,128)(2,1)S(1)}, bf16[2,480,128]{2,1,0:T(8,128)(2,1)S(1)}, u32[]{:S(2)}, u32[]{:S(2)}) collective-permute-start(bf16[2,480,128]{2,1,0:T(8,128)(2,1)S(1)} %get-tuple-element.18), channel_id=1, source_target_pairs={{0,1},{1,2},{2,3},{3,0},{4,5},{5,6},{6,7},{7,4},{8,9},{9,10},{10,1... | collective-permute-start | bytes 737288 | tf_op jit(solution)/shard_map/ppermute | solution.py:144
  23.3 2.6 %collective-permute-start.8 = (bf16[2,480,128]{2,1,0:T(8,128)(2,1)S(1)}, bf16[2,480,128]{2,1,0:T(8,128)(2,1)S(1)}, u32[]{:S(2)}, u32[]{:S(2)}) collective-permute-start(bf16[2,480,128]{2,1,0:T(8,128)(2,1)S(1)} %get-tuple-element.19), channel_id=1, source_target_pairs={{0,3},{1,0},{2,1},{3,2},{4,7},{5,4},{6,5},{7,6},{8,11},{9,8},{10,9... | collective-permute-start | bytes 737288 | tf_op jit(solution)/shard_map/ppermute | solution.py:144
  25.9 1.3 %collective-permute-done.6 = bf16[2,480,128]{2,1,0:T(8,128)(2,1)S(1)} collective-permute-done((bf16[2,480,128]{2,1,0:T(8,128)(2,1)S(1)}, bf16[2,480,128]{2,1,0:T(8,128)(2,1)S(1)}, u32[]{:S(2)}, u32[]{:S(2)}) %collective-permute-start.6) | collective-permute-done | bytes 245792 | tf_op jit(solution)/shard_map/ppermute | solution.py:144
  27.2 2.9 %collective-permute-done.7 = bf16[2,480,128]{2,1,0:T(8,128)(2,1)S(1)} collective-permute-done((bf16[2,480,128]{2,1,0:T(8,128)(2,1)S(1)}, bf16[2,480,128]{2,1,0:T(8,128)(2,1)S(1)}, u32[]{:S(2)}, u32[]{:S(2)}) %collective-permute-start.7) | collective-permute-done | bytes 245792 | tf_op jit(solution)/shard_map/ppermute | solution.py:144
  30.1 0.1 collective-permute-done.8
  30.2 0.1 pad_maximum_fusion
  30.2 0.3 reshape.96
  30.6 1.9 %copy.13 = bf16[4,2,32,6,2,32]{2,3,4,0,5,1:T(8,128)(2,1)S(1)} copy(bf16[4,2,32,6,2,32]{5,4,3,2,1,0:T(2,128)(2,1)S(1)} %reshape.96) | data formatting | bytes 393216 | tf_op jit(solution)/shard_map/reshape | solution.py:149
  32.5 0.5 %copy.16 = bf16[4,2,6,2,32,128]{5,2,3,0,4,1:T(8,128)(2,1)S(1)} copy(bf16[4,2,6,2,32,128]{5,4,3,2,1,0:T(8,128)(2,1)S(1)} %bitcast.111) | data formatting | bytes 1572864 | tf_op jit(solution)/shard_map/reshape | solution.py:146
  33.0 0.2 fusion.45
  33.2 1.3 %fusion.11 = bf16[2,32,4,8,2,128]{5,3,4,2,1,0:T(8,128)(2,1)S(1)} fusion(bf16[4,2,6,1,32,128]{5,2,3,0,4,1:T(8,128)(2,1)S(1)} %get-tuple-element.13, bf16[4,2,6,1,32,128]{5,2,3,0,4,1:T(8,128)(2,1)S(1)} %get-tuple-element.12, bf16[4,2,6,2,32,128]{5,2,3,0,4,1:T(8,128)(2,1)S(1)} %copy.16, bf16[4,2,32,6,2,32]{2,3,4,0,5,1:T(8,128)(2,1)S(1)} %copy.13), kind=kOutput, calls=%fused_computation.12 | convolution fusion | flops 55574528 | bytes 2818048 | tf_op jit(solution)/shard_map/akscfm,akscfn->kfmn/dot_general | solution.py:153
  34.5 0.0 copy-start.1
  34.5 0.3 copy.17
  34.8 0.1 dynamic-slice_bitcast_fusion.2
  34.9 2.0 %collective-permute-start.10 = (bf16[1024,128]{1,0:T(8,128)(2,1)S(1)}, bf16[1024,128]{1,0:T(8,128)(2,1)S(1)}, u32[]{:S(2)}, u32[]{:S(2)}) collective-permute-start(bf16[1024,128]{1,0:T(8,128)(2,1)S(1)} %get-tuple-element.11), channel_id=1, source_target_pairs={{0,4},{1,5},{2,6},{3,7},{4,8},{5,9},{6,10},{7,11},{8,12},{9,13},{1... | collective-permute-start | bytes 786440 | tf_op jit(solution)/shard_map/ppermute | solution.py:165
  36.8 2.2 %collective-permute-start.11 = (bf16[1024,128]{1,0:T(8,128)(2,1)S(1)}, bf16[1024,128]{1,0:T(8,128)(2,1)S(1)}, u32[]{:S(2)}, u32[]{:S(2)}) collective-permute-start(bf16[1024,128]{1,0:T(8,128)(2,1)S(1)} %get-tuple-element.10), channel_id=1, source_target_pairs={{0,12},{1,13},{2,14},{3,15},{4,0},{5,1},{6,2},{7,3},{8,4},{9,5},{1... | collective-permute-start | bytes 786440 | tf_op jit(solution)/shard_map/ppermute | solution.py:165
  39.0 1.8 %collective-permute-start.9 = (bf16[1024,128]{1,0:T(8,128)(2,1)S(1)}, bf16[1024,128]{1,0:T(8,128)(2,1)S(1)}, u32[]{:S(2)}, u32[]{:S(2)}) collective-permute-start(bf16[1024,128]{1,0:T(8,128)(2,1)S(1)} %get-tuple-element.9), channel_id=1, source_target_pairs={{0,8},{1,9},{2,10},{3,11},{4,12},{5,13},{6,14},{7,15},{8,0},{9,1},... | collective-permute-start | bytes 786440 | tf_op jit(solution)/shard_map/ppermute | solution.py:165
  40.8 0.2 fusion.35
  41.0 0.0 copy-done.1
  41.0 0.6 %dynamic_slice.42 = s32[1]{0:T(128)} dynamic-slice(s32[8]{0:T(128)S(1)} %copy-done.1, s32[]{:T(128)S(6)} %select_n.135), dynamic_slice_sizes={1} | dynamic-slice | bytes 12 | tf_op jit(solution)/shard_map/dynamic_slice | solution.py:99
  41.6 0.6 %compare_convert_fusion = f32[2]{0:T(128)S(1)} fusion(s32[]{:T(128)} %bitcast.48), kind=kLoop, calls=%fused_computation.81 | loop fusion | flops 4 | bytes 12 | tf_op jit(solution)/shard_map/convert_element_type | solution.py:175
  42.3 1.1 %collective-permute-done.10 = bf16[1024,128]{1,0:T(8,128)(2,1)S(1)} collective-permute-done((bf16[1024,128]{1,0:T(8,128)(2,1)S(1)}, bf16[1024,128]{1,0:T(8,128)(2,1)S(1)}, u32[]{:S(2)}, u32[]{:S(2)}) %collective-permute-start.10) | collective-permute-done | bytes 262176 | tf_op jit(solution)/shard_map/ppermute | solution.py:165
  43.3 2.5 %collective-permute-done.11 = bf16[1024,128]{1,0:T(8,128)(2,1)S(1)} collective-permute-done((bf16[1024,128]{1,0:T(8,128)(2,1)S(1)}, bf16[1024,128]{1,0:T(8,128)(2,1)S(1)}, u32[]{:S(2)}, u32[]{:S(2)}) %collective-permute-start.11) | collective-permute-done | bytes 262176 | tf_op jit(solution)/shard_map/ppermute | solution.py:165
  45.8 1.8 %collective-permute-done.9 = bf16[1024,128]{1,0:T(8,128)(2,1)S(1)} collective-permute-done((bf16[1024,128]{1,0:T(8,128)(2,1)S(1)}, bf16[1024,128]{1,0:T(8,128)(2,1)S(1)}, u32[]{:S(2)}, u32[]{:S(2)}) %collective-permute-start.9) | collective-permute-done | bytes 262176 | tf_op jit(solution)/shard_map/ppermute | solution.py:165
  47.6 0.1 fusion.21
  47.7 1.1 %fusion.15 = bf16[1,2,8,128,128]{4,3,2,1,0:T(8,128)(2,1)} fusion(bf16[2,32,128,1,1]{2,1,0,4,3:T(8,128)(2,1)S(1)} %bitcast.131, bf16[2,2,32,8,128]{4,3,2,1,0:T(8,128)(2,1)S(1)} %bitcast.127, f32[2]{0:T(128)S(1)} %compare_convert_fusion), kind=kOutput, calls=%fused_computation.14 | convolution fusion | flops 34078720 | bytes 802824 | tf_op jit(solution)/shard_map/kpfrj,pft->krjt/dot_general | solution.py:168
  (18 shorter events, 0.3 us)
Async XLA Ops:
  0.0 8.4 %copy-start = (s32[8,2,2]{0,2,1:T(2,128)S(1)}, s32[8,2,2]{0,2,1:T(2,128)}, u32[]{:S(2)}) copy-start(s32[8,2,2]{0,2,1:T(2,128)} %param.5) | copy-start | bytes 388
  5.2 3.8 %collective-permute-start = (bf16[384,128]{1,0:T(8,128)(2,1)S(1)}, bf16[384,128]{1,0:T(8,128)(2,1)S(1)}, u32[]{:S(2)}, u32[]{:S(2)}) collective-permute-start(bf16[384,128]{1,0:T(8,128)(2,1)S(1)} %bitcast.119), channel_id=1, source_target_pairs={{0,16},{16,0},{32,48},{48,32},{64,80},{80,64},{96,112},{112,96},{1... | collective-permute-start | bytes 294920 | tf_op jit(solution)/shard_map/ppermute | solution.py:87
  5.3 11.2 %collective-permute-start.2 = (bf16[384,128]{1,0:T(8,128)(2,1)S(1)}, bf16[384,128]{1,0:T(8,128)(2,1)S(1)}, u32[]{:S(2)}, u32[]{:S(2)}) collective-permute-start(bf16[384,128]{1,0:T(8,128)(2,1)S(1)} %bitcast.120), channel_id=1, source_target_pairs={{0,64},{16,80},{32,96},{48,112},{64,0},{80,16},{96,32},{112,48},{1... | collective-permute-start | bytes 294920 | tf_op jit(solution)/shard_map/ppermute | solution.py:86
  10.2 6.1 %collective-permute-start.3 = (bf16[384,128]{1,0:T(8,128)(2,1)S(1)}, bf16[384,128]{1,0:T(8,128)(2,1)S(1)}, u32[]{:S(2)}, u32[]{:S(2)}) collective-permute-start(bf16[384,128]{1,0:T(8,128)(2,1)S(1)} %broadcast_add_fusion), channel_id=1, source_target_pairs={{0,32},{16,48},{32,64},{48,80},{64,96},{80,112},{96,0},{112,16},{1... | collective-permute-start | bytes 294920 | tf_op jit(solution)/shard_map/ppermute | solution.py:89
  10.8 5.5 %collective-permute-start.1 = (bf16[384,128]{1,0:T(8,128)(2,1)S(1)}, bf16[384,128]{1,0:T(8,128)(2,1)S(1)}, u32[]{:S(2)}, u32[]{:S(2)}) collective-permute-start(bf16[384,128]{1,0:T(8,128)(2,1)S(1)} %broadcast_add_fusion), channel_id=1, source_target_pairs={{0,96},{16,112},{32,0},{48,16},{64,32},{80,48},{96,64},{112,80},{1... | collective-permute-start | bytes 294920 | tf_op jit(solution)/shard_map/ppermute | solution.py:90
  16.3 1.5 %collective-permute-start.4 = (bf16[2,384,128]{2,1,0:T(8,128)(2,1)S(1)}, bf16[2,384,128]{2,1,0:T(8,128)(2,1)S(1)}, u32[]{:S(2)}, u32[]{:S(2)}) collective-permute-start(bf16[2,384,128]{2,1,0:T(8,128)(2,1)S(1)} %pad_maximum_fusion.7), channel_id=1, source_target_pairs={{0,16},{16,0},{32,48},{48,32},{64,80},{80,64},{96,112},{112,96},{1... | collective-permute-start | bytes 589832 | tf_op jit(solution)/shard_map/ppermute | solution.py:92
  16.4 1.5 %collective-permute-start.5 = (bf16[384,128]{1,0:T(8,128)(2,1)S(1)}, bf16[384,128]{1,0:T(8,128)(2,1)S(1)}, u32[]{:S(2)}, u32[]{:S(2)}) collective-permute-start(bf16[384,128]{1,0:T(8,128)(2,1)S(1)} %collective-permute-done.2), channel_id=1, source_target_pairs={{0,16},{16,0},{32,48},{48,32},{64,80},{80,64},{96,112},{112,96},{1... | collective-permute-start | bytes 294920 | tf_op jit(solution)/shard_map/ppermute | solution.py:93
  19.4 7.8 %collective-permute-start.6 = (bf16[2,480,128]{2,1,0:T(8,128)(2,1)S(1)}, bf16[2,480,128]{2,1,0:T(8,128)(2,1)S(1)}, u32[]{:S(2)}, u32[]{:S(2)}) collective-permute-start(bf16[2,480,128]{2,1,0:T(8,128)(2,1)S(1)} %get-tuple-element.17), channel_id=1, source_target_pairs={{0,2},{1,3},{2,0},{3,1},{4,6},{5,7},{6,4},{7,5},{8,10},{9,11},{10,... | collective-permute-start | bytes 737288 | tf_op jit(solution)/shard_map/ppermute | solution.py:144
  22.7 7.4 %collective-permute-start.7 = (bf16[2,480,128]{2,1,0:T(8,128)(2,1)S(1)}, bf16[2,480,128]{2,1,0:T(8,128)(2,1)S(1)}, u32[]{:S(2)}, u32[]{:S(2)}) collective-permute-start(bf16[2,480,128]{2,1,0:T(8,128)(2,1)S(1)} %get-tuple-element.18), channel_id=1, source_target_pairs={{0,1},{1,2},{2,3},{3,0},{4,5},{5,6},{6,7},{7,4},{8,9},{9,10},{10,1... | collective-permute-start | bytes 737288 | tf_op jit(solution)/shard_map/ppermute | solution.py:144
  23.3 6.8 %collective-permute-start.8 = (bf16[2,480,128]{2,1,0:T(8,128)(2,1)S(1)}, bf16[2,480,128]{2,1,0:T(8,128)(2,1)S(1)}, u32[]{:S(2)}, u32[]{:S(2)}) collective-permute-start(bf16[2,480,128]{2,1,0:T(8,128)(2,1)S(1)} %get-tuple-element.19), channel_id=1, source_target_pairs={{0,3},{1,0},{2,1},{3,2},{4,7},{5,4},{6,5},{7,6},{8,11},{9,8},{10,9... | collective-permute-start | bytes 737288 | tf_op jit(solution)/shard_map/ppermute | solution.py:144
  34.5 6.5 %copy-start.1 = (s32[8]{0:T(128)S(1)}, s32[8]{0:T(128)}, u32[]{:S(2)}) copy-start(s32[8]{0:T(128)} %param.6) | copy-start | bytes 100
  34.9 8.5 %collective-permute-start.10 = (bf16[1024,128]{1,0:T(8,128)(2,1)S(1)}, bf16[1024,128]{1,0:T(8,128)(2,1)S(1)}, u32[]{:S(2)}, u32[]{:S(2)}) collective-permute-start(bf16[1024,128]{1,0:T(8,128)(2,1)S(1)} %get-tuple-element.11), channel_id=1, source_target_pairs={{0,4},{1,5},{2,6},{3,7},{4,8},{5,9},{6,10},{7,11},{8,12},{9,13},{1... | collective-permute-start | bytes 786440 | tf_op jit(solution)/shard_map/ppermute | solution.py:165
  36.8 8.9 %collective-permute-start.11 = (bf16[1024,128]{1,0:T(8,128)(2,1)S(1)}, bf16[1024,128]{1,0:T(8,128)(2,1)S(1)}, u32[]{:S(2)}, u32[]{:S(2)}) collective-permute-start(bf16[1024,128]{1,0:T(8,128)(2,1)S(1)} %get-tuple-element.10), channel_id=1, source_target_pairs={{0,12},{1,13},{2,14},{3,15},{4,0},{5,1},{6,2},{7,3},{8,4},{9,5},{1... | collective-permute-start | bytes 786440 | tf_op jit(solution)/shard_map/ppermute | solution.py:165
  39.0 8.5 %collective-permute-start.9 = (bf16[1024,128]{1,0:T(8,128)(2,1)S(1)}, bf16[1024,128]{1,0:T(8,128)(2,1)S(1)}, u32[]{:S(2)}, u32[]{:S(2)}) collective-permute-start(bf16[1024,128]{1,0:T(8,128)(2,1)S(1)} %get-tuple-element.9), channel_id=1, source_target_pairs={{0,8},{1,9},{2,10},{3,11},{4,12},{5,13},{6,14},{7,15},{8,0},{9,1},... | collective-permute-start | bytes 786440 | tf_op jit(solution)/shard_map/ppermute | solution.py:165

commit v18 on v16

--- a/solution.py
+++ b/solution.py
@@ -97,7 +97,7 @@
     own_pairs = lax.dynamic_index_in_dim(pair_list, owner_index, 0, keepdims=False)
     live_slots = jnp.arange(slot_count, dtype=jnp.int32) < pair_count[owner_index]
     position = ((own_pairs // 2 - chip) % chips) * 2 + own_pairs % 2
-    chosen = jnp.take(table, position.T.reshape(-1), axis=0)
+    chosen = jnp.take(table, position.T.reshape(-1), axis=0, mode="clip")
     left = chosen[:slot_count]
     right = chosen[slot_count:]
     left_t = jnp.transpose(left, (0, 2, 1)).reshape((slot_count, side, side, rows, spec_rows))

time: 47 us -> 48.3 us (1.028)
  waiting for transfers between devices: 14.3 us -> 15.3 us
    ppermute x1, waiting for transfers between devices: 0.11 us -> 4.79 us  [shards(): from_below = lax.ppermute(own, 'pairs', chip_shift(1))]
    ppermute x1, waiting for transfers between devices: 2.33 us -> 0.01 us  [shards(): from_far = lax.ppermute(own, 'pairs', chip_shift(2))]
    ppermute x1, starting transfers between devices: 1.64 us -> 0.01 us  [shards(): from_below = lax.ppermute(own, 'pairs', chip_shift(1))]
    ppermute x1, starting transfers between devices: 1.66 us -> 2.91 us  [shards(): from_above = lax.ppermute(own, 'pairs', chip_shift(-1))]
    ppermute x1, waiting for transfers between devices: 1.2 us -> 0.11 us  [shards(): theirs_far = lax.ppermute(from_far, 'pairs', swap)]
    ppermute x1, waiting for transfers between devices: 1.07 us -> 0.01 us  [shards(): from_above = lax.ppermute(own, 'pairs', chip_shift(-1))]
    ppermute x1, waiting for transfers between devices: 0.01 us -> 0.79 us  [shards(): lax.ppermute(jnp.stack([from_above, from_below]), 'pairs', swap)]
    ppermute x1, starting transfers between devices: 0.01 us -> 0.56 us  [shards(): theirs_far = lax.ppermute(from_far, 'pairs', swap)]
  transfers between devices with their start and end apart: 12 -> 12, of which waited for: 10 -> 9; matrix products, arithmetic and copies ran while one was open for 4% -> 4% of each run, Pallas kernels for 0% -> 0%
where the time goes in v18:
time: 48.3 us; the launch traced here: 48.1 us
  starting transfers between devices  18.3 us (38%)
  waiting for transfers between devices  15.3 us (32%)
  matrix products  7.46 us (15%)
  local copies, waits for them, and re-layouts  5.04 us (10%)
  other arithmetic  1.7 us (4%)
    ppermute x3, starting transfers between devices, shards(): pieces.append(lax.ppermute(message, axes, gather_perm(d)))  6.51 us
    ppermute x3, starting transfers between devices, shards(): lax.ppermute(chunk, axes, reduce_perm(e)).astype(jnp.float32)  5.98 us
    ppermute x3, waiting for transfers between devices, shards(): lax.ppermute(chunk, axes, reduce_perm(e)).astype(jnp.float32)  5.32 us
    dot_general x1, matrix products, shards(): jnp.dot(records[0], band_table(), preferred_element_type=jnp.float32)  5 us
    ppermute x1, waiting for transfers between devices, shards(): from_below = lax.ppermute(own, 'pairs', chip_shift(1))  4.79 us
    ppermute x3, waiting for transfers between devices, shards(): pieces.append(lax.ppermute(message, axes, gather_perm(d)))  4.23 us
    ppermute x1, starting transfers between devices, shards(): from_above = lax.ppermute(own, 'pairs', chip_shift(-1))  2.91 us
    ppermute x1, starting transfers between devices, shards(): from_far = lax.ppermute(own, 'pairs', chip_shift(2))  2.29 us
  transfers between devices with their start and end apart: 12, of which 9 were waited for; matrix products, arithmetic and copies ran while one was open for 4% of the time, Pallas kernels for 0%

profile of v18, /device:TPU:0, one launch (start us, length us, event | category | flops | bytes accessed | tf_op | source)
XLA Modules:
  0.0 48.1 jit_solution(12969992194634473050)
XLA Ops:
  0.0 0.0 copy-start
  0.0 5.0 %fusion.16 = f32[6,128,64]{1,2,0:T(8,128)S(1)} fusion(bf16[4096,64,1]{0,1,2:T(8,128)(2,1)} %constant.162, bf16[1,6,128,4096]{3,2,1,0:T(8,128)(2,1)} %param.4), kind=kOutput, calls=%fused_computation.15 | convolution fusion | flops 402653184 | bytes 7012352 | tf_op jit(solution)/shard_map/dot_general | solution.py:70
  5.1 0.1 multiply_convert_fusion.1
  5.2 2.9 %collective-permute-start = (bf16[384,128]{1,0:T(8,128)(2,1)S(1)}, bf16[384,128]{1,0:T(8,128)(2,1)S(1)}, u32[]{:S(2)}, u32[]{:S(2)}) collective-permute-start(bf16[384,128]{1,0:T(8,128)(2,1)S(1)} %bitcast.116), channel_id=1, source_target_pairs={{0,96},{16,112},{32,0},{48,16},{64,32},{80,48},{96,64},{112,80},{1... | collective-permute-start | bytes 294920 | tf_op jit(solution)/shard_map/ppermute | solution.py:88
  8.1 0.0 collective-permute-start.2
  8.1 2.3 %collective-permute-start.1 = (bf16[384,128]{1,0:T(8,128)(2,1)S(1)}, bf16[384,128]{1,0:T(8,128)(2,1)S(1)}, u32[]{:S(2)}, u32[]{:S(2)}) collective-permute-start(bf16[384,128]{1,0:T(8,128)(2,1)S(1)} %bitcast.118), channel_id=1, source_target_pairs={{0,64},{16,80},{32,96},{48,112},{64,0},{80,16},{96,32},{112,48},{1... | collective-permute-start | bytes 294920 | tf_op jit(solution)/shard_map/ppermute | solution.py:89
  10.4 0.0 collective-permute-start.3
  10.4 0.0 copy-done
  10.4 0.2 fusion.36
  10.7 0.1 copy.8
  10.8 0.1 reshape.64
  10.9 0.0 collective-permute-done
  10.9 4.8 %collective-permute-done.2 = bf16[384,128]{1,0:T(8,128)(2,1)S(1)} collective-permute-done((bf16[384,128]{1,0:T(8,128)(2,1)S(1)}, bf16[384,128]{1,0:T(8,128)(2,1)S(1)}, u32[]{:S(2)}, u32[]{:S(2)}) %collective-permute-start.2) | collective-permute-done | bytes 98336 | tf_op jit(solution)/shard_map/ppermute | solution.py:87
  15.7 0.1 collective-permute-start.4
  15.8 0.0 collective-permute-done.1
  15.8 0.6 %collective-permute-start.5 = (bf16[384,128]{1,0:T(8,128)(2,1)S(1)}, bf16[384,128]{1,0:T(8,128)(2,1)S(1)}, u32[]{:S(2)}, u32[]{:S(2)}) collective-permute-start(bf16[384,128]{1,0:T(8,128)(2,1)S(1)} %collective-permute-done.1), channel_id=1, source_target_pairs={{0,16},{16,0},{32,48},{48,32},{64,80},{80,64},{96,112},{112,96},{1... | collective-permute-start | bytes 294920 | tf_op jit(solution)/shard_map/ppermute | solution.py:92
  16.4 0.1 maximum_bitcast_fusion
  16.4 0.8 %collective-permute-done.4 = bf16[2,384,128]{2,1,0:T(8,128)(2,1)S(1)} collective-permute-done((bf16[2,384,128]{2,1,0:T(8,128)(2,1)S(1)}, bf16[2,384,128]{2,1,0:T(8,128)(2,1)S(1)}, u32[]{:S(2)}, u32[]{:S(2)}) %collective-permute-start.4) | collective-permute-done | bytes 196640 | tf_op jit(solution)/shard_map/ppermute | solution.py:91
  17.2 0.0 collective-permute-done.3
  17.2 0.1 collective-permute-done.5
  17.3 0.1 maximum_bitcast_fusion.1
  17.4 0.1 maximum_select_fusion
  17.5 0.6 %gather_fusion = bf16[4,384,128]{2,1,0:T(8,128)(2,1)S(1)} fusion(bf16[8,384,128]{2,1,0:T(8,128)(2,1)S(1)} %bitcast.108, s32[1024]{0:T(1024)S(1)} %pad_clamp_fusion), kind=kCustom, calls=%fused_computation | custom fusion | bytes 786448 | tf_op jit(solution)/shard_map/jit(_take)/gather | solution.py:100
  18.1 0.2 copy.9
  18.4 0.1 reshape.56
  18.5 0.1 maximum_bitcast_fusion.2
  18.6 3.3 %collective-permute-start.6 = (bf16[2,480,128]{2,1,0:T(8,128)(2,1)S(1)}, bf16[2,480,128]{2,1,0:T(8,128)(2,1)S(1)}, u32[]{:S(2)}, u32[]{:S(2)}) collective-permute-start(bf16[2,480,128]{2,1,0:T(8,128)(2,1)S(1)} %get-tuple-element.17), channel_id=1, source_target_pairs={{0,2},{1,3},{2,0},{3,1},{4,6},{5,7},{6,4},{7,5},{8,10},{9,11},{10,... | collective-permute-start | bytes 737288 | tf_op jit(solution)/shard_map/ppermute | solution.py:143
  21.9 0.7 %collective-permute-start.7 = (bf16[2,480,128]{2,1,0:T(8,128)(2,1)S(1)}, bf16[2,480,128]{2,1,0:T(8,128)(2,1)S(1)}, u32[]{:S(2)}, u32[]{:S(2)}) collective-permute-start(bf16[2,480,128]{2,1,0:T(8,128)(2,1)S(1)} %get-tuple-element.18), channel_id=1, source_target_pairs={{0,1},{1,2},{2,3},{3,0},{4,5},{5,6},{6,7},{7,4},{8,9},{9,10},{10,1... | collective-permute-start | bytes 737288 | tf_op jit(solution)/shard_map/ppermute | solution.py:143
  22.6 2.6 %collective-permute-start.8 = (bf16[2,480,128]{2,1,0:T(8,128)(2,1)S(1)}, bf16[2,480,128]{2,1,0:T(8,128)(2,1)S(1)}, u32[]{:S(2)}, u32[]{:S(2)}) collective-permute-start(bf16[2,480,128]{2,1,0:T(8,128)(2,1)S(1)} %get-tuple-element.19), channel_id=1, source_target_pairs={{0,3},{1,0},{2,1},{3,2},{4,7},{5,4},{6,5},{7,6},{8,11},{9,8},{10,9... | collective-permute-start | bytes 737288 | tf_op jit(solution)/shard_map/ppermute | solution.py:143
  25.1 1.3 %collective-permute-done.6 = bf16[2,480,128]{2,1,0:T(8,128)(2,1)S(1)} collective-permute-done((bf16[2,480,128]{2,1,0:T(8,128)(2,1)S(1)}, bf16[2,480,128]{2,1,0:T(8,128)(2,1)S(1)}, u32[]{:S(2)}, u32[]{:S(2)}) %collective-permute-start.6) | collective-permute-done | bytes 245792 | tf_op jit(solution)/shard_map/ppermute | solution.py:143
  26.4 2.9 %collective-permute-done.7 = bf16[2,480,128]{2,1,0:T(8,128)(2,1)S(1)} collective-permute-done((bf16[2,480,128]{2,1,0:T(8,128)(2,1)S(1)}, bf16[2,480,128]{2,1,0:T(8,128)(2,1)S(1)}, u32[]{:S(2)}, u32[]{:S(2)}) %collective-permute-start.7) | collective-permute-done | bytes 245792 | tf_op jit(solution)/shard_map/ppermute | solution.py:143
  29.3 0.1 collective-permute-done.8
  29.4 0.1 pad_maximum_fusion
  29.5 0.3 reshape.57
  29.8 1.9 %copy.15 = bf16[4,2,32,6,2,32]{2,3,4,0,5,1:T(8,128)(2,1)S(1)} copy(bf16[4,2,32,6,2,32]{5,4,3,2,1,0:T(2,128)(2,1)S(1)} %reshape.57) | data formatting | bytes 393216 | tf_op jit(solution)/shard_map/reshape | solution.py:148
  31.7 0.5 %copy.18 = bf16[4,2,6,2,32,128]{5,2,3,0,4,1:T(8,128)(2,1)S(1)} copy(bf16[4,2,6,2,32,128]{5,4,3,2,1,0:T(8,128)(2,1)S(1)} %bitcast.107) | data formatting | bytes 1572864 | tf_op jit(solution)/shard_map/reshape | solution.py:145
  32.2 0.2 fusion.44
  32.4 1.3 %fusion.11 = bf16[2,32,4,8,2,128]{5,3,4,2,1,0:T(8,128)(2,1)S(1)} fusion(bf16[4,2,6,1,32,128]{5,2,3,0,4,1:T(8,128)(2,1)S(1)} %get-tuple-element.13, bf16[4,2,6,1,32,128]{5,2,3,0,4,1:T(8,128)(2,1)S(1)} %get-tuple-element.12, bf16[4,2,6,2,32,128]{5,2,3,0,4,1:T(8,128)(2,1)S(1)} %copy.18, bf16[4,2,32,6,2,32]{2,3,4,0,5,1:T(8,128)(2,1)S(1)} %copy.15), kind=kOutput, calls=%fused_computation.12 | convolution fusion | flops 55574528 | bytes 2818048 | tf_op jit(solution)/shard_map/akscfm,akscfn->kfmn/dot_general | solution.py:152
  33.7 0.0 copy-start.1
  33.8 0.3 copy.19
  34.0 0.1 dynamic-slice_bitcast_fusion.2
  34.1 2.0 %collective-permute-start.10 = (bf16[1024,128]{1,0:T(8,128)(2,1)S(1)}, bf16[1024,128]{1,0:T(8,128)(2,1)S(1)}, u32[]{:S(2)}, u32[]{:S(2)}) collective-permute-start(bf16[1024,128]{1,0:T(8,128)(2,1)S(1)} %get-tuple-element.11), channel_id=1, source_target_pairs={{0,4},{1,5},{2,6},{3,7},{4,8},{5,9},{6,10},{7,11},{8,12},{9,13},{1... | collective-permute-start | bytes 786440 | tf_op jit(solution)/shard_map/ppermute | solution.py:164
  36.1 2.2 %collective-permute-start.11 = (bf16[1024,128]{1,0:T(8,128)(2,1)S(1)}, bf16[1024,128]{1,0:T(8,128)(2,1)S(1)}, u32[]{:S(2)}, u32[]{:S(2)}) collective-permute-start(bf16[1024,128]{1,0:T(8,128)(2,1)S(1)} %get-tuple-element.10), channel_id=1, source_target_pairs={{0,12},{1,13},{2,14},{3,15},{4,0},{5,1},{6,2},{7,3},{8,4},{9,5},{1... | collective-permute-start | bytes 786440 | tf_op jit(solution)/shard_map/ppermute | solution.py:164
  38.3 1.8 %collective-permute-start.9 = (bf16[1024,128]{1,0:T(8,128)(2,1)S(1)}, bf16[1024,128]{1,0:T(8,128)(2,1)S(1)}, u32[]{:S(2)}, u32[]{:S(2)}) collective-permute-start(bf16[1024,128]{1,0:T(8,128)(2,1)S(1)} %get-tuple-element.9), channel_id=1, source_target_pairs={{0,8},{1,9},{2,10},{3,11},{4,12},{5,13},{6,14},{7,15},{8,0},{9,1},... | collective-permute-start | bytes 786440 | tf_op jit(solution)/shard_map/ppermute | solution.py:164
  40.1 0.2 fusion.35
  40.2 0.0 copy-done.1
  40.2 0.6 %dynamic_slice.42 = s32[1]{0:T(128)} dynamic-slice(s32[8]{0:T(128)S(1)} %copy-done.1, s32[]{:T(128)S(6)} %select_n.119), dynamic_slice_sizes={1} | dynamic-slice | bytes 12 | tf_op jit(solution)/shard_map/dynamic_slice | solution.py:98
  40.8 0.6 %compare_convert_fusion = f32[2]{0:T(128)S(1)} fusion(s32[]{:T(128)} %bitcast.46), kind=kLoop, calls=%fused_computation.77 | loop fusion | flops 4 | bytes 12 | tf_op jit(solution)/shard_map/convert_element_type | solution.py:174
  41.5 1.1 %collective-permute-done.10 = bf16[1024,128]{1,0:T(8,128)(2,1)S(1)} collective-permute-done((bf16[1024,128]{1,0:T(8,128)(2,1)S(1)}, bf16[1024,128]{1,0:T(8,128)(2,1)S(1)}, u32[]{:S(2)}, u32[]{:S(2)}) %collective-permute-start.10) | collective-permute-done | bytes 262176 | tf_op jit(solution)/shard_map/ppermute | solution.py:164
  42.6 2.5 %collective-permute-done.11 = bf16[1024,128]{1,0:T(8,128)(2,1)S(1)} collective-permute-done((bf16[1024,128]{1,0:T(8,128)(2,1)S(1)}, bf16[1024,128]{1,0:T(8,128)(2,1)S(1)}, u32[]{:S(2)}, u32[]{:S(2)}) %collective-permute-start.11) | collective-permute-done | bytes 262176 | tf_op jit(solution)/shard_map/ppermute | solution.py:164
  45.0 1.8 %collective-permute-done.9 = bf16[1024,128]{1,0:T(8,128)(2,1)S(1)} collective-permute-done((bf16[1024,128]{1,0:T(8,128)(2,1)S(1)}, bf16[1024,128]{1,0:T(8,128)(2,1)S(1)}, u32[]{:S(2)}, u32[]{:S(2)}) %collective-permute-start.9) | collective-permute-done | bytes 262176 | tf_op jit(solution)/shard_map/ppermute | solution.py:164
  46.8 0.1 fusion.21
  47.0 1.1 %fusion.15 = bf16[1,2,8,128,128]{4,3,2,1,0:T(8,128)(2,1)} fusion(bf16[2,32,128,1,1]{2,1,0,4,3:T(8,128)(2,1)S(1)} %bitcast.129, bf16[2,2,32,8,128]{4,3,2,1,0:T(8,128)(2,1)S(1)} %bitcast.125, f32[2]{0:T(128)S(1)} %compare_convert_fusion), kind=kOutput, calls=%fused_computation.14 | convolution fusion | flops 34078720 | bytes 802824 | tf_op jit(solution)/shard_map/kpfrj,pft->krjt/dot_general | solution.py:167
  (15 shorter events, 0.2 us)
Async XLA Ops:
  0.0 10.4 %copy-start = (s32[8,2,2]{0,2,1:T(2,128)S(1)}, s32[8,2,2]{0,2,1:T(2,128)}, u32[]{:S(2)}) copy-start(s32[8,2,2]{0,2,1:T(2,128)} %param.5) | copy-start | bytes 388
  5.2 5.7 %collective-permute-start = (bf16[384,128]{1,0:T(8,128)(2,1)S(1)}, bf16[384,128]{1,0:T(8,128)(2,1)S(1)}, u32[]{:S(2)}, u32[]{:S(2)}) collective-permute-start(bf16[384,128]{1,0:T(8,128)(2,1)S(1)} %bitcast.116), channel_id=1, source_target_pairs={{0,96},{16,112},{32,0},{48,16},{64,32},{80,48},{96,64},{112,80},{1... | collective-permute-start | bytes 294920 | tf_op jit(solution)/shard_map/ppermute | solution.py:88
  8.1 7.6 %collective-permute-start.2 = (bf16[384,128]{1,0:T(8,128)(2,1)S(1)}, bf16[384,128]{1,0:T(8,128)(2,1)S(1)}, u32[]{:S(2)}, u32[]{:S(2)}) collective-permute-start(bf16[384,128]{1,0:T(8,128)(2,1)S(1)} %bitcast.117), channel_id=1, source_target_pairs={{0,32},{16,48},{32,64},{48,80},{64,96},{80,112},{96,0},{112,16},{1... | collective-permute-start | bytes 294920 | tf_op jit(solution)/shard_map/ppermute | solution.py:87
  8.1 7.7 %collective-permute-start.1 = (bf16[384,128]{1,0:T(8,128)(2,1)S(1)}, bf16[384,128]{1,0:T(8,128)(2,1)S(1)}, u32[]{:S(2)}, u32[]{:S(2)}) collective-permute-start(bf16[384,128]{1,0:T(8,128)(2,1)S(1)} %bitcast.118), channel_id=1, source_target_pairs={{0,64},{16,80},{32,96},{48,112},{64,0},{80,16},{96,32},{112,48},{1... | collective-permute-start | bytes 294920 | tf_op jit(solution)/shard_map/ppermute | solution.py:89
  10.4 6.8 %collective-permute-start.3 = (bf16[384,128]{1,0:T(8,128)(2,1)S(1)}, bf16[384,128]{1,0:T(8,128)(2,1)S(1)}, u32[]{:S(2)}, u32[]{:S(2)}) collective-permute-start(bf16[384,128]{1,0:T(8,128)(2,1)S(1)} %bitcast.119), channel_id=1, source_target_pairs={{0,16},{16,0},{32,48},{48,32},{64,80},{80,64},{96,112},{112,96},{1... | collective-permute-start | bytes 294920 | tf_op jit(solution)/shard_map/ppermute | solution.py:86
  15.7 1.5 %collective-permute-start.4 = (bf16[2,384,128]{2,1,0:T(8,128)(2,1)S(1)}, bf16[2,384,128]{2,1,0:T(8,128)(2,1)S(1)}, u32[]{:S(2)}, u32[]{:S(2)}) collective-permute-start(bf16[2,384,128]{2,1,0:T(8,128)(2,1)S(1)} %pad_maximum_fusion.7), channel_id=1, source_target_pairs={{0,16},{16,0},{32,48},{48,32},{64,80},{80,64},{96,112},{112,96},{1... | collective-permute-start | bytes 589832 | tf_op jit(solution)/shard_map/ppermute | solution.py:91
  15.8 1.5 %collective-permute-start.5 = (bf16[384,128]{1,0:T(8,128)(2,1)S(1)}, bf16[384,128]{1,0:T(8,128)(2,1)S(1)}, u32[]{:S(2)}, u32[]{:S(2)}) collective-permute-start(bf16[384,128]{1,0:T(8,128)(2,1)S(1)} %collective-permute-done.1), channel_id=1, source_target_pairs={{0,16},{16,0},{32,48},{48,32},{64,80},{80,64},{96,112},{112,96},{1... | collective-permute-start | bytes 294920 | tf_op jit(solution)/shard_map/ppermute | solution.py:92
  18.6 7.8 %collective-permute-start.6 = (bf16[2,480,128]{2,1,0:T(8,128)(2,1)S(1)}, bf16[2,480,128]{2,1,0:T(8,128)(2,1)S(1)}, u32[]{:S(2)}, u32[]{:S(2)}) collective-permute-start(bf16[2,480,128]{2,1,0:T(8,128)(2,1)S(1)} %get-tuple-element.17), channel_id=1, source_target_pairs={{0,2},{1,3},{2,0},{3,1},{4,6},{5,7},{6,4},{7,5},{8,10},{9,11},{10,... | collective-permute-start | bytes 737288 | tf_op jit(solution)/shard_map/ppermute | solution.py:143
  21.9 7.4 %collective-permute-start.7 = (bf16[2,480,128]{2,1,0:T(8,128)(2,1)S(1)}, bf16[2,480,128]{2,1,0:T(8,128)(2,1)S(1)}, u32[]{:S(2)}, u32[]{:S(2)}) collective-permute-start(bf16[2,480,128]{2,1,0:T(8,128)(2,1)S(1)} %get-tuple-element.18), channel_id=1, source_target_pairs={{0,1},{1,2},{2,3},{3,0},{4,5},{5,6},{6,7},{7,4},{8,9},{9,10},{10,1... | collective-permute-start | bytes 737288 | tf_op jit(solution)/shard_map/ppermute | solution.py:143
  22.6 6.8 %collective-permute-start.8 = (bf16[2,480,128]{2,1,0:T(8,128)(2,1)S(1)}, bf16[2,480,128]{2,1,0:T(8,128)(2,1)S(1)}, u32[]{:S(2)}, u32[]{:S(2)}) collective-permute-start(bf16[2,480,128]{2,1,0:T(8,128)(2,1)S(1)} %get-tuple-element.19), channel_id=1, source_target_pairs={{0,3},{1,0},{2,1},{3,2},{4,7},{5,4},{6,5},{7,6},{8,11},{9,8},{10,9... | collective-permute-start | bytes 737288 | tf_op jit(solution)/shard_map/ppermute | solution.py:143
  33.7 6.5 %copy-start.1 = (s32[8]{0:T(128)S(1)}, s32[8]{0:T(128)}, u32[]{:S(2)}) copy-start(s32[8]{0:T(128)} %param.6) | copy-start | bytes 100
  34.1 8.5 %collective-permute-start.10 = (bf16[1024,128]{1,0:T(8,128)(2,1)S(1)}, bf16[1024,128]{1,0:T(8,128)(2,1)S(1)}, u32[]{:S(2)}, u32[]{:S(2)}) collective-permute-start(bf16[1024,128]{1,0:T(8,128)(2,1)S(1)} %get-tuple-element.11), channel_id=1, source_target_pairs={{0,4},{1,5},{2,6},{3,7},{4,8},{5,9},{6,10},{7,11},{8,12},{9,13},{1... | collective-permute-start | bytes 786440 | tf_op jit(solution)/shard_map/ppermute | solution.py:164
  36.1 8.9 %collective-permute-start.11 = (bf16[1024,128]{1,0:T(8,128)(2,1)S(1)}, bf16[1024,128]{1,0:T(8,128)(2,1)S(1)}, u32[]{:S(2)}, u32[]{:S(2)}) collective-permute-start(bf16[1024,128]{1,0:T(8,128)(2,1)S(1)} %get-tuple-element.10), channel_id=1, source_target_pairs={{0,12},{1,13},{2,14},{3,15},{4,0},{5,1},{6,2},{7,3},{8,4},{9,5},{1... | collective-permute-start | bytes 786440 | tf_op jit(solution)/shard_map/ppermute | solution.py:164
  38.3 8.5 %collective-permute-start.9 = (bf16[1024,128]{1,0:T(8,128)(2,1)S(1)}, bf16[1024,128]{1,0:T(8,128)(2,1)S(1)}, u32[]{:S(2)}, u32[]{:S(2)}) collective-permute-start(bf16[1024,128]{1,0:T(8,128)(2,1)S(1)} %get-tuple-element.9), channel_id=1, source_target_pairs={{0,8},{1,9},{2,10},{3,11},{4,12},{5,13},{6,14},{7,15},{8,0},{9,1},... | collective-permute-start | bytes 786440 | tf_op jit(solution)/shard_map/ppermute | solution.py:164

commit v19 on v16

--- a/solution.py
+++ b/solution.py
@@ -88,9 +88,10 @@
     from_above = lax.ppermute(own, "pairs", chip_shift(-1))
     from_far = lax.ppermute(own, "pairs", chip_shift(2))
     mine = jnp.stack([own, from_above, from_far, from_below])
-    theirs_near = lax.ppermute(jnp.stack([from_above, from_below]), "pairs", swap)
+    theirs_above = lax.ppermute(from_above, "pairs", swap)
+    theirs_below = lax.ppermute(from_below, "pairs", swap)
     theirs_far = lax.ppermute(from_far, "pairs", swap)
-    theirs = jnp.stack([partner, theirs_near[0], theirs_far, theirs_near[1]])
+    theirs = jnp.stack([partner, theirs_above, theirs_far, theirs_below])
     table = jnp.where(
         first_core, jnp.stack([mine, theirs], axis=1), jnp.stack([theirs, mine], axis=1)
     ).reshape((pairs_count,) + own.shape)

time: 47 us -> 47.7 us (1.015)
    ppermute x3, waiting for transfers between devices: 5.33 us -> 3.5 us  [shards(): lax.ppermute(chunk, axes, reduce_perm(e)).astype(jnp.float32)]
    ppermute x1, starting transfers between devices: 1.66 us -> 2.91 us  [shards(): from_above = lax.ppermute(own, 'pairs', chip_shift(-1))]
    ppermute x3, starting transfers between devices: 5.97 us -> 7.19 us  [shards(): lax.ppermute(chunk, axes, reduce_perm(e)).astype(jnp.float32)]
    ppermute x1, starting transfers between devices: 1.89 us -> 0.8 us  [shards(): from_far = lax.ppermute(own, 'pairs', chip_shift(2))]
    ppermute x1 -> x2, waiting for transfers between devices: 0.01 us -> 1.01 us  [the longest x1 1.01 us: shards(): theirs_below = lax.ppermute(from_below, 'pairs', swap)]
    ppermute x1, waiting for transfers between devices: 1.2 us -> 0.21 us  [shards(): theirs_far = lax.ppermute(from_far, 'pairs', swap)]
    ppermute x1, waiting for transfers between devices: 0.11 us -> 1.01 us  [shards(): from_below = lax.ppermute(own, 'pairs', chip_shift(1))]
    ppermute x1, waiting for transfers between devices: 1.07 us -> 1.94 us  [shards(): from_above = lax.ppermute(own, 'pairs', chip_shift(-1))]
  transfers between devices with their start and end apart: 12 -> 13, of which waited for: 10 -> 10; matrix products, arithmetic and copies ran while one was open for 4% -> 4% of each run, Pallas kernels for 0% -> 0%
where the time goes in v19:
time: 47.7 us; the launch traced here: 47.5 us
  starting transfers between devices  18.3 us (38%)
  waiting for transfers between devices  14.6 us (31%)
  matrix products  7.46 us (16%)
  local copies, waits for them, and re-layouts  5.11 us (11%)
  other arithmetic  1.8 us (4%)
    ppermute x3, starting transfers between devices, shards(): lax.ppermute(chunk, axes, reduce_perm(e)).astype(jnp.float32)  7.19 us
    ppermute x3, starting transfers between devices, shards(): pieces.append(lax.ppermute(message, axes, gather_perm(d)))  6.51 us
    dot_general x1, matrix products, shards(): jnp.dot(records[0], band_table(), preferred_element_type=jnp.float32)  5 us
    ppermute x3, waiting for transfers between devices, shards(): pieces.append(lax.ppermute(message, axes, gather_perm(d)))  4.23 us
    ppermute x3, waiting for transfers between devices, shards(): lax.ppermute(chunk, axes, reduce_perm(e)).astype(jnp.float32)  3.5 us
    ppermute x1, starting transfers between devices, shards(): from_above = lax.ppermute(own, 'pairs', chip_shift(-1))  2.91 us
    ppermute x1, waiting for transfers between devices, shards(): from_far = lax.ppermute(own, 'pairs', chip_shift(2))  2.66 us
    reshape x2, local copies, waits for them, and re-layouts, shards(): gathered[:, :, spec_rows:]  2.22 us
  transfers between devices with their start and end apart: 13, of which 10 were waited for; matrix products, arithmetic and copies ran while one was open for 4% of the time, Pallas kernels for 0%

profile of v19, /device:TPU:0, one launch (start us, length us, event | category | flops | bytes accessed | tf_op | source)
XLA Modules:
  0.0 47.5 jit_solution(9299084349616561063)
XLA Ops:
  0.0 0.0 copy-start
  0.0 5.0 %fusion.16 = f32[6,128,64]{1,2,0:T(8,128)S(1)} fusion(bf16[4096,64,1]{0,1,2:T(8,128)(2,1)} %constant.176, bf16[1,6,128,4096]{3,2,1,0:T(8,128)(2,1)} %param.4), kind=kOutput, calls=%fused_computation.15 | convolution fusion | flops 402653184 | bytes 7012352 | tf_op jit(solution)/shard_map/dot_general | solution.py:70
  5.1 0.1 multiply_convert_fusion.1
  5.2 2.9 %collective-permute-start = (bf16[384,128]{1,0:T(8,128)(2,1)S(1)}, bf16[384,128]{1,0:T(8,128)(2,1)S(1)}, u32[]{:S(2)}, u32[]{:S(2)}) collective-permute-start(bf16[384,128]{1,0:T(8,128)(2,1)S(1)} %bitcast.120), channel_id=1, source_target_pairs={{0,96},{16,112},{32,0},{48,16},{64,32},{80,48},{96,64},{112,80},{1... | collective-permute-start | bytes 294920 | tf_op jit(solution)/shard_map/ppermute | solution.py:88
  8.1 0.8 %collective-permute-start.1 = (bf16[384,128]{1,0:T(8,128)(2,1)S(1)}, bf16[384,128]{1,0:T(8,128)(2,1)S(1)}, u32[]{:S(2)}, u32[]{:S(2)}) collective-permute-start(bf16[384,128]{1,0:T(8,128)(2,1)S(1)} %bitcast.121), channel_id=1, source_target_pairs={{0,64},{16,80},{32,96},{48,112},{64,0},{80,16},{96,32},{112,48},{1... | collective-permute-start | bytes 294920 | tf_op jit(solution)/shard_map/ppermute | solution.py:89
  8.9 0.9 %collective-permute-start.2 = (bf16[384,128]{1,0:T(8,128)(2,1)S(1)}, bf16[384,128]{1,0:T(8,128)(2,1)S(1)}, u32[]{:S(2)}, u32[]{:S(2)}) collective-permute-start(bf16[384,128]{1,0:T(8,128)(2,1)S(1)} %bitcast.122), channel_id=1, source_target_pairs={{0,32},{16,48},{32,64},{48,80},{64,96},{80,112},{96,0},{112,16},{1... | collective-permute-start | bytes 294920 | tf_op jit(solution)/shard_map/ppermute | solution.py:87
  9.8 0.0 collective-permute-start.3
  9.8 0.0 copy-done
  9.8 0.2 fusion.36
  10.0 0.1 copy.8
  10.1 0.1 reshape.93
  10.2 0.1 reshape.91
  10.3 1.9 %collective-permute-done = bf16[384,128]{1,0:T(8,128)(2,1)S(1)} collective-permute-done((bf16[384,128]{1,0:T(8,128)(2,1)S(1)}, bf16[384,128]{1,0:T(8,128)(2,1)S(1)}, u32[]{:S(2)}, u32[]{:S(2)}) %collective-permute-start) | collective-permute-done | bytes 98336 | tf_op jit(solution)/shard_map/ppermute | solution.py:88
  12.3 0.0 collective-permute-start.4
  12.3 2.7 %collective-permute-done.1 = bf16[384,128]{1,0:T(8,128)(2,1)S(1)} collective-permute-done((bf16[384,128]{1,0:T(8,128)(2,1)S(1)}, bf16[384,128]{1,0:T(8,128)(2,1)S(1)}, u32[]{:S(2)}, u32[]{:S(2)}) %collective-permute-start.1) | collective-permute-done | bytes 98336 | tf_op jit(solution)/shard_map/ppermute | solution.py:89
  14.9 0.0 collective-permute-start.5
  14.9 1.0 %collective-permute-done.2 = bf16[384,128]{1,0:T(8,128)(2,1)S(1)} collective-permute-done((bf16[384,128]{1,0:T(8,128)(2,1)S(1)}, bf16[384,128]{1,0:T(8,128)(2,1)S(1)}, u32[]{:S(2)}, u32[]{:S(2)}) %collective-permute-start.2) | collective-permute-done | bytes 98336 | tf_op jit(solution)/shard_map/ppermute | solution.py:87
  15.9 0.0 collective-permute-start.6
  15.9 0.1 maximum_bitcast_fusion
  16.0 0.0 collective-permute-done.3
  16.0 0.0 collective-permute-done.4
  16.0 0.2 collective-permute-done.5
  16.2 1.0 %collective-permute-done.6 = bf16[384,128]{1,0:T(8,128)(2,1)S(1)} collective-permute-done((bf16[384,128]{1,0:T(8,128)(2,1)S(1)}, bf16[384,128]{1,0:T(8,128)(2,1)S(1)}, u32[]{:S(2)}, u32[]{:S(2)}) %collective-permute-start.6) | collective-permute-done | bytes 98336 | tf_op jit(solution)/shard_map/ppermute | solution.py:92
  17.2 0.1 maximum_bitcast_fusion.1
  17.3 0.1 maximum_select_fusion
  17.4 0.6 %gather_fusion = bf16[4,384,128]{2,1,0:T(8,128)(2,1)S(1)} fusion(bf16[8,384,128]{2,1,0:T(8,128)(2,1)S(1)} %bitcast.112, s32[1024]{0:T(1024)S(1)} %pad_clamp_fusion), kind=kCustom, calls=%fused_computation | custom fusion | bytes 786448 | tf_op jit(solution)/shard_map/jit(_take)/gather | solution.py:101
  18.0 0.1 broadcast_select_fusion
  18.2 0.2 copy.10
  18.4 0.1 reshape.113
  18.5 0.1 maximum_bitcast_fusion.2
  18.6 3.3 %collective-permute-start.7 = (bf16[2,480,128]{2,1,0:T(8,128)(2,1)S(1)}, bf16[2,480,128]{2,1,0:T(8,128)(2,1)S(1)}, u32[]{:S(2)}, u32[]{:S(2)}) collective-permute-start(bf16[2,480,128]{2,1,0:T(8,128)(2,1)S(1)} %get-tuple-element.17), channel_id=1, source_target_pairs={{0,2},{1,3},{2,0},{3,1},{4,6},{5,7},{6,4},{7,5},{8,10},{9,11},{10,... | collective-permute-start | bytes 737288 | tf_op jit(solution)/shard_map/ppermute | solution.py:144
  21.9 0.7 %collective-permute-start.8 = (bf16[2,480,128]{2,1,0:T(8,128)(2,1)S(1)}, bf16[2,480,128]{2,1,0:T(8,128)(2,1)S(1)}, u32[]{:S(2)}, u32[]{:S(2)}) collective-permute-start(bf16[2,480,128]{2,1,0:T(8,128)(2,1)S(1)} %get-tuple-element.18), channel_id=1, source_target_pairs={{0,1},{1,2},{2,3},{3,0},{4,5},{5,6},{6,7},{7,4},{8,9},{9,10},{10,1... | collective-permute-start | bytes 737288 | tf_op jit(solution)/shard_map/ppermute | solution.py:144
  22.6 2.6 %collective-permute-start.9 = (bf16[2,480,128]{2,1,0:T(8,128)(2,1)S(1)}, bf16[2,480,128]{2,1,0:T(8,128)(2,1)S(1)}, u32[]{:S(2)}, u32[]{:S(2)}) collective-permute-start(bf16[2,480,128]{2,1,0:T(8,128)(2,1)S(1)} %get-tuple-element.19), channel_id=1, source_target_pairs={{0,3},{1,0},{2,1},{3,2},{4,7},{5,4},{6,5},{7,6},{8,11},{9,8},{10,9... | collective-permute-start | bytes 737288 | tf_op jit(solution)/shard_map/ppermute | solution.py:144
  25.2 1.3 %collective-permute-done.7 = bf16[2,480,128]{2,1,0:T(8,128)(2,1)S(1)} collective-permute-done((bf16[2,480,128]{2,1,0:T(8,128)(2,1)S(1)}, bf16[2,480,128]{2,1,0:T(8,128)(2,1)S(1)}, u32[]{:S(2)}, u32[]{:S(2)}) %collective-permute-start.7) | collective-permute-done | bytes 245792 | tf_op jit(solution)/shard_map/ppermute | solution.py:144
  26.4 2.9 %collective-permute-done.8 = bf16[2,480,128]{2,1,0:T(8,128)(2,1)S(1)} collective-permute-done((bf16[2,480,128]{2,1,0:T(8,128)(2,1)S(1)}, bf16[2,480,128]{2,1,0:T(8,128)(2,1)S(1)}, u32[]{:S(2)}, u32[]{:S(2)}) %collective-permute-start.8) | collective-permute-done | bytes 245792 | tf_op jit(solution)/shard_map/ppermute | solution.py:144
  29.3 0.1 collective-permute-done.9
  29.4 0.1 pad_maximum_fusion
  29.5 0.3 reshape.96
  29.8 1.9 %copy.13 = bf16[4,2,32,6,2,32]{2,3,4,0,5,1:T(8,128)(2,1)S(1)} copy(bf16[4,2,32,6,2,32]{5,4,3,2,1,0:T(2,128)(2,1)S(1)} %reshape.96) | data formatting | bytes 393216 | tf_op jit(solution)/shard_map/reshape | solution.py:149
  31.7 0.5 %copy.16 = bf16[4,2,6,2,32,128]{5,2,3,0,4,1:T(8,128)(2,1)S(1)} copy(bf16[4,2,6,2,32,128]{5,4,3,2,1,0:T(8,128)(2,1)S(1)} %bitcast.111) | data formatting | bytes 1572864 | tf_op jit(solution)/shard_map/reshape | solution.py:146
  32.3 0.2 fusion.45
  32.4 1.3 %fusion.11 = bf16[2,32,4,8,2,128]{5,3,4,2,1,0:T(8,128)(2,1)S(1)} fusion(bf16[4,2,6,1,32,128]{5,2,3,0,4,1:T(8,128)(2,1)S(1)} %get-tuple-element.13, bf16[4,2,6,1,32,128]{5,2,3,0,4,1:T(8,128)(2,1)S(1)} %get-tuple-element.12, bf16[4,2,6,2,32,128]{5,2,3,0,4,1:T(8,128)(2,1)S(1)} %copy.16, bf16[4,2,32,6,2,32]{2,3,4,0,5,1:T(8,128)(2,1)S(1)} %copy.13), kind=kOutput, calls=%fused_computation.12 | convolution fusion | flops 55574528 | bytes 2818048 | tf_op jit(solution)/shard_map/akscfm,akscfn->kfmn/dot_general | solution.py:153
  33.8 0.0 copy-start.1
  33.8 0.3 copy.17
  34.0 0.1 dynamic-slice_bitcast_fusion.2
  34.1 4.0 %collective-permute-start.10 = (bf16[1024,128]{1,0:T(8,128)(2,1)S(1)}, bf16[1024,128]{1,0:T(8,128)(2,1)S(1)}, u32[]{:S(2)}, u32[]{:S(2)}) collective-permute-start(bf16[1024,128]{1,0:T(8,128)(2,1)S(1)} %get-tuple-element.9), channel_id=1, source_target_pairs={{0,8},{1,9},{2,10},{3,11},{4,12},{5,13},{6,14},{7,15},{8,0},{9,1},... | collective-permute-start | bytes 786440 | tf_op jit(solution)/shard_map/ppermute | solution.py:165
  38.1 1.0 %collective-permute-start.11 = (bf16[1024,128]{1,0:T(8,128)(2,1)S(1)}, bf16[1024,128]{1,0:T(8,128)(2,1)S(1)}, u32[]{:S(2)}, u32[]{:S(2)}) collective-permute-start(bf16[1024,128]{1,0:T(8,128)(2,1)S(1)} %get-tuple-element.11), channel_id=1, source_target_pairs={{0,4},{1,5},{2,6},{3,7},{4,8},{5,9},{6,10},{7,11},{8,12},{9,13},{1... | collective-permute-start | bytes 786440 | tf_op jit(solution)/shard_map/ppermute | solution.py:165
  39.1 2.2 %collective-permute-start.12 = (bf16[1024,128]{1,0:T(8,128)(2,1)S(1)}, bf16[1024,128]{1,0:T(8,128)(2,1)S(1)}, u32[]{:S(2)}, u32[]{:S(2)}) collective-permute-start(bf16[1024,128]{1,0:T(8,128)(2,1)S(1)} %get-tuple-element.10), channel_id=1, source_target_pairs={{0,12},{1,13},{2,14},{3,15},{4,0},{5,1},{6,2},{7,3},{8,4},{9,5},{1... | collective-permute-start | bytes 786440 | tf_op jit(solution)/shard_map/ppermute | solution.py:165
  41.3 0.2 fusion.35
  41.5 0.0 copy-done.1
  41.5 0.6 %dynamic_slice.42 = s32[1]{0:T(128)} dynamic-slice(s32[8]{0:T(128)S(1)} %copy-done.1, s32[]{:T(128)S(6)} %select_n.135), dynamic_slice_sizes={1} | dynamic-slice | bytes 12 | tf_op jit(solution)/shard_map/dynamic_slice | solution.py:99
  42.1 0.6 %compare_convert_fusion = f32[2]{0:T(128)S(1)} fusion(s32[]{:T(128)} %bitcast.49), kind=kLoop, calls=%fused_computation.79 | loop fusion | flops 4 | bytes 12 | tf_op jit(solution)/shard_map/convert_element_type | solution.py:175
  42.7 0.0 collective-permute-done.10
  42.7 2.9 %collective-permute-done.11 = bf16[1024,128]{1,0:T(8,128)(2,1)S(1)} collective-permute-done((bf16[1024,128]{1,0:T(8,128)(2,1)S(1)}, bf16[1024,128]{1,0:T(8,128)(2,1)S(1)}, u32[]{:S(2)}, u32[]{:S(2)}) %collective-permute-start.11) | collective-permute-done | bytes 262176 | tf_op jit(solution)/shard_map/ppermute | solution.py:165
  45.7 0.6 %collective-permute-done.12 = bf16[1024,128]{1,0:T(8,128)(2,1)S(1)} collective-permute-done((bf16[1024,128]{1,0:T(8,128)(2,1)S(1)}, bf16[1024,128]{1,0:T(8,128)(2,1)S(1)}, u32[]{:S(2)}, u32[]{:S(2)}) %collective-permute-start.12) | collective-permute-done | bytes 262176 | tf_op jit(solution)/shard_map/ppermute | solution.py:165
  46.2 0.1 fusion.21
  46.4 1.1 %fusion.15 = bf16[1,2,8,128,128]{4,3,2,1,0:T(8,128)(2,1)} fusion(bf16[2,32,128,1,1]{2,1,0,4,3:T(8,128)(2,1)S(1)} %bitcast.133, bf16[2,2,32,8,128]{4,3,2,1,0:T(8,128)(2,1)S(1)} %bitcast.125, f32[2]{0:T(128)S(1)} %compare_convert_fusion), kind=kOutput, calls=%fused_computation.14 | convolution fusion | flops 34078720 | bytes 802824 | tf_op jit(solution)/shard_map/kpfrj,pft->krjt/dot_general | solution.py:168
  (15 shorter events, 0.2 us)
Async XLA Ops:
  0.0 9.8 %copy-start = (s32[8,2,2]{0,2,1:T(2,128)S(1)}, s32[8,2,2]{0,2,1:T(2,128)}, u32[]{:S(2)}) copy-start(s32[8,2,2]{0,2,1:T(2,128)} %param.5) | copy-start | bytes 388
  5.2 7.1 %collective-permute-start = (bf16[384,128]{1,0:T(8,128)(2,1)S(1)}, bf16[384,128]{1,0:T(8,128)(2,1)S(1)}, u32[]{:S(2)}, u32[]{:S(2)}) collective-permute-start(bf16[384,128]{1,0:T(8,128)(2,1)S(1)} %bitcast.120), channel_id=1, source_target_pairs={{0,96},{16,112},{32,0},{48,16},{64,32},{80,48},{96,64},{112,80},{1... | collective-permute-start | bytes 294920 | tf_op jit(solution)/shard_map/ppermute | solution.py:88
  8.1 6.9 %collective-permute-start.1 = (bf16[384,128]{1,0:T(8,128)(2,1)S(1)}, bf16[384,128]{1,0:T(8,128)(2,1)S(1)}, u32[]{:S(2)}, u32[]{:S(2)}) collective-permute-start(bf16[384,128]{1,0:T(8,128)(2,1)S(1)} %bitcast.121), channel_id=1, source_target_pairs={{0,64},{16,80},{32,96},{48,112},{64,0},{80,16},{96,32},{112,48},{1... | collective-permute-start | bytes 294920 | tf_op jit(solution)/shard_map/ppermute | solution.py:89
  8.9 7.1 %collective-permute-start.2 = (bf16[384,128]{1,0:T(8,128)(2,1)S(1)}, bf16[384,128]{1,0:T(8,128)(2,1)S(1)}, u32[]{:S(2)}, u32[]{:S(2)}) collective-permute-start(bf16[384,128]{1,0:T(8,128)(2,1)S(1)} %bitcast.122), channel_id=1, source_target_pairs={{0,32},{16,48},{32,64},{48,80},{64,96},{80,112},{96,0},{112,16},{1... | collective-permute-start | bytes 294920 | tf_op jit(solution)/shard_map/ppermute | solution.py:87
  9.8 6.2 %collective-permute-start.3 = (bf16[384,128]{1,0:T(8,128)(2,1)S(1)}, bf16[384,128]{1,0:T(8,128)(2,1)S(1)}, u32[]{:S(2)}, u32[]{:S(2)}) collective-permute-start(bf16[384,128]{1,0:T(8,128)(2,1)S(1)} %bitcast.123), channel_id=1, source_target_pairs={{0,16},{16,0},{32,48},{48,32},{64,80},{80,64},{96,112},{112,96},{1... | collective-permute-start | bytes 294920 | tf_op jit(solution)/shard_map/ppermute | solution.py:86
  12.3 3.7 %collective-permute-start.4 = (bf16[384,128]{1,0:T(8,128)(2,1)S(1)}, bf16[384,128]{1,0:T(8,128)(2,1)S(1)}, u32[]{:S(2)}, u32[]{:S(2)}) collective-permute-start(bf16[384,128]{1,0:T(8,128)(2,1)S(1)} %collective-permute-done), channel_id=1, source_target_pairs={{0,16},{16,0},{32,48},{48,32},{64,80},{80,64},{96,112},{112,96},{1... | collective-permute-start | bytes 294920 | tf_op jit(solution)/shard_map/ppermute | solution.py:91
  14.9 1.3 %collective-permute-start.5 = (bf16[384,128]{1,0:T(8,128)(2,1)S(1)}, bf16[384,128]{1,0:T(8,128)(2,1)S(1)}, u32[]{:S(2)}, u32[]{:S(2)}) collective-permute-start(bf16[384,128]{1,0:T(8,128)(2,1)S(1)} %collective-permute-done.1), channel_id=1, source_target_pairs={{0,16},{16,0},{32,48},{48,32},{64,80},{80,64},{96,112},{112,96},{1... | collective-permute-start | bytes 294920 | tf_op jit(solution)/shard_map/ppermute | solution.py:93
  15.9 1.3 %collective-permute-start.6 = (bf16[384,128]{1,0:T(8,128)(2,1)S(1)}, bf16[384,128]{1,0:T(8,128)(2,1)S(1)}, u32[]{:S(2)}, u32[]{:S(2)}) collective-permute-start(bf16[384,128]{1,0:T(8,128)(2,1)S(1)} %collective-permute-done.2), channel_id=1, source_target_pairs={{0,16},{16,0},{32,48},{48,32},{64,80},{80,64},{96,112},{112,96},{1... | collective-permute-start | bytes 294920 | tf_op jit(solution)/shard_map/ppermute | solution.py:92
  18.6 7.8 %collective-permute-start.7 = (bf16[2,480,128]{2,1,0:T(8,128)(2,1)S(1)}, bf16[2,480,128]{2,1,0:T(8,128)(2,1)S(1)}, u32[]{:S(2)}, u32[]{:S(2)}) collective-permute-start(bf16[2,480,128]{2,1,0:T(8,128)(2,1)S(1)} %get-tuple-element.17), channel_id=1, source_target_pairs={{0,2},{1,3},{2,0},{3,1},{4,6},{5,7},{6,4},{7,5},{8,10},{9,11},{10,... | collective-permute-start | bytes 737288 | tf_op jit(solution)/shard_map/ppermute | solution.py:144
  21.9 7.4 %collective-permute-start.8 = (bf16[2,480,128]{2,1,0:T(8,128)(2,1)S(1)}, bf16[2,480,128]{2,1,0:T(8,128)(2,1)S(1)}, u32[]{:S(2)}, u32[]{:S(2)}) collective-permute-start(bf16[2,480,128]{2,1,0:T(8,128)(2,1)S(1)} %get-tuple-element.18), channel_id=1, source_target_pairs={{0,1},{1,2},{2,3},{3,0},{4,5},{5,6},{6,7},{7,4},{8,9},{9,10},{10,1... | collective-permute-start | bytes 737288 | tf_op jit(solution)/shard_map/ppermute | solution.py:144
  22.6 6.8 %collective-permute-start.9 = (bf16[2,480,128]{2,1,0:T(8,128)(2,1)S(1)}, bf16[2,480,128]{2,1,0:T(8,128)(2,1)S(1)}, u32[]{:S(2)}, u32[]{:S(2)}) collective-permute-start(bf16[2,480,128]{2,1,0:T(8,128)(2,1)S(1)} %get-tuple-element.19), channel_id=1, source_target_pairs={{0,3},{1,0},{2,1},{3,2},{4,7},{5,4},{6,5},{7,6},{8,11},{9,8},{10,9... | collective-permute-start | bytes 737288 | tf_op jit(solution)/shard_map/ppermute | solution.py:144
  33.8 7.7 %copy-start.1 = (s32[8]{0:T(128)S(1)}, s32[8]{0:T(128)}, u32[]{:S(2)}) copy-start(s32[8]{0:T(128)} %param.6) | copy-start | bytes 100
  34.1 8.6 %collective-permute-start.10 = (bf16[1024,128]{1,0:T(8,128)(2,1)S(1)}, bf16[1024,128]{1,0:T(8,128)(2,1)S(1)}, u32[]{:S(2)}, u32[]{:S(2)}) collective-permute-start(bf16[1024,128]{1,0:T(8,128)(2,1)S(1)} %get-tuple-element.9), channel_id=1, source_target_pairs={{0,8},{1,9},{2,10},{3,11},{4,12},{5,13},{6,14},{7,15},{8,0},{9,1},... | collective-permute-start | bytes 786440 | tf_op jit(solution)/shard_map/ppermute | solution.py:165
  38.1 7.6 %collective-permute-start.11 = (bf16[1024,128]{1,0:T(8,128)(2,1)S(1)}, bf16[1024,128]{1,0:T(8,128)(2,1)S(1)}, u32[]{:S(2)}, u32[]{:S(2)}) collective-permute-start(bf16[1024,128]{1,0:T(8,128)(2,1)S(1)} %get-tuple-element.11), channel_id=1, source_target_pairs={{0,4},{1,5},{2,6},{3,7},{4,8},{5,9},{6,10},{7,11},{8,12},{9,13},{1... | collective-permute-start | bytes 786440 | tf_op jit(solution)/shard_map/ppermute | solution.py:165
  39.1 7.2 %collective-permute-start.12 = (bf16[1024,128]{1,0:T(8,128)(2,1)S(1)}, bf16[1024,128]{1,0:T(8,128)(2,1)S(1)}, u32[]{:S(2)}, u32[]{:S(2)}) collective-permute-start(bf16[1024,128]{1,0:T(8,128)(2,1)S(1)} %get-tuple-element.10), channel_id=1, source_target_pairs={{0,12},{1,13},{2,14},{3,15},{4,0},{5,1},{6,2},{7,3},{8,4},{9,5},{1... | collective-permute-start | bytes 786440 | tf_op jit(solution)/shard_map/ppermute | solution.py:165

commit v20 on v16

--- a/solution.py
+++ b/solution.py
@@ -28,14 +28,15 @@
 
 
 def lag_table(segments):
-    bin_idx = jnp.arange(FREQS, dtype=jnp.int32) + LOW_BIN
-    lag_idx = (jnp.arange(LAGS, dtype=jnp.int32) - LAGS // 2) * (NSAMP // LAGS)
-    phase = (bin_idx[:, None] * lag_idx[None, :] % NSAMP).astype(jnp.float32) * (
+    bin_idx = np.arange(FREQS, dtype=np.int64) + LOW_BIN
+    lag_idx = (np.arange(LAGS, dtype=np.int64) - LAGS // 2) * (NSAMP // LAGS)
+    phase = (bin_idx[:, None] * lag_idx[None, :] % NSAMP).astype(np.float32) * np.float32(
         2.0 * math.pi / NSAMP
     )
-    return jnp.concatenate([jnp.cos(phase), -jnp.sin(phase)], axis=0) * (
+    table = np.concatenate([np.cos(phase), -np.sin(phase)], axis=0) * np.float32(
         1.0 / math.sqrt(segments * FREQS)
     )
+    return jnp.asarray(table.astype(np.float32))
 
 
 def whiten(spectra):

time: 47 us -> 47.1 us (level)
  no operation moved by 1% of the time
where the time goes in v20:
time: 47.1 us; the launch traced here: 46.9 us
  starting transfers between devices  17.9 us (38%)
  waiting for transfers between devices  14.5 us (31%)
  matrix products  7.46 us (16%)
  local copies, waits for them, and re-layouts  5.12 us (11%)
  other arithmetic  1.65 us (4%)
    ppermute x3, starting transfers between devices, shards(): pieces.append(lax.ppermute(message, axes, gather_perm(d)))  6.59 us
    ppermute x3, starting transfers between devices, shards(): lax.ppermute(chunk, axes, reduce_perm(e)).astype(jnp.float32)  5.97 us
    ppermute x3, waiting for transfers between devices, shards(): lax.ppermute(chunk, axes, reduce_perm(e)).astype(jnp.float32)  5.51 us
    dot_general x1, matrix products, shards(): jnp.dot(records[0], band_table(), preferred_element_type=jnp.float32)  5 us
    ppermute x3, waiting for transfers between devices, shards(): pieces.append(lax.ppermute(message, axes, gather_perm(d)))  4.24 us
    ppermute x1, waiting for transfers between devices, shards(): from_far = lax.ppermute(own, 'pairs', chip_shift(2))  2.33 us
    reshape x2, local copies, waits for them, and re-layouts, shards(): gathered[:, :, spec_rows:]  2.22 us
    ppermute x1, starting transfers between devices, shards(): from_far = lax.ppermute(own, 'pairs', chip_shift(2))  1.89 us
  transfers between devices with their start and end apart: 12, of which 10 were waited for; matrix products, arithmetic and copies ran while one was open for 4% of the time, Pallas kernels for 0%

profile of v20, /device:TPU:0, one launch (start us, length us, event | category | flops | bytes accessed | tf_op | source)
XLA Modules:
  0.0 46.9 jit_solution(11029995597098308267)
XLA Ops:
  0.0 0.0 copy-start
  0.0 5.0 %fusion.16 = f32[6,128,64]{1,2,0:T(8,128)S(1)} fusion(bf16[4096,64,1]{0,1,2:T(8,128)(2,1)} %constant.155, bf16[1,6,128,4096]{3,2,1,0:T(8,128)(2,1)} %param.5), kind=kOutput, calls=%fused_computation.15 | convolution fusion | flops 402653184 | bytes 7012352 | tf_op jit(solution)/shard_map/dot_general | solution.py:71
  5.1 0.1 multiply_convert_fusion.1
  5.2 1.6 %collective-permute-start.2 = (bf16[384,128]{1,0:T(8,128)(2,1)S(1)}, bf16[384,128]{1,0:T(8,128)(2,1)S(1)}, u32[]{:S(2)}, u32[]{:S(2)}) collective-permute-start(bf16[384,128]{1,0:T(8,128)(2,1)S(1)} %bitcast.116), channel_id=1, source_target_pairs={{0,32},{16,48},{32,64},{48,80},{64,96},{80,112},{96,0},{112,16},{1... | collective-permute-start | bytes 294920 | tf_op jit(solution)/shard_map/ppermute | solution.py:88
  6.8 1.7 %collective-permute-start = (bf16[384,128]{1,0:T(8,128)(2,1)S(1)}, bf16[384,128]{1,0:T(8,128)(2,1)S(1)}, u32[]{:S(2)}, u32[]{:S(2)}) collective-permute-start(bf16[384,128]{1,0:T(8,128)(2,1)S(1)} %bitcast.117), channel_id=1, source_target_pairs={{0,96},{16,112},{32,0},{48,16},{64,32},{80,48},{96,64},{112,80},{1... | collective-permute-start | bytes 294920 | tf_op jit(solution)/shard_map/ppermute | solution.py:89
  8.5 1.9 %collective-permute-start.1 = (bf16[384,128]{1,0:T(8,128)(2,1)S(1)}, bf16[384,128]{1,0:T(8,128)(2,1)S(1)}, u32[]{:S(2)}, u32[]{:S(2)}) collective-permute-start(bf16[384,128]{1,0:T(8,128)(2,1)S(1)} %bitcast.118), channel_id=1, source_target_pairs={{0,64},{16,80},{32,96},{48,112},{64,0},{80,16},{96,32},{112,48},{1... | collective-permute-start | bytes 294920 | tf_op jit(solution)/shard_map/ppermute | solution.py:90
  10.4 0.0 collective-permute-start.3
  10.4 0.0 copy-done
  10.4 0.2 fusion.32
  10.6 0.1 copy.9
  10.7 0.1 reshape.83
  10.8 0.1 reshape.81
  11.0 0.1 collective-permute-done.2
  11.1 1.1 %collective-permute-done = bf16[384,128]{1,0:T(8,128)(2,1)S(1)} collective-permute-done((bf16[384,128]{1,0:T(8,128)(2,1)S(1)}, bf16[384,128]{1,0:T(8,128)(2,1)S(1)}, u32[]{:S(2)}, u32[]{:S(2)}) %collective-permute-start) | collective-permute-done | bytes 98336 | tf_op jit(solution)/shard_map/ppermute | solution.py:89
  12.2 0.1 collective-permute-start.4
  12.3 2.3 %collective-permute-done.1 = bf16[384,128]{1,0:T(8,128)(2,1)S(1)} collective-permute-done((bf16[384,128]{1,0:T(8,128)(2,1)S(1)}, bf16[384,128]{1,0:T(8,128)(2,1)S(1)}, u32[]{:S(2)}, u32[]{:S(2)}) %collective-permute-start.1) | collective-permute-done | bytes 98336 | tf_op jit(solution)/shard_map/ppermute | solution.py:90
  14.6 0.0 collective-permute-start.5
  14.6 0.1 maximum_bitcast_fusion
  14.7 0.0 collective-permute-done.4
  14.7 0.0 collective-permute-done.3
  14.7 1.2 %collective-permute-done.5 = bf16[384,128]{1,0:T(8,128)(2,1)S(1)} collective-permute-done((bf16[384,128]{1,0:T(8,128)(2,1)S(1)}, bf16[384,128]{1,0:T(8,128)(2,1)S(1)}, u32[]{:S(2)}, u32[]{:S(2)}) %collective-permute-start.5) | collective-permute-done | bytes 98336 | tf_op jit(solution)/shard_map/ppermute | solution.py:93
  15.9 0.1 maximum_bitcast_fusion.1
  16.0 0.1 maximum_select_fusion
  16.0 0.6 %gather_fusion = bf16[4,384,128]{2,1,0:T(8,128)(2,1)S(1)} fusion(bf16[8,384,128]{2,1,0:T(8,128)(2,1)S(1)} %bitcast.108, s32[1024]{0:T(1024)S(1)} %pad_clamp_fusion), kind=kCustom, calls=%fused_computation | custom fusion | bytes 786448 | tf_op jit(solution)/shard_map/jit(_take)/gather | solution.py:101
  16.7 0.1 broadcast_select_fusion
  16.8 0.2 copy.11
  17.0 0.1 reshape.104
  17.2 0.1 maximum_bitcast_fusion.2
  17.3 3.4 %collective-permute-start.6 = (bf16[2,480,128]{2,1,0:T(8,128)(2,1)S(1)}, bf16[2,480,128]{2,1,0:T(8,128)(2,1)S(1)}, u32[]{:S(2)}, u32[]{:S(2)}) collective-permute-start(bf16[2,480,128]{2,1,0:T(8,128)(2,1)S(1)} %get-tuple-element.17), channel_id=1, source_target_pairs={{0,2},{1,3},{2,0},{3,1},{4,6},{5,7},{6,4},{7,5},{8,10},{9,11},{10,... | collective-permute-start | bytes 737288 | tf_op jit(solution)/shard_map/ppermute | solution.py:144
  20.7 0.7 %collective-permute-start.7 = (bf16[2,480,128]{2,1,0:T(8,128)(2,1)S(1)}, bf16[2,480,128]{2,1,0:T(8,128)(2,1)S(1)}, u32[]{:S(2)}, u32[]{:S(2)}) collective-permute-start(bf16[2,480,128]{2,1,0:T(8,128)(2,1)S(1)} %get-tuple-element.18), channel_id=1, source_target_pairs={{0,1},{1,2},{2,3},{3,0},{4,5},{5,6},{6,7},{7,4},{8,9},{9,10},{10,1... | collective-permute-start | bytes 737288 | tf_op jit(solution)/shard_map/ppermute | solution.py:144
  21.3 2.6 %collective-permute-start.8 = (bf16[2,480,128]{2,1,0:T(8,128)(2,1)S(1)}, bf16[2,480,128]{2,1,0:T(8,128)(2,1)S(1)}, u32[]{:S(2)}, u32[]{:S(2)}) collective-permute-start(bf16[2,480,128]{2,1,0:T(8,128)(2,1)S(1)} %get-tuple-element.19), channel_id=1, source_target_pairs={{0,3},{1,0},{2,1},{3,2},{4,7},{5,4},{6,5},{7,6},{8,11},{9,8},{10,9... | collective-permute-start | bytes 737288 | tf_op jit(solution)/shard_map/ppermute | solution.py:144
  23.9 1.2 %collective-permute-done.6 = bf16[2,480,128]{2,1,0:T(8,128)(2,1)S(1)} collective-permute-done((bf16[2,480,128]{2,1,0:T(8,128)(2,1)S(1)}, bf16[2,480,128]{2,1,0:T(8,128)(2,1)S(1)}, u32[]{:S(2)}, u32[]{:S(2)}) %collective-permute-start.6) | collective-permute-done | bytes 245792 | tf_op jit(solution)/shard_map/ppermute | solution.py:144
  25.1 3.0 %collective-permute-done.7 = bf16[2,480,128]{2,1,0:T(8,128)(2,1)S(1)} collective-permute-done((bf16[2,480,128]{2,1,0:T(8,128)(2,1)S(1)}, bf16[2,480,128]{2,1,0:T(8,128)(2,1)S(1)}, u32[]{:S(2)}, u32[]{:S(2)}) %collective-permute-start.7) | collective-permute-done | bytes 245792 | tf_op jit(solution)/shard_map/ppermute | solution.py:144
  28.1 0.1 collective-permute-done.8
  28.2 0.1 pad_maximum_fusion
  28.2 0.3 reshape.86
  28.5 1.9 %copy.14 = bf16[4,2,32,6,2,32]{2,3,4,0,5,1:T(8,128)(2,1)S(1)} copy(bf16[4,2,32,6,2,32]{5,4,3,2,1,0:T(2,128)(2,1)S(1)} %reshape.86) | data formatting | bytes 393216 | tf_op jit(solution)/shard_map/reshape | solution.py:149
  30.4 0.5 %copy.17 = bf16[4,2,6,2,32,128]{5,2,3,0,4,1:T(8,128)(2,1)S(1)} copy(bf16[4,2,6,2,32,128]{5,4,3,2,1,0:T(8,128)(2,1)S(1)} %bitcast.107) | data formatting | bytes 1572864 | tf_op jit(solution)/shard_map/reshape | solution.py:146
  31.0 0.2 fusion.41
  31.2 1.3 %fusion.11 = bf16[2,32,4,8,2,128]{5,3,4,2,1,0:T(8,128)(2,1)S(1)} fusion(bf16[4,2,6,1,32,128]{5,2,3,0,4,1:T(8,128)(2,1)S(1)} %get-tuple-element.13, bf16[4,2,6,1,32,128]{5,2,3,0,4,1:T(8,128)(2,1)S(1)} %get-tuple-element.12, bf16[4,2,6,2,32,128]{5,2,3,0,4,1:T(8,128)(2,1)S(1)} %copy.17, bf16[4,2,32,6,2,32]{2,3,4,0,5,1:T(8,128)(2,1)S(1)} %copy.14), kind=kOutput, calls=%fused_computation.12 | convolution fusion | flops 55574528 | bytes 2818048 | tf_op jit(solution)/shard_map/akscfm,akscfn->kfmn/dot_general | solution.py:153
  32.5 0.0 copy-start.1
  32.5 0.0 copy-start.2
  32.5 0.3 copy.18
  32.8 0.1 dynamic-slice_bitcast_fusion.2
  32.9 2.0 %collective-permute-start.10 = (bf16[1024,128]{1,0:T(8,128)(2,1)S(1)}, bf16[1024,128]{1,0:T(8,128)(2,1)S(1)}, u32[]{:S(2)}, u32[]{:S(2)}) collective-permute-start(bf16[1024,128]{1,0:T(8,128)(2,1)S(1)} %get-tuple-element.11), channel_id=1, source_target_pairs={{0,4},{1,5},{2,6},{3,7},{4,8},{5,9},{6,10},{7,11},{8,12},{9,13},{1... | collective-permute-start | bytes 786440 | tf_op jit(solution)/shard_map/ppermute | solution.py:165
  34.9 2.2 %collective-permute-start.11 = (bf16[1024,128]{1,0:T(8,128)(2,1)S(1)}, bf16[1024,128]{1,0:T(8,128)(2,1)S(1)}, u32[]{:S(2)}, u32[]{:S(2)}) collective-permute-start(bf16[1024,128]{1,0:T(8,128)(2,1)S(1)} %get-tuple-element.10), channel_id=1, source_target_pairs={{0,12},{1,13},{2,14},{3,15},{4,0},{5,1},{6,2},{7,3},{8,4},{9,5},{1... | collective-permute-start | bytes 786440 | tf_op jit(solution)/shard_map/ppermute | solution.py:165
  37.1 1.8 %collective-permute-start.9 = (bf16[1024,128]{1,0:T(8,128)(2,1)S(1)}, bf16[1024,128]{1,0:T(8,128)(2,1)S(1)}, u32[]{:S(2)}, u32[]{:S(2)}) collective-permute-start(bf16[1024,128]{1,0:T(8,128)(2,1)S(1)} %get-tuple-element.9), channel_id=1, source_target_pairs={{0,8},{1,9},{2,10},{3,11},{4,12},{5,13},{6,14},{7,15},{8,0},{9,1},... | collective-permute-start | bytes 786440 | tf_op jit(solution)/shard_map/ppermute | solution.py:165
  38.8 0.0 copy-done.1
  38.8 0.6 %dynamic_slice.42 = s32[1]{0:T(128)} dynamic-slice(s32[8]{0:T(128)S(1)} %copy-done.1, s32[]{:T(128)S(6)} %select_n.127), dynamic_slice_sizes={1} | dynamic-slice | bytes 12 | tf_op jit(solution)/shard_map/dynamic_slice | solution.py:99
  39.4 0.6 %compare_convert_fusion = f32[2]{0:T(128)S(1)} fusion(s32[]{:T(128)} %bitcast.46), kind=kLoop, calls=%fused_computation.69 | loop fusion | flops 4 | bytes 12 | tf_op jit(solution)/shard_map/convert_element_type | solution.py:175
  40.1 1.2 %collective-permute-done.10 = bf16[1024,128]{1,0:T(8,128)(2,1)S(1)} collective-permute-done((bf16[1024,128]{1,0:T(8,128)(2,1)S(1)}, bf16[1024,128]{1,0:T(8,128)(2,1)S(1)}, u32[]{:S(2)}, u32[]{:S(2)}) %collective-permute-start.10) | collective-permute-done | bytes 262176 | tf_op jit(solution)/shard_map/ppermute | solution.py:165
  41.3 2.5 %collective-permute-done.11 = bf16[1024,128]{1,0:T(8,128)(2,1)S(1)} collective-permute-done((bf16[1024,128]{1,0:T(8,128)(2,1)S(1)}, bf16[1024,128]{1,0:T(8,128)(2,1)S(1)}, u32[]{:S(2)}, u32[]{:S(2)}) %collective-permute-start.11) | collective-permute-done | bytes 262176 | tf_op jit(solution)/shard_map/ppermute | solution.py:165
  43.8 1.8 %collective-permute-done.9 = bf16[1024,128]{1,0:T(8,128)(2,1)S(1)} collective-permute-done((bf16[1024,128]{1,0:T(8,128)(2,1)S(1)}, bf16[1024,128]{1,0:T(8,128)(2,1)S(1)}, u32[]{:S(2)}, u32[]{:S(2)}) %collective-permute-start.9) | collective-permute-done | bytes 262176 | tf_op jit(solution)/shard_map/ppermute | solution.py:165
  45.6 0.1 fusion.21
  45.7 0.0 copy-done.2
  45.7 1.1 %fusion.15 = bf16[1,2,8,128,128]{4,3,2,1,0:T(8,128)(2,1)} fusion(bf16[2,32,128,1,1]{2,1,0,4,3:T(8,128)(2,1)S(1)} %copy-done.2, bf16[2,2,32,8,128]{4,3,2,1,0:T(8,128)(2,1)S(1)} %bitcast.125, f32[2]{0:T(128)S(1)} %compare_convert_fusion), kind=kOutput, calls=%fused_computation.14 | convolution fusion | flops 34078720 | bytes 802824 | tf_op jit(solution)/shard_map/kpfrj,pft->krjt/dot_general | solution.py:168
  (14 shorter events, 0.2 us)
Async XLA Ops:
  0.0 10.4 %copy-start = (s32[8,2,2]{0,2,1:T(2,128)S(1)}, s32[8,2,2]{0,2,1:T(2,128)}, u32[]{:S(2)}) copy-start(s32[8,2,2]{0,2,1:T(2,128)} %param.6) | copy-start | bytes 388
  5.2 5.9 %collective-permute-start.2 = (bf16[384,128]{1,0:T(8,128)(2,1)S(1)}, bf16[384,128]{1,0:T(8,128)(2,1)S(1)}, u32[]{:S(2)}, u32[]{:S(2)}) collective-permute-start(bf16[384,128]{1,0:T(8,128)(2,1)S(1)} %bitcast.116), channel_id=1, source_target_pairs={{0,32},{16,48},{32,64},{48,80},{64,96},{80,112},{96,0},{112,16},{1... | collective-permute-start | bytes 294920 | tf_op jit(solution)/shard_map/ppermute | solution.py:88
  6.8 5.3 %collective-permute-start = (bf16[384,128]{1,0:T(8,128)(2,1)S(1)}, bf16[384,128]{1,0:T(8,128)(2,1)S(1)}, u32[]{:S(2)}, u32[]{:S(2)}) collective-permute-start(bf16[384,128]{1,0:T(8,128)(2,1)S(1)} %bitcast.117), channel_id=1, source_target_pairs={{0,96},{16,112},{32,0},{48,16},{64,32},{80,48},{96,64},{112,80},{1... | collective-permute-start | bytes 294920 | tf_op jit(solution)/shard_map/ppermute | solution.py:89
  8.5 6.1 %collective-permute-start.1 = (bf16[384,128]{1,0:T(8,128)(2,1)S(1)}, bf16[384,128]{1,0:T(8,128)(2,1)S(1)}, u32[]{:S(2)}, u32[]{:S(2)}) collective-permute-start(bf16[384,128]{1,0:T(8,128)(2,1)S(1)} %bitcast.118), channel_id=1, source_target_pairs={{0,64},{16,80},{32,96},{48,112},{64,0},{80,16},{96,32},{112,48},{1... | collective-permute-start | bytes 294920 | tf_op jit(solution)/shard_map/ppermute | solution.py:90
  10.4 4.3 %collective-permute-start.3 = (bf16[384,128]{1,0:T(8,128)(2,1)S(1)}, bf16[384,128]{1,0:T(8,128)(2,1)S(1)}, u32[]{:S(2)}, u32[]{:S(2)}) collective-permute-start(bf16[384,128]{1,0:T(8,128)(2,1)S(1)} %bitcast.119), channel_id=1, source_target_pairs={{0,16},{16,0},{32,48},{48,32},{64,80},{80,64},{96,112},{112,96},{1... | collective-permute-start | bytes 294920 | tf_op jit(solution)/shard_map/ppermute | solution.py:87
  12.2 2.5 %collective-permute-start.4 = (bf16[2,384,128]{2,1,0:T(8,128)(2,1)S(1)}, bf16[2,384,128]{2,1,0:T(8,128)(2,1)S(1)}, u32[]{:S(2)}, u32[]{:S(2)}) collective-permute-start(bf16[2,384,128]{2,1,0:T(8,128)(2,1)S(1)} %pad_maximum_fusion.7), channel_id=1, source_target_pairs={{0,16},{16,0},{32,48},{48,32},{64,80},{80,64},{96,112},{112,96},{1... | collective-permute-start | bytes 589832 | tf_op jit(solution)/shard_map/ppermute | solution.py:92
  14.6 1.3 %collective-permute-start.5 = (bf16[384,128]{1,0:T(8,128)(2,1)S(1)}, bf16[384,128]{1,0:T(8,128)(2,1)S(1)}, u32[]{:S(2)}, u32[]{:S(2)}) collective-permute-start(bf16[384,128]{1,0:T(8,128)(2,1)S(1)} %collective-permute-done.1), channel_id=1, source_target_pairs={{0,16},{16,0},{32,48},{48,32},{64,80},{80,64},{96,112},{112,96},{1... | collective-permute-start | bytes 294920 | tf_op jit(solution)/shard_map/ppermute | solution.py:93
  17.3 7.8 %collective-permute-start.6 = (bf16[2,480,128]{2,1,0:T(8,128)(2,1)S(1)}, bf16[2,480,128]{2,1,0:T(8,128)(2,1)S(1)}, u32[]{:S(2)}, u32[]{:S(2)}) collective-permute-start(bf16[2,480,128]{2,1,0:T(8,128)(2,1)S(1)} %get-tuple-element.17), channel_id=1, source_target_pairs={{0,2},{1,3},{2,0},{3,1},{4,6},{5,7},{6,4},{7,5},{8,10},{9,11},{10,... | collective-permute-start | bytes 737288 | tf_op jit(solution)/shard_map/ppermute | solution.py:144
  20.7 7.4 %collective-permute-start.7 = (bf16[2,480,128]{2,1,0:T(8,128)(2,1)S(1)}, bf16[2,480,128]{2,1,0:T(8,128)(2,1)S(1)}, u32[]{:S(2)}, u32[]{:S(2)}) collective-permute-start(bf16[2,480,128]{2,1,0:T(8,128)(2,1)S(1)} %get-tuple-element.18), channel_id=1, source_target_pairs={{0,1},{1,2},{2,3},{3,0},{4,5},{5,6},{6,7},{7,4},{8,9},{9,10},{10,1... | collective-permute-start | bytes 737288 | tf_op jit(solution)/shard_map/ppermute | solution.py:144
  21.3 6.8 %collective-permute-start.8 = (bf16[2,480,128]{2,1,0:T(8,128)(2,1)S(1)}, bf16[2,480,128]{2,1,0:T(8,128)(2,1)S(1)}, u32[]{:S(2)}, u32[]{:S(2)}) collective-permute-start(bf16[2,480,128]{2,1,0:T(8,128)(2,1)S(1)} %get-tuple-element.19), channel_id=1, source_target_pairs={{0,3},{1,0},{2,1},{3,2},{4,7},{5,4},{6,5},{7,6},{8,11},{9,8},{10,9... | collective-permute-start | bytes 737288 | tf_op jit(solution)/shard_map/ppermute | solution.py:144
  32.5 6.3 %copy-start.1 = (s32[8]{0:T(128)S(1)}, s32[8]{0:T(128)}, u32[]{:S(2)}) copy-start(s32[8]{0:T(128)} %param.7) | copy-start | bytes 100
  32.5 13.2 %copy-start.2 = (bf16[2,32,128,1,1]{2,1,0,4,3:T(8,128)(2,1)S(1)}, bf16[2,32,128,1,1]{2,1,0,4,3:T(8,128)(2,1)}, u32[]{:S(2)}) copy-start(bf16[2,32,128,1,1]{2,1,0,4,3:T(8,128)(2,1)} %constant.232) | copy-start | bytes 49156
  32.9 8.5 %collective-permute-start.10 = (bf16[1024,128]{1,0:T(8,128)(2,1)S(1)}, bf16[1024,128]{1,0:T(8,128)(2,1)S(1)}, u32[]{:S(2)}, u32[]{:S(2)}) collective-permute-start(bf16[1024,128]{1,0:T(8,128)(2,1)S(1)} %get-tuple-element.11), channel_id=1, source_target_pairs={{0,4},{1,5},{2,6},{3,7},{4,8},{5,9},{6,10},{7,11},{8,12},{9,13},{1... | collective-permute-start | bytes 786440 | tf_op jit(solution)/shard_map/ppermute | solution.py:165
  34.9 8.9 %collective-permute-start.11 = (bf16[1024,128]{1,0:T(8,128)(2,1)S(1)}, bf16[1024,128]{1,0:T(8,128)(2,1)S(1)}, u32[]{:S(2)}, u32[]{:S(2)}) collective-permute-start(bf16[1024,128]{1,0:T(8,128)(2,1)S(1)} %get-tuple-element.10), channel_id=1, source_target_pairs={{0,12},{1,13},{2,14},{3,15},{4,0},{5,1},{6,2},{7,3},{8,4},{9,5},{1... | collective-permute-start | bytes 786440 | tf_op jit(solution)/shard_map/ppermute | solution.py:165
  37.1 8.5 %collective-permute-start.9 = (bf16[1024,128]{1,0:T(8,128)(2,1)S(1)}, bf16[1024,128]{1,0:T(8,128)(2,1)S(1)}, u32[]{:S(2)}, u32[]{:S(2)}) collective-permute-start(bf16[1024,128]{1,0:T(8,128)(2,1)S(1)} %get-tuple-element.9), channel_id=1, source_target_pairs={{0,8},{1,9},{2,10},{3,11},{4,12},{5,13},{6,14},{7,15},{8,0},{9,1},... | collective-permute-start | bytes 786440 | tf_op jit(solution)/shard_map/ppermute | solution.py:165
